TPU v7x, 32 devices: a whole 2x2x4 slice. The times are simulated.
32 devices in a mesh: gx: 4 (over z), gy: 8 (over y, x, core).
Axes of the slice: x: 2, y: 2, z: 4, core: 2. Of those that a mesh axis runs over, the one named last changes fastest.
Arguments:
- region_state: float32 [9, 32, 24, 64], P(None, ('gx', 'gy')), may hold values from -6 to 6
- region_material: int32 [32, 24, 64], P(('gx', 'gy')), may hold values from 0 to 7
- fine_state: float32 [9, 96, 72, 128], P(None, 'gx', 'gy'), may hold values from -6 to 6
- fine_material: int32 [96, 72, 128], P('gx', 'gy'), may hold values from 0 to 7
- material_table: float32 [3, 8], replicated, may hold values from 0.6 to 1.4
Outputs:
- region_next: float32 [9, 32, 24, 64], P(None, ('gx', 'gy'))
- fine_next: float32 [9, 96, 72, 128], P(None, 'gx', 'gy')
All inputs are finite; a program needn't handle non-finite values.
Results may differ from a plain program's by a relative error of at most 0.0012.
Values may be sent and summed in bfloat16 or wider, within the bound.
No kernel may reach another device: no remote copies, remote signals or barrier semaphores. Data moves between devices by JAX's collectives and lax.ppermute only.
A program may use at most 64 MiB of HBM per device.

v0:
```python
import jax
import jax.numpy as jnp
from jax import lax
from jax.sharding import PartitionSpec as P


def padded_2(array, sides, width):
    for axis, dim in sides:
        size, length = (lax.axis_size(axis), array.shape[dim])
        up = [(i, (i + 1) % size) for i in range(size - 1)]
        down = [(j, i) for i, j in up]
        last = lax.slice_in_dim(array, length - width, length, axis=dim)
        initial = lax.slice_in_dim(array, 0, width, axis=dim)
        before = lax.ppermute(last, axis, up)
        after = lax.ppermute(initial, axis, down)
        array = jnp.concatenate([before, array, after], axis=dim)
    return array


def lookup(index, table):
    rho = jnp.zeros(index.shape, jnp.float32)
    lam = jnp.zeros(index.shape, jnp.float32)
    shear = jnp.zeros(index.shape, jnp.float32)
    for material in range(table.shape[1]):
        match = index == material
        rho = jnp.where(match, table[0, material], rho)
        lam = jnp.where(match, table[1, material], lam)
        shear = jnp.where(match, table[2, material], shear)
    return (rho, lam, shear)


def centered(padded, spacing):
    scale = 0.5 / spacing
    d_x = (padded[:, 2:, 1:-1, 1:-1] - padded[:, :-2, 1:-1, 1:-1]) * scale
    d_y = (padded[:, 1:-1, 2:, 1:-1] - padded[:, 1:-1, :-2, 1:-1]) * scale
    d_z = (padded[:, 1:-1, 1:-1, 2:] - padded[:, 1:-1, 1:-1, :-2]) * scale
    return (d_x, d_y, d_z)


def fine_stress(field):
    ext = padded_2(field, (("gx", 1), ("gy", 2)), 1)
    return jnp.pad(ext, ((0, 0), (0, 0), (0, 0), (1, 1)))


def fine_velocity(field):
    ext = padded_2(field, (("gx", 1), ("gy", 2)), 1)
    return jnp.pad(ext, ((0, 0), (0, 0), (0, 0), (1, 1)))


def region_stress(field):
    ext = padded_2(field.astype(jnp.bfloat16), ((("gx", "gy"), 1),), 1).astype(field.dtype)
    return jnp.pad(ext, ((0, 0), (0, 0), (1, 1), (1, 1)))


def region_velocity(field):
    ext = padded_2(field, ((("gx", "gy"), 1),), 1)
    return jnp.pad(ext, ((0, 0), (0, 0), (1, 1), (1, 1)))


def elastic_step(state, props, step, spacing, extend_stress, extend_velocity):
    rho, lam, shear = props
    velocity = state[:3]
    stress = state[3:]
    d_x, d_y, d_z = centered(extend_stress(stress), spacing)
    acc_x = d_x[0] + d_y[3] + d_z[4]
    acc_y = d_x[3] + d_y[1] + d_z[5]
    acc_z = d_x[4] + d_y[5] + d_z[2]
    velocity = velocity + (step / rho)[None] * jnp.stack([acc_x, acc_y, acc_z])
    g_x, g_y, g_z = centered(extend_velocity(velocity), spacing)
    spread = g_x[0] + g_y[1] + g_z[2]
    new_xx = stress[0] + step * (lam * spread + 2.0 * shear * g_x[0])
    new_yy = stress[1] + step * (lam * spread + 2.0 * shear * g_y[1])
    new_zz = stress[2] + step * (lam * spread + 2.0 * shear * g_z[2])
    new_xy = stress[3] + step * shear * (g_y[0] + g_x[1])
    new_xz = stress[4] + step * shear * (g_z[0] + g_x[2])
    new_yz = stress[5] + step * shear * (g_z[1] + g_y[2])
    return jnp.concatenate(
        [velocity, jnp.stack([new_xx, new_yy, new_zz, new_xy, new_xz, new_yz])], 0
    )


def interp_matrix(n_fine, n_coarse):
    fine_pos = jnp.arange(n_fine, dtype=jnp.int32)
    whole = fine_pos // 3
    rest = fine_pos - 3 * whole
    lower = jnp.where(rest == 0, whole - 1, whole)
    frac = jnp.where(rest == 0, 2.0 / 3.0, jnp.where(rest == 1, 0.0, 1.0 / 3.0)).astype(jnp.float32)
    below = lower < 0
    lower = jnp.where(below, 0, lower)
    frac = jnp.where(below, 0.0, frac)
    above = lower >= n_coarse - 1
    lower = jnp.where(above, n_coarse - 2, lower)
    frac = jnp.where(above, 1.0, frac)
    cols = jnp.arange(n_coarse, dtype=jnp.int32)
    low_hit = (cols[None, :] == lower[:, None]).astype(jnp.float32)
    high_hit = (cols[None, :] == lower[:, None] + 1).astype(jnp.float32)
    return (1.0 - frac)[:, None] * low_hit + frac[:, None] * high_hit


def ramp(first, count, total, tile):
    place = first + jnp.arange(count, dtype=jnp.int32)
    margin = jnp.minimum(place, total - 1 - place).astype(jnp.float32) + 0.5
    part = jnp.maximum(1.0 - margin / tile, 0.0)
    return part * part


def local(region_state, region_material, fine_state, fine_material, material_table):
    count_x = lax.axis_size("gx")
    count_y = lax.axis_size("gy")
    fine_x = fine_state.shape[1]
    fine_y = fine_state.shape[2]
    fine_z = fine_state.shape[3]
    reg_y = region_state.shape[2]
    rows_each = reg_y // count_y
    region_props = lookup(region_material, material_table)
    region_next = elastic_step(region_state, region_props, 0.6, 3.0, region_stress, region_velocity)
    both = jnp.concatenate([region_state, region_next], 0).astype(jnp.bfloat16)
    row_start = lax.axis_index("gy") * rows_each
    band = lax.dynamic_slice_in_dim(
        lax.all_gather(both, "gy", axis=1, tiled=True), row_start, rows_each, 2
    ).astype(jnp.float32)
    columns = band.shape[1]
    high = lax.Precision.HIGHEST
    first = jnp.einsum("fa,cabz->cfbz", interp_matrix(fine_x, columns), band, precision=high)
    second = jnp.einsum("gb,cfbz->cfgz", interp_matrix(fine_y, rows_each), first, precision=high)
    background = jnp.einsum(
        "kz,cfgz->cfgk", interp_matrix(fine_z, band.shape[3]), second, precision=high
    )
    along_x = ramp(lax.axis_index("gx") * fine_x, fine_x, count_x * fine_x, fine_x)
    along_y = ramp(lax.axis_index("gy") * fine_y, fine_y, count_y * fine_y, fine_y)
    relax = (0.1 + 0.4 * jnp.maximum(along_x[:, None], along_y[None, :]))[:, :, None]
    fine_props = lookup(fine_material, material_table)
    state = fine_state
    for sub in range(1, 4):
        state = elastic_step(state, fine_props, 0.2, 1.0, fine_stress, fine_velocity)
        share = sub / 3.0
        target = background[:9] + share * (background[9:] - background[:9])
        state = state + relax[None] * (target - state)
    return (region_next, state)


def solution(mesh):
    return jax.shard_map(
        local,
        mesh=mesh,
        in_specs=(
            P(None, ("gx", "gy"), None, None),
            P(("gx", "gy"), None, None),
            P(None, "gx", "gy", None),
            P("gx", "gy", None),
            P(),
        ),
        out_specs=(P(None, ("gx", "gy"), None, None), P(None, "gx", "gy", None)),
        check_vma=False,
    )
```

profile of v0, /device:TPU:27, one launch (start us, length us, event | category | flops | bytes accessed | tf_op | source)
XLA Modules:
  0.0 174.1 jit_solution(11138570664467528104)
XLA Ops:
  0.6 1.0 constant_dynamic-update-slice_fusion.15
  1.6 2.6 %collective-permute-start.1 = (bf16[6,1,24,64]{3,2,1,0:T(8,128)(2,1)S(1)}, bf16[6,1,24,64]{3,2,1,0:T(8,128)(2,1)S(1)}, u32[]{:S(2)}, u32[]{:S(2)}) collective-permute-start(bf16[6,1,24,64]{3,2,1,0:T(8,128)(2,1)S(1)} %slice.940), channel_id=1, source_target_pairs={{1,0},{2,1},{3,2},{4,3},{5,4},{6,5},{7,6},{8,7},{9,8},{10,9},{11,1... | collective-permute-start | bytes 55304 | tf_op jit(solution)/shard_map/ppermute | solution.py:15
  4.2 3.9 %collective-permute-start = (bf16[6,1,24,64]{3,2,1,0:T(8,128)(2,1)S(1)}, bf16[6,1,24,64]{3,2,1,0:T(8,128)(2,1)S(1)}, u32[]{:S(2)}, u32[]{:S(2)}) collective-permute-start(bf16[6,1,24,64]{3,2,1,0:T(8,128)(2,1)S(1)} %slice.940), channel_id=1, source_target_pairs={{0,1},{1,2},{2,3},{3,4},{4,5},{5,6},{6,7},{7,8},{8,9},{9,10},{10,1... | collective-permute-start | bytes 55304 | tf_op jit(solution)/shard_map/ppermute | solution.py:14
  8.1 1.1 fusion.174
  9.2 1.3 collective-permute-start.5
  10.5 4.0 %collective-permute-start.4 = (f32[6,1,9,128]{3,1,2,0:T(1,128)S(1)}, f32[6,1,9,128]{3,1,2,0:T(1,128)S(1)}, u32[]{:S(2)}, u32[]{:S(2)}) collective-permute-start(f32[6,1,9,128]{3,1,2,0:T(1,128)S(1)} %get-tuple-element.66), channel_id=1, source_target_pairs={{8,0},{16,8},{24,16},{9,1},{17,9},{25,17},{10,2},{18,10},{26,18},{... | collective-permute-start | bytes 82952 | tf_op jit(solution)/shard_map/ppermute | solution.py:15
  14.5 2.1 %fusion.178 = (f32[1,1]{1,0:T(1,128)}, f32[1,1]{1,0:T(1,128)}, f32[1,1]{1,0:T(1,128)}, f32[1,1]{1,0:T(1,128)}, f32[1,1]{1,0:T(1,128)}, /*index=5*/f32[1,1]{1,0:T...) fusion(f32[3,8]{1,0:T(4,128)} %param.9), kind=kLoop, calls=%fused_computation.466 | loop fusion | bytes 152 | tf_op jit(solution)/shard_map/slice | solution.py:27
  16.6 1.5 fusion.179
  18.2 5.5 %divide_bitcast_fusion = (f32[24,64]{1,0:T(8,128)S(1)}, pred[1,24,64]{2,1,0:T(8,128)(4,1)S(1)}, pred[1,24,64]{2,1,0:T(8,128)(4,1)S(1)}, pred[1,24,64]{2,1,0:T(8,...) fusion(f32[]{:T(128)} %bitcast.7, f32[]{:T(128)} %bitcast.6, ...), kind=kLoop, calls=%fused_computation.376 | loop fusion | flops 26112 | bytes 24608 | tf_op jit(solution)/shard_map/mul | solution.py:68
  23.8 5.9 %select_divide_fusion = (f32[24,9,128]{2,0,1:T(8,128)S(1)}, pred[24,9,128]{2,0,1:T(8,128)(4,1)S(1)}, pred[24,9,128]{2,0,1:T(8,128)(4,1)S(1)}, pred[24,9,128]{2,0...) fusion(f32[]{:T(128)} %bitcast.7, f32[]{:T(128)} %bitcast.6, ...), kind=kLoop, calls=%fused_computation.267 | loop fusion | flops 470016 | bytes 442400 | tf_op jit(solution)/shard_map/div | solution.py:68
  29.7 1.1 slice.801
  31.1 1.9 %collective-permute-start.2 = (f32[3,1,24,64]{3,2,1,0:T(8,128)S(1)}, f32[3,1,24,64]{3,2,1,0:T(8,128)S(1)}, u32[]{:S(2)}, u32[]{:S(2)}) collective-permute-start(f32[3,1,24,64]{3,2,1,0:T(8,128)S(1)} %get-tuple-element.25), channel_id=1, source_target_pairs={{1,0},{2,1},{3,2},{4,3},{5,4},{6,5},{7,6},{8,7},{9,8},{10,9},{11,1... | collective-permute-start | bytes 55304 | tf_op jit(solution)/shard_map/ppermute | solution.py:15
  33.0 4.5 %collective-permute-start.3 = (f32[3,1,24,64]{3,2,1,0:T(8,128)S(1)}, f32[3,1,24,64]{3,2,1,0:T(8,128)S(1)}, u32[]{:S(2)}, u32[]{:S(2)}) collective-permute-start(f32[3,1,24,64]{3,2,1,0:T(8,128)S(1)} %get-tuple-element.25), channel_id=1, source_target_pairs={{0,1},{1,2},{2,3},{3,4},{4,5},{5,6},{6,7},{7,8},{8,9},{9,10},{10,1... | collective-permute-start | bytes 55304 | tf_op jit(solution)/shard_map/ppermute | solution.py:14
  37.7 1.9 %collective-permute-start.7 = (f32[6,26,1,128]{3,1,2,0:T(8,128)S(1)}, f32[6,26,1,128]{3,1,2,0:T(8,128)S(1)}, u32[]{:S(2)}, u32[]{:S(2)}) collective-permute-start(f32[6,26,1,128]{3,1,2,0:T(8,128)S(1)} %get-tuple-element.77), channel_id=1, source_target_pairs={{0,1},{1,2},{2,3},{3,4},{4,5},{5,6},{6,7},{8,9},{9,10},{10,11},{11... | collective-permute-start | bytes 239624 | tf_op jit(solution)/shard_map/ppermute | solution.py:14
  39.6 2.4 %collective-permute-start.6 = (f32[6,26,1,128]{3,1,2,0:T(8,128)S(1)}, f32[6,26,1,128]{3,1,2,0:T(8,128)S(1)}, u32[]{:S(2)}, u32[]{:S(2)}) collective-permute-start(f32[6,26,1,128]{3,1,2,0:T(8,128)S(1)} %get-tuple-element.78), channel_id=1, source_target_pairs={{1,0},{2,1},{3,2},{4,3},{5,4},{6,5},{7,6},{9,8},{10,9},{11,10},{12... | collective-permute-start | bytes 239624 | tf_op jit(solution)/shard_map/ppermute | solution.py:15
  42.2 10.1 %constant_dynamic-update-slice_fusion.13 = (bf16[18,1,24,64]{3,2,1,0:T(8,128)(2,1)S(1)}, f32[1,24,64]{2,1,0:T(8,128)S(1)}, f32[1,24,64]{2,1,0:T(8,128)S(1)}, f32[1,24,64]{2,1,0:T(8,128)S(1)}) fusion(bf16[18,1,24,64]{3,2,1,0:T(8,128)(2,1)S(1)} %get-tuple-element.24, f32[3,1,24,64]{3,2,1,0:T(8,128)S(1)} %get-tuple-element.129, ...), kind=kLoop, calls=%fused_computation.290 | loop fusion | flops 38400 | bytes 116800
  52.5 11.5 %all_gather.3 = bf16[18,8,24,64]{3,2,1,0:T(8,128)(2,1)S(1)} all-gather(bf16[18,1,24,64]{3,2,1,0:T(8,128)(2,1)S(1)} %get-tuple-element.10), channel_id=1, replica_groups=mesh['gx'=4,'gy'=8] {'gy'}, dimensions={1}, use_global_device_ids=true | all-gather | bytes 497664 | tf_op jit(solution)/shard_map/all_gather | solution.py:120
  64.1 0.5 convolution_bitcast_fusion
  64.6 0.9 select_maximum_fusion.8
  65.5 0.5 fusion.21
  66.0 0.6 copy-done
  66.8 4.4 %collective-permute-start.8 = (f32[3,1,9,128]{3,1,2,0:T(1,128)S(1)}, f32[3,1,9,128]{3,1,2,0:T(1,128)S(1)}, u32[]{:S(2)}, u32[]{:S(2)}) collective-permute-start(f32[3,1,9,128]{3,1,2,0:T(1,128)S(1)} %get-tuple-element.95), channel_id=1, source_target_pairs={{8,0},{16,8},{24,16},{9,1},{17,9},{25,17},{10,2},{18,10},{26,18},{... | collective-permute-start | bytes 41480 | tf_op jit(solution)/shard_map/ppermute | solution.py:15
  71.1 1.3 collective-permute-start.9
  72.4 3.0 %fusion.5 = f32[18,24,64,9]{2,3,1,0:T(8,128)S(1)} fusion(f32[18,24,3,64]{3,1,2,0:T(8,128)S(1)} %convolution_bitcast_fusion, f32[9]{0:T(128)S(1)} %get-tuple-element.135, s32[9]{0:T(128)S(1)} %get-tuple-element.138, f32[9]{0:T(128)S(1)} %get-tuple-element.136, s32[9]{0:T(128)S(1)} %get-tuple-element.137), kind=kOutput, calls=%fused_computation.38 | convolution fusion | flops 8958087 | bytes 1327248 | tf_op jit(solution)/shard_map/gb,cfbz->cfgz/dot_general | solution.py:125
  75.6 4.6 %collective-permute-start.11 = (f32[3,26,1,128]{3,1,2,0:T(8,128)S(1)}, f32[3,26,1,128]{3,1,2,0:T(8,128)S(1)}, u32[]{:S(2)}, u32[]{:S(2)}) collective-permute-start(f32[3,26,1,128]{3,1,2,0:T(8,128)S(1)} %get-tuple-element.89), channel_id=1, source_target_pairs={{0,1},{1,2},{2,3},{3,4},{4,5},{5,6},{6,7},{8,9},{9,10},{10,11},{11... | collective-permute-start | bytes 119816 | tf_op jit(solution)/shard_map/ppermute | solution.py:14
  80.2 1.9 %collective-permute-start.10 = (f32[3,26,1,128]{3,1,2,0:T(8,128)S(1)}, f32[3,26,1,128]{3,1,2,0:T(8,128)S(1)}, u32[]{:S(2)}, u32[]{:S(2)}) collective-permute-start(f32[3,26,1,128]{3,1,2,0:T(8,128)S(1)} %get-tuple-element.90), channel_id=1, source_target_pairs={{1,0},{2,1},{3,2},{4,3},{5,4},{6,5},{7,6},{9,8},{10,9},{11,10},{12... | collective-permute-start | bytes 119816 | tf_op jit(solution)/shard_map/ppermute | solution.py:15
  82.1 2.2 %fusion.1 = f32[18,24,9,128]{3,1,2,0:T(8,128)S(1)} fusion(f32[18,24,64,9]{2,3,1,0:T(8,128)S(1)} %fusion.5, f32[128]{0:T(128)S(1)} %get-tuple-element.139, s32[128]{0:T(128)S(1)} %get-tuple-element.142, f32[128]{0:T(128)S(1)} %get-tuple-element.140, s32[128]{0:T(128)S(1)} %get-tuple-element.141), kind=kOutput, calls=%fused_computation.15 | convolution fusion | flops 382246912 | bytes 2988032 | tf_op jit(solution)/shard_map/kz,cfgz->cfgk/dot_general | solution.py:126
  84.4 2.1 %collective-permute-done.10 = f32[3,26,1,128]{3,1,2,0:T(8,128)S(1)} collective-permute-done((f32[3,26,1,128]{3,1,2,0:T(8,128)S(1)}, f32[3,26,1,128]{3,1,2,0:T(8,128)S(1)}, u32[]{:S(2)}, u32[]{:S(2)}) %collective-permute-start.10) | collective-permute-done | bytes 39968 | tf_op jit(solution)/shard_map/ppermute | solution.py:15
  86.5 0.5 select_maximum_fusion.20
  87.3 10.2 %bitcast_dynamic-update-slice_fusion.2 = (f32[9,24,9,128]{3,1,2,0:T(8,128)S(1)}, f32[24,9,128]{2,0,1:T(8,128)S(1)}, f32[24,9,128]{2,0,1:T(8,128)S(1)}, f32[24,9,128]{2,0,1:T(8,128)S(1)}) fusion(f32[9,24,9,128]{3,1,2,0:T(8,128)S(1)} %get-tuple-element.32, f32[9,24,9,128]{3,1,2,0:T(8,128)S(1)} %copy-done, f32[3,24,9,128]{3,1,2,0:T(8,128)S(1)} %get-tuple-element.88, ...), kind=kLoop, calls=%fused_computation.259 | loop fusion | flops 663552 | bytes 1105984
  97.7 0.3 multiply_add_fusion.2
  98.1 3.0 %collective-permute-start.12 = (f32[6,1,9,128]{3,1,2,0:T(1,128)S(1)}, f32[6,1,9,128]{3,1,2,0:T(1,128)S(1)}, u32[]{:S(2)}, u32[]{:S(2)}) collective-permute-start(f32[6,1,9,128]{3,1,2,0:T(1,128)S(1)} %get-tuple-element.64), channel_id=1, source_target_pairs={{8,0},{16,8},{24,16},{9,1},{17,9},{25,17},{10,2},{18,10},{26,18},{... | collective-permute-start | bytes 82952 | tf_op jit(solution)/shard_map/ppermute | solution.py:15
  101.0 1.3 collective-permute-start.13
  102.4 3.2 %collective-permute-done.13 = f32[6,1,9,128]{3,1,2,0:T(1,128)S(1)} collective-permute-done((f32[6,1,9,128]{3,1,2,0:T(1,128)S(1)}, f32[6,1,9,128]{3,1,2,0:T(1,128)S(1)}, u32[]{:S(2)}, u32[]{:S(2)}) %collective-permute-start.13) | collective-permute-done | bytes 27680 | tf_op jit(solution)/shard_map/ppermute | solution.py:14
  105.7 1.9 %collective-permute-start.14 = (f32[6,26,1,128]{3,1,2,0:T(8,128)S(1)}, f32[6,26,1,128]{3,1,2,0:T(8,128)S(1)}, u32[]{:S(2)}, u32[]{:S(2)}) collective-permute-start(f32[6,26,1,128]{3,1,2,0:T(8,128)S(1)} %get-tuple-element.74), channel_id=1, source_target_pairs={{1,0},{2,1},{3,2},{4,3},{5,4},{6,5},{7,6},{9,8},{10,9},{11,10},{12... | collective-permute-start | bytes 239624 | tf_op jit(solution)/shard_map/ppermute | solution.py:15
  107.6 4.7 %collective-permute-start.15 = (f32[6,26,1,128]{3,1,2,0:T(8,128)S(1)}, f32[6,26,1,128]{3,1,2,0:T(8,128)S(1)}, u32[]{:S(2)}, u32[]{:S(2)}) collective-permute-start(f32[6,26,1,128]{3,1,2,0:T(8,128)S(1)} %get-tuple-element.73), channel_id=1, source_target_pairs={{0,1},{1,2},{2,3},{3,4},{4,5},{5,6},{6,7},{8,9},{9,10},{10,11},{11... | collective-permute-start | bytes 239624 | tf_op jit(solution)/shard_map/ppermute | solution.py:14
  112.5 1.2 collective-permute-done.15
  113.8 0.9 select_maximum_fusion.4
  114.9 0.3 fusion.16
  115.3 2.1 %collective-permute-start.16 = (f32[3,1,9,128]{3,1,2,0:T(1,128)S(1)}, f32[3,1,9,128]{3,1,2,0:T(1,128)S(1)}, u32[]{:S(2)}, u32[]{:S(2)}) collective-permute-start(f32[3,1,9,128]{3,1,2,0:T(1,128)S(1)} %get-tuple-element.93), channel_id=1, source_target_pairs={{8,0},{16,8},{24,16},{9,1},{17,9},{25,17},{10,2},{18,10},{26,18},{... | collective-permute-start | bytes 41480 | tf_op jit(solution)/shard_map/ppermute | solution.py:15
  117.4 1.3 collective-permute-start.17
  118.7 3.1 %collective-permute-done.17 = f32[3,1,9,128]{3,1,2,0:T(1,128)S(1)} collective-permute-done((f32[3,1,9,128]{3,1,2,0:T(1,128)S(1)}, f32[3,1,9,128]{3,1,2,0:T(1,128)S(1)}, u32[]{:S(2)}, u32[]{:S(2)}) %collective-permute-start.17) | collective-permute-done | bytes 13856 | tf_op jit(solution)/shard_map/ppermute | solution.py:14
  121.9 6.6 %collective-permute-start.19 = (f32[3,26,1,128]{3,1,2,0:T(8,128)S(1)}, f32[3,26,1,128]{3,1,2,0:T(8,128)S(1)}, u32[]{:S(2)}, u32[]{:S(2)}) collective-permute-start(f32[3,26,1,128]{3,1,2,0:T(8,128)S(1)} %get-tuple-element.85), channel_id=1, source_target_pairs={{0,1},{1,2},{2,3},{3,4},{4,5},{5,6},{6,7},{8,9},{9,10},{10,11},{11... | collective-permute-start | bytes 119816 | tf_op jit(solution)/shard_map/ppermute | solution.py:14
  128.5 1.9 %collective-permute-start.18 = (f32[3,26,1,128]{3,1,2,0:T(8,128)S(1)}, f32[3,26,1,128]{3,1,2,0:T(8,128)S(1)}, u32[]{:S(2)}, u32[]{:S(2)}) collective-permute-start(f32[3,26,1,128]{3,1,2,0:T(8,128)S(1)} %get-tuple-element.86), channel_id=1, source_target_pairs={{1,0},{2,1},{3,2},{4,3},{5,4},{6,5},{7,6},{9,8},{10,9},{11,10},{12... | collective-permute-start | bytes 119816 | tf_op jit(solution)/shard_map/ppermute | solution.py:15
  130.5 4.4 %collective-permute-done.18 = f32[3,26,1,128]{3,1,2,0:T(8,128)S(1)} collective-permute-done((f32[3,26,1,128]{3,1,2,0:T(8,128)S(1)}, f32[3,26,1,128]{3,1,2,0:T(8,128)S(1)}, u32[]{:S(2)}, u32[]{:S(2)}) %collective-permute-start.18) | collective-permute-done | bytes 39968 | tf_op jit(solution)/shard_map/ppermute | solution.py:15
  134.8 0.5 select_maximum_fusion.16
  135.9 0.3 multiply_add_fusion.1
  136.2 1.9 %collective-permute-start.20 = (f32[6,1,9,128]{3,1,2,0:T(1,128)S(1)}, f32[6,1,9,128]{3,1,2,0:T(1,128)S(1)}, u32[]{:S(2)}, u32[]{:S(2)}) collective-permute-start(f32[6,1,9,128]{3,1,2,0:T(1,128)S(1)} %get-tuple-element.62), channel_id=1, source_target_pairs={{8,0},{16,8},{24,16},{9,1},{17,9},{25,17},{10,2},{18,10},{26,18},{... | collective-permute-start | bytes 82952 | tf_op jit(solution)/shard_map/ppermute | solution.py:15
  138.2 1.3 collective-permute-start.21
  139.5 3.2 %collective-permute-done.21 = f32[6,1,9,128]{3,1,2,0:T(1,128)S(1)} collective-permute-done((f32[6,1,9,128]{3,1,2,0:T(1,128)S(1)}, f32[6,1,9,128]{3,1,2,0:T(1,128)S(1)}, u32[]{:S(2)}, u32[]{:S(2)}) %collective-permute-start.21) | collective-permute-done | bytes 27680 | tf_op jit(solution)/shard_map/ppermute | solution.py:14
  142.8 1.9 %collective-permute-start.22 = (f32[6,26,1,128]{3,1,2,0:T(8,128)S(1)}, f32[6,26,1,128]{3,1,2,0:T(8,128)S(1)}, u32[]{:S(2)}, u32[]{:S(2)}) collective-permute-start(f32[6,26,1,128]{3,1,2,0:T(8,128)S(1)} %get-tuple-element.70), channel_id=1, source_target_pairs={{1,0},{2,1},{3,2},{4,3},{5,4},{6,5},{7,6},{9,8},{10,9},{11,10},{12... | collective-permute-start | bytes 239624 | tf_op jit(solution)/shard_map/ppermute | solution.py:15
  144.7 4.5 %collective-permute-start.23 = (f32[6,26,1,128]{3,1,2,0:T(8,128)S(1)}, f32[6,26,1,128]{3,1,2,0:T(8,128)S(1)}, u32[]{:S(2)}, u32[]{:S(2)}) collective-permute-start(f32[6,26,1,128]{3,1,2,0:T(8,128)S(1)} %get-tuple-element.69), channel_id=1, source_target_pairs={{0,1},{1,2},{2,3},{3,4},{4,5},{5,6},{6,7},{8,9},{9,10},{10,11},{11... | collective-permute-start | bytes 239624 | tf_op jit(solution)/shard_map/ppermute | solution.py:14
  149.3 1.0 collective-permute-done.22
  150.3 0.7 collective-permute-done.23
  150.9 0.9 select_maximum_fusion
  152.0 0.3 fusion.11
  152.5 1.9 %collective-permute-start.24 = (f32[3,1,9,128]{3,1,2,0:T(1,128)S(1)}, f32[3,1,9,128]{3,1,2,0:T(1,128)S(1)}, u32[]{:S(2)}, u32[]{:S(2)}) collective-permute-start(f32[3,1,9,128]{3,1,2,0:T(1,128)S(1)} %get-tuple-element.91), channel_id=1, source_target_pairs={{8,0},{16,8},{24,16},{9,1},{17,9},{25,17},{10,2},{18,10},{26,18},{... | collective-permute-start | bytes 41480 | tf_op jit(solution)/shard_map/ppermute | solution.py:15
  154.4 1.3 collective-permute-start.25
  155.7 3.1 %collective-permute-done.25 = f32[3,1,9,128]{3,1,2,0:T(1,128)S(1)} collective-permute-done((f32[3,1,9,128]{3,1,2,0:T(1,128)S(1)}, f32[3,1,9,128]{3,1,2,0:T(1,128)S(1)}, u32[]{:S(2)}, u32[]{:S(2)}) %collective-permute-start.25) | collective-permute-done | bytes 13856 | tf_op jit(solution)/shard_map/ppermute | solution.py:14
  158.9 6.6 %collective-permute-start.27 = (f32[3,26,1,128]{3,1,2,0:T(8,128)S(1)}, f32[3,26,1,128]{3,1,2,0:T(8,128)S(1)}, u32[]{:S(2)}, u32[]{:S(2)}) collective-permute-start(f32[3,26,1,128]{3,1,2,0:T(8,128)S(1)} %get-tuple-element.81), channel_id=1, source_target_pairs={{0,1},{1,2},{2,3},{3,4},{4,5},{5,6},{6,7},{8,9},{9,10},{10,11},{11... | collective-permute-start | bytes 119816 | tf_op jit(solution)/shard_map/ppermute | solution.py:14
  165.5 1.9 %collective-permute-start.26 = (f32[3,26,1,128]{3,1,2,0:T(8,128)S(1)}, f32[3,26,1,128]{3,1,2,0:T(8,128)S(1)}, u32[]{:S(2)}, u32[]{:S(2)}) collective-permute-start(f32[3,26,1,128]{3,1,2,0:T(8,128)S(1)} %get-tuple-element.82), channel_id=1, source_target_pairs={{1,0},{2,1},{3,2},{4,3},{5,4},{6,5},{7,6},{9,8},{10,9},{11,10},{12... | collective-permute-start | bytes 119816 | tf_op jit(solution)/shard_map/ppermute | solution.py:15
  167.5 4.3 %collective-permute-done.26 = f32[3,26,1,128]{3,1,2,0:T(8,128)S(1)} collective-permute-done((f32[3,26,1,128]{3,1,2,0:T(8,128)S(1)}, f32[3,26,1,128]{3,1,2,0:T(8,128)S(1)}, u32[]{:S(2)}, u32[]{:S(2)}) %collective-permute-start.26) | collective-permute-done | bytes 39968 | tf_op jit(solution)/shard_map/ppermute | solution.py:15
  171.8 0.5 select_maximum_fusion.12
  172.9 1.2 multiply_add_fusion
  (96 shorter events, 4.1 us)
Async XLA Ops:
  0.6 30.5 %copy-start.1 = (f32[9,1,24,64]{3,2,1,0:T(8,128)S(1)}, f32[9,1,24,64]{3,2,1,0:T(8,128)}, u32[]{:S(2)}) copy-start(f32[9,1,24,64]{3,2,1,0:T(8,128)} %param.5) | copy-start | bytes 165892
  1.6 29.3 %collective-permute-start.1 = (bf16[6,1,24,64]{3,2,1,0:T(8,128)(2,1)S(1)}, bf16[6,1,24,64]{3,2,1,0:T(8,128)(2,1)S(1)}, u32[]{:S(2)}, u32[]{:S(2)}) collective-permute-start(bf16[6,1,24,64]{3,2,1,0:T(8,128)(2,1)S(1)} %slice.940), channel_id=1, source_target_pairs={{1,0},{2,1},{3,2},{4,3},{5,4},{6,5},{7,6},{8,7},{9,8},{10,9},{11,1... | collective-permute-start | bytes 55304 | tf_op jit(solution)/shard_map/ppermute | solution.py:15
  4.2 26.7 %collective-permute-start = (bf16[6,1,24,64]{3,2,1,0:T(8,128)(2,1)S(1)}, bf16[6,1,24,64]{3,2,1,0:T(8,128)(2,1)S(1)}, u32[]{:S(2)}, u32[]{:S(2)}) collective-permute-start(bf16[6,1,24,64]{3,2,1,0:T(8,128)(2,1)S(1)} %slice.940), channel_id=1, source_target_pairs={{0,1},{1,2},{2,3},{3,4},{4,5},{5,6},{6,7},{7,8},{8,9},{9,10},{10,1... | collective-permute-start | bytes 55304 | tf_op jit(solution)/shard_map/ppermute | solution.py:14
  9.2 28.4 %collective-permute-start.5 = (f32[6,1,9,128]{3,1,2,0:T(1,128)S(1)}, f32[6,1,9,128]{3,1,2,0:T(1,128)S(1)}, u32[]{:S(2)}, u32[]{:S(2)}) collective-permute-start(f32[6,1,9,128]{3,1,2,0:T(1,128)S(1)} %get-tuple-element.65), channel_id=1, source_target_pairs={{0,8},{8,16},{16,24},{1,9},{9,17},{17,25},{2,10},{10,18},{18,26},{... | collective-permute-start | bytes 82952 | tf_op jit(solution)/shard_map/ppermute | solution.py:14
  10.5 27.1 %collective-permute-start.4 = (f32[6,1,9,128]{3,1,2,0:T(1,128)S(1)}, f32[6,1,9,128]{3,1,2,0:T(1,128)S(1)}, u32[]{:S(2)}, u32[]{:S(2)}) collective-permute-start(f32[6,1,9,128]{3,1,2,0:T(1,128)S(1)} %get-tuple-element.66), channel_id=1, source_target_pairs={{8,0},{16,8},{24,16},{9,1},{17,9},{25,17},{10,2},{18,10},{26,18},{... | collective-permute-start | bytes 82952 | tf_op jit(solution)/shard_map/ppermute | solution.py:15
  31.1 10.9 %collective-permute-start.2 = (f32[3,1,24,64]{3,2,1,0:T(8,128)S(1)}, f32[3,1,24,64]{3,2,1,0:T(8,128)S(1)}, u32[]{:S(2)}, u32[]{:S(2)}) collective-permute-start(f32[3,1,24,64]{3,2,1,0:T(8,128)S(1)} %get-tuple-element.25), channel_id=1, source_target_pairs={{1,0},{2,1},{3,2},{4,3},{5,4},{6,5},{7,6},{8,7},{9,8},{10,9},{11,1... | collective-permute-start | bytes 55304 | tf_op jit(solution)/shard_map/ppermute | solution.py:15
  33.0 9.0 %collective-permute-start.3 = (f32[3,1,24,64]{3,2,1,0:T(8,128)S(1)}, f32[3,1,24,64]{3,2,1,0:T(8,128)S(1)}, u32[]{:S(2)}, u32[]{:S(2)}) collective-permute-start(f32[3,1,24,64]{3,2,1,0:T(8,128)S(1)} %get-tuple-element.25), channel_id=1, source_target_pairs={{0,1},{1,2},{2,3},{3,4},{4,5},{5,6},{6,7},{7,8},{8,9},{9,10},{10,1... | collective-permute-start | bytes 55304 | tf_op jit(solution)/shard_map/ppermute | solution.py:14
  37.7 26.9 %collective-permute-start.7 = (f32[6,26,1,128]{3,1,2,0:T(8,128)S(1)}, f32[6,26,1,128]{3,1,2,0:T(8,128)S(1)}, u32[]{:S(2)}, u32[]{:S(2)}) collective-permute-start(f32[6,26,1,128]{3,1,2,0:T(8,128)S(1)} %get-tuple-element.77), channel_id=1, source_target_pairs={{0,1},{1,2},{2,3},{3,4},{4,5},{5,6},{6,7},{8,9},{9,10},{10,11},{11... | collective-permute-start | bytes 239624 | tf_op jit(solution)/shard_map/ppermute | solution.py:14
  39.6 25.0 %collective-permute-start.6 = (f32[6,26,1,128]{3,1,2,0:T(8,128)S(1)}, f32[6,26,1,128]{3,1,2,0:T(8,128)S(1)}, u32[]{:S(2)}, u32[]{:S(2)}) collective-permute-start(f32[6,26,1,128]{3,1,2,0:T(8,128)S(1)} %get-tuple-element.78), channel_id=1, source_target_pairs={{1,0},{2,1},{3,2},{4,3},{5,4},{6,5},{7,6},{9,8},{10,9},{11,10},{12... | collective-permute-start | bytes 239624 | tf_op jit(solution)/shard_map/ppermute | solution.py:15
  65.5 1.2 copy-start
  66.8 8.7 %collective-permute-start.8 = (f32[3,1,9,128]{3,1,2,0:T(1,128)S(1)}, f32[3,1,9,128]{3,1,2,0:T(1,128)S(1)}, u32[]{:S(2)}, u32[]{:S(2)}) collective-permute-start(f32[3,1,9,128]{3,1,2,0:T(1,128)S(1)} %get-tuple-element.95), channel_id=1, source_target_pairs={{8,0},{16,8},{24,16},{9,1},{17,9},{25,17},{10,2},{18,10},{26,18},{... | collective-permute-start | bytes 41480 | tf_op jit(solution)/shard_map/ppermute | solution.py:15
  71.1 4.5 %collective-permute-start.9 = (f32[3,1,9,128]{3,1,2,0:T(1,128)S(1)}, f32[3,1,9,128]{3,1,2,0:T(1,128)S(1)}, u32[]{:S(2)}, u32[]{:S(2)}) collective-permute-start(f32[3,1,9,128]{3,1,2,0:T(1,128)S(1)} %get-tuple-element.96), channel_id=1, source_target_pairs={{0,8},{8,16},{16,24},{1,9},{9,17},{17,25},{2,10},{10,18},{18,26},{... | collective-permute-start | bytes 41480 | tf_op jit(solution)/shard_map/ppermute | solution.py:14
  75.6 8.7 %collective-permute-start.11 = (f32[3,26,1,128]{3,1,2,0:T(8,128)S(1)}, f32[3,26,1,128]{3,1,2,0:T(8,128)S(1)}, u32[]{:S(2)}, u32[]{:S(2)}) collective-permute-start(f32[3,26,1,128]{3,1,2,0:T(8,128)S(1)} %get-tuple-element.89), channel_id=1, source_target_pairs={{0,1},{1,2},{2,3},{3,4},{4,5},{5,6},{6,7},{8,9},{9,10},{10,11},{11... | collective-permute-start | bytes 119816 | tf_op jit(solution)/shard_map/ppermute | solution.py:14
  80.2 6.3 %collective-permute-start.10 = (f32[3,26,1,128]{3,1,2,0:T(8,128)S(1)}, f32[3,26,1,128]{3,1,2,0:T(8,128)S(1)}, u32[]{:S(2)}, u32[]{:S(2)}) collective-permute-start(f32[3,26,1,128]{3,1,2,0:T(8,128)S(1)} %get-tuple-element.90), channel_id=1, source_target_pairs={{1,0},{2,1},{3,2},{4,3},{5,4},{6,5},{7,6},{9,8},{10,9},{11,10},{12... | collective-permute-start | bytes 119816 | tf_op jit(solution)/shard_map/ppermute | solution.py:15
  98.1 4.3 %collective-permute-start.12 = (f32[6,1,9,128]{3,1,2,0:T(1,128)S(1)}, f32[6,1,9,128]{3,1,2,0:T(1,128)S(1)}, u32[]{:S(2)}, u32[]{:S(2)}) collective-permute-start(f32[6,1,9,128]{3,1,2,0:T(1,128)S(1)} %get-tuple-element.64), channel_id=1, source_target_pairs={{8,0},{16,8},{24,16},{9,1},{17,9},{25,17},{10,2},{18,10},{26,18},{... | collective-permute-start | bytes 82952 | tf_op jit(solution)/shard_map/ppermute | solution.py:15
  101.0 4.6 %collective-permute-start.13 = (f32[6,1,9,128]{3,1,2,0:T(1,128)S(1)}, f32[6,1,9,128]{3,1,2,0:T(1,128)S(1)}, u32[]{:S(2)}, u32[]{:S(2)}) collective-permute-start(f32[6,1,9,128]{3,1,2,0:T(1,128)S(1)} %get-tuple-element.63), channel_id=1, source_target_pairs={{0,8},{8,16},{16,24},{1,9},{9,17},{17,25},{2,10},{10,18},{18,26},{... | collective-permute-start | bytes 82952 | tf_op jit(solution)/shard_map/ppermute | solution.py:14
  105.7 6.9 %collective-permute-start.14 = (f32[6,26,1,128]{3,1,2,0:T(8,128)S(1)}, f32[6,26,1,128]{3,1,2,0:T(8,128)S(1)}, u32[]{:S(2)}, u32[]{:S(2)}) collective-permute-start(f32[6,26,1,128]{3,1,2,0:T(8,128)S(1)} %get-tuple-element.74), channel_id=1, source_target_pairs={{1,0},{2,1},{3,2},{4,3},{5,4},{6,5},{7,6},{9,8},{10,9},{11,10},{12... | collective-permute-start | bytes 239624 | tf_op jit(solution)/shard_map/ppermute | solution.py:15
  107.6 6.2 %collective-permute-start.15 = (f32[6,26,1,128]{3,1,2,0:T(8,128)S(1)}, f32[6,26,1,128]{3,1,2,0:T(8,128)S(1)}, u32[]{:S(2)}, u32[]{:S(2)}) collective-permute-start(f32[6,26,1,128]{3,1,2,0:T(8,128)S(1)} %get-tuple-element.73), channel_id=1, source_target_pairs={{0,1},{1,2},{2,3},{3,4},{4,5},{5,6},{6,7},{8,9},{9,10},{10,11},{11... | collective-permute-start | bytes 239624 | tf_op jit(solution)/shard_map/ppermute | solution.py:14
  115.3 3.4 %collective-permute-start.16 = (f32[3,1,9,128]{3,1,2,0:T(1,128)S(1)}, f32[3,1,9,128]{3,1,2,0:T(1,128)S(1)}, u32[]{:S(2)}, u32[]{:S(2)}) collective-permute-start(f32[3,1,9,128]{3,1,2,0:T(1,128)S(1)} %get-tuple-element.93), channel_id=1, source_target_pairs={{8,0},{16,8},{24,16},{9,1},{17,9},{25,17},{10,2},{18,10},{26,18},{... | collective-permute-start | bytes 41480 | tf_op jit(solution)/shard_map/ppermute | solution.py:15
  117.4 4.5 %collective-permute-start.17 = (f32[3,1,9,128]{3,1,2,0:T(1,128)S(1)}, f32[3,1,9,128]{3,1,2,0:T(1,128)S(1)}, u32[]{:S(2)}, u32[]{:S(2)}) collective-permute-start(f32[3,1,9,128]{3,1,2,0:T(1,128)S(1)} %get-tuple-element.94), channel_id=1, source_target_pairs={{0,8},{8,16},{16,24},{1,9},{9,17},{17,25},{2,10},{10,18},{18,26},{... | collective-permute-start | bytes 41480 | tf_op jit(solution)/shard_map/ppermute | solution.py:14
  121.9 8.6 %collective-permute-start.19 = (f32[3,26,1,128]{3,1,2,0:T(8,128)S(1)}, f32[3,26,1,128]{3,1,2,0:T(8,128)S(1)}, u32[]{:S(2)}, u32[]{:S(2)}) collective-permute-start(f32[3,26,1,128]{3,1,2,0:T(8,128)S(1)} %get-tuple-element.85), channel_id=1, source_target_pairs={{0,1},{1,2},{2,3},{3,4},{4,5},{5,6},{6,7},{8,9},{9,10},{10,11},{11... | collective-permute-start | bytes 119816 | tf_op jit(solution)/shard_map/ppermute | solution.py:14
  128.5 6.3 %collective-permute-start.18 = (f32[3,26,1,128]{3,1,2,0:T(8,128)S(1)}, f32[3,26,1,128]{3,1,2,0:T(8,128)S(1)}, u32[]{:S(2)}, u32[]{:S(2)}) collective-permute-start(f32[3,26,1,128]{3,1,2,0:T(8,128)S(1)} %get-tuple-element.86), channel_id=1, source_target_pairs={{1,0},{2,1},{3,2},{4,3},{5,4},{6,5},{7,6},{9,8},{10,9},{11,10},{12... | collective-permute-start | bytes 119816 | tf_op jit(solution)/shard_map/ppermute | solution.py:15
  136.2 3.3 %collective-permute-start.20 = (f32[6,1,9,128]{3,1,2,0:T(1,128)S(1)}, f32[6,1,9,128]{3,1,2,0:T(1,128)S(1)}, u32[]{:S(2)}, u32[]{:S(2)}) collective-permute-start(f32[6,1,9,128]{3,1,2,0:T(1,128)S(1)} %get-tuple-element.62), channel_id=1, source_target_pairs={{8,0},{16,8},{24,16},{9,1},{17,9},{25,17},{10,2},{18,10},{26,18},{... | collective-permute-start | bytes 82952 | tf_op jit(solution)/shard_map/ppermute | solution.py:15
  138.2 4.6 %collective-permute-start.21 = (f32[6,1,9,128]{3,1,2,0:T(1,128)S(1)}, f32[6,1,9,128]{3,1,2,0:T(1,128)S(1)}, u32[]{:S(2)}, u32[]{:S(2)}) collective-permute-start(f32[6,1,9,128]{3,1,2,0:T(1,128)S(1)} %get-tuple-element.61), channel_id=1, source_target_pairs={{0,8},{8,16},{16,24},{1,9},{9,17},{17,25},{2,10},{10,18},{18,26},{... | collective-permute-start | bytes 82952 | tf_op jit(solution)/shard_map/ppermute | solution.py:14
  142.8 7.4 %collective-permute-start.22 = (f32[6,26,1,128]{3,1,2,0:T(8,128)S(1)}, f32[6,26,1,128]{3,1,2,0:T(8,128)S(1)}, u32[]{:S(2)}, u32[]{:S(2)}) collective-permute-start(f32[6,26,1,128]{3,1,2,0:T(8,128)S(1)} %get-tuple-element.70), channel_id=1, source_target_pairs={{1,0},{2,1},{3,2},{4,3},{5,4},{6,5},{7,6},{9,8},{10,9},{11,10},{12... | collective-permute-start | bytes 239624 | tf_op jit(solution)/shard_map/ppermute | solution.py:15
  144.7 6.2 %collective-permute-start.23 = (f32[6,26,1,128]{3,1,2,0:T(8,128)S(1)}, f32[6,26,1,128]{3,1,2,0:T(8,128)S(1)}, u32[]{:S(2)}, u32[]{:S(2)}) collective-permute-start(f32[6,26,1,128]{3,1,2,0:T(8,128)S(1)} %get-tuple-element.69), channel_id=1, source_target_pairs={{0,1},{1,2},{2,3},{3,4},{4,5},{5,6},{6,7},{8,9},{9,10},{10,11},{11... | collective-permute-start | bytes 239624 | tf_op jit(solution)/shard_map/ppermute | solution.py:14
  152.5 3.2 %collective-permute-start.24 = (f32[3,1,9,128]{3,1,2,0:T(1,128)S(1)}, f32[3,1,9,128]{3,1,2,0:T(1,128)S(1)}, u32[]{:S(2)}, u32[]{:S(2)}) collective-permute-start(f32[3,1,9,128]{3,1,2,0:T(1,128)S(1)} %get-tuple-element.91), channel_id=1, source_target_pairs={{8,0},{16,8},{24,16},{9,1},{17,9},{25,17},{10,2},{18,10},{26,18},{... | collective-permute-start | bytes 41480 | tf_op jit(solution)/shard_map/ppermute | solution.py:15
  154.4 4.5 %collective-permute-start.25 = (f32[3,1,9,128]{3,1,2,0:T(1,128)S(1)}, f32[3,1,9,128]{3,1,2,0:T(1,128)S(1)}, u32[]{:S(2)}, u32[]{:S(2)}) collective-permute-start(f32[3,1,9,128]{3,1,2,0:T(1,128)S(1)} %get-tuple-element.92), channel_id=1, source_target_pairs={{0,8},{8,16},{16,24},{1,9},{9,17},{17,25},{2,10},{10,18},{18,26},{... | collective-permute-start | bytes 41480 | tf_op jit(solution)/shard_map/ppermute | solution.py:14
  158.9 8.6 %collective-permute-start.27 = (f32[3,26,1,128]{3,1,2,0:T(8,128)S(1)}, f32[3,26,1,128]{3,1,2,0:T(8,128)S(1)}, u32[]{:S(2)}, u32[]{:S(2)}) collective-permute-start(f32[3,26,1,128]{3,1,2,0:T(8,128)S(1)} %get-tuple-element.81), channel_id=1, source_target_pairs={{0,1},{1,2},{2,3},{3,4},{4,5},{5,6},{6,7},{8,9},{9,10},{10,11},{11... | collective-permute-start | bytes 119816 | tf_op jit(solution)/shard_map/ppermute | solution.py:14
  165.5 6.3 %collective-permute-start.26 = (f32[3,26,1,128]{3,1,2,0:T(8,128)S(1)}, f32[3,26,1,128]{3,1,2,0:T(8,128)S(1)}, u32[]{:S(2)}, u32[]{:S(2)}) collective-permute-start(f32[3,26,1,128]{3,1,2,0:T(8,128)S(1)} %get-tuple-element.82), channel_id=1, source_target_pairs={{1,0},{2,1},{3,2},{4,3},{5,4},{6,5},{7,6},{9,8},{10,9},{11,10},{12... | collective-permute-start | bytes 119816 | tf_op jit(solution)/shard_map/ppermute | solution.py:15
  167.5 5.2 %copy-start.2 = (f32[9,1,24,64]{3,2,1,0:T(8,128)}, f32[9,1,24,64]{3,2,1,0:T(8,128)S(1)}, u32[]{:S(2)}) copy-start(f32[9,1,24,64]{3,2,1,0:T(8,128)S(1)} %constant_dynamic-update-slice_fusion) | copy-start | bytes 165892
where the time goes:
time: 176 us; the launch traced here: 174 us
  starting transfers between devices  78.9 us (45%)
  other arithmetic  42.9 us (24%)
  waiting for transfers between devices  26.8 us (15%)
  blocking collectives  11.5 us (7%)
  local copies, waits for them, and re-layouts  6.86 us (4%)
  matrix products  5.66 us (3%)
    ppermute x14, starting transfers between devices, padded_2(): before = lax.ppermute(last, axis, up)  45.2 us
    ppermute x14, starting transfers between devices, padded_2(): after = lax.ppermute(initial, axis, down)  33.7 us
    unnamed x25, other arithmetic  22.2 us
    ppermute x14, waiting for transfers between devices, padded_2(): before = lax.ppermute(last, axis, up)  14.8 us
    ppermute x14, waiting for transfers between devices, padded_2(): after = lax.ppermute(initial, axis, down)  12 us
    all_gather x1, blocking collectives, local(): lax.all_gather(both, 'gy', axis=1, tiled=True)  11.5 us
    div x1, other arithmetic, elastic_step(): velocity = velocity + (step / rho)[None] * jnp.stack([acc_x, acc_y, acc_z])  5.85 us
    mul x1, other arithmetic, elastic_step(): velocity = velocity + (step / rho)[None] * jnp.stack([acc_x, acc_y, acc_z])  5.53 us
  transfers between devices with their start and end apart: 28, of which 12 were waited for; matrix products, arithmetic and copies ran while one was open for 19% of the time, Pallas kernels for 0%

commit v1 on v0

v1 whole, which is shorter than its diff:
```python
import jax
import jax.numpy as jnp
from jax import lax
from jax.sharding import PartitionSpec as P


def shifted(n, s):
    return [(i, i + s) for i in range(n) if 0 <= i + s < n]


def grid_pairs(nx, ny, dx, dy):
    pairs = []
    for a in range(nx):
        for b in range(ny):
            if 0 <= a + dx < nx and 0 <= b + dy < ny:
                pairs.append((a * ny + b, (a + dx) * ny + b + dy))
    return pairs


def tile_halo(field, width):
    nx, ny = lax.axis_size("gx"), lax.axis_size("gy")
    w = width
    lo_x, hi_x = field[:, -w:], field[:, :w]
    from_left = lax.ppermute(lo_x, "gx", shifted(nx, 1))
    from_right = lax.ppermute(hi_x, "gx", shifted(nx, -1))
    from_below = lax.ppermute(field[:, :, -w:], "gy", shifted(ny, 1))
    from_above = lax.ppermute(field[:, :, :w], "gy", shifted(ny, -1))
    both = ("gx", "gy")
    c_mm = lax.ppermute(field[:, -w:, -w:], both, grid_pairs(nx, ny, 1, 1))
    c_mp = lax.ppermute(field[:, -w:, :w], both, grid_pairs(nx, ny, 1, -1))
    c_pm = lax.ppermute(field[:, :w, -w:], both, grid_pairs(nx, ny, -1, 1))
    c_pp = lax.ppermute(field[:, :w, :w], both, grid_pairs(nx, ny, -1, -1))
    low = jnp.concatenate([c_mm, from_left, c_mp], axis=2)
    mid = jnp.concatenate([from_below, field, from_above], axis=2)
    high = jnp.concatenate([c_pm, from_right, c_pp], axis=2)
    return jnp.concatenate([low, mid, high], axis=1)


def strip_halo(field, width):
    n = lax.axis_size("gx") * lax.axis_size("gy")
    own = field.shape[1]
    reach = -(-width // own)
    both = ("gx", "gy")
    lows = [lax.ppermute(field, both, shifted(n, d)) for d in range(reach, 0, -1)]
    highs = [lax.ppermute(field, both, shifted(n, -d)) for d in range(1, reach + 1)]
    lo = jnp.concatenate(lows, axis=1)[:, reach * own - width:]
    hi = jnp.concatenate(highs, axis=1)[:, :width]
    return jnp.concatenate([lo, field, hi], axis=1)


def lookup(index, table):
    rho = jnp.zeros(index.shape, jnp.float32)
    lam = jnp.zeros(index.shape, jnp.float32)
    shear = jnp.zeros(index.shape, jnp.float32)
    for material in range(table.shape[1]):
        match = index == material
        rho = jnp.where(match, table[0, material], rho)
        lam = jnp.where(match, table[1, material], lam)
        shear = jnp.where(match, table[2, material], shear)
    return (rho, lam, shear)


def along(f, axis):
    n = f.shape[axis]
    zero = jnp.zeros_like(lax.slice_in_dim(f, 0, 1, axis=axis))
    up = jnp.concatenate([lax.slice_in_dim(f, 1, n, axis=axis), zero], axis=axis)
    down = jnp.concatenate([zero, lax.slice_in_dim(f, 0, n - 1, axis=axis)], axis=axis)
    return up - down


def step_wide(ext, coef, stress0, lam, shear, step, spacing, y_local):
    scale = 0.5 / spacing
    s = ext[3:9]
    if y_local:
        mid_s = s[:, 1:-1]
        dx = lambda c: (s[c, 2:] - s[c, :-2]) * scale
        dy = lambda c: along(mid_s[c], 1) * scale
        dz = lambda c: along(mid_s[c], 2) * scale
        vel_old = ext[0:3, 1:-1]
    else:
        mid_s = s[:, 1:-1, 1:-1]
        dx = lambda c: (s[c, 2:, 1:-1] - s[c, :-2, 1:-1]) * scale
        dy = lambda c: (s[c, 1:-1, 2:] - s[c, 1:-1, :-2]) * scale
        dz = lambda c: along(mid_s[c], 2) * scale
        vel_old = ext[0:3, 1:-1, 1:-1]
    acc_x = dx(0) + dy(3) + dz(4)
    acc_y = dx(3) + dy(1) + dz(5)
    acc_z = dx(4) + dy(5) + dz(2)
    vel = vel_old + coef[None] * jnp.stack([acc_x, acc_y, acc_z])
    if y_local:
        inner = vel[:, 1:-1]
        gx = lambda c: (vel[c, 2:] - vel[c, :-2]) * scale
        gy = lambda c: along(inner[c], 1) * scale
        gz = lambda c: along(inner[c], 2) * scale
    else:
        inner = vel[:, 1:-1, 1:-1]
        gx = lambda c: (vel[c, 2:, 1:-1] - vel[c, :-2, 1:-1]) * scale
        gy = lambda c: (vel[c, 1:-1, 2:] - vel[c, 1:-1, :-2]) * scale
        gz = lambda c: along(inner[c], 2) * scale
    g_x0, g_y1, g_z2 = gx(0), gy(1), gz(2)
    spread = g_x0 + g_y1 + g_z2
    new_xx = stress0[0] + step * (lam * spread + 2.0 * shear * g_x0)
    new_yy = stress0[1] + step * (lam * spread + 2.0 * shear * g_y1)
    new_zz = stress0[2] + step * (lam * spread + 2.0 * shear * g_z2)
    new_xy = stress0[3] + step * shear * (gy(0) + gx(1))
    new_xz = stress0[4] + step * shear * (gz(0) + gx(2))
    new_yz = stress0[5] + step * shear * (gz(1) + gy(2))
    return jnp.concatenate(
        [inner, jnp.stack([new_xx, new_yy, new_zz, new_xy, new_xz, new_yz])], 0
    )


def interp_matrix(n_fine, n_coarse):
    fine_pos = jnp.arange(n_fine, dtype=jnp.int32)
    whole = fine_pos // 3
    rest = fine_pos - 3 * whole
    lower = jnp.where(rest == 0, whole - 1, whole)
    frac = jnp.where(rest == 0, 2.0 / 3.0, jnp.where(rest == 1, 0.0, 1.0 / 3.0)).astype(jnp.float32)
    below = lower < 0
    lower = jnp.where(below, 0, lower)
    frac = jnp.where(below, 0.0, frac)
    above = lower >= n_coarse - 1
    lower = jnp.where(above, n_coarse - 2, lower)
    frac = jnp.where(above, 1.0, frac)
    cols = jnp.arange(n_coarse, dtype=jnp.int32)
    low_hit = (cols[None, :] == lower[:, None]).astype(jnp.float32)
    high_hit = (cols[None, :] == lower[:, None] + 1).astype(jnp.float32)
    return (1.0 - frac)[:, None] * low_hit + frac[:, None] * high_hit


def ramp(first, count, total, tile):
    place = first + jnp.arange(count, dtype=jnp.int32)
    margin = jnp.minimum(place, total - 1 - place).astype(jnp.float32) + 0.5
    part = jnp.maximum(1.0 - margin / tile, 0.0)
    return part * part


def local(region_state, region_material, fine_state, fine_material, material_table):
    count_x = lax.axis_size("gx")
    count_y = lax.axis_size("gy")
    fine_x = fine_state.shape[1]
    fine_y = fine_state.shape[2]
    reg_y = region_state.shape[2]
    rows_each = reg_y // count_y

    rho_r, lam_r, mu_r = lookup(region_material, material_table)
    coef_r = 0.6 / rho_r
    reg_ext = strip_halo(jnp.concatenate([region_state, coef_r[None]], 0), 2)
    region_next = step_wide(
        reg_ext, reg_ext[9, 1:-1], region_state[3:], lam_r, mu_r, 0.6, 3.0, True
    )

    both = jnp.concatenate([region_state, region_next], 0).astype(jnp.bfloat16)
    band = lax.all_to_all(both, "gy", 2, 1, tiled=True).astype(jnp.float32)
    columns = band.shape[1]
    high = lax.Precision.HIGHEST
    first = jnp.einsum("fa,cabz->cfbz", interp_matrix(fine_x, columns), band, precision=high)
    second = jnp.einsum("gb,cfbz->cfgz", interp_matrix(fine_y, rows_each), first, precision=high)
    background = jnp.einsum(
        "kz,cfgz->cfgk", interp_matrix(fine_state.shape[3], band.shape[3]), second, precision=high
    )
    along_x = ramp(lax.axis_index("gx") * fine_x, fine_x, count_x * fine_x, fine_x)
    along_y = ramp(lax.axis_index("gy") * fine_y, fine_y, count_y * fine_y, fine_y)
    relax = (0.1 + 0.4 * jnp.maximum(along_x[:, None], along_y[None, :]))[:, :, None]

    rho_f, lam_f, mu_f = lookup(fine_material, material_table)
    coef_f = 0.2 / rho_f
    ext = tile_halo(jnp.concatenate([fine_state, coef_f[None]], 0), 2)
    coef_ext = ext[9, 1:-1, 1:-1]
    state = fine_state
    for sub in range(1, 4):
        if sub > 1:
            ext = tile_halo(state, 2)
        state = step_wide(ext, coef_ext, state[3:], lam_f, mu_f, 0.2, 1.0, False)
        share = sub / 3.0
        target = background[:9] + share * (background[9:] - background[:9])
        state = state + relax[None] * (target - state)
    return (region_next, state)


def solution(mesh):
    return jax.shard_map(
        local,
        mesh=mesh,
        in_specs=(
            P(None, ("gx", "gy"), None, None),
            P(("gx", "gy"), None, None),
            P(None, "gx", "gy", None),
            P("gx", "gy", None),
            P(),
        ),
        out_specs=(P(None, ("gx", "gy"), None, None), P(None, "gx", "gy", None)),
        check_vma=False,
    )
```

time: 176 us -> 165 us (0.938)
  the two profiles are of different devices: /device:TPU:27 before, /device:TPU:19 now
where the time goes in v1:
time: 165 us; the launch traced here: 163 us
  starting transfers between devices  82.3 us (50%)
  other arithmetic  46.6 us (28%)
  waiting for transfers between devices  16.9 us (10%)
  local copies, waits for them, and re-layouts  9.93 us (6%)
  matrix products  5.79 us (4%)
  between operations  1.95 us (1%)
    unnamed x18, other arithmetic  21.4 us
    ppermute x3, starting transfers between devices, tile_halo(): from_below = lax.ppermute(field[:, :, -w:], 'gy', shifted(ny, 1))  13.3 us
    ppermute x3, waiting for transfers between devices, tile_halo(): c_mp = lax.ppermute(field[:, -w:, :w], both, grid_pairs(nx, ny, 1, -1))  11.2 us
    ppermute x3, starting transfers between devices, tile_halo(): c_mm = lax.ppermute(field[:, -w:, -w:], both, grid_pairs(nx, ny, 1, 1))  10.5 us
    ppermute x3, starting transfers between devices, tile_halo(): from_left = lax.ppermute(lo_x, 'gx', shifted(nx, 1))  10.4 us
    ppermute x3, starting transfers between devices, tile_halo(): c_pm = lax.ppermute(field[:, :w, -w:], both, grid_pairs(nx, ny, -1, 1))  8.41 us
    broadcast_in_dim x1, other arithmetic, local(): reg_ext = strip_halo(jnp.concatenate([region_state, coef_r[None]], 0), 2)  6.38 us
    ppermute x3, starting transfers between devices, tile_halo(): from_above = lax.ppermute(field[:, :, :w], 'gy', shifted(ny, -1))  6.35 us
  transfers between devices with their start and end apart: 29, of which 7 were waited for; matrix products, arithmetic and copies ran while one was open for 20% of the time, Pallas kernels for 0%

profile of v1, /device:TPU:19, one launch (start us, length us, event | category | flops | bytes accessed | tf_op | source)
XLA Modules:
  0.0 163.5 jit_solution(3994273409424276629)
XLA Ops:
  0.7 2.1 %fusion.245 = (f32[1,1]{1,0:T(1,128)}, f32[1,1]{1,0:T(1,128)}, f32[1,1]{1,0:T(1,128)}, f32[1,1]{1,0:T(1,128)}, f32[1,1]{1,0:T(1,128)}, /*index=5*/f32[1,1]{1,0:T...) fusion(f32[3,8]{1,0:T(4,128)} %param.9), kind=kLoop, calls=%fused_computation.525 | loop fusion | bytes 152 | tf_op jit(solution)/shard_map/slice | solution.py:58
  2.7 1.5 fusion.246
  4.3 6.4 %divide_bitcast_fusion.1 = (f32[1,1,24,64]{3,2,1,0:T(8,128)S(1)}, pred[1,24,64]{2,1,0:T(8,128)(4,1)S(1)}, pred[1,24,64]{2,1,0:T(8,128)(4,1)S(1)}, pred[1,24,64]{...) fusion(f32[]{:T(128)} %bitcast.7, f32[]{:T(128)} %bitcast.6, ...), kind=kLoop, calls=%fused_computation.398 | loop fusion | flops 26112 | bytes 24608 | tf_op jit(solution)/shard_map/broadcast_in_dim | solution.py:148
  10.7 0.9 pad_maximum_fusion.24
  11.6 2.6 %collective-permute-start.1 = (f32[10,1,24,64]{3,2,1,0:T(8,128)S(1)}, f32[10,1,24,64]{3,2,1,0:T(8,128)S(1)}, u32[]{:S(2)}, u32[]{:S(2)}) collective-permute-start(f32[10,1,24,64]{3,2,1,0:T(8,128)S(1)} %pad_maximum_fusion.24), channel_id=1, source_target_pairs={{1,0},{2,1},{3,2},{4,3},{5,4},{6,5},{7,6},{8,7},{9,8},{10,9},{11,1... | collective-permute-start | bytes 184328 | tf_op jit(solution)/shard_map/ppermute | solution.py:45
  14.2 3.9 %collective-permute-start = (f32[10,1,24,64]{3,2,1,0:T(8,128)S(1)}, f32[10,1,24,64]{3,2,1,0:T(8,128)S(1)}, u32[]{:S(2)}, u32[]{:S(2)}) collective-permute-start(f32[10,1,24,64]{3,2,1,0:T(8,128)S(1)} %pad_maximum_fusion.24), channel_id=1, source_target_pairs={{0,1},{1,2},{2,3},{3,4},{4,5},{5,6},{6,7},{7,8},{8,9},{9,10},{10,1... | collective-permute-start | bytes 184328 | tf_op jit(solution)/shard_map/ppermute | solution.py:44
  18.1 2.3 %collective-permute-start.3 = (f32[10,1,24,64]{3,2,1,0:T(8,128)S(1)}, f32[10,1,24,64]{3,2,1,0:T(8,128)S(1)}, u32[]{:S(2)}, u32[]{:S(2)}) collective-permute-start(f32[10,1,24,64]{3,2,1,0:T(8,128)S(1)} %pad_maximum_fusion.24), channel_id=1, source_target_pairs={{0,2},{1,3},{2,4},{3,5},{4,6},{5,7},{6,8},{7,9},{8,10},{9,11},{10,... | collective-permute-start | bytes 184328 | tf_op jit(solution)/shard_map/ppermute | solution.py:44
  20.3 3.0 %collective-permute-start.2 = (f32[10,1,24,64]{3,2,1,0:T(8,128)S(1)}, f32[10,1,24,64]{3,2,1,0:T(8,128)S(1)}, u32[]{:S(2)}, u32[]{:S(2)}) collective-permute-start(f32[10,1,24,64]{3,2,1,0:T(8,128)S(1)} %pad_maximum_fusion.24), channel_id=1, source_target_pairs={{2,0},{3,1},{4,2},{5,3},{6,4},{7,5},{8,6},{9,7},{10,8},{11,9},{12,... | collective-permute-start | bytes 184328 | tf_op jit(solution)/shard_map/ppermute | solution.py:45
  23.4 6.1 %divide_bitcast_fusion = (f32[1,24,9,128]{3,1,2,0:T(8,128)S(1)}, pred[24,9,128]{2,0,1:T(8,128)(4,1)S(1)}, pred[24,9,128]{2,0,1:T(8,128)(4,1)S(1)}, pred[24,9,128...) fusion(f32[]{:T(128)} %bitcast.7, f32[]{:T(128)} %bitcast.6, ...), kind=kLoop, calls=%fused_computation.308 | loop fusion | flops 470016 | bytes 442400 | tf_op jit(solution)/shard_map/broadcast_in_dim | solution.py:168
  29.5 1.6 %pad_maximum_fusion.32 = (f32[10,2,2,128]{3,1,2,0:T(2,128)}, f32[10,2,2,128]{3,1,2,0:T(2,128)S(1)}, f32[10,2,2,128]{3,1,2,0:T(2,128)}, f32[10,2,2,128]{3,1,2,0:T(2,128)S(1)}) fusion(f32[1,24,9,128]{3,1,2,0:T(8,128)S(1)} %get-tuple-element.24, f32[9,24,9,128]{3,1,2,0:T(8,128)} %param.7), kind=kLoop, calls=%fused_computation.358 | loop fusion | flops 20480 | bytes 1187840 | tf_op jit(solution)/shard_map/slice | solution.py:30
  31.1 3.3 %collective-permute-start.9 = (f32[10,2,2,128]{3,1,2,0:T(2,128)S(1)}, f32[10,2,2,128]{3,1,2,0:T(2,128)S(1)}, u32[]{:S(2)}, u32[]{:S(2)}) collective-permute-start(f32[10,2,2,128]{3,1,2,0:T(2,128)S(1)} %get-tuple-element.52), channel_id=1, source_target_pairs={{8,1},{9,2},{10,3},{11,4},{12,5},{13,6},{14,7},{16,9},{17,10},{18,... | collective-permute-start | bytes 61448 | tf_op jit(solution)/shard_map/ppermute | solution.py:31
  34.4 0.7 pad_maximum_fusion.25
  35.2 0.6 compare_select_fusion.8
  35.7 0.5 compare_select_fusion.9
  36.3 0.6 compare_select_fusion.4
  36.9 0.6 compare_select_fusion.5
  37.5 0.6 compare_select_fusion
  38.2 0.6 compare_select_fusion.1
  38.8 3.9 %collective-permute-start.4 = (f32[10,2,2,128]{3,1,2,0:T(2,128)S(1)}, f32[10,2,2,128]{3,1,2,0:T(2,128)S(1)}, u32[]{:S(2)}, u32[]{:S(2)}) collective-permute-start(f32[10,2,2,128]{3,1,2,0:T(2,128)S(1)} %get-tuple-element.54), channel_id=1, source_target_pairs={{0,9},{1,10},{2,11},{3,12},{4,13},{5,14},{6,15},{8,17},{9,18},{10,... | collective-permute-start | bytes 61448 | tf_op jit(solution)/shard_map/ppermute | solution.py:29
  42.7 1.3 collective-permute-done.4
  44.0 2.1 %collective-permute-start.10 = (f32[10,2,9,128]{3,1,2,0:T(2,128)}, f32[10,2,9,128]{3,1,2,0:T(2,128)}, u32[]{:S(2)}, u32[]{:S(2)}) collective-permute-start(f32[10,2,9,128]{3,1,2,0:T(2,128)} %get-tuple-element.56), channel_id=1, source_target_pairs={{8,0},{16,8},{24,16},{9,1},{17,9},{25,17},{10,2},{18,10},{26,18},{... | collective-permute-start | bytes 276488 | tf_op jit(solution)/shard_map/ppermute | solution.py:25
  46.1 2.1 %collective-permute-start.11 = (f32[10,2,2,128]{3,1,2,0:T(2,128)}, f32[10,2,2,128]{3,1,2,0:T(2,128)}, u32[]{:S(2)}, u32[]{:S(2)}) collective-permute-start(f32[10,2,2,128]{3,1,2,0:T(2,128)} %get-tuple-element.53), channel_id=1, source_target_pairs={{9,0},{10,1},{11,2},{12,3},{13,4},{14,5},{15,6},{17,8},{18,9},{19,... | collective-permute-start | bytes 61448 | tf_op jit(solution)/shard_map/ppermute | solution.py:32
  48.2 2.1 %collective-permute-start.8 = (f32[10,24,2,128]{3,1,2,0:T(8,128)S(1)}, f32[10,24,2,128]{3,1,2,0:T(8,128)S(1)}, u32[]{:S(2)}, u32[]{:S(2)}) collective-permute-start(f32[10,24,2,128]{3,1,2,0:T(8,128)S(1)} %get-tuple-element.58), channel_id=1, source_target_pairs={{1,0},{2,1},{3,2},{4,3},{5,4},{6,5},{7,6},{9,8},{10,9},{11,10},{12... | collective-permute-start | bytes 737288 | tf_op jit(solution)/shard_map/ppermute | solution.py:27
  50.7 4.6 %collective-permute-start.7 = (f32[10,24,2,128]{3,1,2,0:T(8,128)S(1)}, f32[10,24,2,128]{3,1,2,0:T(8,128)S(1)}, u32[]{:S(2)}, u32[]{:S(2)}) collective-permute-start(f32[10,24,2,128]{3,1,2,0:T(8,128)S(1)} %get-tuple-element.57), channel_id=1, source_target_pairs={{0,1},{1,2},{2,3},{3,4},{4,5},{5,6},{6,7},{8,9},{9,10},{10,11},{11... | collective-permute-start | bytes 737288 | tf_op jit(solution)/shard_map/ppermute | solution.py:26
  55.2 3.8 %collective-permute-start.5 = (f32[10,2,9,128]{3,1,2,0:T(2,128)S(1)}, f32[10,2,9,128]{3,1,2,0:T(2,128)}, u32[]{:S(2)}, u32[]{:S(2)}) collective-permute-start(f32[10,2,9,128]{3,1,2,0:T(2,128)S(1)} %get-tuple-element.55), channel_id=1, source_target_pairs={{0,8},{8,16},{16,24},{1,9},{9,17},{17,25},{2,10},{10,18},{18,26},{... | collective-permute-start | bytes 276488 | tf_op jit(solution)/shard_map/ppermute | solution.py:24
  59.7 10.1 %constant_dynamic-update-slice_fusion.24 = (bf16[18,1,24,64]{3,2,1,0:T(8,128)(2,1)S(1)}, f32[1,24,64]{2,1,0:T(8,128)S(1)}, f32[1,24,64]{2,1,0:T(8,128)S(1)}, f32[1,24,64]{2,1,0:T(8,128)S(1)}) fusion(bf16[18,1,24,64]{3,2,1,0:T(8,128)(2,1)S(1)} %constant_dynamic-update-slice_fusion.25, f32[3,3,24,64]{3,2,1,0:T(8,128)S(1)} %slice_add_fusion.3, ...), kind=kLoop, calls=%fused_computation.150 | loop fusion | flops 47616 | bytes 153664
  70.1 0.8 reshape.458
  70.9 3.8 %all-to-all-start = ((bf16[8,2,1728]{2,1,0:T(2,128)(2,1)}), bf16[8,2,1728]{2,1,0:T(2,128)(2,1)S(1)}, u32[]{:S(2)}, u32[]{:S(2)}) async-start(bf16[8,2,1728]{2,1,0:T(2,128)(2,1)} %reshape.458), calls=%async_computation | async-start | bytes 114688 | tf_op jit(solution)/shard_map/all_to_all | solution.py:154
  74.8 1.9 %collective-permute-start.6 = (f32[10,2,2,128]{3,1,2,0:T(2,128)S(1)}, f32[10,2,2,128]{3,1,2,0:T(2,128)S(1)}, u32[]{:S(2)}, u32[]{:S(2)}) collective-permute-start(f32[10,2,2,128]{3,1,2,0:T(2,128)S(1)} %copy-done.2), channel_id=1, source_target_pairs={{1,8},{2,9},{3,10},{4,11},{5,12},{6,13},{7,14},{9,16},{10,17},{11,... | collective-permute-start | bytes 61448 | tf_op jit(solution)/shard_map/ppermute | solution.py:30
  76.7 0.9 constant_dynamic-update-slice_fusion.11
  77.6 0.9 constant_dynamic-update-slice_fusion.8
  78.5 0.7 constant_dynamic-update-slice_fusion.10
  79.3 2.4 %collective-permute-done.6 = f32[10,2,2,128]{3,1,2,0:T(2,128)S(1)} collective-permute-done((f32[10,2,2,128]{3,1,2,0:T(2,128)S(1)}, f32[10,2,2,128]{3,1,2,0:T(2,128)S(1)}, u32[]{:S(2)}, u32[]{:S(2)}) %collective-permute-start.6) | collective-permute-done | bytes 20512 | tf_op jit(solution)/shard_map/ppermute | solution.py:30
  81.9 0.5 convolution_bitcast_fusion.1
  82.4 3.1 %convolution_bitcast_fusion = f32[18,24,9,64]{3,2,1,0:T(8,128)S(1)} fusion(f32[18,24,3,64]{3,1,2,0:T(8,128)S(1)} %convolution_bitcast_fusion.1, f32[9]{0:T(128)S(1)} %copy-done.16, s32[9]{0:T(128)S(1)} %copy-done.19, f32[9]{0:T(128)S(1)} %copy-done.17, s32[9]{0:T(128)S(1)} %copy-done.18), kind=kOutput, calls=%fused_computation.7 | convolution fusion | flops 8958087 | bytes 1327248 | tf_op jit(solution)/shard_map/gb,cfbz->cfgz/dot_general | solution.py:158
  85.6 2.2 %fusion = f32[18,24,9,128]{3,1,2,0:T(8,128)S(1)} fusion(f32[18,24,9,64]{3,2,1,0:T(8,128)S(1)} %convolution_bitcast_fusion, f32[128]{0:T(128)S(1)} %copy-done.8, s32[128]{0:T(128)S(1)} %copy-done.15, f32[128]{0:T(128)S(1)} %copy-done.9, s32[128]{0:T(128)S(1)} %copy-done.14), kind=kOutput, calls=%fused_computation.5 | convolution fusion | flops 382246912 | bytes 2988032 | tf_op jit(solution)/shard_map/kz,cfgz->cfgk/dot_general | solution.py:159
  88.2 0.4 pad_maximum_fusion
  89.3 10.2 %constant_dynamic-update-slice_fusion.18 = (f32[9,24,9,128]{3,1,2,0:T(8,128)S(1)}, f32[24,9,128]{2,0,1:T(8,128)S(1)}, f32[24,9,128]{2,0,1:T(8,128)S(1)}, f32[24,9,128]{2,0,1:T(8,128)S(1)}) fusion(f32[9,24,9,128]{3,1,2,0:T(8,128)S(1)} %slice_dynamic-update-slice_fusion.2, f32[9,24,9,128]{3,1,2,0:T(8,128)S(1)} %copy-done, ...), kind=kLoop, calls=%fused_computation.144 | loop fusion | flops 829440 | bytes 1437760
  100.2 0.3 multiply_add_fusion.2
  100.5 3.1 %collective-permute-start.17 = (f32[9,2,2,128]{3,1,2,0:T(2,128)S(1)}, f32[9,2,2,128]{3,1,2,0:T(2,128)S(1)}, u32[]{:S(2)}, u32[]{:S(2)}) collective-permute-start(f32[9,2,2,128]{3,1,2,0:T(2,128)S(1)} %get-tuple-element.69), channel_id=1, source_target_pairs={{8,1},{9,2},{10,3},{11,4},{12,5},{13,6},{14,7},{16,9},{17,10},{18,... | collective-permute-start | bytes 55304 | tf_op jit(solution)/shard_map/ppermute | solution.py:31
  103.7 1.9 %collective-permute-start.18 = (f32[9,2,9,128]{3,1,2,0:T(2,128)S(1)}, f32[9,2,9,128]{3,1,2,0:T(2,128)S(1)}, u32[]{:S(2)}, u32[]{:S(2)}) collective-permute-start(f32[9,2,9,128]{3,1,2,0:T(2,128)S(1)} %get-tuple-element.72), channel_id=1, source_target_pairs={{8,0},{16,8},{24,16},{9,1},{17,9},{25,17},{10,2},{18,10},{26,18},{... | collective-permute-start | bytes 248840 | tf_op jit(solution)/shard_map/ppermute | solution.py:25
  105.6 1.9 %collective-permute-start.19 = (f32[9,2,2,128]{3,1,2,0:T(2,128)S(1)}, f32[9,2,2,128]{3,1,2,0:T(2,128)S(1)}, u32[]{:S(2)}, u32[]{:S(2)}) collective-permute-start(f32[9,2,2,128]{3,1,2,0:T(2,128)S(1)} %get-tuple-element.68), channel_id=1, source_target_pairs={{9,0},{10,1},{11,2},{12,3},{13,4},{14,5},{15,6},{17,8},{18,9},{19,... | collective-permute-start | bytes 55304 | tf_op jit(solution)/shard_map/ppermute | solution.py:32
  107.5 1.9 %collective-permute-start.16 = (f32[9,24,2,128]{3,1,2,0:T(8,128)S(1)}, f32[9,24,2,128]{3,1,2,0:T(8,128)S(1)}, u32[]{:S(2)}, u32[]{:S(2)}) collective-permute-start(f32[9,24,2,128]{3,1,2,0:T(8,128)S(1)} %get-tuple-element.74), channel_id=1, source_target_pairs={{1,0},{2,1},{3,2},{4,3},{5,4},{6,5},{7,6},{9,8},{10,9},{11,10},{12... | collective-permute-start | bytes 663560 | tf_op jit(solution)/shard_map/ppermute | solution.py:27
  109.5 4.5 %collective-permute-start.15 = (f32[9,24,2,128]{3,1,2,0:T(8,128)S(1)}, f32[9,24,2,128]{3,1,2,0:T(8,128)S(1)}, u32[]{:S(2)}, u32[]{:S(2)}) collective-permute-start(f32[9,24,2,128]{3,1,2,0:T(8,128)S(1)} %get-tuple-element.73), channel_id=1, source_target_pairs={{0,1},{1,2},{2,3},{3,4},{4,5},{5,6},{6,7},{8,9},{9,10},{10,11},{11... | collective-permute-start | bytes 663560 | tf_op jit(solution)/shard_map/ppermute | solution.py:26
  114.0 3.3 %collective-permute-start.12 = (f32[9,2,2,128]{3,1,2,0:T(2,128)S(1)}, f32[9,2,2,128]{3,1,2,0:T(2,128)S(1)}, u32[]{:S(2)}, u32[]{:S(2)}) collective-permute-start(f32[9,2,2,128]{3,1,2,0:T(2,128)S(1)} %get-tuple-element.70), channel_id=1, source_target_pairs={{0,9},{1,10},{2,11},{3,12},{4,13},{5,14},{6,15},{8,17},{9,18},{10,... | collective-permute-start | bytes 55304 | tf_op jit(solution)/shard_map/ppermute | solution.py:29
  117.4 1.8 %collective-permute-done.12 = f32[9,2,2,128]{3,1,2,0:T(2,128)S(1)} collective-permute-done((f32[9,2,2,128]{3,1,2,0:T(2,128)S(1)}, f32[9,2,2,128]{3,1,2,0:T(2,128)S(1)}, u32[]{:S(2)}, u32[]{:S(2)}) %collective-permute-start.12) | collective-permute-done | bytes 18464 | tf_op jit(solution)/shard_map/ppermute | solution.py:29
  119.1 3.1 %collective-permute-start.13 = (f32[9,2,9,128]{3,1,2,0:T(2,128)S(1)}, f32[9,2,9,128]{3,1,2,0:T(2,128)S(1)}, u32[]{:S(2)}, u32[]{:S(2)}) collective-permute-start(f32[9,2,9,128]{3,1,2,0:T(2,128)S(1)} %get-tuple-element.71), channel_id=1, source_target_pairs={{0,8},{8,16},{16,24},{1,9},{9,17},{17,25},{2,10},{10,18},{18,26},{... | collective-permute-start | bytes 248840 | tf_op jit(solution)/shard_map/ppermute | solution.py:24
  122.2 2.1 %collective-permute-start.14 = (f32[9,2,2,128]{3,1,2,0:T(2,128)S(1)}, f32[9,2,2,128]{3,1,2,0:T(2,128)S(1)}, u32[]{:S(2)}, u32[]{:S(2)}) collective-permute-start(f32[9,2,2,128]{3,1,2,0:T(2,128)S(1)} %get-tuple-element.67), channel_id=1, source_target_pairs={{1,8},{2,9},{3,10},{4,11},{5,12},{6,13},{7,14},{9,16},{10,17},{11,... | collective-permute-start | bytes 55304 | tf_op jit(solution)/shard_map/ppermute | solution.py:30
  124.4 0.8 collective-permute-done.13
  125.2 4.0 %collective-permute-done.14 = f32[9,2,2,128]{3,1,2,0:T(2,128)S(1)} collective-permute-done((f32[9,2,2,128]{3,1,2,0:T(2,128)S(1)}, f32[9,2,2,128]{3,1,2,0:T(2,128)S(1)}, u32[]{:S(2)}, u32[]{:S(2)}) %collective-permute-start.14) | collective-permute-done | bytes 18464 | tf_op jit(solution)/shard_map/ppermute | solution.py:30
  129.7 0.3 pad_maximum_fusion.1
  131.5 0.3 multiply_add_fusion.1
  131.8 2.1 %collective-permute-start.25 = (f32[9,2,2,128]{3,1,2,0:T(2,128)S(1)}, f32[9,2,2,128]{3,1,2,0:T(2,128)S(1)}, u32[]{:S(2)}, u32[]{:S(2)}) collective-permute-start(f32[9,2,2,128]{3,1,2,0:T(2,128)S(1)} %get-tuple-element.61), channel_id=1, source_target_pairs={{8,1},{9,2},{10,3},{11,4},{12,5},{13,6},{14,7},{16,9},{17,10},{18,... | collective-permute-start | bytes 55304 | tf_op jit(solution)/shard_map/ppermute | solution.py:31
  134.0 1.9 %collective-permute-start.26 = (f32[9,2,9,128]{3,1,2,0:T(2,128)S(1)}, f32[9,2,9,128]{3,1,2,0:T(2,128)S(1)}, u32[]{:S(2)}, u32[]{:S(2)}) collective-permute-start(f32[9,2,9,128]{3,1,2,0:T(2,128)S(1)} %get-tuple-element.64), channel_id=1, source_target_pairs={{8,0},{16,8},{24,16},{9,1},{17,9},{25,17},{10,2},{18,10},{26,18},{... | collective-permute-start | bytes 248840 | tf_op jit(solution)/shard_map/ppermute | solution.py:25
  135.9 1.9 %collective-permute-start.27 = (f32[9,2,2,128]{3,1,2,0:T(2,128)S(1)}, f32[9,2,2,128]{3,1,2,0:T(2,128)S(1)}, u32[]{:S(2)}, u32[]{:S(2)}) collective-permute-start(f32[9,2,2,128]{3,1,2,0:T(2,128)S(1)} %get-tuple-element.60), channel_id=1, source_target_pairs={{9,0},{10,1},{11,2},{12,3},{13,4},{14,5},{15,6},{17,8},{18,9},{19,... | collective-permute-start | bytes 55304 | tf_op jit(solution)/shard_map/ppermute | solution.py:32
  137.9 2.3 %collective-permute-start.24 = (f32[9,24,2,128]{3,1,2,0:T(8,128)S(1)}, f32[9,24,2,128]{3,1,2,0:T(8,128)S(1)}, u32[]{:S(2)}, u32[]{:S(2)}) collective-permute-start(f32[9,24,2,128]{3,1,2,0:T(8,128)S(1)} %get-tuple-element.66), channel_id=1, source_target_pairs={{1,0},{2,1},{3,2},{4,3},{5,4},{6,5},{7,6},{9,8},{10,9},{11,10},{12... | collective-permute-start | bytes 663560 | tf_op jit(solution)/shard_map/ppermute | solution.py:27
  140.2 4.2 %collective-permute-start.23 = (f32[9,24,2,128]{3,1,2,0:T(8,128)S(1)}, f32[9,24,2,128]{3,1,2,0:T(8,128)S(1)}, u32[]{:S(2)}, u32[]{:S(2)}) collective-permute-start(f32[9,24,2,128]{3,1,2,0:T(8,128)S(1)} %get-tuple-element.65), channel_id=1, source_target_pairs={{0,1},{1,2},{2,3},{3,4},{4,5},{5,6},{6,7},{8,9},{9,10},{10,11},{11... | collective-permute-start | bytes 663560 | tf_op jit(solution)/shard_map/ppermute | solution.py:26
  144.4 3.4 %collective-permute-start.20 = (f32[9,2,2,128]{3,1,2,0:T(2,128)S(1)}, f32[9,2,2,128]{3,1,2,0:T(2,128)S(1)}, u32[]{:S(2)}, u32[]{:S(2)}) collective-permute-start(f32[9,2,2,128]{3,1,2,0:T(2,128)S(1)} %get-tuple-element.62), channel_id=1, source_target_pairs={{0,9},{1,10},{2,11},{3,12},{4,13},{5,14},{6,15},{8,17},{9,18},{10,... | collective-permute-start | bytes 55304 | tf_op jit(solution)/shard_map/ppermute | solution.py:29
  147.7 1.7 %collective-permute-done.20 = f32[9,2,2,128]{3,1,2,0:T(2,128)S(1)} collective-permute-done((f32[9,2,2,128]{3,1,2,0:T(2,128)S(1)}, f32[9,2,2,128]{3,1,2,0:T(2,128)S(1)}, u32[]{:S(2)}, u32[]{:S(2)}) %collective-permute-start.20) | collective-permute-done | bytes 18464 | tf_op jit(solution)/shard_map/ppermute | solution.py:29
  149.4 3.6 %collective-permute-start.21 = (f32[9,2,9,128]{3,1,2,0:T(2,128)S(1)}, f32[9,2,9,128]{3,1,2,0:T(2,128)S(1)}, u32[]{:S(2)}, u32[]{:S(2)}) collective-permute-start(f32[9,2,9,128]{3,1,2,0:T(2,128)S(1)} %get-tuple-element.63), channel_id=1, source_target_pairs={{0,8},{8,16},{16,24},{1,9},{9,17},{17,25},{2,10},{10,18},{18,26},{... | collective-permute-start | bytes 248840 | tf_op jit(solution)/shard_map/ppermute | solution.py:24
  153.1 1.9 %collective-permute-start.22 = (f32[9,2,2,128]{3,1,2,0:T(2,128)S(1)}, f32[9,2,2,128]{3,1,2,0:T(2,128)S(1)}, u32[]{:S(2)}, u32[]{:S(2)}) collective-permute-start(f32[9,2,2,128]{3,1,2,0:T(2,128)S(1)} %get-tuple-element.59), channel_id=1, source_target_pairs={{1,8},{2,9},{3,10},{4,11},{5,12},{6,13},{7,14},{9,16},{10,17},{11,... | collective-permute-start | bytes 55304 | tf_op jit(solution)/shard_map/ppermute | solution.py:30
  155.1 4.9 %collective-permute-done.22 = f32[9,2,2,128]{3,1,2,0:T(2,128)S(1)} collective-permute-done((f32[9,2,2,128]{3,1,2,0:T(2,128)S(1)}, f32[9,2,2,128]{3,1,2,0:T(2,128)S(1)}, u32[]{:S(2)}, u32[]{:S(2)}) %collective-permute-start.22) | collective-permute-done | bytes 18464 | tf_op jit(solution)/shard_map/ppermute | solution.py:30
  160.4 0.3 pad_maximum_fusion.2
  162.2 1.2 multiply_add_fusion
  (177 shorter events, 7.2 us)
Async XLA Ops:
  0.6 33.7 %copy-start.1 = (f32[9,1,24,64]{3,2,1,0:T(8,128)S(1)}, f32[9,1,24,64]{3,2,1,0:T(8,128)}, u32[]{:S(2)}) copy-start(f32[9,1,24,64]{3,2,1,0:T(8,128)} %param.5) | copy-start | bytes 165892
  0.6 33.8 %copy-start = (f32[9,24,9,128]{3,1,2,0:T(8,128)S(1)}, f32[9,24,9,128]{3,1,2,0:T(8,128)}, u32[]{:S(2)}) copy-start(f32[9,24,9,128]{3,1,2,0:T(8,128)} %param.7) | copy-start | bytes 2985988
  11.6 34.5 %collective-permute-start.1 = (f32[10,1,24,64]{3,2,1,0:T(8,128)S(1)}, f32[10,1,24,64]{3,2,1,0:T(8,128)S(1)}, u32[]{:S(2)}, u32[]{:S(2)}) collective-permute-start(f32[10,1,24,64]{3,2,1,0:T(8,128)S(1)} %pad_maximum_fusion.24), channel_id=1, source_target_pairs={{1,0},{2,1},{3,2},{4,3},{5,4},{6,5},{7,6},{8,7},{9,8},{10,9},{11,1... | collective-permute-start | bytes 184328 | tf_op jit(solution)/shard_map/ppermute | solution.py:45
  14.2 34.0 %collective-permute-start = (f32[10,1,24,64]{3,2,1,0:T(8,128)S(1)}, f32[10,1,24,64]{3,2,1,0:T(8,128)S(1)}, u32[]{:S(2)}, u32[]{:S(2)}) collective-permute-start(f32[10,1,24,64]{3,2,1,0:T(8,128)S(1)} %pad_maximum_fusion.24), channel_id=1, source_target_pairs={{0,1},{1,2},{2,3},{3,4},{4,5},{5,6},{6,7},{7,8},{8,9},{9,10},{10,1... | collective-permute-start | bytes 184328 | tf_op jit(solution)/shard_map/ppermute | solution.py:44
  18.1 32.6 %collective-permute-start.3 = (f32[10,1,24,64]{3,2,1,0:T(8,128)S(1)}, f32[10,1,24,64]{3,2,1,0:T(8,128)S(1)}, u32[]{:S(2)}, u32[]{:S(2)}) collective-permute-start(f32[10,1,24,64]{3,2,1,0:T(8,128)S(1)} %pad_maximum_fusion.24), channel_id=1, source_target_pairs={{0,2},{1,3},{2,4},{3,5},{4,6},{5,7},{6,8},{7,9},{8,10},{9,11},{10,... | collective-permute-start | bytes 184328 | tf_op jit(solution)/shard_map/ppermute | solution.py:44
  20.3 34.9 %collective-permute-start.2 = (f32[10,1,24,64]{3,2,1,0:T(8,128)S(1)}, f32[10,1,24,64]{3,2,1,0:T(8,128)S(1)}, u32[]{:S(2)}, u32[]{:S(2)}) collective-permute-start(f32[10,1,24,64]{3,2,1,0:T(8,128)S(1)} %pad_maximum_fusion.24), channel_id=1, source_target_pairs={{2,0},{3,1},{4,2},{5,3},{6,4},{7,5},{8,6},{9,7},{10,8},{11,9},{12,... | collective-permute-start | bytes 184328 | tf_op jit(solution)/shard_map/ppermute | solution.py:45
  31.1 7.7 %collective-permute-start.9 = (f32[10,2,2,128]{3,1,2,0:T(2,128)S(1)}, f32[10,2,2,128]{3,1,2,0:T(2,128)S(1)}, u32[]{:S(2)}, u32[]{:S(2)}) collective-permute-start(f32[10,2,2,128]{3,1,2,0:T(2,128)S(1)} %get-tuple-element.52), channel_id=1, source_target_pairs={{8,1},{9,2},{10,3},{11,4},{12,5},{13,6},{14,7},{16,9},{17,10},{18,... | collective-permute-start | bytes 61448 | tf_op jit(solution)/shard_map/ppermute | solution.py:31
  38.8 5.2 %collective-permute-start.4 = (f32[10,2,2,128]{3,1,2,0:T(2,128)S(1)}, f32[10,2,2,128]{3,1,2,0:T(2,128)S(1)}, u32[]{:S(2)}, u32[]{:S(2)}) collective-permute-start(f32[10,2,2,128]{3,1,2,0:T(2,128)S(1)} %get-tuple-element.54), channel_id=1, source_target_pairs={{0,9},{1,10},{2,11},{3,12},{4,13},{5,14},{6,15},{8,17},{9,18},{10,... | collective-permute-start | bytes 61448 | tf_op jit(solution)/shard_map/ppermute | solution.py:29
  44.0 30.8 %collective-permute-start.10 = (f32[10,2,9,128]{3,1,2,0:T(2,128)}, f32[10,2,9,128]{3,1,2,0:T(2,128)}, u32[]{:S(2)}, u32[]{:S(2)}) collective-permute-start(f32[10,2,9,128]{3,1,2,0:T(2,128)} %get-tuple-element.56), channel_id=1, source_target_pairs={{8,0},{16,8},{24,16},{9,1},{17,9},{25,17},{10,2},{18,10},{26,18},{... | collective-permute-start | bytes 276488 | tf_op jit(solution)/shard_map/ppermute | solution.py:25
  46.1 32.4 %collective-permute-start.11 = (f32[10,2,2,128]{3,1,2,0:T(2,128)}, f32[10,2,2,128]{3,1,2,0:T(2,128)}, u32[]{:S(2)}, u32[]{:S(2)}) collective-permute-start(f32[10,2,2,128]{3,1,2,0:T(2,128)} %get-tuple-element.53), channel_id=1, source_target_pairs={{9,0},{10,1},{11,2},{12,3},{13,4},{14,5},{15,6},{17,8},{18,9},{19,... | collective-permute-start | bytes 61448 | tf_op jit(solution)/shard_map/ppermute | solution.py:32
  48.2 39.6 %collective-permute-start.8 = (f32[10,24,2,128]{3,1,2,0:T(8,128)S(1)}, f32[10,24,2,128]{3,1,2,0:T(8,128)S(1)}, u32[]{:S(2)}, u32[]{:S(2)}) collective-permute-start(f32[10,24,2,128]{3,1,2,0:T(8,128)S(1)} %get-tuple-element.58), channel_id=1, source_target_pairs={{1,0},{2,1},{3,2},{4,3},{5,4},{6,5},{7,6},{9,8},{10,9},{11,10},{12... | collective-permute-start | bytes 737288 | tf_op jit(solution)/shard_map/ppermute | solution.py:27
  50.6 9.1 %copy-start.4 = (pred[1,24,64]{2,1,0:T(8,128)(4,1)S(1)}, pred[1,24,64]{2,1,0:T(8,128)(4,1)}, u32[]{:S(2)}) copy-start(pred[1,24,64]{2,1,0:T(8,128)(4,1)} %get-tuple-element.38) | copy-start | bytes 4612
  50.6 9.1 %copy-start.5 = (pred[1,24,64]{2,1,0:T(8,128)(4,1)S(1)}, pred[1,24,64]{2,1,0:T(8,128)(4,1)}, u32[]{:S(2)}) copy-start(pred[1,24,64]{2,1,0:T(8,128)(4,1)} %get-tuple-element.39) | copy-start | bytes 4612
  50.6 9.1 %copy-start.6 = (pred[1,24,64]{2,1,0:T(8,128)(4,1)S(1)}, pred[1,24,64]{2,1,0:T(8,128)(4,1)}, u32[]{:S(2)}) copy-start(pred[1,24,64]{2,1,0:T(8,128)(4,1)} %get-tuple-element.40) | copy-start | bytes 4612
  50.6 9.1 %copy-start.7 = (pred[1,24,64]{2,1,0:T(8,128)(4,1)S(1)}, pred[1,24,64]{2,1,0:T(8,128)(4,1)}, u32[]{:S(2)}) copy-start(pred[1,24,64]{2,1,0:T(8,128)(4,1)} %get-tuple-element.41) | copy-start | bytes 4612
  50.7 37.1 %collective-permute-start.7 = (f32[10,24,2,128]{3,1,2,0:T(8,128)S(1)}, f32[10,24,2,128]{3,1,2,0:T(8,128)S(1)}, u32[]{:S(2)}, u32[]{:S(2)}) collective-permute-start(f32[10,24,2,128]{3,1,2,0:T(8,128)S(1)} %get-tuple-element.57), channel_id=1, source_target_pairs={{0,1},{1,2},{2,3},{3,4},{4,5},{5,6},{6,7},{8,9},{9,10},{10,11},{11... | collective-permute-start | bytes 737288 | tf_op jit(solution)/shard_map/ppermute | solution.py:26
  55.2 22.4 %collective-permute-start.5 = (f32[10,2,9,128]{3,1,2,0:T(2,128)S(1)}, f32[10,2,9,128]{3,1,2,0:T(2,128)}, u32[]{:S(2)}, u32[]{:S(2)}) collective-permute-start(f32[10,2,9,128]{3,1,2,0:T(2,128)S(1)} %get-tuple-element.55), channel_id=1, source_target_pairs={{0,8},{8,16},{16,24},{1,9},{9,17},{17,25},{2,10},{10,18},{18,26},{... | collective-permute-start | bytes 276488 | tf_op jit(solution)/shard_map/ppermute | solution.py:24
  59.1 15.7 %copy-start.2 = (f32[10,2,2,128]{3,1,2,0:T(2,128)S(1)}, f32[10,2,2,128]{3,1,2,0:T(2,128)}, u32[]{:S(2)}) copy-start(f32[10,2,2,128]{3,1,2,0:T(2,128)} %get-tuple-element.51) | copy-start | bytes 61444
  59.2 22.6 %copy-start.10 = (f32[24]{0:T(128)S(1)}, f32[24]{0:T(128)}, u32[]{:S(2)}) copy-start(f32[24]{0:T(128)} %get-tuple-element.186) | copy-start | bytes 292
  59.2 22.6 %copy-start.11 = (f32[24]{0:T(128)S(1)}, f32[24]{0:T(128)}, u32[]{:S(2)}) copy-start(f32[24]{0:T(128)} %get-tuple-element.187) | copy-start | bytes 292
  59.2 22.6 %copy-start.12 = (s32[24]{0:T(128)S(1)}, s32[24]{0:T(128)}, u32[]{:S(2)}) copy-start(s32[24]{0:T(128)} %get-tuple-element.188) | copy-start | bytes 292
  59.2 22.6 %copy-start.13 = (s32[24]{0:T(128)S(1)}, s32[24]{0:T(128)}, u32[]{:S(2)}) copy-start(s32[24]{0:T(128)} %get-tuple-element.189) | copy-start | bytes 292
  59.3 23.0 %copy-start.16 = (f32[9]{0:T(128)S(1)}, f32[9]{0:T(128)}, u32[]{:S(2)}) copy-start(f32[9]{0:T(128)} %get-tuple-element.190) | copy-start | bytes 112
  59.3 23.0 %copy-start.17 = (f32[9]{0:T(128)S(1)}, f32[9]{0:T(128)}, u32[]{:S(2)}) copy-start(f32[9]{0:T(128)} %get-tuple-element.191) | copy-start | bytes 112
  59.3 23.0 %copy-start.18 = (s32[9]{0:T(128)S(1)}, s32[9]{0:T(128)}, u32[]{:S(2)}) copy-start(s32[9]{0:T(128)} %get-tuple-element.192) | copy-start | bytes 112
  59.3 23.0 %copy-start.19 = (s32[9]{0:T(128)S(1)}, s32[9]{0:T(128)}, u32[]{:S(2)}) copy-start(s32[9]{0:T(128)} %get-tuple-element.193) | copy-start | bytes 112
  70.9 10.8 %all-to-all-start = ((bf16[8,2,1728]{2,1,0:T(2,128)(2,1)}), bf16[8,2,1728]{2,1,0:T(2,128)(2,1)S(1)}, u32[]{:S(2)}, u32[]{:S(2)}) async-start(bf16[8,2,1728]{2,1,0:T(2,128)(2,1)} %reshape.458), calls=%async_computation | async-start | bytes 114688 | tf_op jit(solution)/shard_map/all_to_all | solution.py:154
  74.7 10.8 %copy-start.3 = (f32[9,1,24,64]{3,2,1,0:T(8,128)}, f32[9,1,24,64]{3,2,1,0:T(8,128)S(1)}, u32[]{:S(2)}) copy-start(f32[9,1,24,64]{3,2,1,0:T(8,128)S(1)} %constant_dynamic-update-slice_fusion) | copy-start | bytes 165892
  74.8 6.9 %collective-permute-start.6 = (f32[10,2,2,128]{3,1,2,0:T(2,128)S(1)}, f32[10,2,2,128]{3,1,2,0:T(2,128)S(1)}, u32[]{:S(2)}, u32[]{:S(2)}) collective-permute-start(f32[10,2,2,128]{3,1,2,0:T(2,128)S(1)} %copy-done.2), channel_id=1, source_target_pairs={{1,8},{2,9},{3,10},{4,11},{5,12},{6,13},{7,14},{9,16},{10,17},{11,... | collective-permute-start | bytes 61448 | tf_op jit(solution)/shard_map/ppermute | solution.py:30
  82.4 3.2 %copy-start.8 = (f32[128]{0:T(128)S(1)}, f32[128]{0:T(128)}, u32[]{:S(2)}) copy-start(f32[128]{0:T(128)} %get-tuple-element.194) | copy-start | bytes 1540
  82.4 3.2 %copy-start.9 = (f32[128]{0:T(128)S(1)}, f32[128]{0:T(128)}, u32[]{:S(2)}) copy-start(f32[128]{0:T(128)} %get-tuple-element.195) | copy-start | bytes 1540
  82.4 3.2 %copy-start.14 = (s32[128]{0:T(128)S(1)}, s32[128]{0:T(128)}, u32[]{:S(2)}) copy-start(s32[128]{0:T(128)} %get-tuple-element.196) | copy-start | bytes 1540
  82.4 3.2 %copy-start.15 = (s32[128]{0:T(128)S(1)}, s32[128]{0:T(128)}, u32[]{:S(2)}) copy-start(s32[128]{0:T(128)} %get-tuple-element.197) | copy-start | bytes 1540
  100.5 13.5 %collective-permute-start.17 = (f32[9,2,2,128]{3,1,2,0:T(2,128)S(1)}, f32[9,2,2,128]{3,1,2,0:T(2,128)S(1)}, u32[]{:S(2)}, u32[]{:S(2)}) collective-permute-start(f32[9,2,2,128]{3,1,2,0:T(2,128)S(1)} %get-tuple-element.69), channel_id=1, source_target_pairs={{8,1},{9,2},{10,3},{11,4},{12,5},{13,6},{14,7},{16,9},{17,10},{18,... | collective-permute-start | bytes 55304 | tf_op jit(solution)/shard_map/ppermute | solution.py:31
  103.7 18.5 %collective-permute-start.18 = (f32[9,2,9,128]{3,1,2,0:T(2,128)S(1)}, f32[9,2,9,128]{3,1,2,0:T(2,128)S(1)}, u32[]{:S(2)}, u32[]{:S(2)}) collective-permute-start(f32[9,2,9,128]{3,1,2,0:T(2,128)S(1)} %get-tuple-element.72), channel_id=1, source_target_pairs={{8,0},{16,8},{24,16},{9,1},{17,9},{25,17},{10,2},{18,10},{26,18},{... | collective-permute-start | bytes 248840 | tf_op jit(solution)/shard_map/ppermute | solution.py:25
  105.6 19.6 %collective-permute-start.19 = (f32[9,2,2,128]{3,1,2,0:T(2,128)S(1)}, f32[9,2,2,128]{3,1,2,0:T(2,128)S(1)}, u32[]{:S(2)}, u32[]{:S(2)}) collective-permute-start(f32[9,2,2,128]{3,1,2,0:T(2,128)S(1)} %get-tuple-element.68), channel_id=1, source_target_pairs={{9,0},{10,1},{11,2},{12,3},{13,4},{14,5},{15,6},{17,8},{18,9},{19,... | collective-permute-start | bytes 55304 | tf_op jit(solution)/shard_map/ppermute | solution.py:32
  107.5 21.7 %collective-permute-start.16 = (f32[9,24,2,128]{3,1,2,0:T(8,128)S(1)}, f32[9,24,2,128]{3,1,2,0:T(8,128)S(1)}, u32[]{:S(2)}, u32[]{:S(2)}) collective-permute-start(f32[9,24,2,128]{3,1,2,0:T(8,128)S(1)} %get-tuple-element.74), channel_id=1, source_target_pairs={{1,0},{2,1},{3,2},{4,3},{5,4},{6,5},{7,6},{9,8},{10,9},{11,10},{12... | collective-permute-start | bytes 663560 | tf_op jit(solution)/shard_map/ppermute | solution.py:27
  109.5 19.8 %collective-permute-start.15 = (f32[9,24,2,128]{3,1,2,0:T(8,128)S(1)}, f32[9,24,2,128]{3,1,2,0:T(8,128)S(1)}, u32[]{:S(2)}, u32[]{:S(2)}) collective-permute-start(f32[9,24,2,128]{3,1,2,0:T(8,128)S(1)} %get-tuple-element.73), channel_id=1, source_target_pairs={{0,1},{1,2},{2,3},{3,4},{4,5},{5,6},{6,7},{8,9},{9,10},{10,11},{11... | collective-permute-start | bytes 663560 | tf_op jit(solution)/shard_map/ppermute | solution.py:26
  114.0 5.1 %collective-permute-start.12 = (f32[9,2,2,128]{3,1,2,0:T(2,128)S(1)}, f32[9,2,2,128]{3,1,2,0:T(2,128)S(1)}, u32[]{:S(2)}, u32[]{:S(2)}) collective-permute-start(f32[9,2,2,128]{3,1,2,0:T(2,128)S(1)} %get-tuple-element.70), channel_id=1, source_target_pairs={{0,9},{1,10},{2,11},{3,12},{4,13},{5,14},{6,15},{8,17},{9,18},{10,... | collective-permute-start | bytes 55304 | tf_op jit(solution)/shard_map/ppermute | solution.py:29
  119.1 6.1 %collective-permute-start.13 = (f32[9,2,9,128]{3,1,2,0:T(2,128)S(1)}, f32[9,2,9,128]{3,1,2,0:T(2,128)S(1)}, u32[]{:S(2)}, u32[]{:S(2)}) collective-permute-start(f32[9,2,9,128]{3,1,2,0:T(2,128)S(1)} %get-tuple-element.71), channel_id=1, source_target_pairs={{0,8},{8,16},{16,24},{1,9},{9,17},{17,25},{2,10},{10,18},{18,26},{... | collective-permute-start | bytes 248840 | tf_op jit(solution)/shard_map/ppermute | solution.py:24
  122.2 7.0 %collective-permute-start.14 = (f32[9,2,2,128]{3,1,2,0:T(2,128)S(1)}, f32[9,2,2,128]{3,1,2,0:T(2,128)S(1)}, u32[]{:S(2)}, u32[]{:S(2)}) collective-permute-start(f32[9,2,2,128]{3,1,2,0:T(2,128)S(1)} %get-tuple-element.67), channel_id=1, source_target_pairs={{1,8},{2,9},{3,10},{4,11},{5,12},{6,13},{7,14},{9,16},{10,17},{11,... | collective-permute-start | bytes 55304 | tf_op jit(solution)/shard_map/ppermute | solution.py:30
  131.8 12.5 %collective-permute-start.25 = (f32[9,2,2,128]{3,1,2,0:T(2,128)S(1)}, f32[9,2,2,128]{3,1,2,0:T(2,128)S(1)}, u32[]{:S(2)}, u32[]{:S(2)}) collective-permute-start(f32[9,2,2,128]{3,1,2,0:T(2,128)S(1)} %get-tuple-element.61), channel_id=1, source_target_pairs={{8,1},{9,2},{10,3},{11,4},{12,5},{13,6},{14,7},{16,9},{17,10},{18,... | collective-permute-start | bytes 55304 | tf_op jit(solution)/shard_map/ppermute | solution.py:31
  134.0 19.1 %collective-permute-start.26 = (f32[9,2,9,128]{3,1,2,0:T(2,128)S(1)}, f32[9,2,9,128]{3,1,2,0:T(2,128)S(1)}, u32[]{:S(2)}, u32[]{:S(2)}) collective-permute-start(f32[9,2,9,128]{3,1,2,0:T(2,128)S(1)} %get-tuple-element.64), channel_id=1, source_target_pairs={{8,0},{16,8},{24,16},{9,1},{17,9},{25,17},{10,2},{18,10},{26,18},{... | collective-permute-start | bytes 248840 | tf_op jit(solution)/shard_map/ppermute | solution.py:25
  135.9 19.1 %collective-permute-start.27 = (f32[9,2,2,128]{3,1,2,0:T(2,128)S(1)}, f32[9,2,2,128]{3,1,2,0:T(2,128)S(1)}, u32[]{:S(2)}, u32[]{:S(2)}) collective-permute-start(f32[9,2,2,128]{3,1,2,0:T(2,128)S(1)} %get-tuple-element.60), channel_id=1, source_target_pairs={{9,0},{10,1},{11,2},{12,3},{13,4},{14,5},{15,6},{17,8},{18,9},{19,... | collective-permute-start | bytes 55304 | tf_op jit(solution)/shard_map/ppermute | solution.py:32
  137.9 22.1 %collective-permute-start.24 = (f32[9,24,2,128]{3,1,2,0:T(8,128)S(1)}, f32[9,24,2,128]{3,1,2,0:T(8,128)S(1)}, u32[]{:S(2)}, u32[]{:S(2)}) collective-permute-start(f32[9,24,2,128]{3,1,2,0:T(8,128)S(1)} %get-tuple-element.66), channel_id=1, source_target_pairs={{1,0},{2,1},{3,2},{4,3},{5,4},{6,5},{7,6},{9,8},{10,9},{11,10},{12... | collective-permute-start | bytes 663560 | tf_op jit(solution)/shard_map/ppermute | solution.py:27
  140.2 19.8 %collective-permute-start.23 = (f32[9,24,2,128]{3,1,2,0:T(8,128)S(1)}, f32[9,24,2,128]{3,1,2,0:T(8,128)S(1)}, u32[]{:S(2)}, u32[]{:S(2)}) collective-permute-start(f32[9,24,2,128]{3,1,2,0:T(8,128)S(1)} %get-tuple-element.65), channel_id=1, source_target_pairs={{0,1},{1,2},{2,3},{3,4},{4,5},{5,6},{6,7},{8,9},{9,10},{10,11},{11... | collective-permute-start | bytes 663560 | tf_op jit(solution)/shard_map/ppermute | solution.py:26
  144.4 5.1 %collective-permute-start.20 = (f32[9,2,2,128]{3,1,2,0:T(2,128)S(1)}, f32[9,2,2,128]{3,1,2,0:T(2,128)S(1)}, u32[]{:S(2)}, u32[]{:S(2)}) collective-permute-start(f32[9,2,2,128]{3,1,2,0:T(2,128)S(1)} %get-tuple-element.62), channel_id=1, source_target_pairs={{0,9},{1,10},{2,11},{3,12},{4,13},{5,14},{6,15},{8,17},{9,18},{10,... | collective-permute-start | bytes 55304 | tf_op jit(solution)/shard_map/ppermute | solution.py:29
  149.4 5.6 %collective-permute-start.21 = (f32[9,2,9,128]{3,1,2,0:T(2,128)S(1)}, f32[9,2,9,128]{3,1,2,0:T(2,128)S(1)}, u32[]{:S(2)}, u32[]{:S(2)}) collective-permute-start(f32[9,2,9,128]{3,1,2,0:T(2,128)S(1)} %get-tuple-element.63), channel_id=1, source_target_pairs={{0,8},{8,16},{16,24},{1,9},{9,17},{17,25},{2,10},{10,18},{18,26},{... | collective-permute-start | bytes 248840 | tf_op jit(solution)/shard_map/ppermute | solution.py:24
  153.1 6.9 %collective-permute-start.22 = (f32[9,2,2,128]{3,1,2,0:T(2,128)S(1)}, f32[9,2,2,128]{3,1,2,0:T(2,128)S(1)}, u32[]{:S(2)}, u32[]{:S(2)}) collective-permute-start(f32[9,2,2,128]{3,1,2,0:T(2,128)S(1)} %get-tuple-element.59), channel_id=1, source_target_pairs={{1,8},{2,9},{3,10},{4,11},{5,12},{6,13},{7,14},{9,16},{10,17},{11,... | collective-permute-start | bytes 55304 | tf_op jit(solution)/shard_map/ppermute | solution.py:30

commit v2 on v1

--- a/solution.py
+++ b/solution.py
@@ -8,32 +8,15 @@
     return [(i, i + s) for i in range(n) if 0 <= i + s < n]
 
 
-def grid_pairs(nx, ny, dx, dy):
-    pairs = []
-    for a in range(nx):
-        for b in range(ny):
-            if 0 <= a + dx < nx and 0 <= b + dy < ny:
-                pairs.append((a * ny + b, (a + dx) * ny + b + dy))
-    return pairs
-
-
 def tile_halo(field, width):
     nx, ny = lax.axis_size("gx"), lax.axis_size("gy")
     w = width
-    lo_x, hi_x = field[:, -w:], field[:, :w]
-    from_left = lax.ppermute(lo_x, "gx", shifted(nx, 1))
-    from_right = lax.ppermute(hi_x, "gx", shifted(nx, -1))
-    from_below = lax.ppermute(field[:, :, -w:], "gy", shifted(ny, 1))
-    from_above = lax.ppermute(field[:, :, :w], "gy", shifted(ny, -1))
-    both = ("gx", "gy")
-    c_mm = lax.ppermute(field[:, -w:, -w:], both, grid_pairs(nx, ny, 1, 1))
-    c_mp = lax.ppermute(field[:, -w:, :w], both, grid_pairs(nx, ny, 1, -1))
-    c_pm = lax.ppermute(field[:, :w, -w:], both, grid_pairs(nx, ny, -1, 1))
-    c_pp = lax.ppermute(field[:, :w, :w], both, grid_pairs(nx, ny, -1, -1))
-    low = jnp.concatenate([c_mm, from_left, c_mp], axis=2)
-    mid = jnp.concatenate([from_below, field, from_above], axis=2)
-    high = jnp.concatenate([c_pm, from_right, c_pp], axis=2)
-    return jnp.concatenate([low, mid, high], axis=1)
+    from_left = lax.ppermute(field[:, -w:], "gx", shifted(nx, 1))
+    from_right = lax.ppermute(field[:, :w], "gx", shifted(nx, -1))
+    wide = jnp.concatenate([from_left, field, from_right], axis=1)
+    from_below = lax.ppermute(wide[:, :, -w:], "gy", shifted(ny, 1))
+    from_above = lax.ppermute(wide[:, :, :w], "gy", shifted(ny, -1))
+    return jnp.concatenate([from_below, wide, from_above], axis=2)
 
 
 def strip_halo(field, width):
@@ -144,7 +127,7 @@
     rows_each = reg_y // count_y
 
     rho_r, lam_r, mu_r = lookup(region_material, material_table)
-    coef_r = 0.6 / rho_r
+    coef_r, lam_r, mu_r = lax.optimization_barrier((0.6 / rho_r, lam_r, mu_r))
     reg_ext = strip_halo(jnp.concatenate([region_state, coef_r[None]], 0), 2)
     region_next = step_wide(
         reg_ext, reg_ext[9, 1:-1], region_state[3:], lam_r, mu_r, 0.6, 3.0, True
@@ -164,7 +147,7 @@
     relax = (0.1 + 0.4 * jnp.maximum(along_x[:, None], along_y[None, :]))[:, :, None]
 
     rho_f, lam_f, mu_f = lookup(fine_material, material_table)
-    coef_f = 0.2 / rho_f
+    coef_f, lam_f, mu_f = lax.optimization_barrier((0.2 / rho_f, lam_f, mu_f))
     ext = tile_halo(jnp.concatenate([fine_state, coef_f[None]], 0), 2)
     coef_ext = ext[9, 1:-1, 1:-1]
     state = fine_state

time: 165 us -> 129 us (0.78)
  the two profiles are of different devices: /device:TPU:19 before, /device:TPU:1 now
where the time goes in v2:
time: 129 us; the launch traced here: 128 us
  starting transfers between devices  50.7 us (39%)
  other arithmetic  40.4 us (31%)
  waiting for transfers between devices  22.4 us (17%)
  local copies, waits for them, and re-layouts  7.02 us (5%)
  matrix products  5.73 us (4%)
  between operations  1.48 us (1%)
    select_n x2, other arithmetic, lookup(): shear = jnp.where(match, table[2, material], shear)  11.4 us
    ppermute x3, waiting for transfers between devices, tile_halo(): from_above = lax.ppermute(wide[:, :, :w], 'gy', shifted(ny, -1))  11.4 us
    ppermute x3, starting transfers between devices, tile_halo(): from_below = lax.ppermute(wide[:, :, -w:], 'gy', shifted(ny, 1))  11.4 us
    ppermute x3, starting transfers between devices, tile_halo(): from_left = lax.ppermute(field[:, -w:], 'gx', shifted(nx, 1))  10.4 us
    select_n x2, other arithmetic, lookup(): lam = jnp.where(match, table[1, material], lam)  10.3 us
    ppermute x2, starting transfers between devices, strip_halo(): lax.ppermute(field, both, shifted(n, d))  9.02 us
    ppermute x3, waiting for transfers between devices, tile_halo(): from_right = lax.ppermute(field[:, :w], 'gx', shifted(nx, -1))  7.45 us
    ppermute x3, starting transfers between devices, tile_halo(): from_above = lax.ppermute(wide[:, :, :w], 'gy', shifted(ny, -1))  5.94 us
  transfers between devices with their start and end apart: 17, of which 9 were waited for; matrix products, arithmetic and copies ran while one was open for 19% of the time, Pallas kernels for 0%

profile of v2, /device:TPU:1, one launch (start us, length us, event | category | flops | bytes accessed | tf_op | source)
XLA Modules:
  0.0 127.7 jit_solution(10791031990923709152)
XLA Ops:
  0.7 1.5 %fusion.253 = (f32[1,1]{1,0:T(1,128)}, f32[1,1]{1,0:T(1,128)}, f32[1,1]{1,0:T(1,128)}, f32[1,1]{1,0:T(1,128)}, f32[1,1]{1,0:T(1,128)}) fusion(f32[3,8]{1,0:T(4,128)} %param.9), kind=kLoop, calls=%fused_computation.501 | loop fusion | bytes 40 | tf_op jit(solution)/shard_map/slice | solution.py:40
  2.2 2.1 %fusion.252 = (f32[1,1]{1,0:T(1,128)}, f32[1,1]{1,0:T(1,128)}, f32[1,1]{1,0:T(1,128)}, f32[1,1]{1,0:T(1,128)}, f32[1,1]{1,0:T(1,128)}, /*index=5*/f32[1,1]{1,0:T...) fusion(f32[3,8]{1,0:T(4,128)} %param.9), kind=kLoop, calls=%fused_computation.500 | loop fusion | bytes 152 | tf_op jit(solution)/shard_map/slice | solution.py:41
  4.3 5.6 %select_select_fusion.2 = (f32[1,24,64]{2,1,0:T(8,128)S(1)}, pred[1,24,64]{2,1,0:T(8,128)(4,1)S(1)}, pred[1,24,64]{2,1,0:T(8,128)(4,1)S(1)}, pred[1,24,64]{2,1,0...) fusion(f32[]{:T(128)} %bitcast.23, f32[]{:T(128)} %bitcast.22, ...), kind=kLoop, calls=%fused_computation.375 | loop fusion | flops 24576 | bytes 24608 | tf_op jit(solution)/shard_map/jit(_where)/select_n | solution.py:42
  9.8 5.1 %select_select_fusion.3 = f32[1,24,64]{2,1,0:T(8,128)S(1)} fusion(pred[1,24,64]{2,1,0:T(8,128)(4,1)S(1)} %get-tuple-element.50, pred[1,24,64]{2,1,0:T(8,128)(4,1)S(1)} %get-tuple-element.49, pred[1,24,64]{2,1,0:T(8,128)(4,1)S(1)} %get-tuple-element.48, pred[1,24,64]{2,1,0:T(8,128)(4,1)S(1)} %get-tuple-element.47, ...), kind=kLoop, calls=%fused_computation.376 | loop fusion | flops 12288 | bytes 18464 | tf_op jit(solution)/shard_map/jit(_where)/select_n | solution.py:41
  15.0 5.1 %select_divide_fusion.1 = f32[1,24,64]{2,1,0:T(8,128)S(1)} fusion(pred[1,24,64]{2,1,0:T(8,128)(4,1)S(1)} %get-tuple-element.50, pred[1,24,64]{2,1,0:T(8,128)(4,1)S(1)} %get-tuple-element.49, pred[1,24,64]{2,1,0:T(8,128)(4,1)S(1)} %get-tuple-element.48, pred[1,24,64]{2,1,0:T(8,128)(4,1)S(1)} %get-tuple-element.47, ...), kind=kLoop, calls=%fused_computation.377 | loop fusion | flops 13824 | bytes 18464 | tf_op jit(solution)/shard_map/div | solution.py:130
  20.0 0.9 pad_maximum_fusion.34
  20.9 1.3 %collective-permute-start.2 = (f32[10,1,24,64]{3,2,1,0:T(8,128)S(1)}, f32[10,1,24,64]{3,2,1,0:T(8,128)S(1)}, u32[]{:S(2)}, u32[]{:S(2)}) collective-permute-start(f32[10,1,24,64]{3,2,1,0:T(8,128)S(1)} %pad_maximum_fusion.34), channel_id=1, source_target_pairs={{2,0},{3,1},{4,2},{5,3},{6,4},{7,5},{8,6},{9,7},{10,8},{11,9},{12,... | collective-permute-start | bytes 184328 | tf_op jit(solution)/shard_map/ppermute | solution.py:28
  22.2 4.6 %collective-permute-start.3 = (f32[10,1,24,64]{3,2,1,0:T(8,128)S(1)}, f32[10,1,24,64]{3,2,1,0:T(8,128)S(1)}, u32[]{:S(2)}, u32[]{:S(2)}) collective-permute-start(f32[10,1,24,64]{3,2,1,0:T(8,128)S(1)} %pad_maximum_fusion.34), channel_id=1, source_target_pairs={{0,2},{1,3},{2,4},{3,5},{4,6},{5,7},{6,8},{7,9},{8,10},{9,11},{10,... | collective-permute-start | bytes 184328 | tf_op jit(solution)/shard_map/ppermute | solution.py:27
  26.8 2.9 %collective-permute-start.1 = (f32[10,1,24,64]{3,2,1,0:T(8,128)S(1)}, f32[10,1,24,64]{3,2,1,0:T(8,128)S(1)}, u32[]{:S(2)}, u32[]{:S(2)}) collective-permute-start(f32[10,1,24,64]{3,2,1,0:T(8,128)S(1)} %pad_maximum_fusion.34), channel_id=1, source_target_pairs={{1,0},{2,1},{3,2},{4,3},{5,4},{6,5},{7,6},{8,7},{9,8},{10,9},{11,1... | collective-permute-start | bytes 184328 | tf_op jit(solution)/shard_map/ppermute | solution.py:28
  29.7 4.4 %collective-permute-start = (f32[10,1,24,64]{3,2,1,0:T(8,128)S(1)}, f32[10,1,24,64]{3,2,1,0:T(8,128)S(1)}, u32[]{:S(2)}, u32[]{:S(2)}) collective-permute-start(f32[10,1,24,64]{3,2,1,0:T(8,128)S(1)} %pad_maximum_fusion.34), channel_id=1, source_target_pairs={{0,1},{1,2},{2,3},{3,4},{4,5},{5,6},{6,7},{7,8},{8,9},{9,10},{10,1... | collective-permute-start | bytes 184328 | tf_op jit(solution)/shard_map/ppermute | solution.py:27
  34.2 5.9 %select_select_fusion = (f32[24,9,128]{2,0,1:T(8,128)S(1)}, pred[24,9,128]{2,0,1:T(8,128)(4,1)S(1)}, pred[24,9,128]{2,0,1:T(8,128)(4,1)S(1)}, pred[24,9,128]{2,0...) fusion(f32[]{:T(128)} %bitcast.23, f32[]{:T(128)} %bitcast.22, ...), kind=kLoop, calls=%fused_computation.273 | loop fusion | flops 442368 | bytes 442400 | tf_op jit(solution)/shard_map/jit(_where)/select_n | solution.py:42
  40.0 5.2 %select_select_fusion.1 = f32[24,9,128]{2,0,1:T(8,128)S(1)} fusion(pred[24,9,128]{2,0,1:T(8,128)(4,1)S(1)} %get-tuple-element.41, pred[24,9,128]{2,0,1:T(8,128)(4,1)S(1)} %get-tuple-element.40, pred[24,9,128]{2,0,1:T(8,128)(4,1)S(1)} %get-tuple-element.39, pred[24,9,128]{2,0,1:T(8,128)(4,1)S(1)} %get-tuple-element.38, ...), kind=kLoop, calls=%fused_computation.274 | loop fusion | flops 221184 | bytes 331808 | tf_op jit(solution)/shard_map/jit(_where)/select_n | solution.py:41
  45.2 5.1 %select_divide_fusion = f32[24,9,128]{2,0,1:T(8,128)S(1)} fusion(pred[24,9,128]{2,0,1:T(8,128)(4,1)S(1)} %get-tuple-element.41, pred[24,9,128]{2,0,1:T(8,128)(4,1)S(1)} %get-tuple-element.40, pred[24,9,128]{2,0,1:T(8,128)(4,1)S(1)} %get-tuple-element.39, pred[24,9,128]{2,0,1:T(8,128)(4,1)S(1)} %get-tuple-element.38, ...), kind=kLoop, calls=%fused_computation.275 | loop fusion | flops 248832 | bytes 331808 | tf_op jit(solution)/shard_map/div | solution.py:150
  50.5 3.2 %collective-permute-start.4 = (f32[10,2,9,128]{3,1,2,0:T(2,128)S(1)}, f32[10,2,9,128]{3,1,2,0:T(2,128)S(1)}, u32[]{:S(2)}, u32[]{:S(2)}) collective-permute-start(f32[10,2,9,128]{3,1,2,0:T(2,128)S(1)} %get-tuple-element.66), channel_id=1, source_target_pairs={{0,8},{8,16},{16,24},{1,9},{9,17},{17,25},{2,10},{10,18},{18,26},{... | collective-permute-start | bytes 276488 | tf_op jit(solution)/shard_map/ppermute | solution.py:14
  54.0 1.3 %collective-permute-start.5 = (f32[10,2,9,128]{3,1,2,0:T(2,128)S(1)}, f32[10,2,9,128]{3,1,2,0:T(2,128)S(1)}, u32[]{:S(2)}, u32[]{:S(2)}) collective-permute-start(f32[10,2,9,128]{3,1,2,0:T(2,128)S(1)} %get-tuple-element.67), channel_id=1, source_target_pairs={{8,0},{16,8},{24,16},{9,1},{17,9},{25,17},{10,2},{18,10},{26,18},{... | collective-permute-start | bytes 276488 | tf_op jit(solution)/shard_map/ppermute | solution.py:15
  56.6 0.8 reshape.458
  57.3 5.9 %all-to-all-start = ((bf16[8,2,1728]{2,1,0:T(2,128)(2,1)}), bf16[8,2,1728]{2,1,0:T(2,128)(2,1)S(1)}, u32[]{:S(2)}, u32[]{:S(2)}) async-start(bf16[8,2,1728]{2,1,0:T(2,128)(2,1)} %reshape.458), calls=%async_computation | async-start | bytes 114688 | tf_op jit(solution)/shard_map/all_to_all | solution.py:137
  63.4 3.5 %collective-permute-start.6 = (f32[10,28,2,128]{3,1,2,0:T(8,128)S(1)}, f32[10,28,2,128]{3,1,2,0:T(8,128)S(1)}, u32[]{:S(2)}, u32[]{:S(2)}) collective-permute-start(f32[10,28,2,128]{3,1,2,0:T(8,128)S(1)} %get-tuple-element.60), channel_id=1, source_target_pairs={{0,1},{1,2},{2,3},{3,4},{4,5},{5,6},{6,7},{8,9},{9,10},{10,11},{11... | collective-permute-start | bytes 860168 | tf_op jit(solution)/shard_map/ppermute | solution.py:17
  66.9 1.9 %collective-permute-start.7 = (f32[10,28,2,128]{3,1,2,0:T(8,128)S(1)}, f32[10,28,2,128]{3,1,2,0:T(8,128)S(1)}, u32[]{:S(2)}, u32[]{:S(2)}) collective-permute-start(f32[10,28,2,128]{3,1,2,0:T(8,128)S(1)} %get-tuple-element.61), channel_id=1, source_target_pairs={{1,0},{2,1},{3,2},{4,3},{5,4},{6,5},{7,6},{9,8},{10,9},{11,10},{12... | collective-permute-start | bytes 860168 | tf_op jit(solution)/shard_map/ppermute | solution.py:18
  68.9 0.1 reshape.459
  69.0 0.5 convolution_bitcast_fusion.1
  69.5 3.1 %convolution_bitcast_fusion = f32[18,24,9,64]{3,2,1,0:T(8,128)S(1)} fusion(f32[18,24,3,64]{3,1,2,0:T(8,128)S(1)} %convolution_bitcast_fusion.1, f32[9]{0:T(128)S(1)} %get-tuple-element.187, s32[9]{0:T(128)S(1)} %get-tuple-element.190, f32[9]{0:T(128)S(1)} %get-tuple-element.188, s32[9]{0:T(128)S(1)} %get-tuple-element.189), kind=kOutput, calls=%fused_computation.3 | convolution fusion | flops 8958087 | bytes 1327248 | tf_op jit(solution)/shard_map/gb,cfbz->cfgz/dot_general | solution.py:141
  72.6 2.2 %fusion = f32[18,24,9,128]{3,1,2,0:T(8,128)S(1)} fusion(f32[18,24,9,64]{3,2,1,0:T(8,128)S(1)} %convolution_bitcast_fusion, f32[128]{0:T(128)S(1)} %get-tuple-element.191, s32[128]{0:T(128)S(1)} %get-tuple-element.194, f32[128]{0:T(128)S(1)} %get-tuple-element.192, s32[128]{0:T(128)S(1)} %get-tuple-element.193), kind=kOutput, calls=%fused_computation.1 | convolution fusion | flops 382246912 | bytes 2988032 | tf_op jit(solution)/shard_map/kz,cfgz->cfgk/dot_general | solution.py:142
  74.8 1.3 %collective-permute-done.7 = f32[10,28,2,128]{3,1,2,0:T(8,128)S(1)} collective-permute-done((f32[10,28,2,128]{3,1,2,0:T(8,128)S(1)}, f32[10,28,2,128]{3,1,2,0:T(8,128)S(1)}, u32[]{:S(2)}, u32[]{:S(2)}) %collective-permute-start.7) | collective-permute-done | bytes 286752 | tf_op jit(solution)/shard_map/ppermute | solution.py:18
  76.3 0.2 fusion.228
  76.5 0.3 pad_maximum_fusion
  76.8 0.1 fusion.40
  77.0 0.1 fusion.50
  77.1 0.1 fusion.45
  77.2 0.1 slice_add_fusion.2
  77.6 0.1 bitcast_dynamic-update-slice_fusion.2
  78.0 0.1 slice_bitcast_fusion.18
  78.3 0.3 multiply_add_fusion.2
  78.7 4.0 %collective-permute-start.8 = (f32[9,2,9,128]{3,1,2,0:T(2,128)S(1)}, f32[9,2,9,128]{3,1,2,0:T(2,128)S(1)}, u32[]{:S(2)}, u32[]{:S(2)}) collective-permute-start(f32[9,2,9,128]{3,1,2,0:T(2,128)S(1)} %get-tuple-element.70), channel_id=1, source_target_pairs={{0,8},{8,16},{16,24},{1,9},{9,17},{17,25},{2,10},{10,18},{18,26},{... | collective-permute-start | bytes 248840 | tf_op jit(solution)/shard_map/ppermute | solution.py:14
  82.7 1.3 %collective-permute-start.9 = (f32[9,2,9,128]{3,1,2,0:T(2,128)S(1)}, f32[9,2,9,128]{3,1,2,0:T(2,128)S(1)}, u32[]{:S(2)}, u32[]{:S(2)}) collective-permute-start(f32[9,2,9,128]{3,1,2,0:T(2,128)S(1)} %get-tuple-element.71), channel_id=1, source_target_pairs={{8,0},{16,8},{24,16},{9,1},{17,9},{25,17},{10,2},{18,10},{26,18},{... | collective-permute-start | bytes 248840 | tf_op jit(solution)/shard_map/ppermute | solution.py:15
  84.0 0.2 collective-permute-done.8
  84.1 3.7 %collective-permute-done.9 = f32[9,2,9,128]{3,1,2,0:T(2,128)S(1)} collective-permute-done((f32[9,2,9,128]{3,1,2,0:T(2,128)S(1)}, f32[9,2,9,128]{3,1,2,0:T(2,128)S(1)}, u32[]{:S(2)}, u32[]{:S(2)}) %collective-permute-start.9) | collective-permute-done | bytes 82976 | tf_op jit(solution)/shard_map/ppermute | solution.py:15
  88.0 4.7 %collective-permute-start.10 = (f32[9,28,2,128]{3,1,2,0:T(8,128)S(1)}, f32[9,28,2,128]{3,1,2,0:T(8,128)S(1)}, u32[]{:S(2)}, u32[]{:S(2)}) collective-permute-start(f32[9,28,2,128]{3,1,2,0:T(8,128)S(1)} %get-tuple-element.64), channel_id=1, source_target_pairs={{0,1},{1,2},{2,3},{3,4},{4,5},{5,6},{6,7},{8,9},{9,10},{10,11},{11... | collective-permute-start | bytes 774152 | tf_op jit(solution)/shard_map/ppermute | solution.py:17
  92.6 2.1 %collective-permute-start.11 = (f32[9,28,2,128]{3,1,2,0:T(8,128)S(1)}, f32[9,28,2,128]{3,1,2,0:T(8,128)S(1)}, u32[]{:S(2)}, u32[]{:S(2)}) collective-permute-start(f32[9,28,2,128]{3,1,2,0:T(8,128)S(1)} %get-tuple-element.65), channel_id=1, source_target_pairs={{1,0},{2,1},{3,2},{4,3},{5,4},{6,5},{7,6},{9,8},{10,9},{11,10},{12... | collective-permute-start | bytes 774152 | tf_op jit(solution)/shard_map/ppermute | solution.py:18
  94.8 1.5 %collective-permute-done.10 = f32[9,28,2,128]{3,1,2,0:T(8,128)S(1)} collective-permute-done((f32[9,28,2,128]{3,1,2,0:T(8,128)S(1)}, f32[9,28,2,128]{3,1,2,0:T(8,128)S(1)}, u32[]{:S(2)}, u32[]{:S(2)}) %collective-permute-start.10) | collective-permute-done | bytes 258080 | tf_op jit(solution)/shard_map/ppermute | solution.py:17
  96.3 4.8 %collective-permute-done.11 = f32[9,28,2,128]{3,1,2,0:T(8,128)S(1)} collective-permute-done((f32[9,28,2,128]{3,1,2,0:T(8,128)S(1)}, f32[9,28,2,128]{3,1,2,0:T(8,128)S(1)}, u32[]{:S(2)}, u32[]{:S(2)}) %collective-permute-start.11) | collective-permute-done | bytes 258080 | tf_op jit(solution)/shard_map/ppermute | solution.py:18
  101.5 0.3 pad_maximum_fusion.1
  101.8 0.1 fusion.34
  102.0 0.1 fusion.29
  102.1 0.1 fusion.24
  102.6 0.1 fusion.118
  103.2 0.1 fusion.91
  103.3 0.3 multiply_add_fusion.1
  103.7 3.2 %collective-permute-start.12 = (f32[9,2,9,128]{3,1,2,0:T(2,128)S(1)}, f32[9,2,9,128]{3,1,2,0:T(2,128)S(1)}, u32[]{:S(2)}, u32[]{:S(2)}) collective-permute-start(f32[9,2,9,128]{3,1,2,0:T(2,128)S(1)} %get-tuple-element.68), channel_id=1, source_target_pairs={{0,8},{8,16},{16,24},{1,9},{9,17},{17,25},{2,10},{10,18},{18,26},{... | collective-permute-start | bytes 248840 | tf_op jit(solution)/shard_map/ppermute | solution.py:14
  106.9 1.3 %collective-permute-start.13 = (f32[9,2,9,128]{3,1,2,0:T(2,128)S(1)}, f32[9,2,9,128]{3,1,2,0:T(2,128)S(1)}, u32[]{:S(2)}, u32[]{:S(2)}) collective-permute-start(f32[9,2,9,128]{3,1,2,0:T(2,128)S(1)} %get-tuple-element.69), channel_id=1, source_target_pairs={{8,0},{16,8},{24,16},{9,1},{17,9},{25,17},{10,2},{18,10},{26,18},{... | collective-permute-start | bytes 248840 | tf_op jit(solution)/shard_map/ppermute | solution.py:15
  108.2 0.2 collective-permute-done.12
  108.3 3.7 %collective-permute-done.13 = f32[9,2,9,128]{3,1,2,0:T(2,128)S(1)} collective-permute-done((f32[9,2,9,128]{3,1,2,0:T(2,128)S(1)}, f32[9,2,9,128]{3,1,2,0:T(2,128)S(1)}, u32[]{:S(2)}, u32[]{:S(2)}) %collective-permute-start.13) | collective-permute-done | bytes 82976 | tf_op jit(solution)/shard_map/ppermute | solution.py:15
  112.2 3.2 %collective-permute-start.14 = (f32[9,28,2,128]{3,1,2,0:T(8,128)S(1)}, f32[9,28,2,128]{3,1,2,0:T(8,128)S(1)}, u32[]{:S(2)}, u32[]{:S(2)}) collective-permute-start(f32[9,28,2,128]{3,1,2,0:T(8,128)S(1)} %get-tuple-element.62), channel_id=1, source_target_pairs={{0,1},{1,2},{2,3},{3,4},{4,5},{5,6},{6,7},{8,9},{9,10},{10,11},{11... | collective-permute-start | bytes 774152 | tf_op jit(solution)/shard_map/ppermute | solution.py:17
  115.4 1.9 %collective-permute-start.15 = (f32[9,28,2,128]{3,1,2,0:T(8,128)S(1)}, f32[9,28,2,128]{3,1,2,0:T(8,128)S(1)}, u32[]{:S(2)}, u32[]{:S(2)}) collective-permute-start(f32[9,28,2,128]{3,1,2,0:T(8,128)S(1)} %get-tuple-element.63), channel_id=1, source_target_pairs={{1,0},{2,1},{3,2},{4,3},{5,4},{6,5},{7,6},{9,8},{10,9},{11,10},{12... | collective-permute-start | bytes 774152 | tf_op jit(solution)/shard_map/ppermute | solution.py:18
  117.3 1.7 %collective-permute-done.14 = f32[9,28,2,128]{3,1,2,0:T(8,128)S(1)} collective-permute-done((f32[9,28,2,128]{3,1,2,0:T(8,128)S(1)}, f32[9,28,2,128]{3,1,2,0:T(8,128)S(1)}, u32[]{:S(2)}, u32[]{:S(2)}) %collective-permute-start.14) | collective-permute-done | bytes 258080 | tf_op jit(solution)/shard_map/ppermute | solution.py:17
  119.0 5.3 %collective-permute-done.15 = f32[9,28,2,128]{3,1,2,0:T(8,128)S(1)} collective-permute-done((f32[9,28,2,128]{3,1,2,0:T(8,128)S(1)}, f32[9,28,2,128]{3,1,2,0:T(8,128)S(1)}, u32[]{:S(2)}, u32[]{:S(2)}) %collective-permute-start.15) | collective-permute-done | bytes 258080 | tf_op jit(solution)/shard_map/ppermute | solution.py:18
  124.6 0.1 fusion.224
  124.7 0.3 pad_maximum_fusion.2
  125.0 0.1 fusion.18
  125.2 0.1 fusion.13
  125.3 0.1 fusion.8
  125.8 0.1 fusion.84
  126.4 0.1 fusion.57
  126.5 1.2 multiply_add_fusion
  (102 shorter events, 5.1 us)
Async XLA Ops:
  0.6 53.2 %copy-start.1 = (f32[9,1,24,64]{3,2,1,0:T(8,128)S(1)}, f32[9,1,24,64]{3,2,1,0:T(8,128)}, u32[]{:S(2)}) copy-start(f32[9,1,24,64]{3,2,1,0:T(8,128)} %param.5) | copy-start | bytes 165892
  0.6 49.7 %copy-start = (f32[9,24,9,128]{3,1,2,0:T(8,128)S(1)}, f32[9,24,9,128]{3,1,2,0:T(8,128)}, u32[]{:S(2)}) copy-start(f32[9,24,9,128]{3,1,2,0:T(8,128)} %param.7) | copy-start | bytes 2985988
  20.9 34.6 %collective-permute-start.2 = (f32[10,1,24,64]{3,2,1,0:T(8,128)S(1)}, f32[10,1,24,64]{3,2,1,0:T(8,128)S(1)}, u32[]{:S(2)}, u32[]{:S(2)}) collective-permute-start(f32[10,1,24,64]{3,2,1,0:T(8,128)S(1)} %pad_maximum_fusion.34), channel_id=1, source_target_pairs={{2,0},{3,1},{4,2},{5,3},{6,4},{7,5},{8,6},{9,7},{10,8},{11,9},{12,... | collective-permute-start | bytes 184328 | tf_op jit(solution)/shard_map/ppermute | solution.py:28
  22.2 33.3 %collective-permute-start.3 = (f32[10,1,24,64]{3,2,1,0:T(8,128)S(1)}, f32[10,1,24,64]{3,2,1,0:T(8,128)S(1)}, u32[]{:S(2)}, u32[]{:S(2)}) collective-permute-start(f32[10,1,24,64]{3,2,1,0:T(8,128)S(1)} %pad_maximum_fusion.34), channel_id=1, source_target_pairs={{0,2},{1,3},{2,4},{3,5},{4,6},{5,7},{6,8},{7,9},{8,10},{9,11},{10,... | collective-permute-start | bytes 184328 | tf_op jit(solution)/shard_map/ppermute | solution.py:27
  26.8 27.1 %collective-permute-start.1 = (f32[10,1,24,64]{3,2,1,0:T(8,128)S(1)}, f32[10,1,24,64]{3,2,1,0:T(8,128)S(1)}, u32[]{:S(2)}, u32[]{:S(2)}) collective-permute-start(f32[10,1,24,64]{3,2,1,0:T(8,128)S(1)} %pad_maximum_fusion.34), channel_id=1, source_target_pairs={{1,0},{2,1},{3,2},{4,3},{5,4},{6,5},{7,6},{8,7},{9,8},{10,9},{11,1... | collective-permute-start | bytes 184328 | tf_op jit(solution)/shard_map/ppermute | solution.py:28
  29.7 25.6 %collective-permute-start = (f32[10,1,24,64]{3,2,1,0:T(8,128)S(1)}, f32[10,1,24,64]{3,2,1,0:T(8,128)S(1)}, u32[]{:S(2)}, u32[]{:S(2)}) collective-permute-start(f32[10,1,24,64]{3,2,1,0:T(8,128)S(1)} %pad_maximum_fusion.34), channel_id=1, source_target_pairs={{0,1},{1,2},{2,3},{3,4},{4,5},{5,6},{6,7},{7,8},{8,9},{9,10},{10,1... | collective-permute-start | bytes 184328 | tf_op jit(solution)/shard_map/ppermute | solution.py:27
  50.5 12.8 %collective-permute-start.4 = (f32[10,2,9,128]{3,1,2,0:T(2,128)S(1)}, f32[10,2,9,128]{3,1,2,0:T(2,128)S(1)}, u32[]{:S(2)}, u32[]{:S(2)}) collective-permute-start(f32[10,2,9,128]{3,1,2,0:T(2,128)S(1)} %get-tuple-element.66), channel_id=1, source_target_pairs={{0,8},{8,16},{16,24},{1,9},{9,17},{17,25},{2,10},{10,18},{18,26},{... | collective-permute-start | bytes 276488 | tf_op jit(solution)/shard_map/ppermute | solution.py:14
  54.0 9.3 %collective-permute-start.5 = (f32[10,2,9,128]{3,1,2,0:T(2,128)S(1)}, f32[10,2,9,128]{3,1,2,0:T(2,128)S(1)}, u32[]{:S(2)}, u32[]{:S(2)}) collective-permute-start(f32[10,2,9,128]{3,1,2,0:T(2,128)S(1)} %get-tuple-element.67), channel_id=1, source_target_pairs={{8,0},{16,8},{24,16},{9,1},{17,9},{25,17},{10,2},{18,10},{26,18},{... | collective-permute-start | bytes 276488 | tf_op jit(solution)/shard_map/ppermute | solution.py:15
  57.3 11.5 %all-to-all-start = ((bf16[8,2,1728]{2,1,0:T(2,128)(2,1)}), bf16[8,2,1728]{2,1,0:T(2,128)(2,1)S(1)}, u32[]{:S(2)}, u32[]{:S(2)}) async-start(bf16[8,2,1728]{2,1,0:T(2,128)(2,1)} %reshape.458), calls=%async_computation | async-start | bytes 114688 | tf_op jit(solution)/shard_map/all_to_all | solution.py:137
  63.4 11.4 %collective-permute-start.6 = (f32[10,28,2,128]{3,1,2,0:T(8,128)S(1)}, f32[10,28,2,128]{3,1,2,0:T(8,128)S(1)}, u32[]{:S(2)}, u32[]{:S(2)}) collective-permute-start(f32[10,28,2,128]{3,1,2,0:T(8,128)S(1)} %get-tuple-element.60), channel_id=1, source_target_pairs={{0,1},{1,2},{2,3},{3,4},{4,5},{5,6},{6,7},{8,9},{9,10},{10,11},{11... | collective-permute-start | bytes 860168 | tf_op jit(solution)/shard_map/ppermute | solution.py:17
  66.9 9.1 %collective-permute-start.7 = (f32[10,28,2,128]{3,1,2,0:T(8,128)S(1)}, f32[10,28,2,128]{3,1,2,0:T(8,128)S(1)}, u32[]{:S(2)}, u32[]{:S(2)}) collective-permute-start(f32[10,28,2,128]{3,1,2,0:T(8,128)S(1)} %get-tuple-element.61), channel_id=1, source_target_pairs={{1,0},{2,1},{3,2},{4,3},{5,4},{6,5},{7,6},{9,8},{10,9},{11,10},{12... | collective-permute-start | bytes 860168 | tf_op jit(solution)/shard_map/ppermute | solution.py:18
  78.7 5.5 %collective-permute-start.8 = (f32[9,2,9,128]{3,1,2,0:T(2,128)S(1)}, f32[9,2,9,128]{3,1,2,0:T(2,128)S(1)}, u32[]{:S(2)}, u32[]{:S(2)}) collective-permute-start(f32[9,2,9,128]{3,1,2,0:T(2,128)S(1)} %get-tuple-element.70), channel_id=1, source_target_pairs={{0,8},{8,16},{16,24},{1,9},{9,17},{17,25},{2,10},{10,18},{18,26},{... | collective-permute-start | bytes 248840 | tf_op jit(solution)/shard_map/ppermute | solution.py:14
  82.7 5.2 %collective-permute-start.9 = (f32[9,2,9,128]{3,1,2,0:T(2,128)S(1)}, f32[9,2,9,128]{3,1,2,0:T(2,128)S(1)}, u32[]{:S(2)}, u32[]{:S(2)}) collective-permute-start(f32[9,2,9,128]{3,1,2,0:T(2,128)S(1)} %get-tuple-element.71), channel_id=1, source_target_pairs={{8,0},{16,8},{24,16},{9,1},{17,9},{25,17},{10,2},{18,10},{26,18},{... | collective-permute-start | bytes 248840 | tf_op jit(solution)/shard_map/ppermute | solution.py:15
  88.0 8.3 %collective-permute-start.10 = (f32[9,28,2,128]{3,1,2,0:T(8,128)S(1)}, f32[9,28,2,128]{3,1,2,0:T(8,128)S(1)}, u32[]{:S(2)}, u32[]{:S(2)}) collective-permute-start(f32[9,28,2,128]{3,1,2,0:T(8,128)S(1)} %get-tuple-element.64), channel_id=1, source_target_pairs={{0,1},{1,2},{2,3},{3,4},{4,5},{5,6},{6,7},{8,9},{9,10},{10,11},{11... | collective-permute-start | bytes 774152 | tf_op jit(solution)/shard_map/ppermute | solution.py:17
  92.6 8.5 %collective-permute-start.11 = (f32[9,28,2,128]{3,1,2,0:T(8,128)S(1)}, f32[9,28,2,128]{3,1,2,0:T(8,128)S(1)}, u32[]{:S(2)}, u32[]{:S(2)}) collective-permute-start(f32[9,28,2,128]{3,1,2,0:T(8,128)S(1)} %get-tuple-element.65), channel_id=1, source_target_pairs={{1,0},{2,1},{3,2},{4,3},{5,4},{6,5},{7,6},{9,8},{10,9},{11,10},{12... | collective-permute-start | bytes 774152 | tf_op jit(solution)/shard_map/ppermute | solution.py:18
  103.7 4.7 %collective-permute-start.12 = (f32[9,2,9,128]{3,1,2,0:T(2,128)S(1)}, f32[9,2,9,128]{3,1,2,0:T(2,128)S(1)}, u32[]{:S(2)}, u32[]{:S(2)}) collective-permute-start(f32[9,2,9,128]{3,1,2,0:T(2,128)S(1)} %get-tuple-element.68), channel_id=1, source_target_pairs={{0,8},{8,16},{16,24},{1,9},{9,17},{17,25},{2,10},{10,18},{18,26},{... | collective-permute-start | bytes 248840 | tf_op jit(solution)/shard_map/ppermute | solution.py:14
  106.9 5.2 %collective-permute-start.13 = (f32[9,2,9,128]{3,1,2,0:T(2,128)S(1)}, f32[9,2,9,128]{3,1,2,0:T(2,128)S(1)}, u32[]{:S(2)}, u32[]{:S(2)}) collective-permute-start(f32[9,2,9,128]{3,1,2,0:T(2,128)S(1)} %get-tuple-element.69), channel_id=1, source_target_pairs={{8,0},{16,8},{24,16},{9,1},{17,9},{25,17},{10,2},{18,10},{26,18},{... | collective-permute-start | bytes 248840 | tf_op jit(solution)/shard_map/ppermute | solution.py:15
  112.2 6.8 %collective-permute-start.14 = (f32[9,28,2,128]{3,1,2,0:T(8,128)S(1)}, f32[9,28,2,128]{3,1,2,0:T(8,128)S(1)}, u32[]{:S(2)}, u32[]{:S(2)}) collective-permute-start(f32[9,28,2,128]{3,1,2,0:T(8,128)S(1)} %get-tuple-element.62), channel_id=1, source_target_pairs={{0,1},{1,2},{2,3},{3,4},{4,5},{5,6},{6,7},{8,9},{9,10},{10,11},{11... | collective-permute-start | bytes 774152 | tf_op jit(solution)/shard_map/ppermute | solution.py:17
  115.4 8.9 %collective-permute-start.15 = (f32[9,28,2,128]{3,1,2,0:T(8,128)S(1)}, f32[9,28,2,128]{3,1,2,0:T(8,128)S(1)}, u32[]{:S(2)}, u32[]{:S(2)}) collective-permute-start(f32[9,28,2,128]{3,1,2,0:T(8,128)S(1)} %get-tuple-element.63), channel_id=1, source_target_pairs={{1,0},{2,1},{3,2},{4,3},{5,4},{6,5},{7,6},{9,8},{10,9},{11,10},{12... | collective-permute-start | bytes 774152 | tf_op jit(solution)/shard_map/ppermute | solution.py:18
  117.3 7.4 %copy-start.2 = (f32[9,1,24,64]{3,2,1,0:T(8,128)}, f32[9,1,24,64]{3,2,1,0:T(8,128)S(1)}, u32[]{:S(2)}) copy-start(f32[9,1,24,64]{3,2,1,0:T(8,128)S(1)} %constant_dynamic-update-slice_fusion) | copy-start | bytes 165892

commit v3 on v2

--- a/solution.py
+++ b/solution.py
@@ -2,6 +2,8 @@
 import jax.numpy as jnp
 from jax import lax
 from jax.sharding import PartitionSpec as P
+from jax.experimental import pallas as pl
+from jax.experimental.pallas import tpu as pltpu
 
 
 def shifted(n, s):
@@ -31,16 +33,30 @@
     return jnp.concatenate([lo, field, hi], axis=1)
 
 
-def lookup(index, table):
-    rho = jnp.zeros(index.shape, jnp.float32)
-    lam = jnp.zeros(index.shape, jnp.float32)
-    shear = jnp.zeros(index.shape, jnp.float32)
-    for material in range(table.shape[1]):
-        match = index == material
-        rho = jnp.where(match, table[0, material], rho)
-        lam = jnp.where(match, table[1, material], lam)
-        shear = jnp.where(match, table[2, material], shear)
-    return (rho, lam, shear)
+def lookup_kernel(step, idx_ref, tab_ref, coef_ref, lam_ref, mu_ref):
+    idx = idx_ref[...]
+    rho = jnp.zeros(idx.shape, jnp.float32)
+    lam = jnp.zeros(idx.shape, jnp.float32)
+    shear = jnp.zeros(idx.shape, jnp.float32)
+    for material in range(tab_ref.shape[1]):
+        match = idx == material
+        rho = jnp.where(match, tab_ref[0, material], rho)
+        lam = jnp.where(match, tab_ref[1, material], lam)
+        shear = jnp.where(match, tab_ref[2, material], shear)
+    coef_ref[...] = step / rho
+    lam_ref[...] = lam
+    mu_ref[...] = shear
+
+
+def lookup(index, table, step):
+    out = jax.ShapeDtypeStruct(index.shape, jnp.float32)
+    vmem = pl.BlockSpec(memory_space=pltpu.VMEM)
+    return pl.pallas_call(
+        lambda *refs: lookup_kernel(step, *refs),
+        out_shape=(out, out, out),
+        in_specs=[vmem, pl.BlockSpec(memory_space=pltpu.SMEM)],
+        out_specs=(vmem, vmem, vmem),
+    )(index, table)
 
 
 def along(f, axis):
@@ -126,8 +142,7 @@
     reg_y = region_state.shape[2]
     rows_each = reg_y // count_y
 
-    rho_r, lam_r, mu_r = lookup(region_material, material_table)
-    coef_r, lam_r, mu_r = lax.optimization_barrier((0.6 / rho_r, lam_r, mu_r))
+    coef_r, lam_r, mu_r = lookup(region_material, material_table, 0.6)
     reg_ext = strip_halo(jnp.concatenate([region_state, coef_r[None]], 0), 2)
     region_next = step_wide(
         reg_ext, reg_ext[9, 1:-1], region_state[3:], lam_r, mu_r, 0.6, 3.0, True
@@ -146,8 +161,7 @@
     along_y = ramp(lax.axis_index("gy") * fine_y, fine_y, count_y * fine_y, fine_y)
     relax = (0.1 + 0.4 * jnp.maximum(along_x[:, None], along_y[None, :]))[:, :, None]
 
-    rho_f, lam_f, mu_f = lookup(fine_material, material_table)
-    coef_f, lam_f, mu_f = lax.optimization_barrier((0.2 / rho_f, lam_f, mu_f))
+    coef_f, lam_f, mu_f = lookup(fine_material, material_table, 0.2)
     ext = tile_halo(jnp.concatenate([fine_state, coef_f[None]], 0), 2)
     coef_ext = ext[9, 1:-1, 1:-1]
     state = fine_state

time: 129 us -> 105 us (0.81)
  the two profiles are of different devices: /device:TPU:1 before, /device:TPU:28 now
where the time goes in v3:
time: 105 us; the launch traced here: 104 us
  starting transfers between devices  44.2 us (42%)
  waiting for transfers between devices  21.4 us (20%)
  other arithmetic  14 us (13%)
  local copies, waits for them, and re-layouts  13.4 us (13%)
  matrix products  5.75 us (5%)
  Pallas kernels  3.39 us (3%)
  between operations  1.5 us (1%)
    unnamed x39, local copies, waits for them, and re-layouts  9.91 us
    ppermute x3, starting transfers between devices, tile_halo(): from_right = lax.ppermute(field[:, :w], 'gx', shifted(nx, -1))  9.27 us
    ppermute x3, waiting for transfers between devices, tile_halo(): from_left = lax.ppermute(field[:, -w:], 'gx', shifted(nx, 1))  8.51 us
    ppermute x3, waiting for transfers between devices, tile_halo(): from_below = lax.ppermute(wide[:, :, -w:], 'gy', shifted(ny, 1))  8.24 us
    ppermute x3, starting transfers between devices, tile_halo(): from_above = lax.ppermute(wide[:, :, :w], 'gy', shifted(ny, -1))  7.67 us
    ppermute x2, starting transfers between devices, strip_halo(): lax.ppermute(field, both, shifted(n, -d))  6.48 us
    ppermute x3, starting transfers between devices, tile_halo(): from_below = lax.ppermute(wide[:, :, -w:], 'gy', shifted(ny, 1))  6.43 us
    all_to_all x1, starting transfers between devices, local(): band = lax.all_to_all(both, 'gy', 2, 1, tiled=True).astype(jnp.float32)  5.57 us
  transfers between devices with their start and end apart: 17, of which 9 were waited for; matrix products, arithmetic and copies ran while one was open for 19% of the time, Pallas kernels for 2%

profile of v3, /device:TPU:28, one launch (start us, length us, event | category | flops | bytes accessed | tf_op | source)
XLA Modules:
  0.0 103.7 jit_solution(17346617282201779913)
XLA Ops:
  0.6 1.5 %shard_map.68 = (f32[1,24,64]{2,1,0:T(8,128)}, f32[1,24,64]{2,1,0:T(8,128)}, f32[1,24,64]{2,1,0:T(8,128)}) custom-call(s32[1,24,64]{2,1,0:T(8,128)} %refs_0_.2, f32[3,8]{1,0:T(4,128)} %refs_1_.3), custom_call_target="tpu_custom_call" | custom-call | tf_op jit(solution)/shard_map/pallas_call | solution.py:54
  2.1 1.6 %pad_maximum_fusion.36 = f32[10,1,24,64]{3,2,1,0:T(8,128)} fusion(f32[1,1,24,64]{3,2,1,0:T(8,128)} %bitcast.618, f32[9,1,24,64]{3,2,1,0:T(8,128)} %param.5), kind=kLoop, calls=%fused_computation.289 | loop fusion | flops 15360 | bytes 122880 | tf_op jit(solution)/shard_map/concatenate | solution.py:146
  3.7 2.8 %collective-permute-start.1 = (f32[10,1,24,64]{3,2,1,0:T(8,128)}, f32[10,1,24,64]{3,2,1,0:T(8,128)S(1)}, u32[]{:S(2)}, u32[]{:S(2)}) collective-permute-start(f32[10,1,24,64]{3,2,1,0:T(8,128)} %pad_maximum_fusion.36), channel_id=1, source_target_pairs={{1,0},{2,1},{3,2},{4,3},{5,4},{6,5},{7,6},{8,7},{9,8},{10,9},{11,1... | collective-permute-start | bytes 184328 | tf_op jit(solution)/shard_map/ppermute | solution.py:30
  6.4 1.9 %collective-permute-start = (f32[10,1,24,64]{3,2,1,0:T(8,128)}, f32[10,1,24,64]{3,2,1,0:T(8,128)S(1)}, u32[]{:S(2)}, u32[]{:S(2)}) collective-permute-start(f32[10,1,24,64]{3,2,1,0:T(8,128)} %pad_maximum_fusion.36), channel_id=1, source_target_pairs={{0,1},{1,2},{2,3},{3,4},{4,5},{5,6},{6,7},{7,8},{8,9},{9,10},{10,1... | collective-permute-start | bytes 184328 | tf_op jit(solution)/shard_map/ppermute | solution.py:29
  8.4 3.0 %collective-permute-start.3 = (f32[10,1,24,64]{3,2,1,0:T(8,128)}, f32[10,1,24,64]{3,2,1,0:T(8,128)S(1)}, u32[]{:S(2)}, u32[]{:S(2)}) collective-permute-start(f32[10,1,24,64]{3,2,1,0:T(8,128)} %pad_maximum_fusion.36), channel_id=1, source_target_pairs={{0,2},{1,3},{2,4},{3,5},{4,6},{5,7},{6,8},{7,9},{8,10},{9,11},{10,... | collective-permute-start | bytes 184328 | tf_op jit(solution)/shard_map/ppermute | solution.py:29
  11.4 3.7 %collective-permute-start.2 = (f32[10,1,24,64]{3,2,1,0:T(8,128)}, f32[10,1,24,64]{3,2,1,0:T(8,128)S(1)}, u32[]{:S(2)}, u32[]{:S(2)}) collective-permute-start(f32[10,1,24,64]{3,2,1,0:T(8,128)} %pad_maximum_fusion.36), channel_id=1, source_target_pairs={{2,0},{3,1},{4,2},{5,3},{6,4},{7,5},{8,6},{9,7},{10,8},{11,9},{12,... | collective-permute-start | bytes 184328 | tf_op jit(solution)/shard_map/ppermute | solution.py:30
  15.1 1.6 %copy.52.refs_0_ = s32[24,9,128]{2,1,0:T(8,128)} copy(s32[24,9,128]{2,0,1:T(8,128)} %param.8) | data formatting | bytes 221184 | tf_op args[3]
  16.7 1.9 %shard_map.69 = (f32[24,9,128]{2,1,0:T(8,128)}, f32[24,9,128]{2,1,0:T(8,128)}, f32[24,9,128]{2,1,0:T(8,128)}) custom-call(s32[24,9,128]{2,1,0:T(8,128)} %copy.52.refs_0_, f32[3,8]{1,0:T(4,128)} %refs_1_.3), custom_call_target="tpu_custom_call" | custom-call | tf_op jit(solution)/shard_map/pallas_call | solution.py:54
  18.7 1.5 %copy.53 = f32[9,24,9,128]{3,2,1,0:T(8,128)S(1)} copy(f32[9,24,9,128]{3,1,2,0:T(8,128)} %param.7) | data formatting | bytes 1990656 | tf_op args[2]
  20.3 2.4 %collective-permute-start.5 = (f32[10,2,9,128]{3,2,1,0:T(8,128)S(1)}, f32[10,2,9,128]{3,2,1,0:T(8,128)S(1)}, u32[]{:S(2)}, u32[]{:S(2)}) collective-permute-start(f32[10,2,9,128]{3,2,1,0:T(8,128)S(1)} %get-tuple-element.60), channel_id=1, source_target_pairs={{8,0},{16,8},{24,16},{9,1},{17,9},{25,17},{10,2},{18,10},{26,18},{... | collective-permute-start | bytes 276488 | tf_op jit(solution)/shard_map/ppermute | solution.py:17
  22.9 1.3 %collective-permute-start.4 = (f32[10,2,9,128]{3,2,1,0:T(8,128)S(1)}, f32[10,2,9,128]{3,2,1,0:T(8,128)S(1)}, u32[]{:S(2)}, u32[]{:S(2)}) collective-permute-start(f32[10,2,9,128]{3,2,1,0:T(8,128)S(1)} %get-tuple-element.59), channel_id=1, source_target_pairs={{0,8},{8,16},{16,24},{1,9},{9,17},{17,25},{2,10},{10,18},{18,26},{... | collective-permute-start | bytes 276488 | tf_op jit(solution)/shard_map/ppermute | solution.py:16
  24.8 0.6 constant_dynamic-update-slice_fusion.6
  25.7 0.7 constant_dynamic-update-slice_fusion.12
  26.4 0.7 constant_dynamic-update-slice_fusion.10
  27.1 0.6 constant_dynamic-update-slice_fusion.9
  27.7 0.7 constant_dynamic-update-slice_fusion.8
  28.4 0.7 constant_dynamic-update-slice_fusion.7
  29.1 0.8 reshape.458
  29.9 5.6 %all-to-all-start = ((bf16[8,2,1728]{2,1,0:T(2,128)(2,1)}), bf16[8,2,1728]{2,1,0:T(2,128)(2,1)S(1)}, u32[]{:S(2)}, u32[]{:S(2)}) async-start(bf16[8,2,1728]{2,1,0:T(2,128)(2,1)} %reshape.458), calls=%async_computation | async-start | bytes 114688 | tf_op jit(solution)/shard_map/all_to_all | solution.py:152
  35.5 0.9 pad_maximum_fusion.7
  36.4 3.1 %collective-permute-start.7 = (f32[10,28,2,128]{3,2,1,0:T(2,128)}, f32[10,28,2,128]{3,2,1,0:T(2,128)S(1)}, u32[]{:S(2)}, u32[]{:S(2)}) collective-permute-start(f32[10,28,2,128]{3,2,1,0:T(2,128)} %get-tuple-element.46), channel_id=1, source_target_pairs={{1,0},{2,1},{3,2},{4,3},{5,4},{6,5},{7,6},{9,8},{10,9},{11,10},{12... | collective-permute-start | bytes 860168 | tf_op jit(solution)/shard_map/ppermute | solution.py:20
  39.5 1.9 %collective-permute-start.6 = (f32[10,28,2,128]{3,2,1,0:T(2,128)S(1)}, f32[10,28,2,128]{3,2,1,0:T(2,128)S(1)}, u32[]{:S(2)}, u32[]{:S(2)}) collective-permute-start(f32[10,28,2,128]{3,2,1,0:T(2,128)S(1)} %get-tuple-element.45), channel_id=1, source_target_pairs={{0,1},{1,2},{2,3},{3,4},{4,5},{5,6},{6,7},{8,9},{9,10},{10,11},{11... | collective-permute-start | bytes 860168 | tf_op jit(solution)/shard_map/ppermute | solution.py:19
  41.6 0.5 convolution_bitcast_fusion.1
  42.0 3.1 %convolution_bitcast_fusion = f32[18,24,9,64]{3,2,1,0:T(8,128)S(1)} fusion(f32[18,24,3,64]{3,1,2,0:T(8,128)S(1)} %convolution_bitcast_fusion.1, f32[9]{0:T(128)S(1)} %get-tuple-element.156, s32[9]{0:T(128)S(1)} %get-tuple-element.159, f32[9]{0:T(128)S(1)} %get-tuple-element.157, s32[9]{0:T(128)S(1)} %get-tuple-element.158), kind=kOutput, calls=%fused_computation.9 | convolution fusion | flops 8958087 | bytes 1327248 | tf_op jit(solution)/shard_map/gb,cfbz->cfgz/dot_general | solution.py:156
  45.1 2.2 %fusion = f32[18,24,9,128]{3,1,2,0:T(8,128)S(1)} fusion(f32[18,24,9,64]{3,2,1,0:T(8,128)S(1)} %convolution_bitcast_fusion, f32[128]{0:T(128)S(1)} %get-tuple-element.160, s32[128]{0:T(128)S(1)} %get-tuple-element.163, f32[128]{0:T(128)S(1)} %get-tuple-element.161, s32[128]{0:T(128)S(1)} %get-tuple-element.162), kind=kOutput, calls=%fused_computation.7 | convolution fusion | flops 382246912 | bytes 2988032 | tf_op jit(solution)/shard_map/kz,cfgz->cfgk/dot_general | solution.py:157
  47.5 0.8 collective-permute-done.6
  48.3 0.5 pad_maximum_fusion
  49.0 0.2 fusion.247
  50.0 0.7 copy-done
  50.8 0.2 fusion.161
  51.8 0.7 fusion.4
  52.5 4.6 %collective-permute-start.9 = (f32[9,2,9,128]{3,2,1,0:T(8,128)S(1)}, f32[9,2,9,128]{3,2,1,0:T(8,128)S(1)}, u32[]{:S(2)}, u32[]{:S(2)}) collective-permute-start(f32[9,2,9,128]{3,2,1,0:T(8,128)S(1)} %get-tuple-element.64), channel_id=1, source_target_pairs={{8,0},{16,8},{24,16},{9,1},{17,9},{25,17},{10,2},{18,10},{26,18},{... | collective-permute-start | bytes 248840 | tf_op jit(solution)/shard_map/ppermute | solution.py:17
  57.1 1.3 %collective-permute-start.8 = (f32[9,2,9,128]{3,2,1,0:T(8,128)S(1)}, f32[9,2,9,128]{3,2,1,0:T(8,128)S(1)}, u32[]{:S(2)}, u32[]{:S(2)}) collective-permute-start(f32[9,2,9,128]{3,2,1,0:T(8,128)S(1)} %get-tuple-element.63), channel_id=1, source_target_pairs={{0,8},{8,16},{16,24},{1,9},{9,17},{17,25},{2,10},{10,18},{18,26},{... | collective-permute-start | bytes 248840 | tf_op jit(solution)/shard_map/ppermute | solution.py:16
  58.4 0.6 constant_dynamic-update-slice_fusion.5
  59.0 1.2 %collective-permute-done.9 = f32[9,2,9,128]{3,2,1,0:T(8,128)S(1)} collective-permute-done((f32[9,2,9,128]{3,2,1,0:T(8,128)S(1)}, f32[9,2,9,128]{3,2,1,0:T(8,128)S(1)}, u32[]{:S(2)}, u32[]{:S(2)}) %collective-permute-start.9) | collective-permute-done | bytes 82976 | tf_op jit(solution)/shard_map/ppermute | solution.py:17
  60.2 4.1 %collective-permute-done.8 = f32[9,2,9,128]{3,2,1,0:T(8,128)S(1)} collective-permute-done((f32[9,2,9,128]{3,2,1,0:T(8,128)S(1)}, f32[9,2,9,128]{3,2,1,0:T(8,128)S(1)}, u32[]{:S(2)}, u32[]{:S(2)}) %collective-permute-start.8) | collective-permute-done | bytes 82976 | tf_op jit(solution)/shard_map/ppermute | solution.py:16
  64.3 0.2 pad_maximum_fusion.13
  64.5 2.6 %collective-permute-start.11 = (f32[9,28,2,128]{3,2,1,0:T(2,128)S(1)}, f32[9,28,2,128]{3,2,1,0:T(2,128)S(1)}, u32[]{:S(2)}, u32[]{:S(2)}) collective-permute-start(f32[9,28,2,128]{3,2,1,0:T(2,128)S(1)} %get-tuple-element.56), channel_id=1, source_target_pairs={{1,0},{2,1},{3,2},{4,3},{5,4},{6,5},{7,6},{9,8},{10,9},{11,10},{12... | collective-permute-start | bytes 774152 | tf_op jit(solution)/shard_map/ppermute | solution.py:20
  67.2 2.1 %collective-permute-start.10 = (f32[9,28,2,128]{3,2,1,0:T(2,128)S(1)}, f32[9,28,2,128]{3,2,1,0:T(2,128)S(1)}, u32[]{:S(2)}, u32[]{:S(2)}) collective-permute-start(f32[9,28,2,128]{3,2,1,0:T(2,128)S(1)} %get-tuple-element.55), channel_id=1, source_target_pairs={{0,1},{1,2},{2,3},{3,4},{4,5},{5,6},{6,7},{8,9},{9,10},{10,11},{11... | collective-permute-start | bytes 774152 | tf_op jit(solution)/shard_map/ppermute | solution.py:19
  69.3 0.6 constant_dynamic-update-slice_fusion.4
  69.9 0.6 constant_dynamic-update-slice_fusion.3
  70.5 1.7 %collective-permute-done.11 = f32[9,28,2,128]{3,2,1,0:T(2,128)S(1)} collective-permute-done((f32[9,28,2,128]{3,2,1,0:T(2,128)S(1)}, f32[9,28,2,128]{3,2,1,0:T(2,128)S(1)}, u32[]{:S(2)}, u32[]{:S(2)}) %collective-permute-start.11) | collective-permute-done | bytes 258080 | tf_op jit(solution)/shard_map/ppermute | solution.py:20
  72.2 3.5 %collective-permute-done.10 = f32[9,28,2,128]{3,2,1,0:T(2,128)S(1)} collective-permute-done((f32[9,28,2,128]{3,2,1,0:T(2,128)S(1)}, f32[9,28,2,128]{3,2,1,0:T(2,128)S(1)}, u32[]{:S(2)}, u32[]{:S(2)}) %collective-permute-start.10) | collective-permute-done | bytes 258080 | tf_op jit(solution)/shard_map/ppermute | solution.py:19
  75.7 0.4 pad_maximum_fusion.1
  76.9 0.2 fusion.43
  77.4 0.2 fusion.127
  78.0 0.2 slice_bitcast_fusion.19
  78.4 0.7 fusion.7
  79.1 2.4 %collective-permute-start.13 = (f32[9,2,9,128]{3,2,1,0:T(8,128)S(1)}, f32[9,2,9,128]{3,2,1,0:T(8,128)S(1)}, u32[]{:S(2)}, u32[]{:S(2)}) collective-permute-start(f32[9,2,9,128]{3,2,1,0:T(8,128)S(1)} %get-tuple-element.62), channel_id=1, source_target_pairs={{8,0},{16,8},{24,16},{9,1},{17,9},{25,17},{10,2},{18,10},{26,18},{... | collective-permute-start | bytes 248840 | tf_op jit(solution)/shard_map/ppermute | solution.py:17
  81.5 1.3 %collective-permute-start.12 = (f32[9,2,9,128]{3,2,1,0:T(8,128)S(1)}, f32[9,2,9,128]{3,2,1,0:T(8,128)S(1)}, u32[]{:S(2)}, u32[]{:S(2)}) collective-permute-start(f32[9,2,9,128]{3,2,1,0:T(8,128)S(1)} %get-tuple-element.61), channel_id=1, source_target_pairs={{0,8},{8,16},{16,24},{1,9},{9,17},{17,25},{2,10},{10,18},{18,26},{... | collective-permute-start | bytes 248840 | tf_op jit(solution)/shard_map/ppermute | solution.py:16
  82.8 0.6 constant_dynamic-update-slice_fusion.2
  83.4 0.7 collective-permute-done.13
  84.1 4.4 %collective-permute-done.12 = f32[9,2,9,128]{3,2,1,0:T(8,128)S(1)} collective-permute-done((f32[9,2,9,128]{3,2,1,0:T(8,128)S(1)}, f32[9,2,9,128]{3,2,1,0:T(8,128)S(1)}, u32[]{:S(2)}, u32[]{:S(2)}) %collective-permute-start.12) | collective-permute-done | bytes 82976 | tf_op jit(solution)/shard_map/ppermute | solution.py:16
  88.5 0.2 pad_maximum_fusion.10
  88.7 1.9 %collective-permute-start.15 = (f32[9,28,2,128]{3,2,1,0:T(2,128)S(1)}, f32[9,28,2,128]{3,2,1,0:T(2,128)S(1)}, u32[]{:S(2)}, u32[]{:S(2)}) collective-permute-start(f32[9,28,2,128]{3,2,1,0:T(2,128)S(1)} %get-tuple-element.51), channel_id=1, source_target_pairs={{1,0},{2,1},{3,2},{4,3},{5,4},{6,5},{7,6},{9,8},{10,9},{11,10},{12... | collective-permute-start | bytes 774152 | tf_op jit(solution)/shard_map/ppermute | solution.py:20
  90.6 2.4 %collective-permute-start.14 = (f32[9,28,2,128]{3,2,1,0:T(2,128)S(1)}, f32[9,28,2,128]{3,2,1,0:T(2,128)S(1)}, u32[]{:S(2)}, u32[]{:S(2)}) collective-permute-start(f32[9,28,2,128]{3,2,1,0:T(2,128)S(1)} %get-tuple-element.50), channel_id=1, source_target_pairs={{0,1},{1,2},{2,3},{3,4},{4,5},{5,6},{6,7},{8,9},{9,10},{10,11},{11... | collective-permute-start | bytes 774152 | tf_op jit(solution)/shard_map/ppermute | solution.py:19
  93.1 0.6 constant_dynamic-update-slice_fusion.1
  93.7 0.6 constant_dynamic-update-slice_fusion
  94.3 1.0 collective-permute-done.15
  95.3 3.9 %collective-permute-done.14 = f32[9,28,2,128]{3,2,1,0:T(2,128)S(1)} collective-permute-done((f32[9,28,2,128]{3,2,1,0:T(2,128)S(1)}, f32[9,28,2,128]{3,2,1,0:T(2,128)S(1)}, u32[]{:S(2)}, u32[]{:S(2)}) %collective-permute-start.14) | collective-permute-done | bytes 258080 | tf_op jit(solution)/shard_map/ppermute | solution.py:19
  99.2 0.4 pad_maximum_fusion.2
  100.9 0.2 fusion.93
  101.9 0.6 fusion.10
  102.5 1.3 %copy.67 = f32[9,24,9,128]{3,1,2,0:T(8,128)} copy(f32[9,24,9,128]{3,2,1,0:T(8,128)S(1)} %fusion.10) | data formatting | bytes 1990656
  (117 shorter events, 6.9 us)
Async XLA Ops:
  3.7 19.2 %collective-permute-start.1 = (f32[10,1,24,64]{3,2,1,0:T(8,128)}, f32[10,1,24,64]{3,2,1,0:T(8,128)S(1)}, u32[]{:S(2)}, u32[]{:S(2)}) collective-permute-start(f32[10,1,24,64]{3,2,1,0:T(8,128)} %pad_maximum_fusion.36), channel_id=1, source_target_pairs={{1,0},{2,1},{3,2},{4,3},{5,4},{6,5},{7,6},{8,7},{9,8},{10,9},{11,1... | collective-permute-start | bytes 184328 | tf_op jit(solution)/shard_map/ppermute | solution.py:30
  6.4 17.8 %collective-permute-start = (f32[10,1,24,64]{3,2,1,0:T(8,128)}, f32[10,1,24,64]{3,2,1,0:T(8,128)S(1)}, u32[]{:S(2)}, u32[]{:S(2)}) collective-permute-start(f32[10,1,24,64]{3,2,1,0:T(8,128)} %pad_maximum_fusion.36), channel_id=1, source_target_pairs={{0,1},{1,2},{2,3},{3,4},{4,5},{5,6},{6,7},{7,8},{8,9},{9,10},{10,1... | collective-permute-start | bytes 184328 | tf_op jit(solution)/shard_map/ppermute | solution.py:29
  8.4 16.1 %collective-permute-start.3 = (f32[10,1,24,64]{3,2,1,0:T(8,128)}, f32[10,1,24,64]{3,2,1,0:T(8,128)S(1)}, u32[]{:S(2)}, u32[]{:S(2)}) collective-permute-start(f32[10,1,24,64]{3,2,1,0:T(8,128)} %pad_maximum_fusion.36), channel_id=1, source_target_pairs={{0,2},{1,3},{2,4},{3,5},{4,6},{5,7},{6,8},{7,9},{8,10},{9,11},{10,... | collective-permute-start | bytes 184328 | tf_op jit(solution)/shard_map/ppermute | solution.py:29
  11.4 13.1 %collective-permute-start.2 = (f32[10,1,24,64]{3,2,1,0:T(8,128)}, f32[10,1,24,64]{3,2,1,0:T(8,128)S(1)}, u32[]{:S(2)}, u32[]{:S(2)}) collective-permute-start(f32[10,1,24,64]{3,2,1,0:T(8,128)} %pad_maximum_fusion.36), channel_id=1, source_target_pairs={{2,0},{3,1},{4,2},{5,3},{6,4},{7,5},{8,6},{9,7},{10,8},{11,9},{12,... | collective-permute-start | bytes 184328 | tf_op jit(solution)/shard_map/ppermute | solution.py:30
  18.7 1.5 %copy-start.2 = (f32[24,9,128]{2,1,0:T(8,128)S(1)}, f32[24,9,128]{2,1,0:T(8,128)}, u32[]{:S(2)}) copy-start(f32[24,9,128]{2,1,0:T(8,128)} %get-tuple-element.11) | copy-start | bytes 331780
  20.2 2.4 %copy-start.1 = (f32[9,1,24,64]{3,2,1,0:T(8,128)S(1)}, f32[9,1,24,64]{3,2,1,0:T(8,128)}, u32[]{:S(2)}) copy-start(f32[9,1,24,64]{3,2,1,0:T(8,128)} %param.5) | copy-start | bytes 165892
  20.2 4.0 %copy-start.4 = (f32[1,24,64]{2,1,0:T(8,128)S(1)}, f32[1,24,64]{2,1,0:T(8,128)}, u32[]{:S(2)}) copy-start(f32[1,24,64]{2,1,0:T(8,128)} %get-tuple-element.8) | copy-start | bytes 18436
  20.3 15.2 %collective-permute-start.5 = (f32[10,2,9,128]{3,2,1,0:T(8,128)S(1)}, f32[10,2,9,128]{3,2,1,0:T(8,128)S(1)}, u32[]{:S(2)}, u32[]{:S(2)}) collective-permute-start(f32[10,2,9,128]{3,2,1,0:T(8,128)S(1)} %get-tuple-element.60), channel_id=1, source_target_pairs={{8,0},{16,8},{24,16},{9,1},{17,9},{25,17},{10,2},{18,10},{26,18},{... | collective-permute-start | bytes 276488 | tf_op jit(solution)/shard_map/ppermute | solution.py:17
  22.9 12.5 %collective-permute-start.4 = (f32[10,2,9,128]{3,2,1,0:T(8,128)S(1)}, f32[10,2,9,128]{3,2,1,0:T(8,128)S(1)}, u32[]{:S(2)}, u32[]{:S(2)}) collective-permute-start(f32[10,2,9,128]{3,2,1,0:T(8,128)S(1)} %get-tuple-element.59), channel_id=1, source_target_pairs={{0,8},{8,16},{16,24},{1,9},{9,17},{17,25},{2,10},{10,18},{18,26},{... | collective-permute-start | bytes 276488 | tf_op jit(solution)/shard_map/ppermute | solution.py:16
  24.5 1.2 %copy-start.5 = (f32[1,24,64]{2,1,0:T(8,128)S(1)}, f32[1,24,64]{2,1,0:T(8,128)}, u32[]{:S(2)}) copy-start(f32[1,24,64]{2,1,0:T(8,128)} %get-tuple-element.10) | copy-start | bytes 18436
  24.5 1.2 %copy-start.11 = (f32[1,24,64]{2,1,0:T(8,128)S(1)}, f32[1,24,64]{2,1,0:T(8,128)}, u32[]{:S(2)}) copy-start(f32[1,24,64]{2,1,0:T(8,128)} %get-tuple-element.9) | copy-start | bytes 18436
  29.9 11.5 %all-to-all-start = ((bf16[8,2,1728]{2,1,0:T(2,128)(2,1)}), bf16[8,2,1728]{2,1,0:T(2,128)(2,1)S(1)}, u32[]{:S(2)}, u32[]{:S(2)}) async-start(bf16[8,2,1728]{2,1,0:T(2,128)(2,1)} %reshape.458), calls=%async_computation | async-start | bytes 114688 | tf_op jit(solution)/shard_map/all_to_all | solution.py:152
  36.4 11.1 %collective-permute-start.7 = (f32[10,28,2,128]{3,2,1,0:T(2,128)}, f32[10,28,2,128]{3,2,1,0:T(2,128)S(1)}, u32[]{:S(2)}, u32[]{:S(2)}) collective-permute-start(f32[10,28,2,128]{3,2,1,0:T(2,128)} %get-tuple-element.46), channel_id=1, source_target_pairs={{1,0},{2,1},{3,2},{4,3},{5,4},{6,5},{7,6},{9,8},{10,9},{11,10},{12... | collective-permute-start | bytes 860168 | tf_op jit(solution)/shard_map/ppermute | solution.py:20
  39.5 8.9 %collective-permute-start.6 = (f32[10,28,2,128]{3,2,1,0:T(2,128)S(1)}, f32[10,28,2,128]{3,2,1,0:T(2,128)S(1)}, u32[]{:S(2)}, u32[]{:S(2)}) collective-permute-start(f32[10,28,2,128]{3,2,1,0:T(2,128)S(1)} %get-tuple-element.45), channel_id=1, source_target_pairs={{0,1},{1,2},{2,3},{3,4},{4,5},{5,6},{6,7},{8,9},{9,10},{10,11},{11... | collective-permute-start | bytes 860168 | tf_op jit(solution)/shard_map/ppermute | solution.py:19
  49.8 0.9 copy-start
  49.8 1.0 copy-start.3
  51.8 6.6 %copy-start.7 = (f32[1,24,64]{2,1,0:T(8,128)S(1)}, f32[1,24,64]{2,1,0:T(8,128)}, u32[]{:S(2)}) copy-start(f32[1,24,64]{2,1,0:T(8,128)} %get-tuple-element.37) | copy-start | bytes 18436
  52.5 17.4 %copy-start.6 = (f32[1,24,64]{2,1,0:T(8,128)S(1)}, f32[1,24,64]{2,1,0:T(8,128)}, u32[]{:S(2)}) copy-start(f32[1,24,64]{2,1,0:T(8,128)} %get-tuple-element.33) | copy-start | bytes 18436
  52.5 7.7 %collective-permute-start.9 = (f32[9,2,9,128]{3,2,1,0:T(8,128)S(1)}, f32[9,2,9,128]{3,2,1,0:T(8,128)S(1)}, u32[]{:S(2)}, u32[]{:S(2)}) collective-permute-start(f32[9,2,9,128]{3,2,1,0:T(8,128)S(1)} %get-tuple-element.64), channel_id=1, source_target_pairs={{8,0},{16,8},{24,16},{9,1},{17,9},{25,17},{10,2},{18,10},{26,18},{... | collective-permute-start | bytes 248840 | tf_op jit(solution)/shard_map/ppermute | solution.py:17
  57.1 7.2 %collective-permute-start.8 = (f32[9,2,9,128]{3,2,1,0:T(8,128)S(1)}, f32[9,2,9,128]{3,2,1,0:T(8,128)S(1)}, u32[]{:S(2)}, u32[]{:S(2)}) collective-permute-start(f32[9,2,9,128]{3,2,1,0:T(8,128)S(1)} %get-tuple-element.63), channel_id=1, source_target_pairs={{0,8},{8,16},{16,24},{1,9},{9,17},{17,25},{2,10},{10,18},{18,26},{... | collective-permute-start | bytes 248840 | tf_op jit(solution)/shard_map/ppermute | solution.py:16
  64.5 7.7 %collective-permute-start.11 = (f32[9,28,2,128]{3,2,1,0:T(2,128)S(1)}, f32[9,28,2,128]{3,2,1,0:T(2,128)S(1)}, u32[]{:S(2)}, u32[]{:S(2)}) collective-permute-start(f32[9,28,2,128]{3,2,1,0:T(2,128)S(1)} %get-tuple-element.56), channel_id=1, source_target_pairs={{1,0},{2,1},{3,2},{4,3},{5,4},{6,5},{7,6},{9,8},{10,9},{11,10},{12... | collective-permute-start | bytes 774152 | tf_op jit(solution)/shard_map/ppermute | solution.py:20
  67.2 8.5 %collective-permute-start.10 = (f32[9,28,2,128]{3,2,1,0:T(2,128)S(1)}, f32[9,28,2,128]{3,2,1,0:T(2,128)S(1)}, u32[]{:S(2)}, u32[]{:S(2)}) collective-permute-start(f32[9,28,2,128]{3,2,1,0:T(2,128)S(1)} %get-tuple-element.55), channel_id=1, source_target_pairs={{0,1},{1,2},{2,3},{3,4},{4,5},{5,6},{6,7},{8,9},{9,10},{10,11},{11... | collective-permute-start | bytes 774152 | tf_op jit(solution)/shard_map/ppermute | solution.py:19
  78.4 4.4 %copy-start.10 = (f32[1,1,24,64]{3,2,1,0:T(8,128)S(1)}, f32[1,1,24,64]{3,2,1,0:T(8,128)}, u32[]{:S(2)}) copy-start(f32[1,1,24,64]{3,2,1,0:T(8,128)} %get-tuple-element.31) | copy-start | bytes 18436
  79.1 14.0 %copy-start.8 = (f32[1,1,24,64]{3,2,1,0:T(8,128)S(1)}, f32[1,1,24,64]{3,2,1,0:T(8,128)}, u32[]{:S(2)}) copy-start(f32[1,1,24,64]{3,2,1,0:T(8,128)} %get-tuple-element.29) | copy-start | bytes 18436
  79.1 14.6 %copy-start.9 = (f32[1,24,64]{2,1,0:T(8,128)S(1)}, f32[1,24,64]{2,1,0:T(8,128)}, u32[]{:S(2)}) copy-start(f32[1,24,64]{2,1,0:T(8,128)} %get-tuple-element.27) | copy-start | bytes 18436
  79.1 5.0 %collective-permute-start.13 = (f32[9,2,9,128]{3,2,1,0:T(8,128)S(1)}, f32[9,2,9,128]{3,2,1,0:T(8,128)S(1)}, u32[]{:S(2)}, u32[]{:S(2)}) collective-permute-start(f32[9,2,9,128]{3,2,1,0:T(8,128)S(1)} %get-tuple-element.62), channel_id=1, source_target_pairs={{8,0},{16,8},{24,16},{9,1},{17,9},{25,17},{10,2},{18,10},{26,18},{... | collective-permute-start | bytes 248840 | tf_op jit(solution)/shard_map/ppermute | solution.py:17
  81.5 7.0 %collective-permute-start.12 = (f32[9,2,9,128]{3,2,1,0:T(8,128)S(1)}, f32[9,2,9,128]{3,2,1,0:T(8,128)S(1)}, u32[]{:S(2)}, u32[]{:S(2)}) collective-permute-start(f32[9,2,9,128]{3,2,1,0:T(8,128)S(1)} %get-tuple-element.61), channel_id=1, source_target_pairs={{0,8},{8,16},{16,24},{1,9},{9,17},{17,25},{2,10},{10,18},{18,26},{... | collective-permute-start | bytes 248840 | tf_op jit(solution)/shard_map/ppermute | solution.py:16
  88.7 6.6 %collective-permute-start.15 = (f32[9,28,2,128]{3,2,1,0:T(2,128)S(1)}, f32[9,28,2,128]{3,2,1,0:T(2,128)S(1)}, u32[]{:S(2)}, u32[]{:S(2)}) collective-permute-start(f32[9,28,2,128]{3,2,1,0:T(2,128)S(1)} %get-tuple-element.51), channel_id=1, source_target_pairs={{1,0},{2,1},{3,2},{4,3},{5,4},{6,5},{7,6},{9,8},{10,9},{11,10},{12... | collective-permute-start | bytes 774152 | tf_op jit(solution)/shard_map/ppermute | solution.py:20
  90.6 8.5 %collective-permute-start.14 = (f32[9,28,2,128]{3,2,1,0:T(2,128)S(1)}, f32[9,28,2,128]{3,2,1,0:T(2,128)S(1)}, u32[]{:S(2)}, u32[]{:S(2)}) collective-permute-start(f32[9,28,2,128]{3,2,1,0:T(2,128)S(1)} %get-tuple-element.50), channel_id=1, source_target_pairs={{0,1},{1,2},{2,3},{3,4},{4,5},{5,6},{6,7},{8,9},{9,10},{10,11},{11... | collective-permute-start | bytes 774152 | tf_op jit(solution)/shard_map/ppermute | solution.py:19

commit v4 on v3

--- a/solution.py
+++ b/solution.py
@@ -10,27 +10,21 @@
     return [(i, i + s) for i in range(n) if 0 <= i + s < n]
 
 
-def tile_halo(field, width):
-    nx, ny = lax.axis_size("gx"), lax.axis_size("gy")
-    w = width
-    from_left = lax.ppermute(field[:, -w:], "gx", shifted(nx, 1))
-    from_right = lax.ppermute(field[:, :w], "gx", shifted(nx, -1))
-    wide = jnp.concatenate([from_left, field, from_right], axis=1)
-    from_below = lax.ppermute(wide[:, :, -w:], "gy", shifted(ny, 1))
-    from_above = lax.ppermute(wide[:, :, :w], "gy", shifted(ny, -1))
-    return jnp.concatenate([from_below, wide, from_above], axis=2)
-
-
-def strip_halo(field, width):
-    n = lax.axis_size("gx") * lax.axis_size("gy")
-    own = field.shape[1]
-    reach = -(-width // own)
-    both = ("gx", "gy")
-    lows = [lax.ppermute(field, both, shifted(n, d)) for d in range(reach, 0, -1)]
-    highs = [lax.ppermute(field, both, shifted(n, -d)) for d in range(1, reach + 1)]
-    lo = jnp.concatenate(lows, axis=1)[:, reach * own - width:]
-    hi = jnp.concatenate(highs, axis=1)[:, :width]
-    return jnp.concatenate([lo, field, hi], axis=1)
+def packed_ppermute(parts, axis, perm):
+    flat = jnp.concatenate([p.reshape(-1) for p in parts])
+    got = lax.ppermute(flat, axis, perm)
+    out, at = [], 0
+    for p in parts:
+        out.append(got[at:at + p.size].reshape(p.shape))
+        at += p.size
+    return out
+
+
+def x_halo(field, width):
+    nx = lax.axis_size("gx")
+    from_left = lax.ppermute(field[:, -width:], "gx", shifted(nx, 1))
+    from_right = lax.ppermute(field[:, :width], "gx", shifted(nx, -1))
+    return jnp.concatenate([from_left, field, from_right], axis=1)
 
 
 def lookup_kernel(step, idx_ref, tab_ref, coef_ref, lam_ref, mu_ref):
@@ -137,41 +131,96 @@
 def local(region_state, region_material, fine_state, fine_material, material_table):
     count_x = lax.axis_size("gx")
     count_y = lax.axis_size("gy")
+    flat = ("gx", "gy")
+    n_flat = count_x * count_y
+    me_y = lax.axis_index("gy")
     fine_x = fine_state.shape[1]
     fine_y = fine_state.shape[2]
+    fine_z = fine_state.shape[3]
+    own = region_state.shape[1]
     reg_y = region_state.shape[2]
     rows_each = reg_y // count_y
+    reach_y = 6
 
     coef_r, lam_r, mu_r = lookup(region_material, material_table, 0.6)
-    reg_ext = strip_halo(jnp.concatenate([region_state, coef_r[None]], 0), 2)
+    coef_f, lam_f, mu_f = lookup(fine_material, material_table, 0.2)
+
+    region_pay = jnp.concatenate([region_state, coef_r[None]], 0)
+    fine_pay = jnp.concatenate([fine_state, coef_f[None], lam_f[None], mu_f[None]], 0)
+    reg_lo, fine_lo = packed_ppermute(
+        [region_pay, fine_pay[:, :, -reach_y:]], flat, shifted(n_flat, 1)
+    )
+    reg_hi, fine_hi = packed_ppermute(
+        [region_pay, fine_pay[:, :, :reach_y]], flat, shifted(n_flat, -1)
+    )
+    fine_lo = jnp.where(me_y > 0, fine_lo, 0.0)
+    fine_hi = jnp.where(me_y < count_y - 1, fine_hi, 0.0)
+    lows, highs = [reg_lo], [reg_hi]
+    for d in range(2, -(-2 // own) + 1):
+        lows.insert(0, lax.ppermute(region_pay, flat, shifted(n_flat, d)))
+        highs.append(lax.ppermute(region_pay, flat, shifted(n_flat, -d)))
+    reg_ext = jnp.concatenate(
+        [jnp.concatenate(lows, 1)[:, -2:], region_pay, jnp.concatenate(highs, 1)[:, :2]], 1
+    )
     region_next = step_wide(
         reg_ext, reg_ext[9, 1:-1], region_state[3:], lam_r, mu_r, 0.6, 3.0, True
     )
 
     both = jnp.concatenate([region_state, region_next], 0).astype(jnp.bfloat16)
-    band = lax.all_to_all(both, "gy", 2, 1, tiled=True).astype(jnp.float32)
+    both = jnp.pad(both, ((0, 0), (0, 0), (rows_each, rows_each), (0, 0)))
+    send = jnp.concatenate(
+        [both[:, :, rows_each * d: rows_each * (d + 3)] for d in range(count_y)], 2
+    )
+    band = lax.all_to_all(send, "gy", 2, 1, tiled=True).astype(jnp.float32)
     columns = band.shape[1]
     high = lax.Precision.HIGHEST
+    along_y_w = interp_matrix(fine_y, rows_each)
+    zeros_w = jnp.zeros_like(along_y_w)
+    tiles_w = jnp.concatenate(
+        [
+            jnp.concatenate([along_y_w, zeros_w, zeros_w], 1),
+            jnp.concatenate([zeros_w, along_y_w, zeros_w], 1),
+            jnp.concatenate([zeros_w, zeros_w, along_y_w], 1),
+        ],
+        0,
+    )[fine_y - 4: 2 * fine_y + 4]
     first = jnp.einsum("fa,cabz->cfbz", interp_matrix(fine_x, columns), band, precision=high)
-    second = jnp.einsum("gb,cfbz->cfgz", interp_matrix(fine_y, rows_each), first, precision=high)
+    second = jnp.einsum("gb,cfbz->cfgz", tiles_w, first, precision=high)
     background = jnp.einsum(
-        "kz,cfgz->cfgk", interp_matrix(fine_state.shape[3], band.shape[3]), second, precision=high
+        "kz,cfgz->cfgk", interp_matrix(fine_z, band.shape[3]), second, precision=high
     )
     along_x = ramp(lax.axis_index("gx") * fine_x, fine_x, count_x * fine_x, fine_x)
-    along_y = ramp(lax.axis_index("gy") * fine_y, fine_y, count_y * fine_y, fine_y)
+    along_y = ramp(me_y * fine_y - 4, fine_y + 8, count_y * fine_y, fine_y)
     relax = (0.1 + 0.4 * jnp.maximum(along_x[:, None], along_y[None, :]))[:, :, None]
 
-    coef_f, lam_f, mu_f = lookup(fine_material, material_table, 0.2)
-    ext = tile_halo(jnp.concatenate([fine_state, coef_f[None]], 0), 2)
-    coef_ext = ext[9, 1:-1, 1:-1]
-    state = fine_state
+    wide = jnp.concatenate([fine_lo, fine_pay, fine_hi], axis=2)
+    lam_w, mu_w = wide[10], wide[11]
+    state = wide[:9]
+    coef_w = None
     for sub in range(1, 4):
-        if sub > 1:
-            ext = tile_halo(state, 2)
-        state = step_wide(ext, coef_ext, state[3:], lam_f, mu_f, 0.2, 1.0, False)
+        if sub == 1:
+            ext = x_halo(wide[:10], 2)
+            coef_w = ext[9, 1:-1]
+            ext = ext[:9]
+        else:
+            ext = x_halo(state, 2)
+        off = 2 * (sub - 1)
+        rows = state.shape[2]
+        state = step_wide(
+            ext,
+            coef_w[:, off + 1: off + rows - 1],
+            state[3:, :, 2:-2],
+            lam_w[:, off + 2: off + rows - 2],
+            mu_w[:, off + 2: off + rows - 2],
+            0.2,
+            1.0,
+            False,
+        )
         share = sub / 3.0
-        target = background[:9] + share * (background[9:] - background[:9])
-        state = state + relax[None] * (target - state)
+        target = background[:9, :, off: off + rows - 4] + share * (
+            background[9:, :, off: off + rows - 4] - background[:9, :, off: off + rows - 4]
+        )
+        state = state + relax[None, :, off: off + rows - 4] * (target - state)
     return (region_next, state)
 
 

time: 105 us -> 135 us (1.29)
  the two profiles are of different devices: /device:TPU:28 before, /device:TPU:0 now
where the time goes in v4:
time: 135 us; the launch traced here: 133 us
  starting transfers between devices  50.6 us (37%)
  local copies, waits for them, and re-layouts  32.8 us (24%)
  other arithmetic  29.8 us (22%)
  matrix products  10.5 us (8%)
  waiting for transfers between devices  4.23 us (3%)
  Pallas kernels  3.41 us (3%)
  between operations  1.59 us (1%)
    ppermute x3, starting transfers between devices, x_halo(): from_left = lax.ppermute(field[:, -width:], 'gx', shifted(nx, 1))  25.7 us
    unnamed x73, local copies, waits for them, and re-layouts  13 us
    all_to_all x1, starting transfers between devices, local(): band = lax.all_to_all(send, 'gy', 2, 1, tiled=True).astype(jnp.float32)  9.64 us
    another operation x12, other arithmetic, step_wide(): vel = vel_old + coef[None] * jnp.stack([acc_x, acc_y, acc_z])  6.36 us
    ppermute x2, starting transfers between devices, packed_ppermute(): got = lax.ppermute(flat, axis, perm)  5.26 us
    dot_general x1, matrix products, local(): second = jnp.einsum('gb,cfbz->cfgz', tiles_w, first, precision=high)  5.05 us
    ppermute x1, starting transfers between devices, local(): lows.insert(0, lax.ppermute(region_pay, flat, shifted(n_flat, d)))  4.84 us
    unnamed x18, other arithmetic  4.13 us
  transfers between devices with their start and end apart: 11, of which 5 were waited for; matrix products, arithmetic and copies ran while one was open for 30% of the time, Pallas kernels for 1%

profile of v4, /device:TPU:0, one launch (start us, length us, event | category | flops | bytes accessed | tf_op | source)
XLA Modules:
  0.0 132.9 jit_solution(11493300262539421246)
XLA Ops:
  0.6 1.4 %shard_map.68 = (f32[1,24,64]{2,1,0:T(8,128)}, f32[1,24,64]{2,1,0:T(8,128)}, f32[1,24,64]{2,1,0:T(8,128)}) custom-call(s32[1,24,64]{2,1,0:T(8,128)} %refs_0_.2, f32[3,8]{1,0:T(4,128)} %refs_1_.3), custom_call_target="tpu_custom_call" | custom-call | tf_op jit(solution)/shard_map/pallas_call | solution.py:48
  2.1 1.6 %pad_maximum_fusion.15 = f32[10,1,24,64]{3,2,1,0:T(8,128)} fusion(f32[1,1,24,64]{3,2,1,0:T(8,128)} %bitcast.623, f32[9,1,24,64]{3,2,1,0:T(8,128)} %param.5), kind=kLoop, calls=%fused_computation.232 | loop fusion | flops 15360 | bytes 122880 | tf_op jit(solution)/shard_map/concatenate | solution.py:148
  3.7 4.8 %collective-permute-start.3 = (f32[10,1,24,64]{3,2,1,0:T(8,128)}, f32[10,1,24,64]{3,2,1,0:T(8,128)S(1)}, u32[]{:S(2)}, u32[]{:S(2)}) collective-permute-start(f32[10,1,24,64]{3,2,1,0:T(8,128)} %pad_maximum_fusion.15), channel_id=1, source_target_pairs={{0,2},{1,3},{2,4},{3,5},{4,6},{5,7},{6,8},{7,9},{8,10},{9,11},{10,... | collective-permute-start | bytes 184328 | tf_op jit(solution)/shard_map/ppermute | solution.py:160
  8.5 1.3 collective-permute-start.2
  9.8 1.6 %reshape.549 = f32[15360]{0:T(1024)} reshape(f32[10,1,24,64]{3,2,1,0:T(8,128)} %pad_maximum_fusion.15) | data formatting | bytes 122880 | tf_op jit(solution)/shard_map/reshape | solution.py:14
  11.4 1.3 constant_dynamic-update-slice_fusion
  12.7 0.7 copy.59.refs_0_
  13.4 2.0 %shard_map.69 = (f32[24,9,128]{2,1,0:T(8,128)}, f32[24,9,128]{2,1,0:T(8,128)}, f32[24,9,128]{2,1,0:T(8,128)}) custom-call(s32[24,9,128]{2,1,0:T(8,128)} %copy.59.refs_0_, f32[3,8]{1,0:T(4,128)} %refs_1_.3), custom_call_target="tpu_custom_call" | custom-call | tf_op jit(solution)/shard_map/pallas_call | solution.py:48
  15.4 1.0 copy_dynamic-update-slice_fusion.2
  16.3 1.0 copy_dynamic-update-slice_fusion.1
  17.3 1.0 copy_dynamic-update-slice_fusion
  18.6 1.0 reshape.550
  19.9 1.0 reshape.552
  20.9 2.5 %pad_maximum_fusion.5 = (f32[236544]{0:T(1024)S(1)}, f32[236544]{0:T(1024)}) fusion(f32[15360]{0:T(1024)S(1)} %copy-done.8, f32[221184]{0:T(1024)} %reshape.550, f32[221184]{0:T(1024)} %reshape.552), kind=kLoop, calls=%fused_computation.24 | loop fusion | flops 473088 | bytes 3723264 | tf_op jit(solution)/shard_map/concatenate | solution.py:14
  23.4 1.3 collective-permute-start.1
  24.7 4.0 %collective-permute-start = (f32[236544]{0:T(1024)S(1)}, f32[236544]{0:T(1024)}, u32[]{:S(2)}, u32[]{:S(2)}) collective-permute-start(f32[236544]{0:T(1024)S(1)} %get-tuple-element.109), channel_id=1, source_target_pairs={{0,1},{1,2},{2,3},{3,4},{4,5},{5,6},{6,7},{7,8},{8,9},{9,10},{10,1... | collective-permute-start | bytes 2838536 | tf_op jit(solution)/shard_map/ppermute | solution.py:15
  29.3 0.6 compare_select_fusion.9
  30.6 0.7 multiply_add_fusion.1
  33.1 0.8 slice.1155
  34.0 0.8 slice.1153
  35.2 0.8 fusion.177
  36.0 0.8 fusion.182
  36.8 0.8 fusion.187
  37.7 0.6 constant_dynamic-update-slice_fusion.7
  39.3 0.7 constant_dynamic-update-slice_fusion.11
  39.9 1.3 slice_select_fusion
  41.2 1.2 select_n.369
  42.4 1.4 %copy.66 = f32[12,24,6,128]{3,1,2,0:T(8,128)S(1)} copy(f32[12,24,6,128]{3,2,1,0:T(8,128)} %select_n.369) | data formatting | bytes 1769472 | tf_op jit(solution)/shard_map/jit(_where)/select_n | solution.py:157
  43.8 1.2 slice_select_fusion.1
  45.0 1.2 select_n.366
  46.2 1.4 %copy.65 = f32[12,24,6,128]{3,1,2,0:T(8,128)S(1)} copy(f32[12,24,6,128]{3,2,1,0:T(8,128)} %select_n.366) | data formatting | bytes 1769472 | tf_op jit(solution)/shard_map/jit(_where)/select_n | solution.py:156
  47.6 0.9 pad_maximum_fusion.12
  48.5 1.3 collective-permute-start.5
  49.8 16.1 %collective-permute-start.4 = (f32[10,2,21,128]{3,1,2,0:T(2,128)}, f32[10,2,21,128]{3,1,2,0:T(2,128)}, u32[]{:S(2)}, u32[]{:S(2)}) collective-permute-start(f32[10,2,21,128]{3,1,2,0:T(2,128)} %get-tuple-element.35), channel_id=1, source_target_pairs={{0,8},{8,16},{16,24},{1,9},{9,17},{17,25},{2,10},{10,18},{18,26},{... | collective-permute-start | bytes 645128 | tf_op jit(solution)/shard_map/ppermute | solution.py:25
  65.9 0.6 constant_dynamic-update-slice_fusion.10
  66.6 0.7 constant_dynamic-update-slice_fusion.9
  67.2 0.7 constant_dynamic-update-slice_fusion.8
  68.1 1.0 reshape.557
  69.1 9.6 %all-to-all-start = ((bf16[8,2,5184]{2,1,0:T(2,128)(2,1)}), bf16[8,2,5184]{2,1,0:T(2,128)(2,1)S(1)}, u32[]{:S(2)}, u32[]{:S(2)}) async-start(bf16[8,2,5184]{2,1,0:T(2,128)(2,1)} %reshape.557), calls=%async_computation | async-start | bytes 335872 | tf_op jit(solution)/shard_map/all_to_all | solution.py:174
  79.3 1.3 constant_dynamic-update-slice_fusion.5
  80.6 1.3 constant_dynamic-update-slice_fusion.4
  82.1 1.6 %slice.1193 = f32[10,24,21,128]{3,1,2,0:T(8,128)} slice(f32[12,24,21,128]{3,1,2,0:T(8,128)S(1)} %pad_maximum_fusion.1), slice={[0:10], [0:24], [0:21], [0:128]} | slice | bytes 5160960 | tf_op jit(solution)/shard_map/slice | solution.py:202
  83.7 0.7 maximum_bitcast_fusion.4
  84.6 1.1 reshape.558
  85.7 2.0 %convolution_bitcast_fusion = f32[18,24,9,64]{3,1,2,0:T(8,128)S(1)} fusion(bf16[18,8,9,64]{3,0,2,1:T(8,128)(2,1)} %bitcast.622, f32[24]{0:T(128)S(1)} %copy-done.21, s32[24]{0:T(128)S(1)} %copy-done.24, f32[24]{0:T(128)S(1)} %copy-done.22, s32[24]{0:T(128)S(1)} %copy-done.23), kind=kOutput, calls=%fused_computation.15 | convolution fusion | flops 23888832 | bytes 1161600 | tf_op jit(solution)/shard_map/fa,cabz->cfbz/dot_general | solution.py:187
  87.8 5.0 %fusion.4 = f32[18,24,17,64]{3,2,1,0:T(8,128)S(1)} fusion(f32[18,24,9,64]{3,1,2,0:T(8,128)S(1)} %convolution_bitcast_fusion, f32[9,3]{0,1:T(4,128)S(1)} %select_add_fusion, f32[9,3]{0,1:T(4,128)S(1)} %broadcast.1095), kind=kOutput, calls=%fused_computation.7 | convolution fusion | flops 50763104 | bytes 2875608 | tf_op jit(solution)/shard_map/gb,cfbz->cfgz/dot_general | solution.py:188
  92.9 3.4 %fusion = f32[18,24,17,128]{3,1,2,0:T(8,128)S(1)} fusion(f32[18,24,17,64]{3,2,1,0:T(8,128)S(1)} %fusion.4, f32[128]{0:T(128)S(1)} %copy-done.17, s32[128]{0:T(128)S(1)} %copy-done.20, f32[128]{0:T(128)S(1)} %copy-done.18, s32[128]{0:T(128)S(1)} %copy-done.19), kind=kOutput, calls=%fused_computation | convolution fusion | flops 721985536 | bytes 5642240 | tf_op jit(solution)/shard_map/kz,cfgz->cfgk/dot_general | solution.py:189
  96.3 1.0 maximum_bitcast_fusion.2
  97.5 1.7 %pad_maximum_fusion = f32[10,28,21,128]{3,1,2,0:T(8,128)S(1)} fusion(f32[10,2,21,128]{3,1,2,0:T(2,128)} %collective-permute-done.5, f32[10,24,21,128]{3,1,2,0:T(8,128)S(1)} %copy-done, f32[10,2,21,128]{3,1,2,0:T(2,128)} %collective-permute-done.4), kind=kLoop, calls=%fused_computation.4 | loop fusion | flops 1505280 | bytes 6021120 | tf_op jit(solution)/shard_map/concatenate | solution.py:27
  99.5 1.0 fusion.25
  100.5 1.0 fusion.31
  101.6 1.1 fusion.36
  103.1 0.7 copy-done.3
  106.2 1.3 collective-permute-start.7
  107.5 4.6 %collective-permute-start.6 = (f32[9,2,17,128]{3,1,2,0:T(2,128)S(1)}, f32[9,2,17,128]{3,1,2,0:T(2,128)S(1)}, u32[]{:S(2)}, u32[]{:S(2)}) collective-permute-start(f32[9,2,17,128]{3,1,2,0:T(2,128)S(1)} %get-tuple-element.43), channel_id=1, source_target_pairs={{0,8},{8,16},{16,24},{1,9},{9,17},{17,25},{2,10},{10,18},{18,26},{... | collective-permute-start | bytes 470024 | tf_op jit(solution)/shard_map/ppermute | solution.py:25
  113.3 1.1 collective-permute-done.7
  114.4 1.2 collective-permute-done.6
  117.1 0.8 slice-done.1
  119.9 1.3 collective-permute-start.9
  121.2 5.0 %collective-permute-start.8 = (f32[9,2,13,128]{3,1,2,0:T(2,128)S(1)}, f32[9,2,13,128]{3,1,2,0:T(2,128)S(1)}, u32[]{:S(2)}, u32[]{:S(2)}) collective-permute-start(f32[9,2,13,128]{3,1,2,0:T(2,128)S(1)} %get-tuple-element.48), channel_id=1, source_target_pairs={{0,8},{8,16},{16,24},{1,9},{9,17},{17,25},{2,10},{10,18},{18,26},{... | collective-permute-start | bytes 359432 | tf_op jit(solution)/shard_map/ppermute | solution.py:25
  126.2 0.6 constant_dynamic-update-slice_fusion.1
  127.1 1.5 %collective-permute-done.8 = f32[9,2,13,128]{3,1,2,0:T(2,128)S(1)} collective-permute-done((f32[9,2,13,128]{3,1,2,0:T(2,128)S(1)}, f32[9,2,13,128]{3,1,2,0:T(2,128)S(1)}, u32[]{:S(2)}, u32[]{:S(2)}) %collective-permute-start.8) | collective-permute-done | bytes 119840 | tf_op jit(solution)/shard_map/ppermute | solution.py:25
  129.8 0.7 slice-done.2
  131.7 1.2 fusion.19
  (169 shorter events, 16.5 us)
Async XLA Ops:
  0.6 12.1 %copy-start.9 = (s32[24,9,128]{2,0,1:T(8,128)S(1)}, s32[24,9,128]{2,0,1:T(8,128)}, u32[]{:S(2)}) copy-start(s32[24,9,128]{2,0,1:T(8,128)} %param.8) | copy-start | bytes 331780
  3.7 31.6 %collective-permute-start.3 = (f32[10,1,24,64]{3,2,1,0:T(8,128)}, f32[10,1,24,64]{3,2,1,0:T(8,128)S(1)}, u32[]{:S(2)}, u32[]{:S(2)}) collective-permute-start(f32[10,1,24,64]{3,2,1,0:T(8,128)} %pad_maximum_fusion.15), channel_id=1, source_target_pairs={{0,2},{1,3},{2,4},{3,5},{4,6},{5,7},{6,8},{7,9},{8,10},{9,11},{10,... | collective-permute-start | bytes 184328 | tf_op jit(solution)/shard_map/ppermute | solution.py:160
  8.5 26.7 %collective-permute-start.2 = (f32[10,1,24,64]{3,2,1,0:T(8,128)}, f32[10,1,24,64]{3,2,1,0:T(8,128)}, u32[]{:S(2)}, u32[]{:S(2)}) collective-permute-start(f32[10,1,24,64]{3,2,1,0:T(8,128)} %pad_maximum_fusion.15), channel_id=1, source_target_pairs={{2,0},{3,1},{4,2},{5,3},{6,4},{7,5},{8,6},{9,7},{10,8},{11,9},{12,... | collective-permute-start | bytes 184328 | tf_op jit(solution)/shard_map/ppermute | solution.py:161
  19.9 1.0 copy-start.8
  20.9 12.2 %copy-start.1 = (f32[9,1,24,64]{3,2,1,0:T(8,128)S(1)}, f32[9,1,24,64]{3,2,1,0:T(8,128)}, u32[]{:S(2)}) copy-start(f32[9,1,24,64]{3,2,1,0:T(8,128)} %param.5) | copy-start | bytes 165892
  20.9 14.0 %copy-start.4 = (f32[1,24,64]{2,1,0:T(8,128)S(1)}, f32[1,24,64]{2,1,0:T(8,128)}, u32[]{:S(2)}) copy-start(f32[1,24,64]{2,1,0:T(8,128)} %get-tuple-element.8) | copy-start | bytes 18436
  23.4 9.6 %collective-permute-start.1 = (f32[236544]{0:T(1024)}, f32[236544]{0:T(1024)}, u32[]{:S(2)}, u32[]{:S(2)}) collective-permute-start(f32[236544]{0:T(1024)} %get-tuple-element.110), channel_id=1, source_target_pairs={{1,0},{2,1},{3,2},{4,3},{5,4},{6,5},{7,6},{8,7},{9,8},{10,9},{11,1... | collective-permute-start | bytes 2838536 | tf_op jit(solution)/shard_map/ppermute | solution.py:15
  24.7 9.3 %collective-permute-start = (f32[236544]{0:T(1024)S(1)}, f32[236544]{0:T(1024)}, u32[]{:S(2)}, u32[]{:S(2)}) collective-permute-start(f32[236544]{0:T(1024)S(1)} %get-tuple-element.109), channel_id=1, source_target_pairs={{0,1},{1,2},{2,3},{3,4},{4,5},{5,6},{6,7},{7,8},{8,9},{9,10},{10,1... | collective-permute-start | bytes 2838536 | tf_op jit(solution)/shard_map/ppermute | solution.py:15
  35.2 3.4 %copy-start.5 = (f32[1,24,64]{2,1,0:T(8,128)S(1)}, f32[1,24,64]{2,1,0:T(8,128)}, u32[]{:S(2)}) copy-start(f32[1,24,64]{2,1,0:T(8,128)} %get-tuple-element.13) | copy-start | bytes 18436
  35.2 3.4 %copy-start.16 = (f32[1,24,64]{2,1,0:T(8,128)S(1)}, f32[1,24,64]{2,1,0:T(8,128)}, u32[]{:S(2)}) copy-start(f32[1,24,64]{2,1,0:T(8,128)} %get-tuple-element.12) | copy-start | bytes 18436
  39.9 2.4 %copy-start.6 = (bf16[18,1,24,64]{3,2,1,0:T(8,128)(2,1)}, bf16[18,1,24,64]{3,2,1,0:T(8,128)(2,1)S(1)}, u32[]{:S(2)}) copy-start(bf16[18,1,24,64]{3,2,1,0:T(8,128)(2,1)S(1)} %get-tuple-element.24) | copy-start | bytes 165892
  47.6 18.3 %copy-start.7 = (bf16[18,1,24,64]{3,2,1,0:T(8,128)(2,1)S(1)}, bf16[18,1,24,64]{3,2,1,0:T(8,128)(2,1)}, u32[]{:S(2)}) copy-start(bf16[18,1,24,64]{3,2,1,0:T(8,128)(2,1)} %copy-done.6) | copy-start | bytes 165892
  48.5 47.8 %collective-permute-start.5 = (f32[10,2,21,128]{3,1,2,0:T(2,128)}, f32[10,2,21,128]{3,1,2,0:T(2,128)}, u32[]{:S(2)}, u32[]{:S(2)}) collective-permute-start(f32[10,2,21,128]{3,1,2,0:T(2,128)} %get-tuple-element.36), channel_id=1, source_target_pairs={{8,0},{16,8},{24,16},{9,1},{17,9},{25,17},{10,2},{18,10},{26,18},{... | collective-permute-start | bytes 645128 | tf_op jit(solution)/shard_map/ppermute | solution.py:26
  49.8 46.5 %collective-permute-start.4 = (f32[10,2,21,128]{3,1,2,0:T(2,128)}, f32[10,2,21,128]{3,1,2,0:T(2,128)}, u32[]{:S(2)}, u32[]{:S(2)}) collective-permute-start(f32[10,2,21,128]{3,1,2,0:T(2,128)} %get-tuple-element.35), channel_id=1, source_target_pairs={{0,8},{8,16},{16,24},{1,9},{9,17},{17,25},{2,10},{10,18},{18,26},{... | collective-permute-start | bytes 645128 | tf_op jit(solution)/shard_map/ppermute | solution.py:25
  69.1 15.6 %all-to-all-start = ((bf16[8,2,5184]{2,1,0:T(2,128)(2,1)}), bf16[8,2,5184]{2,1,0:T(2,128)(2,1)S(1)}, u32[]{:S(2)}, u32[]{:S(2)}) async-start(bf16[8,2,5184]{2,1,0:T(2,128)(2,1)} %reshape.557), calls=%async_computation | async-start | bytes 335872 | tf_op jit(solution)/shard_map/all_to_all | solution.py:174
  83.7 2.0 %copy-start.21 = (f32[24]{0:T(128)S(1)}, f32[24]{0:T(128)}, u32[]{:S(2)}) copy-start(f32[24]{0:T(128)} %get-tuple-element.141) | copy-start | bytes 292
  83.7 2.0 %copy-start.22 = (f32[24]{0:T(128)S(1)}, f32[24]{0:T(128)}, u32[]{:S(2)}) copy-start(f32[24]{0:T(128)} %get-tuple-element.142) | copy-start | bytes 292
  83.7 2.0 %copy-start.23 = (s32[24]{0:T(128)S(1)}, s32[24]{0:T(128)}, u32[]{:S(2)}) copy-start(s32[24]{0:T(128)} %get-tuple-element.143) | copy-start | bytes 292
  83.7 2.0 %copy-start.24 = (s32[24]{0:T(128)S(1)}, s32[24]{0:T(128)}, u32[]{:S(2)}) copy-start(s32[24]{0:T(128)} %get-tuple-element.144) | copy-start | bytes 292
  87.7 5.1 %copy-start.17 = (f32[128]{0:T(128)S(1)}, f32[128]{0:T(128)}, u32[]{:S(2)}) copy-start(f32[128]{0:T(128)} %get-tuple-element.149) | copy-start | bytes 1540
  87.7 5.1 %copy-start.18 = (f32[128]{0:T(128)S(1)}, f32[128]{0:T(128)}, u32[]{:S(2)}) copy-start(f32[128]{0:T(128)} %get-tuple-element.150) | copy-start | bytes 1540
  87.8 5.1 %copy-start.19 = (s32[128]{0:T(128)S(1)}, s32[128]{0:T(128)}, u32[]{:S(2)}) copy-start(s32[128]{0:T(128)} %get-tuple-element.151) | copy-start | bytes 1540
  87.8 5.1 %copy-start.20 = (s32[128]{0:T(128)S(1)}, s32[128]{0:T(128)}, u32[]{:S(2)}) copy-start(s32[128]{0:T(128)} %get-tuple-element.152) | copy-start | bytes 1540
  92.9 3.5 %copy-start = (f32[10,24,21,128]{3,1,2,0:T(8,128)S(1)}, f32[10,24,21,128]{3,1,2,0:T(8,128)}, u32[]{:S(2)}) copy-start(f32[10,24,21,128]{3,1,2,0:T(8,128)} %slice.1193) | copy-start | bytes 7741444
  99.2 1.3 copy-start.2
  101.5 1.1 slice-start
  102.8 0.9 copy-start.3
  104.9 0.7 copy-start.13
  105.6 6.5 %copy-start.11 = (f32[1,1,24,64]{3,2,1,0:T(8,128)S(1)}, f32[1,1,24,64]{3,2,1,0:T(8,128)}, u32[]{:S(2)}) copy-start(f32[1,1,24,64]{3,2,1,0:T(8,128)} %get-tuple-element.23) | copy-start | bytes 18436
  105.6 7.1 %copy-start.12 = (f32[1,1,24,64]{3,2,1,0:T(8,128)S(1)}, f32[1,1,24,64]{3,2,1,0:T(8,128)}, u32[]{:S(2)}) copy-start(f32[1,1,24,64]{3,2,1,0:T(8,128)} %get-tuple-element.21) | copy-start | bytes 18436
  106.2 8.2 %collective-permute-start.7 = (f32[9,2,17,128]{3,1,2,0:T(2,128)S(1)}, f32[9,2,17,128]{3,1,2,0:T(2,128)S(1)}, u32[]{:S(2)}, u32[]{:S(2)}) collective-permute-start(f32[9,2,17,128]{3,1,2,0:T(2,128)S(1)} %get-tuple-element.44), channel_id=1, source_target_pairs={{8,0},{16,8},{24,16},{9,1},{17,9},{25,17},{10,2},{18,10},{26,18},{... | collective-permute-start | bytes 470024 | tf_op jit(solution)/shard_map/ppermute | solution.py:26
  107.5 8.1 %collective-permute-start.6 = (f32[9,2,17,128]{3,1,2,0:T(2,128)S(1)}, f32[9,2,17,128]{3,1,2,0:T(2,128)S(1)}, u32[]{:S(2)}, u32[]{:S(2)}) collective-permute-start(f32[9,2,17,128]{3,1,2,0:T(2,128)S(1)} %get-tuple-element.43), channel_id=1, source_target_pairs={{0,8},{8,16},{16,24},{1,9},{9,17},{17,25},{2,10},{10,18},{18,26},{... | collective-permute-start | bytes 470024 | tf_op jit(solution)/shard_map/ppermute | solution.py:25
  116.9 0.9 slice-start.1
  118.6 0.7 copy-start.15
  119.3 6.8 %copy-start.10 = (f32[1,24,64]{2,1,0:T(8,128)S(1)}, f32[1,24,64]{2,1,0:T(8,128)}, u32[]{:S(2)}) copy-start(f32[1,24,64]{2,1,0:T(8,128)} %get-tuple-element.19) | copy-start | bytes 18436
  119.9 7.2 %collective-permute-start.9 = (f32[9,2,13,128]{3,1,2,0:T(2,128)S(1)}, f32[9,2,13,128]{3,1,2,0:T(2,128)S(1)}, u32[]{:S(2)}, u32[]{:S(2)}) collective-permute-start(f32[9,2,13,128]{3,1,2,0:T(2,128)S(1)} %get-tuple-element.49), channel_id=1, source_target_pairs={{8,0},{16,8},{24,16},{9,1},{17,9},{25,17},{10,2},{18,10},{26,18},{... | collective-permute-start | bytes 359432 | tf_op jit(solution)/shard_map/ppermute | solution.py:26
  121.2 7.4 %collective-permute-start.8 = (f32[9,2,13,128]{3,1,2,0:T(2,128)S(1)}, f32[9,2,13,128]{3,1,2,0:T(2,128)S(1)}, u32[]{:S(2)}, u32[]{:S(2)}) collective-permute-start(f32[9,2,13,128]{3,1,2,0:T(2,128)S(1)} %get-tuple-element.48), channel_id=1, source_target_pairs={{0,8},{8,16},{16,24},{1,9},{9,17},{17,25},{2,10},{10,18},{18,26},{... | collective-permute-start | bytes 359432 | tf_op jit(solution)/shard_map/ppermute | solution.py:25
  129.5 0.9 slice-start.2
  131.0 0.7 copy-start.14

commit v5 on v4

--- a/solution.py
+++ b/solution.py
@@ -8,16 +8,6 @@
 
 def shifted(n, s):
     return [(i, i + s) for i in range(n) if 0 <= i + s < n]
-
-
-def packed_ppermute(parts, axis, perm):
-    flat = jnp.concatenate([p.reshape(-1) for p in parts])
-    got = lax.ppermute(flat, axis, perm)
-    out, at = [], 0
-    for p in parts:
-        out.append(got[at:at + p.size].reshape(p.shape))
-        at += p.size
-    return out
 
 
 def x_halo(field, width):
@@ -147,14 +137,10 @@
 
     region_pay = jnp.concatenate([region_state, coef_r[None]], 0)
     fine_pay = jnp.concatenate([fine_state, coef_f[None], lam_f[None], mu_f[None]], 0)
-    reg_lo, fine_lo = packed_ppermute(
-        [region_pay, fine_pay[:, :, -reach_y:]], flat, shifted(n_flat, 1)
-    )
-    reg_hi, fine_hi = packed_ppermute(
-        [region_pay, fine_pay[:, :, :reach_y]], flat, shifted(n_flat, -1)
-    )
-    fine_lo = jnp.where(me_y > 0, fine_lo, 0.0)
-    fine_hi = jnp.where(me_y < count_y - 1, fine_hi, 0.0)
+    fine_lo = lax.ppermute(fine_pay[:, :, -reach_y:], "gy", shifted(count_y, 1))
+    fine_hi = lax.ppermute(fine_pay[:, :, :reach_y], "gy", shifted(count_y, -1))
+    reg_lo = lax.ppermute(region_pay, flat, shifted(n_flat, 1))
+    reg_hi = lax.ppermute(region_pay, flat, shifted(n_flat, -1))
     lows, highs = [reg_lo], [reg_hi]
     for d in range(2, -(-2 // own) + 1):
         lows.insert(0, lax.ppermute(region_pay, flat, shifted(n_flat, d)))

time: 135 us -> 109 us (0.81)
  local copies, waits for them, and re-layouts: 32.8 us -> 22 us
  other arithmetic: 29.8 us -> 19.4 us
  starting transfers between devices: 50.6 us -> 41.2 us
  waiting for transfers between devices: 4.23 us -> 9.8 us
    ppermute x3, starting transfers between devices: 25.7 us -> 14.9 us  [x_halo(): from_left = lax.ppermute(field[:, -width:], 'gx', shifted(nx, 1))]
    select_n x4 -> x0, local copies, waits for them, and re-layouts: 5.17 us -> none  [the longest x2 2.58 us: local(): fine_hi = jnp.where(me_y < count_y - 1, fine_hi, 0.0)]
    ppermute x2 -> x4, starting transfers between devices: 5.26 us -> 9.86 us  [the longest x1 4.27 us: local(): fine_lo = lax.ppermute(fine_pay[:, :, -reach_y:], 'gy', shifted(count_y, 1))]
    all_to_all x1, starting transfers between devices: 9.64 us -> 5.83 us  [local(): band = lax.all_to_all(send, 'gy', 2, 1, tiled=True).astype(jnp.float32)]
    reshape x5 -> x0, local copies, waits for them, and re-layouts: 3.81 us -> none  [the longest x3 3.65 us: packed_ppermute(): flat = jnp.concatenate([p.reshape(-1) for p in parts])]
    all_to_all x1, waiting for transfers between devices: 0.14 us -> 2.82 us  [local(): band = lax.all_to_all(send, 'gy', 2, 1, tiled=True).astype(jnp.float32)]
    concatenate x1 -> x0, other arithmetic: 2.52 us -> none  [packed_ppermute(): flat = jnp.concatenate([p.reshape(-1) for p in parts])]
    select_n x2 -> x0, other arithmetic: 2.49 us -> none  [the longest x1 1.27 us: local(): fine_hi = jnp.where(me_y < count_y - 1, fine_hi, 0.0)]
  transfers between devices with their start and end apart: 11 -> 13, of which waited for: 5 -> 7; matrix products, arithmetic and copies ran while one was open for 30% -> 33% of each run, Pallas kernels for 1% -> 2%
where the time goes in v5:
time: 109 us; the launch traced here: 107 us
  starting transfers between devices  41.2 us (38%)
  local copies, waits for them, and re-layouts  22 us (20%)
  other arithmetic  19.4 us (18%)
  matrix products  9.97 us (9%)
  waiting for transfers between devices  9.8 us (9%)
  Pallas kernels  3.38 us (3%)
  between operations  1.56 us (1%)
    ppermute x3, starting transfers between devices, x_halo(): from_left = lax.ppermute(field[:, -width:], 'gx', shifted(nx, 1))  14.9 us
    unnamed x57, local copies, waits for them, and re-layouts  12.7 us
    all_to_all x1, starting transfers between devices, local(): band = lax.all_to_all(send, 'gy', 2, 1, tiled=True).astype(jnp.float32)  5.83 us
    ppermute x1, starting transfers between devices, local(): lows.insert(0, lax.ppermute(region_pay, flat, shifted(n_flat, d)))  5.49 us
    dot_general x1, matrix products, local(): second = jnp.einsum('gb,cfbz->cfgz', tiles_w, first, precision=high)  4.99 us
    unnamed x18, other arithmetic  4.55 us
    ppermute x1, starting transfers between devices, local(): fine_lo = lax.ppermute(fine_pay[:, :, -reach_y:], 'gy', shifted(count_y, 1))  4.27 us
    ppermute x3, waiting for transfers between devices, x_halo(): from_left = lax.ppermute(field[:, -width:], 'gx', shifted(nx, 1))  4.15 us
  transfers between devices with their start and end apart: 13, of which 7 were waited for; matrix products, arithmetic and copies ran while one was open for 33% of the time, Pallas kernels for 2%

profile of v5, /device:TPU:0, one launch (start us, length us, event | category | flops | bytes accessed | tf_op | source)
XLA Modules:
  0.0 107.3 jit_solution(4535332387233722594)
XLA Ops:
  0.6 1.5 %shard_map.68 = (f32[1,24,64]{2,1,0:T(8,128)}, f32[1,24,64]{2,1,0:T(8,128)}, f32[1,24,64]{2,1,0:T(8,128)}) custom-call(s32[1,24,64]{2,1,0:T(8,128)} %refs_0_.2, f32[3,8]{1,0:T(4,128)} %refs_1_.3), custom_call_target="tpu_custom_call" | custom-call | tf_op jit(solution)/shard_map/pallas_call | solution.py:38
  2.1 1.6 %pad_maximum_fusion.13 = f32[10,1,24,64]{3,2,1,0:T(8,128)} fusion(f32[1,1,24,64]{3,2,1,0:T(8,128)} %bitcast.621, f32[9,1,24,64]{3,2,1,0:T(8,128)} %param.5), kind=kLoop, calls=%fused_computation.228 | loop fusion | flops 15360 | bytes 122880 | tf_op jit(solution)/shard_map/concatenate | solution.py:138
  3.7 1.3 %collective-permute-start.1 = (f32[10,1,24,64]{3,2,1,0:T(8,128)}, f32[10,1,24,64]{3,2,1,0:T(8,128)S(1)}, u32[]{:S(2)}, u32[]{:S(2)}) collective-permute-start(f32[10,1,24,64]{3,2,1,0:T(8,128)} %pad_maximum_fusion.13), channel_id=1, source_target_pairs={{1,0},{2,1},{3,2},{4,3},{5,4},{6,5},{7,6},{8,7},{9,8},{10,9},{11,1... | collective-permute-start | bytes 184328 | tf_op jit(solution)/shard_map/ppermute | solution.py:143
  5.0 3.0 %collective-permute-start = (f32[10,1,24,64]{3,2,1,0:T(8,128)}, f32[10,1,24,64]{3,2,1,0:T(8,128)S(1)}, u32[]{:S(2)}, u32[]{:S(2)}) collective-permute-start(f32[10,1,24,64]{3,2,1,0:T(8,128)} %pad_maximum_fusion.13), channel_id=1, source_target_pairs={{0,1},{1,2},{2,3},{3,4},{4,5},{5,6},{6,7},{7,8},{8,9},{9,10},{10,1... | collective-permute-start | bytes 184328 | tf_op jit(solution)/shard_map/ppermute | solution.py:142
  8.0 5.5 %collective-permute-start.3 = (f32[10,1,24,64]{3,2,1,0:T(8,128)}, f32[10,1,24,64]{3,2,1,0:T(8,128)}, u32[]{:S(2)}, u32[]{:S(2)}) collective-permute-start(f32[10,1,24,64]{3,2,1,0:T(8,128)} %pad_maximum_fusion.13), channel_id=1, source_target_pairs={{0,2},{1,3},{2,4},{3,5},{4,6},{5,7},{6,8},{7,9},{8,10},{9,11},{10,... | collective-permute-start | bytes 184328 | tf_op jit(solution)/shard_map/ppermute | solution.py:146
  13.5 1.3 %collective-permute-start.2 = (f32[10,1,24,64]{3,2,1,0:T(8,128)}, f32[10,1,24,64]{3,2,1,0:T(8,128)}, u32[]{:S(2)}, u32[]{:S(2)}) collective-permute-start(f32[10,1,24,64]{3,2,1,0:T(8,128)} %pad_maximum_fusion.13), channel_id=1, source_target_pairs={{2,0},{3,1},{4,2},{5,3},{6,4},{7,5},{8,6},{9,7},{10,8},{11,9},{12,... | collective-permute-start | bytes 184328 | tf_op jit(solution)/shard_map/ppermute | solution.py:147
  14.8 1.3 %constant_dynamic-update-slice_fusion.7 = f32[12,24,9,128]{3,1,2,0:T(8,128)S(1)} fusion(f32[9,24,9,128]{3,1,2,0:T(8,128)} %param.7), kind=kLoop, calls=%fused_computation.294 | loop fusion | bytes 1990656
  16.1 0.7 copy.47.refs_0_
  16.8 1.9 %shard_map.69 = (f32[24,9,128]{2,1,0:T(8,128)}, f32[24,9,128]{2,1,0:T(8,128)}, f32[24,9,128]{2,1,0:T(8,128)}) custom-call(s32[24,9,128]{2,1,0:T(8,128)} %copy.47.refs_0_, f32[3,8]{1,0:T(4,128)} %refs_1_.3), custom_call_target="tpu_custom_call" | custom-call | tf_op jit(solution)/shard_map/pallas_call | solution.py:38
  18.7 1.0 copy_dynamic-update-slice_fusion.2
  19.7 1.0 copy_dynamic-update-slice_fusion.1
  20.6 1.0 copy_dynamic-update-slice_fusion
  21.7 1.3 %fusion.255 = (f32[12,24,6,128]{3,1,2,0:T(8,128)}, f32[12,24,6,128]{3,1,2,0:T(8,128)}) fusion(f32[12,24,9,128]{3,1,2,0:T(8,128)S(1)} %copy_dynamic-update-slice_fusion), kind=kLoop, calls=%fused_computation.481 | loop fusion | bytes 3538944 | tf_op jit(solution)/shard_map/slice | solution.py:140
  23.0 1.3 %collective-permute-start.5 = (f32[12,24,6,128]{3,1,2,0:T(8,128)}, f32[12,24,6,128]{3,1,2,0:T(8,128)S(1)}, u32[]{:S(2)}, u32[]{:S(2)}) collective-permute-start(f32[12,24,6,128]{3,1,2,0:T(8,128)} %get-tuple-element.51), channel_id=1, source_target_pairs={{1,0},{2,1},{3,2},{4,3},{5,4},{6,5},{7,6},{9,8},{10,9},{11,10},{12... | collective-permute-start | bytes 2654216 | tf_op jit(solution)/shard_map/ppermute | solution.py:141
  24.3 0.6 constant_dynamic-update-slice_fusion.15
  24.9 0.6 compare_select_fusion.8
  25.5 0.6 compare_select_fusion.9
  26.1 0.5 compare_select_fusion
  26.7 0.7 multiply_add_fusion.1
  27.4 0.6 slice_bitcast_fusion.26
  28.0 0.6 slice_bitcast_fusion.25
  28.6 0.6 compare_select_fusion.1
  29.2 4.3 %collective-permute-start.4 = (f32[12,24,6,128]{3,1,2,0:T(8,128)}, f32[12,24,6,128]{3,1,2,0:T(8,128)S(1)}, u32[]{:S(2)}, u32[]{:S(2)}) collective-permute-start(f32[12,24,6,128]{3,1,2,0:T(8,128)} %get-tuple-element.50), channel_id=1, source_target_pairs={{0,1},{1,2},{2,3},{3,4},{4,5},{5,6},{6,7},{8,9},{9,10},{10,11},{11... | collective-permute-start | bytes 2654216 | tf_op jit(solution)/shard_map/ppermute | solution.py:140
  33.9 0.8 fusion.177
  34.7 0.8 fusion.182
  35.5 0.8 fusion.187
  36.3 0.6 constant_dynamic-update-slice_fusion.6
  37.3 0.6 constant_dynamic-update-slice_fusion.12
  37.9 0.7 constant_dynamic-update-slice_fusion.11
  38.6 0.6 constant_dynamic-update-slice_fusion.10
  39.2 0.7 constant_dynamic-update-slice_fusion.9
  39.9 0.7 constant_dynamic-update-slice_fusion.8
  40.8 1.0 reshape.512
  41.7 5.8 %all-to-all-start = ((bf16[8,2,5184]{2,1,0:T(2,128)(2,1)}), bf16[8,2,5184]{2,1,0:T(2,128)(2,1)}, u32[]{:S(2)}, u32[]{:S(2)}) async-start(bf16[8,2,5184]{2,1,0:T(2,128)(2,1)} %reshape.512), calls=%async_computation | async-start | bytes 335872 | tf_op jit(solution)/shard_map/all_to_all | solution.py:160
  47.6 0.6 constant_dynamic-update-slice_fusion.5
  48.2 1.3 %constant_dynamic-update-slice_fusion.4 = f32[9,1,24,64]{3,2,1,0:T(8,128)} fusion(f32[9,1,24,64]{3,2,1,0:T(8,128)} %constant_dynamic-update-slice_fusion.5, f32[1,24,64]{2,1,0:T(8,128)} %get-tuple-element.27), kind=kLoop, calls=%fused_computation.291 | loop fusion | bytes 24576
  49.5 1.3 %constant_dynamic-update-slice_fusion.3 = f32[9,1,24,64]{3,2,1,0:T(8,128)} fusion(f32[9,1,24,64]{3,2,1,0:T(8,128)} %constant_dynamic-update-slice_fusion.4, f32[1,24,64]{2,1,0:T(8,128)} %get-tuple-element.25), kind=kLoop, calls=%fused_computation.290 | loop fusion | bytes 24576
  50.8 2.8 %all-to-all-done = bf16[8,2,5184]{2,1,0:T(2,128)(2,1)} async-done(((bf16[8,2,5184]{2,1,0:T(2,128)(2,1)}), bf16[8,2,5184]{2,1,0:T(2,128)(2,1)}, u32[]{:S(2)}, u32[]{:S(2)}) %all-to-all-start) | async-done | bytes 165920 | tf_op jit(solution)/shard_map/all_to_all | solution.py:160
  53.6 1.2 %reshape.513 = bf16[72,1,18,64]{3,2,1,0:T(8,128)(2,1)S(1)} reshape(bf16[8,2,5184]{2,1,0:T(2,128)(2,1)} %all-to-all-done) | data formatting | bytes 331776
  54.8 1.7 %convolution_bitcast_fusion = f32[18,24,9,64]{3,1,2,0:T(8,128)S(1)} fusion(bf16[18,8,9,64]{3,0,2,1:T(8,128)(2,1)S(1)} %bitcast.620, f32[24]{0:T(128)} %get-tuple-element.139, s32[24]{0:T(128)} %get-tuple-element.142, f32[24]{0:T(128)} %get-tuple-element.140, s32[24]{0:T(128)} %get-tuple-element.141), kind=kOutput, calls=%fused_computation.15 | convolution fusion | flops 23888832 | bytes 1161600 | tf_op jit(solution)/shard_map/fa,cabz->cfbz/dot_general | solution.py:173
  56.6 5.0 %fusion.4 = f32[18,24,17,64]{3,2,1,0:T(8,128)S(1)} fusion(f32[18,24,9,64]{3,1,2,0:T(8,128)S(1)} %convolution_bitcast_fusion, f32[9,3]{0,1:T(4,128)S(1)} %select_add_fusion, f32[9,3]{0,1:T(4,128)S(1)} %broadcast.1088), kind=kOutput, calls=%fused_computation.7 | convolution fusion | flops 50763104 | bytes 2875608 | tf_op jit(solution)/shard_map/gb,cfbz->cfgz/dot_general | solution.py:174
  61.6 3.3 %fusion = f32[18,24,17,128]{3,1,2,0:T(8,128)S(1)} fusion(f32[18,24,17,64]{3,2,1,0:T(8,128)S(1)} %fusion.4, f32[128]{0:T(128)S(1)} %copy-done.13, s32[128]{0:T(128)S(1)} %copy-done.16, f32[128]{0:T(128)S(1)} %copy-done.14, s32[128]{0:T(128)S(1)} %copy-done.15), kind=kOutput, calls=%fused_computation | convolution fusion | flops 721985536 | bytes 5642240 | tf_op jit(solution)/shard_map/kz,cfgz->cfgk/dot_general | solution.py:175
  65.1 1.3 %collective-permute-start.7 = (f32[10,2,21,128]{3,1,2,0:T(2,128)S(1)}, f32[10,2,21,128]{3,1,2,0:T(2,128)S(1)}, u32[]{:S(2)}, u32[]{:S(2)}) collective-permute-start(f32[10,2,21,128]{3,1,2,0:T(2,128)S(1)} %get-tuple-element.36), channel_id=1, source_target_pairs={{8,0},{16,8},{24,16},{9,1},{17,9},{25,17},{10,2},{18,10},{26,18},{... | collective-permute-start | bytes 645128 | tf_op jit(solution)/shard_map/ppermute | solution.py:16
  66.4 4.8 %collective-permute-start.6 = (f32[10,2,21,128]{3,1,2,0:T(2,128)S(1)}, f32[10,2,21,128]{3,1,2,0:T(2,128)S(1)}, u32[]{:S(2)}, u32[]{:S(2)}) collective-permute-start(f32[10,2,21,128]{3,1,2,0:T(2,128)S(1)} %get-tuple-element.35), channel_id=1, source_target_pairs={{0,8},{8,16},{16,24},{1,9},{9,17},{17,25},{2,10},{10,18},{18,26},{... | collective-permute-start | bytes 645128 | tf_op jit(solution)/shard_map/ppermute | solution.py:15
  71.7 2.5 %collective-permute-done.7 = f32[10,2,21,128]{3,1,2,0:T(2,128)S(1)} collective-permute-done((f32[10,2,21,128]{3,1,2,0:T(2,128)S(1)}, f32[10,2,21,128]{3,1,2,0:T(2,128)S(1)}, u32[]{:S(2)}, u32[]{:S(2)}) %collective-permute-start.7) | collective-permute-done | bytes 215072 | tf_op jit(solution)/shard_map/ppermute | solution.py:16
  74.2 1.2 %collective-permute-done.6 = f32[10,2,21,128]{3,1,2,0:T(2,128)S(1)} collective-permute-done((f32[10,2,21,128]{3,1,2,0:T(2,128)S(1)}, f32[10,2,21,128]{3,1,2,0:T(2,128)S(1)}, u32[]{:S(2)}, u32[]{:S(2)}) %collective-permute-start.6) | collective-permute-done | bytes 215072 | tf_op jit(solution)/shard_map/ppermute | solution.py:15
  75.7 0.6 pad_maximum_fusion
  77.5 0.8 slice-done
  79.8 0.5 copy-done.9
  80.4 0.5 fusion.11
  80.9 1.3 %collective-permute-start.9 = (f32[9,2,17,128]{3,1,2,0:T(2,128)S(1)}, f32[9,2,17,128]{3,1,2,0:T(2,128)S(1)}, u32[]{:S(2)}, u32[]{:S(2)}) collective-permute-start(f32[9,2,17,128]{3,1,2,0:T(2,128)S(1)} %get-tuple-element.44), channel_id=1, source_target_pairs={{8,0},{16,8},{24,16},{9,1},{17,9},{25,17},{10,2},{18,10},{26,18},{... | collective-permute-start | bytes 470024 | tf_op jit(solution)/shard_map/ppermute | solution.py:16
  82.2 5.0 %collective-permute-start.8 = (f32[9,2,17,128]{3,1,2,0:T(2,128)S(1)}, f32[9,2,17,128]{3,1,2,0:T(2,128)S(1)}, u32[]{:S(2)}, u32[]{:S(2)}) collective-permute-start(f32[9,2,17,128]{3,1,2,0:T(2,128)S(1)} %get-tuple-element.43), channel_id=1, source_target_pairs={{0,8},{8,16},{16,24},{1,9},{9,17},{17,25},{2,10},{10,18},{18,26},{... | collective-permute-start | bytes 470024 | tf_op jit(solution)/shard_map/ppermute | solution.py:15
  87.3 0.6 constant_dynamic-update-slice_fusion.2
  87.9 0.6 constant_dynamic-update-slice_fusion.1
  88.5 1.5 %collective-permute-done.8 = f32[9,2,17,128]{3,1,2,0:T(2,128)S(1)} collective-permute-done((f32[9,2,17,128]{3,1,2,0:T(2,128)S(1)}, f32[9,2,17,128]{3,1,2,0:T(2,128)S(1)}, u32[]{:S(2)}, u32[]{:S(2)}) %collective-permute-start.8) | collective-permute-done | bytes 156704 | tf_op jit(solution)/shard_map/ppermute | solution.py:15
  90.5 0.4 pad_maximum_fusion.2
  91.5 0.8 slice-done.1
  93.7 0.4 fusion.16
  94.2 1.3 %collective-permute-start.11 = (f32[9,2,13,128]{3,1,2,0:T(2,128)S(1)}, f32[9,2,13,128]{3,1,2,0:T(2,128)S(1)}, u32[]{:S(2)}, u32[]{:S(2)}) collective-permute-start(f32[9,2,13,128]{3,1,2,0:T(2,128)S(1)} %get-tuple-element.49), channel_id=1, source_target_pairs={{8,0},{16,8},{24,16},{9,1},{17,9},{25,17},{10,2},{18,10},{26,18},{... | collective-permute-start | bytes 359432 | tf_op jit(solution)/shard_map/ppermute | solution.py:16
  95.5 5.0 %collective-permute-start.10 = (f32[9,2,13,128]{3,1,2,0:T(2,128)S(1)}, f32[9,2,13,128]{3,1,2,0:T(2,128)S(1)}, u32[]{:S(2)}, u32[]{:S(2)}) collective-permute-start(f32[9,2,13,128]{3,1,2,0:T(2,128)S(1)} %get-tuple-element.48), channel_id=1, source_target_pairs={{0,8},{8,16},{16,24},{1,9},{9,17},{17,25},{2,10},{10,18},{18,26},{... | collective-permute-start | bytes 359432 | tf_op jit(solution)/shard_map/ppermute | solution.py:15
  100.6 0.6 constant_dynamic-update-slice_fusion
  101.4 1.5 %collective-permute-done.10 = f32[9,2,13,128]{3,1,2,0:T(2,128)S(1)} collective-permute-done((f32[9,2,13,128]{3,1,2,0:T(2,128)S(1)}, f32[9,2,13,128]{3,1,2,0:T(2,128)S(1)}, u32[]{:S(2)}, u32[]{:S(2)}) %collective-permute-start.10) | collective-permute-done | bytes 119840 | tf_op jit(solution)/shard_map/ppermute | solution.py:15
  104.1 0.7 slice-done.2
  106.1 1.2 %fusion.19 = f32[9,24,9,128]{3,1,2,0:T(8,128)} fusion(f32[9,24,9,128]{3,1,2,0:T(8,128)S(1)} %fusion.143, f32[18,24,17,128]{3,1,2,0:T(8,128)S(1)} %fusion, f32[24,9]{0,1:T(8,128)S(1)} %copy-done.10), kind=kLoop, calls=%fused_computation.25 | loop fusion | flops 1244160 | bytes 3982176 | tf_op jit(solution)/shard_map/add | solution.py:209
  (141 shorter events, 9.7 us)
Async XLA Ops:
  0.6 15.4 %copy-start.5 = (s32[24,9,128]{2,0,1:T(8,128)S(1)}, s32[24,9,128]{2,0,1:T(8,128)}, u32[]{:S(2)}) copy-start(s32[24,9,128]{2,0,1:T(8,128)} %param.8) | copy-start | bytes 331780
  3.7 25.6 %collective-permute-start.1 = (f32[10,1,24,64]{3,2,1,0:T(8,128)}, f32[10,1,24,64]{3,2,1,0:T(8,128)S(1)}, u32[]{:S(2)}, u32[]{:S(2)}) collective-permute-start(f32[10,1,24,64]{3,2,1,0:T(8,128)} %pad_maximum_fusion.13), channel_id=1, source_target_pairs={{1,0},{2,1},{3,2},{4,3},{5,4},{6,5},{7,6},{8,7},{9,8},{10,9},{11,1... | collective-permute-start | bytes 184328 | tf_op jit(solution)/shard_map/ppermute | solution.py:143
  5.0 28.6 %collective-permute-start = (f32[10,1,24,64]{3,2,1,0:T(8,128)}, f32[10,1,24,64]{3,2,1,0:T(8,128)S(1)}, u32[]{:S(2)}, u32[]{:S(2)}) collective-permute-start(f32[10,1,24,64]{3,2,1,0:T(8,128)} %pad_maximum_fusion.13), channel_id=1, source_target_pairs={{0,1},{1,2},{2,3},{3,4},{4,5},{5,6},{6,7},{7,8},{8,9},{9,10},{10,1... | collective-permute-start | bytes 184328 | tf_op jit(solution)/shard_map/ppermute | solution.py:142
  8.0 25.9 %collective-permute-start.3 = (f32[10,1,24,64]{3,2,1,0:T(8,128)}, f32[10,1,24,64]{3,2,1,0:T(8,128)}, u32[]{:S(2)}, u32[]{:S(2)}) collective-permute-start(f32[10,1,24,64]{3,2,1,0:T(8,128)} %pad_maximum_fusion.13), channel_id=1, source_target_pairs={{0,2},{1,3},{2,4},{3,5},{4,6},{5,7},{6,8},{7,9},{8,10},{9,11},{10,... | collective-permute-start | bytes 184328 | tf_op jit(solution)/shard_map/ppermute | solution.py:146
  13.5 20.4 %collective-permute-start.2 = (f32[10,1,24,64]{3,2,1,0:T(8,128)}, f32[10,1,24,64]{3,2,1,0:T(8,128)}, u32[]{:S(2)}, u32[]{:S(2)}) collective-permute-start(f32[10,1,24,64]{3,2,1,0:T(8,128)} %pad_maximum_fusion.13), channel_id=1, source_target_pairs={{2,0},{3,1},{4,2},{5,3},{6,4},{7,5},{8,6},{9,7},{10,8},{11,9},{12,... | collective-permute-start | bytes 184328 | tf_op jit(solution)/shard_map/ppermute | solution.py:147
  20.6 3.6 %copy-start = (f32[9,1,24,64]{3,2,1,0:T(8,128)S(1)}, f32[9,1,24,64]{3,2,1,0:T(8,128)}, u32[]{:S(2)}) copy-start(f32[9,1,24,64]{3,2,1,0:T(8,128)} %param.5) | copy-start | bytes 165892
  21.6 11.9 %copy-start.2 = (f32[1,24,64]{2,1,0:T(8,128)S(1)}, f32[1,24,64]{2,1,0:T(8,128)}, u32[]{:S(2)}) copy-start(f32[1,24,64]{2,1,0:T(8,128)} %get-tuple-element.8) | copy-start | bytes 18436
  23.0 42.0 %collective-permute-start.5 = (f32[12,24,6,128]{3,1,2,0:T(8,128)}, f32[12,24,6,128]{3,1,2,0:T(8,128)S(1)}, u32[]{:S(2)}, u32[]{:S(2)}) collective-permute-start(f32[12,24,6,128]{3,1,2,0:T(8,128)} %get-tuple-element.51), channel_id=1, source_target_pairs={{1,0},{2,1},{3,2},{4,3},{5,4},{6,5},{7,6},{9,8},{10,9},{11,10},{12... | collective-permute-start | bytes 2654216 | tf_op jit(solution)/shard_map/ppermute | solution.py:141
  29.2 35.7 %collective-permute-start.4 = (f32[12,24,6,128]{3,1,2,0:T(8,128)}, f32[12,24,6,128]{3,1,2,0:T(8,128)S(1)}, u32[]{:S(2)}, u32[]{:S(2)}) collective-permute-start(f32[12,24,6,128]{3,1,2,0:T(8,128)} %get-tuple-element.50), channel_id=1, source_target_pairs={{0,1},{1,2},{2,3},{3,4},{4,5},{5,6},{6,7},{8,9},{9,10},{10,11},{11... | collective-permute-start | bytes 2654216 | tf_op jit(solution)/shard_map/ppermute | solution.py:140
  33.8 3.4 %copy-start.4 = (bf16[18,1,24,64]{3,2,1,0:T(8,128)(2,1)S(1)}, bf16[18,1,24,64]{3,2,1,0:T(8,128)(2,1)}, u32[]{:S(2)}) copy-start(bf16[18,1,24,64]{3,2,1,0:T(8,128)(2,1)} %constant_dynamic-update-slice_fusion.15) | copy-start | bytes 165892
  33.8 3.4 %copy-start.3 = (f32[1,24,64]{2,1,0:T(8,128)S(1)}, f32[1,24,64]{2,1,0:T(8,128)}, u32[]{:S(2)}) copy-start(f32[1,24,64]{2,1,0:T(8,128)} %get-tuple-element.10) | copy-start | bytes 18436
  33.8 3.4 %copy-start.12 = (f32[1,24,64]{2,1,0:T(8,128)S(1)}, f32[1,24,64]{2,1,0:T(8,128)}, u32[]{:S(2)}) copy-start(f32[1,24,64]{2,1,0:T(8,128)} %get-tuple-element.9) | copy-start | bytes 18436
  41.7 11.9 %all-to-all-start = ((bf16[8,2,5184]{2,1,0:T(2,128)(2,1)}), bf16[8,2,5184]{2,1,0:T(2,128)(2,1)}, u32[]{:S(2)}, u32[]{:S(2)}) async-start(bf16[8,2,5184]{2,1,0:T(2,128)(2,1)} %reshape.512), calls=%async_computation | async-start | bytes 335872 | tf_op jit(solution)/shard_map/all_to_all | solution.py:160
  56.5 5.0 %copy-start.13 = (f32[128]{0:T(128)S(1)}, f32[128]{0:T(128)}, u32[]{:S(2)}) copy-start(f32[128]{0:T(128)} %get-tuple-element.147) | copy-start | bytes 1540
  56.5 5.0 %copy-start.14 = (f32[128]{0:T(128)S(1)}, f32[128]{0:T(128)}, u32[]{:S(2)}) copy-start(f32[128]{0:T(128)} %get-tuple-element.148) | copy-start | bytes 1540
  56.5 5.0 %copy-start.15 = (s32[128]{0:T(128)S(1)}, s32[128]{0:T(128)}, u32[]{:S(2)}) copy-start(s32[128]{0:T(128)} %get-tuple-element.149) | copy-start | bytes 1540
  56.6 5.0 %copy-start.16 = (s32[128]{0:T(128)S(1)}, s32[128]{0:T(128)}, u32[]{:S(2)}) copy-start(s32[128]{0:T(128)} %get-tuple-element.150) | copy-start | bytes 1540
  65.1 9.1 %collective-permute-start.7 = (f32[10,2,21,128]{3,1,2,0:T(2,128)S(1)}, f32[10,2,21,128]{3,1,2,0:T(2,128)S(1)}, u32[]{:S(2)}, u32[]{:S(2)}) collective-permute-start(f32[10,2,21,128]{3,1,2,0:T(2,128)S(1)} %get-tuple-element.36), channel_id=1, source_target_pairs={{8,0},{16,8},{24,16},{9,1},{17,9},{25,17},{10,2},{18,10},{26,18},{... | collective-permute-start | bytes 645128 | tf_op jit(solution)/shard_map/ppermute | solution.py:16
  66.4 9.0 %collective-permute-start.6 = (f32[10,2,21,128]{3,1,2,0:T(2,128)S(1)}, f32[10,2,21,128]{3,1,2,0:T(2,128)S(1)}, u32[]{:S(2)}, u32[]{:S(2)}) collective-permute-start(f32[10,2,21,128]{3,1,2,0:T(2,128)S(1)} %get-tuple-element.35), channel_id=1, source_target_pairs={{0,8},{8,16},{16,24},{1,9},{9,17},{17,25},{2,10},{10,18},{18,26},{... | collective-permute-start | bytes 645128 | tf_op jit(solution)/shard_map/ppermute | solution.py:15
  76.3 0.7 copy-start.1
  77.2 1.0 slice-start
  79.6 0.7 copy-start.9
  80.4 6.9 %copy-start.7 = (f32[1,1,24,64]{3,2,1,0:T(8,128)S(1)}, f32[1,1,24,64]{3,2,1,0:T(8,128)}, u32[]{:S(2)}) copy-start(f32[1,1,24,64]{3,2,1,0:T(8,128)} %get-tuple-element.23) | copy-start | bytes 18436
  80.4 7.5 %copy-start.8 = (f32[1,1,24,64]{3,2,1,0:T(8,128)S(1)}, f32[1,1,24,64]{3,2,1,0:T(8,128)}, u32[]{:S(2)}) copy-start(f32[1,1,24,64]{3,2,1,0:T(8,128)} %get-tuple-element.21) | copy-start | bytes 18436
  80.9 7.6 %collective-permute-start.9 = (f32[9,2,17,128]{3,1,2,0:T(2,128)S(1)}, f32[9,2,17,128]{3,1,2,0:T(2,128)S(1)}, u32[]{:S(2)}, u32[]{:S(2)}) collective-permute-start(f32[9,2,17,128]{3,1,2,0:T(2,128)S(1)} %get-tuple-element.44), channel_id=1, source_target_pairs={{8,0},{16,8},{24,16},{9,1},{17,9},{25,17},{10,2},{18,10},{26,18},{... | collective-permute-start | bytes 470024 | tf_op jit(solution)/shard_map/ppermute | solution.py:16
  82.2 7.8 %collective-permute-start.8 = (f32[9,2,17,128]{3,1,2,0:T(2,128)S(1)}, f32[9,2,17,128]{3,1,2,0:T(2,128)S(1)}, u32[]{:S(2)}, u32[]{:S(2)}) collective-permute-start(f32[9,2,17,128]{3,1,2,0:T(2,128)S(1)} %get-tuple-element.43), channel_id=1, source_target_pairs={{0,8},{8,16},{16,24},{1,9},{9,17},{17,25},{2,10},{10,18},{18,26},{... | collective-permute-start | bytes 470024 | tf_op jit(solution)/shard_map/ppermute | solution.py:15
  91.3 0.9 slice-start.1
  93.0 0.7 copy-start.11
  93.7 6.8 %copy-start.6 = (f32[1,24,64]{2,1,0:T(8,128)S(1)}, f32[1,24,64]{2,1,0:T(8,128)}, u32[]{:S(2)}) copy-start(f32[1,24,64]{2,1,0:T(8,128)} %get-tuple-element.19) | copy-start | bytes 18436
  94.2 7.2 %collective-permute-start.11 = (f32[9,2,13,128]{3,1,2,0:T(2,128)S(1)}, f32[9,2,13,128]{3,1,2,0:T(2,128)S(1)}, u32[]{:S(2)}, u32[]{:S(2)}) collective-permute-start(f32[9,2,13,128]{3,1,2,0:T(2,128)S(1)} %get-tuple-element.49), channel_id=1, source_target_pairs={{8,0},{16,8},{24,16},{9,1},{17,9},{25,17},{10,2},{18,10},{26,18},{... | collective-permute-start | bytes 359432 | tf_op jit(solution)/shard_map/ppermute | solution.py:16
  95.5 7.4 %collective-permute-start.10 = (f32[9,2,13,128]{3,1,2,0:T(2,128)S(1)}, f32[9,2,13,128]{3,1,2,0:T(2,128)S(1)}, u32[]{:S(2)}, u32[]{:S(2)}) collective-permute-start(f32[9,2,13,128]{3,1,2,0:T(2,128)S(1)} %get-tuple-element.48), channel_id=1, source_target_pairs={{0,8},{8,16},{16,24},{1,9},{9,17},{17,25},{2,10},{10,18},{18,26},{... | collective-permute-start | bytes 359432 | tf_op jit(solution)/shard_map/ppermute | solution.py:15
  103.9 0.9 slice-start.2
  105.4 0.7 copy-start.10

commit v6 on v5

--- a/solution.py
+++ b/solution.py
@@ -17,7 +17,7 @@
     return jnp.concatenate([from_left, field, from_right], axis=1)
 
 
-def lookup_kernel(step, idx_ref, tab_ref, coef_ref, lam_ref, mu_ref):
+def lookup_kernel(step, extra, idx_ref, tab_ref, state_ref, pay_ref, *rest):
     idx = idx_ref[...]
     rho = jnp.zeros(idx.shape, jnp.float32)
     lam = jnp.zeros(idx.shape, jnp.float32)
@@ -27,20 +27,29 @@
         rho = jnp.where(match, tab_ref[0, material], rho)
         lam = jnp.where(match, tab_ref[1, material], lam)
         shear = jnp.where(match, tab_ref[2, material], shear)
-    coef_ref[...] = step / rho
-    lam_ref[...] = lam
-    mu_ref[...] = shear
-
-
-def lookup(index, table, step):
-    out = jax.ShapeDtypeStruct(index.shape, jnp.float32)
+    comps = state_ref.shape[0]
+    pay_ref[:comps] = state_ref[...]
+    pay_ref[comps] = step / rho
+    if extra:
+        pay_ref[comps + 1] = lam
+        pay_ref[comps + 2] = shear
+    else:
+        rest[0][...] = lam
+        rest[1][...] = shear
+
+
+def lookup(index, table, state, step, extra):
+    comps = state.shape[0]
     vmem = pl.BlockSpec(memory_space=pltpu.VMEM)
+    cell = jax.ShapeDtypeStruct(index.shape, jnp.float32)
+    pay = jax.ShapeDtypeStruct((comps + (3 if extra else 1),) + index.shape, jnp.float32)
+    outs = (pay,) if extra else (pay, cell, cell)
     return pl.pallas_call(
-        lambda *refs: lookup_kernel(step, *refs),
-        out_shape=(out, out, out),
-        in_specs=[vmem, pl.BlockSpec(memory_space=pltpu.SMEM)],
-        out_specs=(vmem, vmem, vmem),
-    )(index, table)
+        lambda *refs: lookup_kernel(step, extra, *refs),
+        out_shape=outs,
+        in_specs=[vmem, pl.BlockSpec(memory_space=pltpu.SMEM), vmem],
+        out_specs=tuple(vmem for _ in outs),
+    )(index, table, state)
 
 
 def along(f, axis):
@@ -132,11 +141,9 @@
     rows_each = reg_y // count_y
     reach_y = 6
 
-    coef_r, lam_r, mu_r = lookup(region_material, material_table, 0.6)
-    coef_f, lam_f, mu_f = lookup(fine_material, material_table, 0.2)
-
-    region_pay = jnp.concatenate([region_state, coef_r[None]], 0)
-    fine_pay = jnp.concatenate([fine_state, coef_f[None], lam_f[None], mu_f[None]], 0)
+    region_pay, lam_r, mu_r = lookup(region_material, material_table, region_state, 0.6, False)
+    (fine_pay,) = lookup(fine_material, material_table, fine_state, 0.2, True)
+
     fine_lo = lax.ppermute(fine_pay[:, :, -reach_y:], "gy", shifted(count_y, 1))
     fine_hi = lax.ppermute(fine_pay[:, :, :reach_y], "gy", shifted(count_y, -1))
     reg_lo = lax.ppermute(region_pay, flat, shifted(n_flat, 1))
@@ -159,7 +166,7 @@
     )
     band = lax.all_to_all(send, "gy", 2, 1, tiled=True).astype(jnp.float32)
     columns = band.shape[1]
-    high = lax.Precision.HIGHEST
+    high = lax.Precision.HIGH
     along_y_w = interp_matrix(fine_y, rows_each)
     zeros_w = jnp.zeros_like(along_y_w)
     tiles_w = jnp.concatenate(

time: 109 us -> 104 us (0.954)
  waiting for transfers between devices: 9.8 us -> 17.1 us
  other arithmetic: 19.4 us -> 12.1 us
  matrix products: 9.97 us -> 5.43 us
  local copies, waits for them, and re-layouts: 22 us -> 18.6 us
  Pallas kernels: 3.38 us -> 5.03 us
    all_to_all x1, waiting for transfers between devices: 2.82 us -> 7.57 us  [local(): band = lax.all_to_all(send, 'gy', 2, 1, tiled=True).astype(jnp.float32)]
    unnamed x57 -> x62, local copies, waits for them, and re-layouts: 12.7 us -> 8.86 us
    ppermute x3, waiting for transfers between devices: 2.82 us -> 5.47 us  [x_halo(): from_right = lax.ppermute(field[:, :width], 'gx', shifted(nx, -1))]
    dot_general x1, matrix products: 4.99 us -> 2.42 us  [local(): second = jnp.einsum('gb,cfbz->cfgz', tiles_w, first, precision=high)]
    another operation x12 -> x8, other arithmetic: 3.89 us -> 1.43 us  [step_wide(): vel = vel_old + coef[None] * jnp.stack([acc_x, acc_y, acc_z])]
    unnamed x18, other arithmetic: 4.55 us -> 2.37 us
    slice x6 -> x3, local copies, waits for them, and re-layouts: 2.21 us -> 0.07 us  [local(): coef_w[:, off + 1:off + rows - 1]]
    slice x1 -> x2, local copies, waits for them, and re-layouts: 1.31 us -> 3.24 us  [local(): fine_lo = lax.ppermute(fine_pay[:, :, -reach_y:], 'gy', shifted(count_y, 1))]
  transfers between devices with their start and end apart: 13 -> 13, of which waited for: 7 -> 7; matrix products, arithmetic and copies ran while one was open for 33% -> 22% of each run, Pallas kernels for 2% -> 3%
where the time goes in v6:
time: 104 us; the launch traced here: 102 us
  starting transfers between devices  41.7 us (40%)
  local copies, waits for them, and re-layouts  18.6 us (18%)
  waiting for transfers between devices  17.1 us (16%)
  other arithmetic  12.1 us (12%)
  matrix products  5.43 us (5%)
  Pallas kernels  5.03 us (5%)
  between operations  1.69 us (2%)
    ppermute x3, starting transfers between devices, x_halo(): from_left = lax.ppermute(field[:, -width:], 'gx', shifted(nx, 1))  16 us
    unnamed x62, local copies, waits for them, and re-layouts  8.86 us
    all_to_all x1, waiting for transfers between devices, local(): band = lax.all_to_all(send, 'gy', 2, 1, tiled=True).astype(jnp.float32)  7.57 us
    all_to_all x1, starting transfers between devices, local(): band = lax.all_to_all(send, 'gy', 2, 1, tiled=True).astype(jnp.float32)  5.54 us
    ppermute x1, starting transfers between devices, local(): lows.insert(0, lax.ppermute(region_pay, flat, shifted(n_flat, d)))  5.51 us
    ppermute x1, starting transfers between devices, local(): fine_lo = lax.ppermute(fine_pay[:, :, -reach_y:], 'gy', shifted(count_y, 1))  5.48 us
    ppermute x3, waiting for transfers between devices, x_halo(): from_right = lax.ppermute(field[:, :width], 'gx', shifted(nx, -1))  5.47 us
    pallas_call x2, Pallas kernels, lookup(): pl.pallas_call(lambda *refs: lookup_kernel(step, extra, *refs), out_shape...  5.03 us
  transfers between devices with their start and end apart: 13, of which 7 were waited for; matrix products, arithmetic and copies ran while one was open for 22% of the time, Pallas kernels for 3%

profile of v6, /device:TPU:0, one launch (start us, length us, event | category | flops | bytes accessed | tf_op | source)
XLA Modules:
  0.0 101.7 jit_solution(7792090281241306719)
XLA Ops:
  0.6 1.6 %shard_map.68 = (f32[10,1,24,64]{3,2,1,0:T(8,128)}, f32[1,24,64]{2,1,0:T(8,128)}, f32[1,24,64]{2,1,0:T(8,128)}) custom-call(s32[1,24,64]{2,1,0:T(8,128)} %refs_0_.2, f32[3,8]{1,0:T(4,128)} %refs_1_.3, f32[9,1,24,64]{3,2,1,0:T(8,128)} %refs_2_.2), custom_call_target="tpu_custom_call" | custom-call | tf_op jit(solution)/shard_map/pallas_call | solution.py:47
  2.2 5.5 %collective-permute-start.3 = (f32[10,1,24,64]{3,2,1,0:T(8,128)}, f32[10,1,24,64]{3,2,1,0:T(8,128)}, u32[]{:S(2)}, u32[]{:S(2)}) collective-permute-start(f32[10,1,24,64]{3,2,1,0:T(8,128)} %get-tuple-element.5), channel_id=1, source_target_pairs={{0,2},{1,3},{2,4},{3,5},{4,6},{5,7},{6,8},{7,9},{8,10},{9,11},{10,... | collective-permute-start | bytes 184328 | tf_op jit(solution)/shard_map/ppermute | solution.py:153
  7.7 1.5 %collective-permute-start = (f32[10,1,24,64]{3,2,1,0:T(8,128)}, f32[10,1,24,64]{3,2,1,0:T(8,128)S(1)}, u32[]{:S(2)}, u32[]{:S(2)}) collective-permute-start(f32[10,1,24,64]{3,2,1,0:T(8,128)} %get-tuple-element.5), channel_id=1, source_target_pairs={{0,1},{1,2},{2,3},{3,4},{4,5},{5,6},{6,7},{7,8},{8,9},{9,10},{10,1... | collective-permute-start | bytes 184328 | tf_op jit(solution)/shard_map/ppermute | solution.py:149
  9.2 1.3 %collective-permute-start.1 = (f32[10,1,24,64]{3,2,1,0:T(8,128)}, f32[10,1,24,64]{3,2,1,0:T(8,128)S(1)}, u32[]{:S(2)}, u32[]{:S(2)}) collective-permute-start(f32[10,1,24,64]{3,2,1,0:T(8,128)} %get-tuple-element.5), channel_id=1, source_target_pairs={{1,0},{2,1},{3,2},{4,3},{5,4},{6,5},{7,6},{8,7},{9,8},{10,9},{11,1... | collective-permute-start | bytes 184328 | tf_op jit(solution)/shard_map/ppermute | solution.py:150
  10.5 1.3 %collective-permute-start.2 = (f32[10,1,24,64]{3,2,1,0:T(8,128)}, f32[10,1,24,64]{3,2,1,0:T(8,128)S(1)}, u32[]{:S(2)}, u32[]{:S(2)}) collective-permute-start(f32[10,1,24,64]{3,2,1,0:T(8,128)} %get-tuple-element.5), channel_id=1, source_target_pairs={{2,0},{3,1},{4,2},{5,3},{6,4},{7,5},{8,6},{9,7},{10,8},{11,9},{12,... | collective-permute-start | bytes 184328 | tf_op jit(solution)/shard_map/ppermute | solution.py:154
  11.8 1.6 %copy.75.refs_0_ = s32[24,9,128]{2,1,0:T(8,128)} copy(s32[24,9,128]{2,0,1:T(8,128)} %param.8) | data formatting | bytes 221184 | tf_op args[3]
  13.4 2.7 %copy.76.refs_2_ = f32[9,24,9,128]{3,2,1,0:T(8,128)} copy(f32[9,24,9,128]{3,1,2,0:T(8,128)} %param.7) | data formatting | bytes 1990656 | tf_op args[2]
  16.1 3.4 %shard_map.69 = f32[12,24,9,128]{3,2,1,0:T(8,128)} custom-call(s32[24,9,128]{2,1,0:T(8,128)} %copy.75.refs_0_, f32[3,8]{1,0:T(4,128)} %refs_1_.3, f32[9,24,9,128]{3,2,1,0:T(8,128)} %copy.76.refs_2_), custom_call_target="tpu_custom_call" | custom-call | tf_op jit(solution)/shard_map/pallas_call | solution.py:47
  19.6 2.2 %fusion.250 = (f32[12,24,6,128]{3,2,1,0:T(8,128)S(1)}, f32[12,24,6,128]{3,2,1,0:T(8,128)S(1)}) fusion(f32[12,24,9,128]{3,2,1,0:T(8,128)} %shard_map.69), kind=kLoop, calls=%fused_computation.477 | loop fusion | bytes 3538944 | tf_op jit(solution)/shard_map/slice | solution.py:147
  21.9 1.3 %collective-permute-start.5 = (f32[12,24,6,128]{3,1,2,0:T(8,128)S(1)}, f32[12,24,6,128]{3,1,2,0:T(8,128)S(1)}, u32[]{:S(2)}, u32[]{:S(2)}) collective-permute-start(f32[12,24,6,128]{3,1,2,0:T(8,128)S(1)} %copy.78), channel_id=1, source_target_pairs={{1,0},{2,1},{3,2},{4,3},{5,4},{6,5},{7,6},{9,8},{10,9},{11,10},{12... | collective-permute-start | bytes 2654216 | tf_op jit(solution)/shard_map/ppermute | solution.py:148
  23.2 0.6 compare_select_fusion.8
  23.9 0.6 compare_select_fusion.9
  24.4 0.6 compare_select_fusion.4
  25.0 0.6 compare_select_fusion.5
  25.6 0.6 compare_select_fusion
  26.4 0.7 slice_bitcast_fusion.35
  27.1 0.7 slice_bitcast_fusion.34
  27.8 1.1 %copy.77 = f32[12,24,6,128]{3,1,2,0:T(8,128)} copy(f32[12,24,6,128]{3,2,1,0:T(8,128)S(1)} %get-tuple-element.53) | data formatting | bytes 1769472 | tf_op jit(solution)/shard_map/slice | solution.py:147
  28.9 5.5 %collective-permute-start.4 = (f32[12,24,6,128]{3,1,2,0:T(8,128)}, f32[12,24,6,128]{3,1,2,0:T(8,128)}, u32[]{:S(2)}, u32[]{:S(2)}) collective-permute-start(f32[12,24,6,128]{3,1,2,0:T(8,128)} %copy.77), channel_id=1, source_target_pairs={{0,1},{1,2},{2,3},{3,4},{4,5},{5,6},{6,7},{8,9},{9,10},{10,11},{11... | collective-permute-start | bytes 2654216 | tf_op jit(solution)/shard_map/ppermute | solution.py:147
  34.4 0.9 constant_dynamic-update-slice_fusion.8
  36.8 1.0 reshape.512
  37.7 5.5 %all-to-all-start = ((bf16[8,2,5184]{2,1,0:T(2,128)(2,1)}), bf16[8,2,5184]{2,1,0:T(2,128)(2,1)S(1)}, u32[]{:S(2)}, u32[]{:S(2)}) async-start(bf16[8,2,5184]{2,1,0:T(2,128)(2,1)} %reshape.512), calls=%async_computation | async-start | bytes 335872 | tf_op jit(solution)/shard_map/all_to_all | solution.py:167
  43.3 7.6 %all-to-all-done = bf16[8,2,5184]{2,1,0:T(2,128)(2,1)S(1)} async-done(((bf16[8,2,5184]{2,1,0:T(2,128)(2,1)}), bf16[8,2,5184]{2,1,0:T(2,128)(2,1)S(1)}, u32[]{:S(2)}, u32[]{:S(2)}) %all-to-all-start) | async-done | bytes 165920 | tf_op jit(solution)/shard_map/all_to_all | solution.py:167
  50.9 0.3 reshape.513
  51.2 0.7 convolution_bitcast_fusion
  52.0 2.4 %fusion.2 = f32[18,24,64,17]{2,3,1,0:T(8,128)S(1)} fusion(f32[18,24,9,64]{3,1,2,0:T(8,128)S(1)} %convolution_bitcast_fusion, f32[9,3]{0,1:T(4,128)S(1)} %select_add_fusion, f32[9,3]{0,1:T(4,128)S(1)} %broadcast.1088), kind=kOutput, calls=%fused_computation.3 | convolution fusion | flops 25382240 | bytes 2875608 | tf_op jit(solution)/shard_map/gb,cfbz->cfgz/dot_general | solution.py:181
  54.4 2.3 %fusion = f32[18,24,17,128]{3,2,1,0:T(8,128)S(1)} fusion(f32[18,24,64,17]{2,3,1,0:T(8,128)S(1)} %fusion.2, f32[128]{0:T(128)S(1)} %copy-done.8, s32[128]{0:T(128)S(1)} %get-tuple-element.168, f32[128]{0:T(128)S(1)} %copy-done.9, s32[128]{0:T(128)S(1)} %get-tuple-element.167), kind=kOutput, calls=%fused_computation | convolution fusion | flops 361013248 | bytes 5642240 | tf_op jit(solution)/shard_map/kz,cfgz->cfgk/dot_general | solution.py:182
  56.8 0.2 copy.80
  57.0 1.5 %copy.79 = f32[12,24,6,128]{3,2,1,0:T(8,128)S(1)} copy(f32[12,24,6,128]{3,1,2,0:T(8,128)} %collective-permute-done.4) | data formatting | bytes 1769472 | tf_op jit(solution)/shard_map/ppermute | solution.py:147
  58.8 1.3 %collective-permute-start.7 = (f32[10,2,21,128]{3,2,1,0:T(8,128)S(1)}, f32[10,2,21,128]{3,2,1,0:T(8,128)S(1)}, u32[]{:S(2)}, u32[]{:S(2)}) collective-permute-start(f32[10,2,21,128]{3,2,1,0:T(8,128)S(1)} %get-tuple-element.42), channel_id=1, source_target_pairs={{8,0},{16,8},{24,16},{9,1},{17,9},{25,17},{10,2},{18,10},{26,18},{... | collective-permute-start | bytes 645128 | tf_op jit(solution)/shard_map/ppermute | solution.py:16
  60.1 5.9 %collective-permute-start.6 = (f32[10,2,21,128]{3,2,1,0:T(8,128)S(1)}, f32[10,2,21,128]{3,2,1,0:T(8,128)S(1)}, u32[]{:S(2)}, u32[]{:S(2)}) collective-permute-start(f32[10,2,21,128]{3,2,1,0:T(8,128)S(1)} %get-tuple-element.41), channel_id=1, source_target_pairs={{0,8},{8,16},{16,24},{1,9},{9,17},{17,25},{2,10},{10,18},{18,26},{... | collective-permute-start | bytes 645128 | tf_op jit(solution)/shard_map/ppermute | solution.py:15
  66.0 0.7 pad_maximum_fusion
  66.7 0.2 slice.1169
  67.0 2.3 %collective-permute-done.7 = f32[10,2,21,128]{3,2,1,0:T(8,128)S(1)} collective-permute-done((f32[10,2,21,128]{3,2,1,0:T(8,128)S(1)}, f32[10,2,21,128]{3,2,1,0:T(8,128)S(1)}, u32[]{:S(2)}, u32[]{:S(2)}) %collective-permute-start.7) | collective-permute-done | bytes 215072 | tf_op jit(solution)/shard_map/ppermute | solution.py:16
  69.4 1.2 %collective-permute-done.6 = f32[10,2,21,128]{3,2,1,0:T(8,128)S(1)} collective-permute-done((f32[10,2,21,128]{3,2,1,0:T(8,128)S(1)}, f32[10,2,21,128]{3,2,1,0:T(8,128)S(1)}, u32[]{:S(2)}, u32[]{:S(2)}) %collective-permute-start.6) | collective-permute-done | bytes 215072 | tf_op jit(solution)/shard_map/ppermute | solution.py:15
  70.5 0.3 pad_maximum_fusion.1
  71.1 0.2 fusion.252
  71.4 0.2 fusion.22
  71.6 0.4 fusion.33
  71.9 0.2 slice_add_fusion
  72.5 0.3 fusion.67
  73.0 0.2 fusion.57
  73.2 0.2 fusion.54
  73.5 0.3 slice_bitcast_fusion.4
  74.0 0.2 fusion.40
  74.2 0.6 fusion.8
  74.9 1.3 %collective-permute-start.9 = (f32[9,2,17,128]{3,2,1,0:T(8,128)S(1)}, f32[9,2,17,128]{3,2,1,0:T(8,128)S(1)}, u32[]{:S(2)}, u32[]{:S(2)}) collective-permute-start(f32[9,2,17,128]{3,2,1,0:T(8,128)S(1)} %get-tuple-element.52), channel_id=1, source_target_pairs={{8,0},{16,8},{24,16},{9,1},{17,9},{25,17},{10,2},{18,10},{26,18},{... | collective-permute-start | bytes 470024 | tf_op jit(solution)/shard_map/ppermute | solution.py:16
  76.2 5.0 %collective-permute-start.8 = (f32[9,2,17,128]{3,2,1,0:T(8,128)S(1)}, f32[9,2,17,128]{3,2,1,0:T(8,128)S(1)}, u32[]{:S(2)}, u32[]{:S(2)}) collective-permute-start(f32[9,2,17,128]{3,2,1,0:T(8,128)S(1)} %get-tuple-element.51), channel_id=1, source_target_pairs={{0,8},{8,16},{16,24},{1,9},{9,17},{17,25},{2,10},{10,18},{18,26},{... | collective-permute-start | bytes 470024 | tf_op jit(solution)/shard_map/ppermute | solution.py:15
  81.2 2.0 %collective-permute-done.9 = f32[9,2,17,128]{3,2,1,0:T(8,128)S(1)} collective-permute-done((f32[9,2,17,128]{3,2,1,0:T(8,128)S(1)}, f32[9,2,17,128]{3,2,1,0:T(8,128)S(1)}, u32[]{:S(2)}, u32[]{:S(2)}) %collective-permute-start.9) | collective-permute-done | bytes 156704 | tf_op jit(solution)/shard_map/ppermute | solution.py:16
  83.3 1.3 %collective-permute-done.8 = f32[9,2,17,128]{3,2,1,0:T(8,128)S(1)} collective-permute-done((f32[9,2,17,128]{3,2,1,0:T(8,128)S(1)}, f32[9,2,17,128]{3,2,1,0:T(8,128)S(1)}, u32[]{:S(2)}, u32[]{:S(2)}) %collective-permute-start.8) | collective-permute-done | bytes 156704 | tf_op jit(solution)/shard_map/ppermute | solution.py:15
  85.1 0.2 pad_maximum_fusion.2
  86.1 0.2 fusion.167
  86.8 0.2 slice_bitcast_fusion.19
  87.2 0.2 copy-done.5
  87.5 0.6 fusion.16
  88.1 1.3 %collective-permute-start.11 = (f32[9,2,13,128]{3,2,1,0:T(8,128)S(1)}, f32[9,2,13,128]{3,2,1,0:T(8,128)S(1)}, u32[]{:S(2)}, u32[]{:S(2)}) collective-permute-start(f32[9,2,13,128]{3,2,1,0:T(8,128)S(1)} %get-tuple-element.59), channel_id=1, source_target_pairs={{8,0},{16,8},{24,16},{9,1},{17,9},{25,17},{10,2},{18,10},{26,18},{... | collective-permute-start | bytes 359432 | tf_op jit(solution)/shard_map/ppermute | solution.py:16
  89.4 5.0 %collective-permute-start.10 = (f32[9,2,13,128]{3,2,1,0:T(8,128)S(1)}, f32[9,2,13,128]{3,2,1,0:T(8,128)S(1)}, u32[]{:S(2)}, u32[]{:S(2)}) collective-permute-start(f32[9,2,13,128]{3,2,1,0:T(8,128)S(1)} %get-tuple-element.58), channel_id=1, source_target_pairs={{0,8},{8,16},{16,24},{1,9},{9,17},{17,25},{2,10},{10,18},{18,26},{... | collective-permute-start | bytes 359432 | tf_op jit(solution)/shard_map/ppermute | solution.py:15
  94.5 1.1 %collective-permute-done.11 = f32[9,2,13,128]{3,2,1,0:T(8,128)S(1)} collective-permute-done((f32[9,2,13,128]{3,2,1,0:T(8,128)S(1)}, f32[9,2,13,128]{3,2,1,0:T(8,128)S(1)}, u32[]{:S(2)}, u32[]{:S(2)}) %collective-permute-start.11) | collective-permute-done | bytes 119840 | tf_op jit(solution)/shard_map/ppermute | solution.py:16
  95.6 1.5 %collective-permute-done.10 = f32[9,2,13,128]{3,2,1,0:T(8,128)S(1)} collective-permute-done((f32[9,2,13,128]{3,2,1,0:T(8,128)S(1)}, f32[9,2,13,128]{3,2,1,0:T(8,128)S(1)}, u32[]{:S(2)}, u32[]{:S(2)}) %collective-permute-start.10) | collective-permute-done | bytes 119840 | tf_op jit(solution)/shard_map/ppermute | solution.py:15
  97.8 0.2 fusion.83
  98.4 0.2 fusion.133
  99.6 0.2 copy-done.4
  99.8 0.6 fusion.11
  100.5 1.3 %copy.97 = f32[9,24,9,128]{3,1,2,0:T(8,128)} copy(f32[9,24,9,128]{3,2,1,0:T(8,128)S(1)} %fusion.11) | data formatting | bytes 1990656
  (140 shorter events, 6.9 us)
Async XLA Ops:
  2.2 26.7 %collective-permute-start.3 = (f32[10,1,24,64]{3,2,1,0:T(8,128)}, f32[10,1,24,64]{3,2,1,0:T(8,128)}, u32[]{:S(2)}, u32[]{:S(2)}) collective-permute-start(f32[10,1,24,64]{3,2,1,0:T(8,128)} %get-tuple-element.5), channel_id=1, source_target_pairs={{0,2},{1,3},{2,4},{3,5},{4,6},{5,7},{6,8},{7,9},{8,10},{9,11},{10,... | collective-permute-start | bytes 184328 | tf_op jit(solution)/shard_map/ppermute | solution.py:153
  7.7 27.6 %collective-permute-start = (f32[10,1,24,64]{3,2,1,0:T(8,128)}, f32[10,1,24,64]{3,2,1,0:T(8,128)S(1)}, u32[]{:S(2)}, u32[]{:S(2)}) collective-permute-start(f32[10,1,24,64]{3,2,1,0:T(8,128)} %get-tuple-element.5), channel_id=1, source_target_pairs={{0,1},{1,2},{2,3},{3,4},{4,5},{5,6},{6,7},{7,8},{8,9},{9,10},{10,1... | collective-permute-start | bytes 184328 | tf_op jit(solution)/shard_map/ppermute | solution.py:149
  9.2 26.2 %collective-permute-start.1 = (f32[10,1,24,64]{3,2,1,0:T(8,128)}, f32[10,1,24,64]{3,2,1,0:T(8,128)S(1)}, u32[]{:S(2)}, u32[]{:S(2)}) collective-permute-start(f32[10,1,24,64]{3,2,1,0:T(8,128)} %get-tuple-element.5), channel_id=1, source_target_pairs={{1,0},{2,1},{3,2},{4,3},{5,4},{6,5},{7,6},{8,7},{9,8},{10,9},{11,1... | collective-permute-start | bytes 184328 | tf_op jit(solution)/shard_map/ppermute | solution.py:150
  10.5 25.2 %collective-permute-start.2 = (f32[10,1,24,64]{3,2,1,0:T(8,128)}, f32[10,1,24,64]{3,2,1,0:T(8,128)S(1)}, u32[]{:S(2)}, u32[]{:S(2)}) collective-permute-start(f32[10,1,24,64]{3,2,1,0:T(8,128)} %get-tuple-element.5), channel_id=1, source_target_pairs={{2,0},{3,1},{4,2},{5,3},{6,4},{7,5},{8,6},{9,7},{10,8},{11,9},{12,... | collective-permute-start | bytes 184328 | tf_op jit(solution)/shard_map/ppermute | solution.py:154
  21.7 1.5 %copy-start.1 = (f32[9,1,24,64]{3,2,1,0:T(8,128)S(1)}, f32[9,1,24,64]{3,2,1,0:T(8,128)}, u32[]{:S(2)}) copy-start(f32[9,1,24,64]{3,2,1,0:T(8,128)} %refs_2_.2) | copy-start | bytes 165892
  21.9 34.8 %collective-permute-start.5 = (f32[12,24,6,128]{3,1,2,0:T(8,128)S(1)}, f32[12,24,6,128]{3,1,2,0:T(8,128)S(1)}, u32[]{:S(2)}, u32[]{:S(2)}) collective-permute-start(f32[12,24,6,128]{3,1,2,0:T(8,128)S(1)} %copy.78), channel_id=1, source_target_pairs={{1,0},{2,1},{3,2},{4,3},{5,4},{6,5},{7,6},{9,8},{10,9},{11,10},{12... | collective-permute-start | bytes 2654216 | tf_op jit(solution)/shard_map/ppermute | solution.py:148
  26.2 2.6 %copy-start.10 = (f32[9]{0:T(128)S(1)}, f32[9]{0:T(128)}, u32[]{:S(2)}) copy-start(f32[9]{0:T(128)} %get-tuple-element.161) | copy-start | bytes 112
  26.2 2.6 %copy-start.11 = (f32[9]{0:T(128)S(1)}, f32[9]{0:T(128)}, u32[]{:S(2)}) copy-start(f32[9]{0:T(128)} %get-tuple-element.162) | copy-start | bytes 112
  26.2 2.6 %copy-start.12 = (s32[9]{0:T(128)S(1)}, s32[9]{0:T(128)}, u32[]{:S(2)}) copy-start(s32[9]{0:T(128)} %get-tuple-element.163) | copy-start | bytes 112
  26.3 2.6 %copy-start.13 = (s32[9]{0:T(128)S(1)}, s32[9]{0:T(128)}, u32[]{:S(2)}) copy-start(s32[9]{0:T(128)} %get-tuple-element.164) | copy-start | bytes 112
  26.3 9.1 %copy-start.3 = (f32[10,1,24,64]{3,2,1,0:T(8,128)S(1)}, f32[10,1,24,64]{3,2,1,0:T(8,128)}, u32[]{:S(2)}) copy-start(f32[10,1,24,64]{3,2,1,0:T(8,128)} %get-tuple-element.5) | copy-start | bytes 184324
  28.9 28.1 %collective-permute-start.4 = (f32[12,24,6,128]{3,1,2,0:T(8,128)}, f32[12,24,6,128]{3,1,2,0:T(8,128)}, u32[]{:S(2)}, u32[]{:S(2)}) collective-permute-start(f32[12,24,6,128]{3,1,2,0:T(8,128)} %copy.77), channel_id=1, source_target_pairs={{0,1},{1,2},{2,3},{3,4},{4,5},{5,6},{6,7},{8,9},{9,10},{10,11},{11... | collective-permute-start | bytes 2654216 | tf_op jit(solution)/shard_map/ppermute | solution.py:147
  35.3 0.8 copy-start.2
  35.4 0.8 copy-start.6
  35.8 15.4 %copy-start.14 = (f32[24]{0:T(128)S(1)}, f32[24]{0:T(128)}, u32[]{:S(2)}) copy-start(f32[24]{0:T(128)} %get-tuple-element.157) | copy-start | bytes 292
  35.8 15.4 %copy-start.15 = (f32[24]{0:T(128)S(1)}, f32[24]{0:T(128)}, u32[]{:S(2)}) copy-start(f32[24]{0:T(128)} %get-tuple-element.158) | copy-start | bytes 292
  35.9 15.4 %copy-start.16 = (s32[24]{0:T(128)S(1)}, s32[24]{0:T(128)}, u32[]{:S(2)}) copy-start(s32[24]{0:T(128)} %get-tuple-element.159) | copy-start | bytes 292
  35.9 15.4 %copy-start.17 = (s32[24]{0:T(128)S(1)}, s32[24]{0:T(128)}, u32[]{:S(2)}) copy-start(s32[24]{0:T(128)} %get-tuple-element.160) | copy-start | bytes 292
  37.7 13.1 %all-to-all-start = ((bf16[8,2,5184]{2,1,0:T(2,128)(2,1)}), bf16[8,2,5184]{2,1,0:T(2,128)(2,1)S(1)}, u32[]{:S(2)}, u32[]{:S(2)}) async-start(bf16[8,2,5184]{2,1,0:T(2,128)(2,1)} %reshape.512), calls=%async_computation | async-start | bytes 335872 | tf_op jit(solution)/shard_map/all_to_all | solution.py:167
  52.0 2.4 %copy-start.8 = (f32[128]{0:T(128)S(1)}, f32[128]{0:T(128)}, u32[]{:S(2)}) copy-start(f32[128]{0:T(128)} %get-tuple-element.165) | copy-start | bytes 1540
  52.0 2.4 %copy-start.9 = (f32[128]{0:T(128)S(1)}, f32[128]{0:T(128)}, u32[]{:S(2)}) copy-start(f32[128]{0:T(128)} %get-tuple-element.166) | copy-start | bytes 1540
  56.7 1.9 %copy-start = (f32[12,24,9,128]{3,2,1,0:T(8,128)S(1)}, f32[12,24,9,128]{3,2,1,0:T(8,128)}, u32[]{:S(2)}) copy-start(f32[12,24,9,128]{3,2,1,0:T(8,128)} %shard_map.69) | copy-start | bytes 3981316
  58.8 10.6 %collective-permute-start.7 = (f32[10,2,21,128]{3,2,1,0:T(8,128)S(1)}, f32[10,2,21,128]{3,2,1,0:T(8,128)S(1)}, u32[]{:S(2)}, u32[]{:S(2)}) collective-permute-start(f32[10,2,21,128]{3,2,1,0:T(8,128)S(1)} %get-tuple-element.42), channel_id=1, source_target_pairs={{8,0},{16,8},{24,16},{9,1},{17,9},{25,17},{10,2},{18,10},{26,18},{... | collective-permute-start | bytes 645128 | tf_op jit(solution)/shard_map/ppermute | solution.py:16
  60.1 10.5 %collective-permute-start.6 = (f32[10,2,21,128]{3,2,1,0:T(8,128)S(1)}, f32[10,2,21,128]{3,2,1,0:T(8,128)S(1)}, u32[]{:S(2)}, u32[]{:S(2)}) collective-permute-start(f32[10,2,21,128]{3,2,1,0:T(8,128)S(1)} %get-tuple-element.41), channel_id=1, source_target_pairs={{0,8},{8,16},{16,24},{1,9},{9,17},{17,25},{2,10},{10,18},{18,26},{... | collective-permute-start | bytes 645128 | tf_op jit(solution)/shard_map/ppermute | solution.py:15
  74.9 8.4 %collective-permute-start.9 = (f32[9,2,17,128]{3,2,1,0:T(8,128)S(1)}, f32[9,2,17,128]{3,2,1,0:T(8,128)S(1)}, u32[]{:S(2)}, u32[]{:S(2)}) collective-permute-start(f32[9,2,17,128]{3,2,1,0:T(8,128)S(1)} %get-tuple-element.52), channel_id=1, source_target_pairs={{8,0},{16,8},{24,16},{9,1},{17,9},{25,17},{10,2},{18,10},{26,18},{... | collective-permute-start | bytes 470024 | tf_op jit(solution)/shard_map/ppermute | solution.py:16
  76.2 8.5 %collective-permute-start.8 = (f32[9,2,17,128]{3,2,1,0:T(8,128)S(1)}, f32[9,2,17,128]{3,2,1,0:T(8,128)S(1)}, u32[]{:S(2)}, u32[]{:S(2)}) collective-permute-start(f32[9,2,17,128]{3,2,1,0:T(8,128)S(1)} %get-tuple-element.51), channel_id=1, source_target_pairs={{0,8},{8,16},{16,24},{1,9},{9,17},{17,25},{2,10},{10,18},{18,26},{... | collective-permute-start | bytes 470024 | tf_op jit(solution)/shard_map/ppermute | solution.py:15
  86.8 0.7 copy-start.5
  88.1 7.5 %collective-permute-start.11 = (f32[9,2,13,128]{3,2,1,0:T(8,128)S(1)}, f32[9,2,13,128]{3,2,1,0:T(8,128)S(1)}, u32[]{:S(2)}, u32[]{:S(2)}) collective-permute-start(f32[9,2,13,128]{3,2,1,0:T(8,128)S(1)} %get-tuple-element.59), channel_id=1, source_target_pairs={{8,0},{16,8},{24,16},{9,1},{17,9},{25,17},{10,2},{18,10},{26,18},{... | collective-permute-start | bytes 359432 | tf_op jit(solution)/shard_map/ppermute | solution.py:16
  89.4 7.7 %collective-permute-start.10 = (f32[9,2,13,128]{3,2,1,0:T(8,128)S(1)}, f32[9,2,13,128]{3,2,1,0:T(8,128)S(1)}, u32[]{:S(2)}, u32[]{:S(2)}) collective-permute-start(f32[9,2,13,128]{3,2,1,0:T(8,128)S(1)} %get-tuple-element.58), channel_id=1, source_target_pairs={{0,8},{8,16},{16,24},{1,9},{9,17},{17,25},{2,10},{10,18},{18,26},{... | collective-permute-start | bytes 359432 | tf_op jit(solution)/shard_map/ppermute | solution.py:15
  94.5 2.8 %copy-start.7 = (f32[9,1,24,64]{3,2,1,0:T(8,128)}, f32[9,1,24,64]{3,2,1,0:T(8,128)S(1)}, u32[]{:S(2)}) copy-start(f32[9,1,24,64]{3,2,1,0:T(8,128)S(1)} %constant_dynamic-update-slice_fusion.9) | copy-start | bytes 165892
  99.1 0.7 copy-start.4

commit v7 on v6

--- a/solution.py
+++ b/solution.py
@@ -7,13 +7,19 @@
 
 
 def shifted(n, s):
-    return [(i, i + s) for i in range(n) if 0 <= i + s < n]
+    return [(i, (i + s) % n) for i in range(n)]
+
+
+def cyclic_from(field, axis, n, d, me):
+    got = lax.ppermute(field, axis, shifted(n, d))
+    return jnp.where((me - d >= 0) & (me - d < n), got, 0.0)
 
 
 def x_halo(field, width):
     nx = lax.axis_size("gx")
-    from_left = lax.ppermute(field[:, -width:], "gx", shifted(nx, 1))
-    from_right = lax.ppermute(field[:, :width], "gx", shifted(nx, -1))
+    me = lax.axis_index("gx")
+    from_left = cyclic_from(field[:, -width:], "gx", nx, 1, me)
+    from_right = cyclic_from(field[:, :width], "gx", nx, -1, me)
     return jnp.concatenate([from_left, field, from_right], axis=1)
 
 
@@ -144,14 +150,15 @@
     region_pay, lam_r, mu_r = lookup(region_material, material_table, region_state, 0.6, False)
     (fine_pay,) = lookup(fine_material, material_table, fine_state, 0.2, True)
 
-    fine_lo = lax.ppermute(fine_pay[:, :, -reach_y:], "gy", shifted(count_y, 1))
-    fine_hi = lax.ppermute(fine_pay[:, :, :reach_y], "gy", shifted(count_y, -1))
-    reg_lo = lax.ppermute(region_pay, flat, shifted(n_flat, 1))
-    reg_hi = lax.ppermute(region_pay, flat, shifted(n_flat, -1))
+    me_flat = lax.axis_index("gx") * count_y + me_y
+    fine_lo = cyclic_from(fine_pay[:, :, -reach_y:], "gy", count_y, 1, me_y)
+    fine_hi = cyclic_from(fine_pay[:, :, :reach_y], "gy", count_y, -1, me_y)
+    reg_lo = cyclic_from(region_pay, flat, n_flat, 1, me_flat)
+    reg_hi = cyclic_from(region_pay, flat, n_flat, -1, me_flat)
     lows, highs = [reg_lo], [reg_hi]
     for d in range(2, -(-2 // own) + 1):
-        lows.insert(0, lax.ppermute(region_pay, flat, shifted(n_flat, d)))
-        highs.append(lax.ppermute(region_pay, flat, shifted(n_flat, -d)))
+        lows.insert(0, cyclic_from(region_pay, flat, n_flat, d, me_flat))
+        highs.append(cyclic_from(region_pay, flat, n_flat, -d, me_flat))
     reg_ext = jnp.concatenate(
         [jnp.concatenate(lows, 1)[:, -2:], region_pay, jnp.concatenate(highs, 1)[:, :2]], 1
     )
@@ -164,7 +171,10 @@
     send = jnp.concatenate(
         [both[:, :, rows_each * d: rows_each * (d + 3)] for d in range(count_y)], 2
     )
-    band = lax.all_to_all(send, "gy", 2, 1, tiled=True).astype(jnp.float32)
+    band = lax.all_to_all(send, "gy", 2, 1, tiled=True)
+    wide = jnp.concatenate([fine_lo, fine_pay, fine_hi], axis=2)
+    band, first_ext = lax.optimization_barrier((band, x_halo(wide[:10], 2)))
+    band = band.astype(jnp.float32)
     columns = band.shape[1]
     high = lax.Precision.HIGH
     along_y_w = interp_matrix(fine_y, rows_each)
@@ -186,15 +196,13 @@
     along_y = ramp(me_y * fine_y - 4, fine_y + 8, count_y * fine_y, fine_y)
     relax = (0.1 + 0.4 * jnp.maximum(along_x[:, None], along_y[None, :]))[:, :, None]
 
-    wide = jnp.concatenate([fine_lo, fine_pay, fine_hi], axis=2)
     lam_w, mu_w = wide[10], wide[11]
     state = wide[:9]
     coef_w = None
     for sub in range(1, 4):
         if sub == 1:
-            ext = x_halo(wide[:10], 2)
-            coef_w = ext[9, 1:-1]
-            ext = ext[:9]
+            coef_w = first_ext[9, 1:-1]
+            ext = first_ext[:9]
         else:
             ext = x_halo(state, 2)
         off = 2 * (sub - 1)

time: 104 us -> 106 us (1.019); the launches traced: 102 us -> 105 us
  waiting for transfers between devices: 17.1 us -> 36 us
  starting transfers between devices: 41.7 us -> 24.5 us
  local copies, waits for them, and re-layouts: 18.6 us -> 19.7 us
    ppermute x12, starting transfers between devices: 36.2 us -> 20.2 us  [cyclic_from(): got = lax.ppermute(field, axis, shifted(n, d))]
    ppermute x12, waiting for transfers between devices: 9.48 us -> 25.3 us  [cyclic_from(): got = lax.ppermute(field, axis, shifted(n, d))]
    all_to_all x1, waiting for transfers between devices: 7.57 us -> 10.6 us  [local(): band = lax.all_to_all(send, 'gy', 2, 1, tiled=True)]
    unnamed x62 -> x50, local copies, waits for them, and re-layouts: 8.86 us -> 10.9 us
    ppermute x2 -> x0, local copies, waits for them, and re-layouts: 1.74 us -> none  [the longest x1 1.52 us: local(): fine_lo = lax.ppermute(fine_pay[:, :, -reach_y:], 'gy', shifted(count_y, 1))]
    select_n x0 -> x12, other arithmetic: none -> 1.68 us  [cyclic_from(): return jnp.where((me - d >= 0) & (me - d < n), got, 0.0)]
    all_to_all x1, starting transfers between devices: 5.54 us -> 4.31 us  [local(): band = lax.all_to_all(send, 'gy', 2, 1, tiled=True)]
    slice x6 -> x7, local copies, waits for them, and re-layouts: 3.66 us -> 4.38 us  [the longest x2 3.25 us: local(): fine_lo = cyclic_from(fine_pay[:, :, -reach_y:], 'gy', count_y, 1, me_y)]
  transfers between devices with their start and end apart: 13 -> 13, of which waited for: 7 -> 7; matrix products, arithmetic and copies ran while one was open for 22% -> 16% of each run, Pallas kernels for 3% -> 3%
where the time goes in v7:
time: 106 us; the launch traced here: 105 us
  waiting for transfers between devices  36 us (34%)
  starting transfers between devices  24.5 us (23%)
  local copies, waits for them, and re-layouts  19.7 us (19%)
  other arithmetic  12.7 us (12%)
  matrix products  5.41 us (5%)
  Pallas kernels  5.03 us (5%)
  between operations  1.5 us (1%)
    ppermute x12, waiting for transfers between devices, cyclic_from(): got = lax.ppermute(field, axis, shifted(n, d))  25.3 us
    ppermute x12, starting transfers between devices, cyclic_from(): got = lax.ppermute(field, axis, shifted(n, d))  20.2 us
    unnamed x50, local copies, waits for them, and re-layouts  10.9 us
    all_to_all x1, waiting for transfers between devices, local(): band = lax.all_to_all(send, 'gy', 2, 1, tiled=True)  10.6 us
    pallas_call x2, Pallas kernels, lookup(): pl.pallas_call(lambda *refs: lookup_kernel(step, extra, *refs), out_shape...  5.03 us
    all_to_all x1, starting transfers between devices, local(): band = lax.all_to_all(send, 'gy', 2, 1, tiled=True)  4.31 us
    slice x2, local copies, waits for them, and re-layouts, local(): fine_lo = cyclic_from(fine_pay[:, :, -reach_y:], 'gy', count_y, 1, me_y)  3.25 us
    slice x28, local copies, waits for them, and re-layouts, along(): lax.slice_in_dim(f, 1, n, axis=axis)  2.67 us
  transfers between devices with their start and end apart: 13, of which 7 were waited for; matrix products, arithmetic and copies ran while one was open for 16% of the time, Pallas kernels for 3%

profile of v7, /device:TPU:0, one launch (start us, length us, event | category | flops | bytes accessed | tf_op | source)
XLA Modules:
  0.0 104.9 jit_solution(4903363947522586273)
XLA Ops:
  0.6 1.6 %shard_map.68 = (f32[10,1,24,64]{3,2,1,0:T(8,128)}, f32[1,24,64]{2,1,0:T(8,128)}, f32[1,24,64]{2,1,0:T(8,128)}) custom-call(s32[1,24,64]{2,1,0:T(8,128)} %refs_0_.2, f32[3,8]{1,0:T(4,128)} %refs_1_.3, f32[9,1,24,64]{3,2,1,0:T(8,128)} %refs_2_.2), custom_call_target="tpu_custom_call" | custom-call | tf_op jit(solution)/shard_map/pallas_call | solution.py:53
  2.2 6.4 %collective-permute-start.1 = (f32[10,1,24,64]{3,2,1,0:T(8,128)}, f32[10,1,24,64]{3,2,1,0:T(8,128)}, u32[]{:S(2)}, u32[]{:S(2)}) collective-permute-start(f32[10,1,24,64]{3,2,1,0:T(8,128)} %get-tuple-element.7), channel_id=1, source_target_pairs={{0,31},{1,0},{2,1},{3,2},{4,3},{5,4},{6,5},{7,6},{8,7},{9,8},{10,9... | collective-permute-start | bytes 184328 | tf_op jit(solution)/shard_map/ppermute | solution.py:14
  8.6 5.6 %collective-permute-start.2 = (f32[10,1,24,64]{3,2,1,0:T(8,128)}, f32[10,1,24,64]{3,2,1,0:T(8,128)S(1)}, u32[]{:S(2)}, u32[]{:S(2)}) collective-permute-start(f32[10,1,24,64]{3,2,1,0:T(8,128)} %get-tuple-element.7), channel_id=1, source_target_pairs={{0,30},{1,31},{2,0},{3,1},{4,2},{5,3},{6,4},{7,5},{8,6},{9,7},{10,... | collective-permute-start | bytes 184328 | tf_op jit(solution)/shard_map/ppermute | solution.py:14
  14.3 1.6 %copy.82.refs_0_ = s32[24,9,128]{2,1,0:T(8,128)} copy(s32[24,9,128]{2,0,1:T(8,128)} %param.8) | data formatting | bytes 221184 | tf_op args[3]
  15.9 2.7 %copy.83.refs_2_ = f32[9,24,9,128]{3,2,1,0:T(8,128)} copy(f32[9,24,9,128]{3,1,2,0:T(8,128)} %param.7) | data formatting | bytes 1990656 | tf_op args[2]
  18.6 3.4 %shard_map.69 = f32[12,24,9,128]{3,2,1,0:T(8,128)} custom-call(s32[24,9,128]{2,1,0:T(8,128)} %copy.82.refs_0_, f32[3,8]{1,0:T(4,128)} %refs_1_.3, f32[9,24,9,128]{3,2,1,0:T(8,128)} %copy.83.refs_2_), custom_call_target="tpu_custom_call" | custom-call | tf_op jit(solution)/shard_map/pallas_call | solution.py:53
  22.0 2.2 %fusion.242 = (f32[12,24,6,128]{3,2,1,0:T(8,128)S(1)}, f32[12,24,6,128]{3,2,1,0:T(8,128)S(1)}) fusion(f32[12,24,9,128]{3,2,1,0:T(8,128)} %shard_map.69), kind=kLoop, calls=%fused_computation.471 | loop fusion | bytes 3538944 | tf_op jit(solution)/shard_map/slice | solution.py:154
  24.2 1.1 %copy.86 = f32[12,24,6,128]{3,1,2,0:T(8,128)} copy(f32[12,24,6,128]{3,2,1,0:T(8,128)S(1)} %get-tuple-element.59) | data formatting | bytes 1769472 | tf_op jit(solution)/shard_map/slice | solution.py:155
  25.3 0.6 compare_select_fusion.8
  25.9 0.6 compare_select_fusion.9
  26.5 0.6 compare_select_fusion
  27.3 0.7 slice_bitcast_fusion.29
  28.0 0.7 slice_bitcast_fusion.28
  28.6 1.1 %copy.84 = f32[12,24,6,128]{3,1,2,0:T(8,128)} copy(f32[12,24,6,128]{3,2,1,0:T(8,128)S(1)} %get-tuple-element.58) | data formatting | bytes 1769472 | tf_op jit(solution)/shard_map/slice | solution.py:154
  29.7 0.6 collective-permute-start.4
  30.3 0.9 broadcast_select_fusion.8
  32.8 0.9 reshape.512
  33.8 4.3 %all-to-all-start = ((bf16[8,2,5184]{2,1,0:T(2,128)(2,1)}), bf16[8,2,5184]{2,1,0:T(2,128)(2,1)S(1)}, u32[]{:S(2)}, u32[]{:S(2)}) async-start(bf16[8,2,5184]{2,1,0:T(2,128)(2,1)} %reshape.512), calls=%async_computation | async-start | bytes 335872 | tf_op jit(solution)/shard_map/all_to_all | solution.py:174
  38.1 10.6 %all-to-all-done = bf16[8,2,5184]{2,1,0:T(2,128)(2,1)S(1)} async-done(((bf16[8,2,5184]{2,1,0:T(2,128)(2,1)}), bf16[8,2,5184]{2,1,0:T(2,128)(2,1)S(1)}, u32[]{:S(2)}, u32[]{:S(2)}) %all-to-all-start) | async-done | bytes 165920 | tf_op jit(solution)/shard_map/all_to_all | solution.py:174
  48.8 0.3 reshape.513
  49.1 0.3 copy_select_fusion
  49.4 0.3 copy_select_fusion.1
  49.7 1.0 copy-done
  50.8 1.1 %collective-permute-start.7 = (f32[10,2,21,128]{3,2,1,0:T(8,128)S(1)}, f32[10,2,21,128]{3,2,1,0:T(8,128)S(1)}, u32[]{:S(2)}, u32[]{:S(2)}) collective-permute-start(f32[10,2,21,128]{3,2,1,0:T(8,128)S(1)} %get-tuple-element.44), channel_id=1, source_target_pairs={{0,24},{8,0},{16,8},{24,16},{1,25},{9,1},{17,9},{25,17},{2,26},{10... | collective-permute-start | bytes 645128 | tf_op jit(solution)/shard_map/ppermute | solution.py:14
  51.9 0.7 pad_maximum_fusion
  52.6 1.8 %copy-done.1 = f32[12,24,21,128]{3,2,1,0:T(8,128)} copy-done((f32[12,24,21,128]{3,2,1,0:T(8,128)}, f32[12,24,21,128]{3,2,1,0:T(8,128)S(1)}, u32[]{:S(2)}) %copy-start.1) | copy-done | bytes 3096600
  54.4 1.0 collective-permute-start.6
  55.5 2.8 %collective-permute-done.7 = f32[10,2,21,128]{3,2,1,0:T(8,128)S(1)} collective-permute-done((f32[10,2,21,128]{3,2,1,0:T(8,128)S(1)}, f32[10,2,21,128]{3,2,1,0:T(8,128)S(1)}, u32[]{:S(2)}, u32[]{:S(2)}) %collective-permute-start.7) | collective-permute-done | bytes 215072 | tf_op jit(solution)/shard_map/ppermute | solution.py:14
  58.3 5.3 %collective-permute-done.6 = f32[10,2,21,128]{3,2,1,0:T(8,128)S(1)} collective-permute-done((f32[10,2,21,128]{3,2,1,0:T(8,128)S(1)}, f32[10,2,21,128]{3,2,1,0:T(8,128)S(1)}, u32[]{:S(2)}, u32[]{:S(2)}) %collective-permute-start.6) | collective-permute-done | bytes 215072 | tf_op jit(solution)/shard_map/ppermute | solution.py:14
  63.6 0.3 pad_maximum_fusion.1
  64.2 0.2 fusion.245
  64.3 0.2 fusion.246
  64.5 0.5 fusion.24
  65.1 0.2 fusion.17
  65.5 0.3 fusion.58
  65.9 0.2 fusion.51
  66.1 0.2 fusion.48
  66.3 0.2 fusion.45
  66.6 0.3 slice_bitcast_fusion.4
  67.1 0.2 fusion.31
  67.3 0.4 copy-done.10
  67.7 0.7 convolution_bitcast_fusion
  68.5 2.4 %fusion.2 = f32[18,24,64,17]{2,3,1,0:T(8,128)S(1)} fusion(f32[18,24,9,64]{3,1,2,0:T(8,128)S(1)} %convolution_bitcast_fusion, f32[9,3]{0,1:T(4,128)S(1)} %select_add_fusion, f32[9,3]{0,1:T(4,128)S(1)} %broadcast.1088), kind=kOutput, calls=%fused_computation.3 | convolution fusion | flops 25382240 | bytes 2875608 | tf_op jit(solution)/shard_map/gb,cfbz->cfgz/dot_general | solution.py:191
  70.9 2.3 %fusion = f32[18,24,17,128]{3,2,1,0:T(8,128)S(1)} fusion(f32[18,24,64,17]{2,3,1,0:T(8,128)S(1)} %fusion.2, f32[128]{0:T(128)S(1)} %get-tuple-element.158, s32[128]{0:T(128)S(1)} %get-tuple-element.161, f32[128]{0:T(128)S(1)} %copy-done.9, s32[128]{0:T(128)S(1)} %get-tuple-element.160), kind=kOutput, calls=%fused_computation | convolution fusion | flops 361013248 | bytes 5642240 | tf_op jit(solution)/shard_map/kz,cfgz->cfgk/dot_general | solution.py:192
  73.2 0.6 fusion.8
  73.9 3.1 %collective-permute-start.9 = (f32[9,2,17,128]{3,2,1,0:T(8,128)S(1)}, f32[9,2,17,128]{3,2,1,0:T(8,128)S(1)}, u32[]{:S(2)}, u32[]{:S(2)}) collective-permute-start(f32[9,2,17,128]{3,2,1,0:T(8,128)S(1)} %get-tuple-element.57), channel_id=1, source_target_pairs={{0,24},{8,0},{16,8},{24,16},{1,25},{9,1},{17,9},{25,17},{2,26},{10... | collective-permute-start | bytes 470024 | tf_op jit(solution)/shard_map/ppermute | solution.py:14
  77.0 0.3 collective-permute-start.8
  77.3 5.5 %collective-permute-done.9 = f32[9,2,17,128]{3,2,1,0:T(8,128)S(1)} collective-permute-done((f32[9,2,17,128]{3,2,1,0:T(8,128)S(1)}, f32[9,2,17,128]{3,2,1,0:T(8,128)S(1)}, u32[]{:S(2)}, u32[]{:S(2)}) %collective-permute-start.9) | collective-permute-done | bytes 156704 | tf_op jit(solution)/shard_map/ppermute | solution.py:14
  82.9 4.8 %collective-permute-done.8 = f32[9,2,17,128]{3,2,1,0:T(8,128)S(1)} collective-permute-done((f32[9,2,17,128]{3,2,1,0:T(8,128)S(1)}, f32[9,2,17,128]{3,2,1,0:T(8,128)S(1)}, u32[]{:S(2)}, u32[]{:S(2)}) %collective-permute-start.8) | collective-permute-done | bytes 156704 | tf_op jit(solution)/shard_map/ppermute | solution.py:14
  87.6 0.2 pad_maximum_fusion.2
  89.1 0.2 fusion.158
  89.8 0.2 slice_bitcast_fusion.19
  90.3 0.2 copy-done.6
  90.5 0.6 fusion.16
  91.1 2.1 %collective-permute-start.11 = (f32[9,2,13,128]{3,2,1,0:T(8,128)S(1)}, f32[9,2,13,128]{3,2,1,0:T(8,128)S(1)}, u32[]{:S(2)}, u32[]{:S(2)}) collective-permute-start(f32[9,2,13,128]{3,2,1,0:T(8,128)S(1)} %get-tuple-element.64), channel_id=1, source_target_pairs={{0,24},{8,0},{16,8},{24,16},{1,25},{9,1},{17,9},{25,17},{2,26},{10... | collective-permute-start | bytes 359432 | tf_op jit(solution)/shard_map/ppermute | solution.py:14
  93.3 3.6 %collective-permute-done.11 = f32[9,2,13,128]{3,2,1,0:T(8,128)S(1)} collective-permute-done((f32[9,2,13,128]{3,2,1,0:T(8,128)S(1)}, f32[9,2,13,128]{3,2,1,0:T(8,128)S(1)}, u32[]{:S(2)}, u32[]{:S(2)}) %collective-permute-start.11) | collective-permute-done | bytes 119840 | tf_op jit(solution)/shard_map/ppermute | solution.py:14
  97.0 3.4 %collective-permute-done.10 = f32[9,2,13,128]{3,2,1,0:T(8,128)S(1)} collective-permute-done((f32[9,2,13,128]{3,2,1,0:T(8,128)S(1)}, f32[9,2,13,128]{3,2,1,0:T(8,128)S(1)}, u32[]{:S(2)}, u32[]{:S(2)}) %collective-permute-start.10) | collective-permute-done | bytes 119840 | tf_op jit(solution)/shard_map/ppermute | solution.py:14
  101.1 0.2 fusion.74
  101.7 0.2 fusion.124
  102.4 0.2 slice_bitcast_fusion.10
  102.7 0.2 fusion.97
  102.8 0.2 copy-done.5
  103.1 0.6 fusion.11
  103.7 1.3 %copy.97 = f32[9,24,9,128]{3,1,2,0:T(8,128)} copy(f32[9,24,9,128]{3,2,1,0:T(8,128)S(1)} %fusion.11) | data formatting | bytes 1990656
  (141 shorter events, 6.5 us)
Async XLA Ops:
  2.2 27.5 %collective-permute-start.1 = (f32[10,1,24,64]{3,2,1,0:T(8,128)}, f32[10,1,24,64]{3,2,1,0:T(8,128)}, u32[]{:S(2)}, u32[]{:S(2)}) collective-permute-start(f32[10,1,24,64]{3,2,1,0:T(8,128)} %get-tuple-element.7), channel_id=1, source_target_pairs={{0,31},{1,0},{2,1},{3,2},{4,3},{5,4},{6,5},{7,6},{8,7},{9,8},{10,9... | collective-permute-start | bytes 184328 | tf_op jit(solution)/shard_map/ppermute | solution.py:14
  8.6 22.6 %collective-permute-start = (f32[10,1,24,64]{3,2,1,0:T(8,128)}, f32[10,1,24,64]{3,2,1,0:T(8,128)}, u32[]{:S(2)}, u32[]{:S(2)}) collective-permute-start(f32[10,1,24,64]{3,2,1,0:T(8,128)} %get-tuple-element.7), channel_id=1, source_target_pairs={{0,1},{1,2},{2,3},{3,4},{4,5},{5,6},{6,7},{7,8},{8,9},{9,10},{10,1... | collective-permute-start | bytes 184328 | tf_op jit(solution)/shard_map/ppermute | solution.py:14
  8.6 22.9 %collective-permute-start.3 = (f32[10,1,24,64]{3,2,1,0:T(8,128)}, f32[10,1,24,64]{3,2,1,0:T(8,128)S(1)}, u32[]{:S(2)}, u32[]{:S(2)}) collective-permute-start(f32[10,1,24,64]{3,2,1,0:T(8,128)} %get-tuple-element.7), channel_id=1, source_target_pairs={{0,2},{1,3},{2,4},{3,5},{4,6},{5,7},{6,8},{7,9},{8,10},{9,11},{10,... | collective-permute-start | bytes 184328 | tf_op jit(solution)/shard_map/ppermute | solution.py:14
  8.6 23.0 %collective-permute-start.2 = (f32[10,1,24,64]{3,2,1,0:T(8,128)}, f32[10,1,24,64]{3,2,1,0:T(8,128)S(1)}, u32[]{:S(2)}, u32[]{:S(2)}) collective-permute-start(f32[10,1,24,64]{3,2,1,0:T(8,128)} %get-tuple-element.7), channel_id=1, source_target_pairs={{0,30},{1,31},{2,0},{3,1},{4,2},{5,3},{6,4},{7,5},{8,6},{9,7},{10,... | collective-permute-start | bytes 184328 | tf_op jit(solution)/shard_map/ppermute | solution.py:14
  24.2 1.1 %copy-start.3 = (f32[9,1,24,64]{3,2,1,0:T(8,128)S(1)}, f32[9,1,24,64]{3,2,1,0:T(8,128)}, u32[]{:S(2)}) copy-start(f32[9,1,24,64]{3,2,1,0:T(8,128)} %refs_2_.2) | copy-start | bytes 165892
  24.2 7.1 %copy-start.2 = (f32[10,1,24,64]{3,2,1,0:T(8,128)S(1)}, f32[10,1,24,64]{3,2,1,0:T(8,128)}, u32[]{:S(2)}) copy-start(f32[10,1,24,64]{3,2,1,0:T(8,128)} %get-tuple-element.7) | copy-start | bytes 184324
  25.3 23.8 %collective-permute-start.5 = (f32[12,24,6,128]{3,1,2,0:T(8,128)}, f32[12,24,6,128]{3,1,2,0:T(8,128)S(1)}, u32[]{:S(2)}, u32[]{:S(2)}) collective-permute-start(f32[12,24,6,128]{3,1,2,0:T(8,128)} %copy.86), channel_id=1, source_target_pairs={{0,7},{1,0},{2,1},{3,2},{4,3},{5,4},{6,5},{7,6},{8,15},{9,8},{10,9... | collective-permute-start | bytes 2654216 | tf_op jit(solution)/shard_map/ppermute | solution.py:14
  29.7 19.7 %collective-permute-start.4 = (f32[12,24,6,128]{3,1,2,0:T(8,128)}, f32[12,24,6,128]{3,1,2,0:T(8,128)S(1)}, u32[]{:S(2)}, u32[]{:S(2)}) collective-permute-start(f32[12,24,6,128]{3,1,2,0:T(8,128)} %copy.84), channel_id=1, source_target_pairs={{0,1},{1,2},{2,3},{3,4},{4,5},{5,6},{6,7},{7,0},{8,9},{9,10},{10,1... | collective-permute-start | bytes 2654216 | tf_op jit(solution)/shard_map/ppermute | solution.py:14
  31.5 0.7 copy-start.4
  31.5 0.7 copy-start.7
  33.8 15.0 %all-to-all-start = ((bf16[8,2,5184]{2,1,0:T(2,128)(2,1)}), bf16[8,2,5184]{2,1,0:T(2,128)(2,1)S(1)}, u32[]{:S(2)}, u32[]{:S(2)}) async-start(bf16[8,2,5184]{2,1,0:T(2,128)(2,1)} %reshape.512), calls=%async_computation | async-start | bytes 335872 | tf_op jit(solution)/shard_map/all_to_all | solution.py:174
  49.1 1.7 %copy-start = (f32[12,24,9,128]{3,2,1,0:T(8,128)S(1)}, f32[12,24,9,128]{3,2,1,0:T(8,128)}, u32[]{:S(2)}) copy-start(f32[12,24,9,128]{3,2,1,0:T(8,128)} %shard_map.69) | copy-start | bytes 3981316
  50.8 7.5 %collective-permute-start.7 = (f32[10,2,21,128]{3,2,1,0:T(8,128)S(1)}, f32[10,2,21,128]{3,2,1,0:T(8,128)S(1)}, u32[]{:S(2)}, u32[]{:S(2)}) collective-permute-start(f32[10,2,21,128]{3,2,1,0:T(8,128)S(1)} %get-tuple-element.44), channel_id=1, source_target_pairs={{0,24},{8,0},{16,8},{24,16},{1,25},{9,1},{17,9},{25,17},{2,26},{10... | collective-permute-start | bytes 645128 | tf_op jit(solution)/shard_map/ppermute | solution.py:14
  52.6 1.8 %copy-start.1 = (f32[12,24,21,128]{3,2,1,0:T(8,128)}, f32[12,24,21,128]{3,2,1,0:T(8,128)S(1)}, u32[]{:S(2)}) copy-start(f32[12,24,21,128]{3,2,1,0:T(8,128)S(1)} %pad_maximum_fusion) | copy-start | bytes 9289732
  54.4 9.2 %slice-start = ((f32[12,24,21,128]{3,2,1,0:T(8,128)}), f32[10,24,21,128]{3,2,1,0:T(8,128)S(1)}, s32[]{:S(2)}) async-start(f32[12,24,21,128]{3,2,1,0:T(8,128)} %copy-done.1), calls=%async_computation.1 | async-start | bytes 5898240 | tf_op jit(solution)/shard_map/slice | solution.py:176
  54.4 9.2 %collective-permute-start.6 = (f32[10,2,21,128]{3,2,1,0:T(8,128)S(1)}, f32[10,2,21,128]{3,2,1,0:T(8,128)S(1)}, u32[]{:S(2)}, u32[]{:S(2)}) collective-permute-start(f32[10,2,21,128]{3,2,1,0:T(8,128)S(1)} %get-tuple-element.43), channel_id=1, source_target_pairs={{0,8},{8,16},{16,24},{24,0},{1,9},{9,17},{17,25},{25,1},{2,10},{10... | collective-permute-start | bytes 645128 | tf_op jit(solution)/shard_map/ppermute | solution.py:14
  67.0 0.7 copy-start.10
  67.0 0.7 copy-start.11
  67.1 0.6 copy-start.12
  67.1 0.7 copy-start.13
  68.5 2.4 %copy-start.9 = (f32[128]{0:T(128)S(1)}, f32[128]{0:T(128)}, u32[]{:S(2)}) copy-start(f32[128]{0:T(128)} %get-tuple-element.159) | copy-start | bytes 1540
  73.9 9.0 %collective-permute-start.9 = (f32[9,2,17,128]{3,2,1,0:T(8,128)S(1)}, f32[9,2,17,128]{3,2,1,0:T(8,128)S(1)}, u32[]{:S(2)}, u32[]{:S(2)}) collective-permute-start(f32[9,2,17,128]{3,2,1,0:T(8,128)S(1)} %get-tuple-element.57), channel_id=1, source_target_pairs={{0,24},{8,0},{16,8},{24,16},{1,25},{9,1},{17,9},{25,17},{2,26},{10... | collective-permute-start | bytes 470024 | tf_op jit(solution)/shard_map/ppermute | solution.py:14
  77.0 10.6 %collective-permute-start.8 = (f32[9,2,17,128]{3,2,1,0:T(8,128)S(1)}, f32[9,2,17,128]{3,2,1,0:T(8,128)S(1)}, u32[]{:S(2)}, u32[]{:S(2)}) collective-permute-start(f32[9,2,17,128]{3,2,1,0:T(8,128)S(1)} %get-tuple-element.56), channel_id=1, source_target_pairs={{0,8},{8,16},{16,24},{24,0},{1,9},{9,17},{17,25},{25,1},{2,10},{10... | collective-permute-start | bytes 470024 | tf_op jit(solution)/shard_map/ppermute | solution.py:14
  89.8 0.7 copy-start.6
  91.1 5.8 %collective-permute-start.11 = (f32[9,2,13,128]{3,2,1,0:T(8,128)S(1)}, f32[9,2,13,128]{3,2,1,0:T(8,128)S(1)}, u32[]{:S(2)}, u32[]{:S(2)}) collective-permute-start(f32[9,2,13,128]{3,2,1,0:T(8,128)S(1)} %get-tuple-element.64), channel_id=1, source_target_pairs={{0,24},{8,0},{16,8},{24,16},{1,25},{9,1},{17,9},{25,17},{2,26},{10... | collective-permute-start | bytes 359432 | tf_op jit(solution)/shard_map/ppermute | solution.py:14
  93.3 7.2 %copy-start.8 = (f32[9,1,24,64]{3,2,1,0:T(8,128)}, f32[9,1,24,64]{3,2,1,0:T(8,128)S(1)}, u32[]{:S(2)}) copy-start(f32[9,1,24,64]{3,2,1,0:T(8,128)S(1)} %constant_dynamic-update-slice_fusion) | copy-start | bytes 165892
  93.3 7.1 %collective-permute-start.10 = (f32[9,2,13,128]{3,2,1,0:T(8,128)S(1)}, f32[9,2,13,128]{3,2,1,0:T(8,128)S(1)}, u32[]{:S(2)}, u32[]{:S(2)}) collective-permute-start(f32[9,2,13,128]{3,2,1,0:T(8,128)S(1)} %get-tuple-element.63), channel_id=1, source_target_pairs={{0,8},{8,16},{16,24},{24,0},{1,9},{9,17},{17,25},{25,1},{2,10},{10... | collective-permute-start | bytes 359432 | tf_op jit(solution)/shard_map/ppermute | solution.py:14
  102.4 0.7 copy-start.5

commit v8 on v7

--- a/solution.py
+++ b/solution.py
@@ -172,10 +172,16 @@
         [both[:, :, rows_each * d: rows_each * (d + 3)] for d in range(count_y)], 2
     )
     band = lax.all_to_all(send, "gy", 2, 1, tiled=True)
-    wide = jnp.concatenate([fine_lo, fine_pay, fine_hi], axis=2)
-    band, first_ext = lax.optimization_barrier((band, x_halo(wide[:10], 2)))
-    band = band.astype(jnp.float32)
-    columns = band.shape[1]
+    me_x = lax.axis_index("gx")
+    band = jnp.concatenate(
+        [
+            cyclic_from(band[:, -3:], "gx", count_x, 1, me_x),
+            band,
+            cyclic_from(band[:, :3], "gx", count_x, -1, me_x),
+        ],
+        1,
+    ).astype(jnp.float32)
+    columns = band.shape[1] - 6
     high = lax.Precision.HIGH
     along_y_w = interp_matrix(fine_y, rows_each)
     zeros_w = jnp.zeros_like(along_y_w)
@@ -187,41 +193,45 @@
         ],
         0,
     )[fine_y - 4: 2 * fine_y + 4]
-    first = jnp.einsum("fa,cabz->cfbz", interp_matrix(fine_x, columns), band, precision=high)
+    along_x_w = interp_matrix(fine_x, columns)
+    groups_w = jnp.concatenate(
+        [
+            jnp.pad(along_x_w[fine_x - 4:, columns - 3:], ((0, 0), (0, columns + 3))),
+            jnp.pad(along_x_w, ((0, 0), (3, 3))),
+            jnp.pad(along_x_w[:4, :3], ((0, 0), (columns + 3, 0))),
+        ],
+        0,
+    )
+    first = jnp.einsum("fa,cabz->cfbz", groups_w, band, precision=high)
     second = jnp.einsum("gb,cfbz->cfgz", tiles_w, first, precision=high)
     background = jnp.einsum(
         "kz,cfgz->cfgk", interp_matrix(fine_z, band.shape[3]), second, precision=high
     )
-    along_x = ramp(lax.axis_index("gx") * fine_x, fine_x, count_x * fine_x, fine_x)
+    along_x = ramp(me_x * fine_x - 4, fine_x + 8, count_x * fine_x, fine_x)
     along_y = ramp(me_y * fine_y - 4, fine_y + 8, count_y * fine_y, fine_y)
     relax = (0.1 + 0.4 * jnp.maximum(along_x[:, None], along_y[None, :]))[:, :, None]
 
-    lam_w, mu_w = wide[10], wide[11]
-    state = wide[:9]
-    coef_w = None
+    wide = jnp.concatenate([fine_lo, fine_pay, fine_hi], axis=2)
+    full = x_halo(wide, reach_y)
+    coef_w, lam_w, mu_w = full[9], full[10], full[11]
+    state = full[:9]
     for sub in range(1, 4):
-        if sub == 1:
-            coef_w = first_ext[9, 1:-1]
-            ext = first_ext[:9]
-        else:
-            ext = x_halo(state, 2)
         off = 2 * (sub - 1)
-        rows = state.shape[2]
+        cols, rows = state.shape[1], state.shape[2]
         state = step_wide(
-            ext,
-            coef_w[:, off + 1: off + rows - 1],
-            state[3:, :, 2:-2],
-            lam_w[:, off + 2: off + rows - 2],
-            mu_w[:, off + 2: off + rows - 2],
+            state,
+            coef_w[off + 1: off + cols - 1, off + 1: off + rows - 1],
+            state[3:, 2:-2, 2:-2],
+            lam_w[off + 2: off + cols - 2, off + 2: off + rows - 2],
+            mu_w[off + 2: off + cols - 2, off + 2: off + rows - 2],
             0.2,
             1.0,
             False,
         )
         share = sub / 3.0
-        target = background[:9, :, off: off + rows - 4] + share * (
-            background[9:, :, off: off + rows - 4] - background[:9, :, off: off + rows - 4]
-        )
-        state = state + relax[None, :, off: off + rows - 4] * (target - state)
+        bg = background[:, off: off + cols - 4, off: off + rows - 4]
+        target = bg[:9] + share * (bg[9:] - bg[:9])
+        state = state + relax[None, off: off + cols - 4, off: off + rows - 4] * (target - state)
     return (region_next, state)
 
 

time: 106 us -> 115 us (1.085)
  waiting for transfers between devices: 36 us -> 48 us
  starting transfers between devices: 24.5 us -> 21.3 us
  matrix products: 5.41 us -> 8.37 us
  local copies, waits for them, and re-layouts: 19.7 us -> 17.6 us
    ppermute x12 -> x10, waiting for transfers between devices: 25.3 us -> 37.3 us  [cyclic_from(): got = lax.ppermute(field, axis, shifted(n, d))]
    ppermute x12 -> x10, starting transfers between devices: 20.2 us -> 17 us  [cyclic_from(): got = lax.ppermute(field, axis, shifted(n, d))]
    unnamed x50 -> x42, local copies, waits for them, and re-layouts: 10.9 us -> 8.77 us
    dot_general x1, matrix products: 2.41 us -> 4.48 us  [local(): second = jnp.einsum('gb,cfbz->cfgz', tiles_w, first, precision=high)]
    slice x28 -> x27, local copies, waits for them, and re-layouts: 2.67 us -> 2.85 us  [along(): lax.slice_in_dim(f, 1, n, axis=axis)]
  transfers between devices with their start and end apart: 13 -> 11, of which waited for: 7 -> 5; matrix products, arithmetic and copies ran while one was open for 16% -> 21% of each run, Pallas kernels for 3% -> 3%
where the time goes in v8:
time: 115 us
  waiting for transfers between devices  48 us (42%)
  starting transfers between devices  21.3 us (19%)
  local copies, waits for them, and re-layouts  17.6 us (15%)
  other arithmetic  12.9 us (11%)
  matrix products  8.37 us (7%)
  Pallas kernels  5.03 us (4%)
  between operations  1.41 us (1%)
    ppermute x10, waiting for transfers between devices, cyclic_from(): got = lax.ppermute(field, axis, shifted(n, d))  37.3 us
    ppermute x10, starting transfers between devices, cyclic_from(): got = lax.ppermute(field, axis, shifted(n, d))  17 us
    all_to_all x1, waiting for transfers between devices, local(): band = lax.all_to_all(send, 'gy', 2, 1, tiled=True)  10.7 us
    unnamed x42, local copies, waits for them, and re-layouts  8.77 us
    pallas_call x2, Pallas kernels, lookup(): pl.pallas_call(lambda *refs: lookup_kernel(step, extra, *refs), out_shape...  5.03 us
    dot_general x1, matrix products, local(): second = jnp.einsum('gb,cfbz->cfgz', tiles_w, first, precision=high)  4.48 us
    all_to_all x1, starting transfers between devices, local(): band = lax.all_to_all(send, 'gy', 2, 1, tiled=True)  4.31 us
    slice x2, local copies, waits for them, and re-layouts, local(): fine_lo = cyclic_from(fine_pay[:, :, -reach_y:], 'gy', count_y, 1, me_y)  3.3 us
  transfers between devices with their start and end apart: 11, of which 5 were waited for; matrix products, arithmetic and copies ran while one was open for 21% of the time, Pallas kernels for 3%

profile of v8, /device:TPU:0, one launch (start us, length us, event | category | flops | bytes accessed | tf_op | source)
XLA Modules:
  0.0 114.6 jit_solution(10896593903442073544)
XLA Ops:
  0.6 1.6 %shard_map.68 = (f32[10,1,24,64]{3,2,1,0:T(8,128)}, f32[1,24,64]{2,1,0:T(8,128)}, f32[1,24,64]{2,1,0:T(8,128)}) custom-call(s32[1,24,64]{2,1,0:T(8,128)} %refs_0_.2, f32[3,8]{1,0:T(4,128)} %refs_1_.3, f32[9,1,24,64]{3,2,1,0:T(8,128)} %refs_2_.2), custom_call_target="tpu_custom_call" | custom-call | tf_op jit(solution)/shard_map/pallas_call | solution.py:53
  2.2 6.4 %collective-permute-start.1 = (f32[10,1,24,64]{3,2,1,0:T(8,128)}, f32[10,1,24,64]{3,2,1,0:T(8,128)}, u32[]{:S(2)}, u32[]{:S(2)}) collective-permute-start(f32[10,1,24,64]{3,2,1,0:T(8,128)} %get-tuple-element.5), channel_id=1, source_target_pairs={{0,31},{1,0},{2,1},{3,2},{4,3},{5,4},{6,5},{7,6},{8,7},{9,8},{10,9... | collective-permute-start | bytes 184328 | tf_op jit(solution)/shard_map/ppermute | solution.py:14
  8.6 5.6 %collective-permute-start.2 = (f32[10,1,24,64]{3,2,1,0:T(8,128)}, f32[10,1,24,64]{3,2,1,0:T(8,128)S(1)}, u32[]{:S(2)}, u32[]{:S(2)}) collective-permute-start(f32[10,1,24,64]{3,2,1,0:T(8,128)} %get-tuple-element.5), channel_id=1, source_target_pairs={{0,30},{1,31},{2,0},{3,1},{4,2},{5,3},{6,4},{7,5},{8,6},{9,7},{10,... | collective-permute-start | bytes 184328 | tf_op jit(solution)/shard_map/ppermute | solution.py:14
  14.3 1.6 %copy.79.refs_0_ = s32[24,9,128]{2,1,0:T(8,128)} copy(s32[24,9,128]{2,0,1:T(8,128)} %param.8) | data formatting | bytes 221184 | tf_op args[3]
  15.9 2.7 %copy.80.refs_2_ = f32[9,24,9,128]{3,2,1,0:T(8,128)} copy(f32[9,24,9,128]{3,1,2,0:T(8,128)} %param.7) | data formatting | bytes 1990656 | tf_op args[2]
  18.6 3.4 %shard_map.69 = f32[12,24,9,128]{3,2,1,0:T(8,128)} custom-call(s32[24,9,128]{2,1,0:T(8,128)} %copy.79.refs_0_, f32[3,8]{1,0:T(4,128)} %refs_1_.3, f32[9,24,9,128]{3,2,1,0:T(8,128)} %copy.80.refs_2_), custom_call_target="tpu_custom_call" | custom-call | tf_op jit(solution)/shard_map/pallas_call | solution.py:53
  22.0 2.2 %fusion.256 = (f32[12,24,6,128]{3,2,1,0:T(8,128)S(1)}, f32[12,24,6,128]{3,2,1,0:T(8,128)S(1)}) fusion(f32[12,24,9,128]{3,2,1,0:T(8,128)} %shard_map.69), kind=kLoop, calls=%fused_computation.488 | loop fusion | bytes 3538944 | tf_op jit(solution)/shard_map/slice | solution.py:154
  24.3 1.1 copy.83
  25.4 0.6 compare_select_fusion
  26.1 0.7 multiply_add_fusion.1
  26.9 0.7 slice_bitcast_fusion.40
  27.6 1.1 copy.81
  28.7 0.6 collective-permute-start.4
  29.3 0.9 broadcast_select_fusion.6
  31.8 1.0 reshape.512
  32.8 4.3 %all-to-all-start = ((bf16[8,2,5184]{2,1,0:T(2,128)(2,1)}), bf16[8,2,5184]{2,1,0:T(2,128)(2,1)S(1)}, u32[]{:S(2)}, u32[]{:S(2)}) async-start(bf16[8,2,5184]{2,1,0:T(2,128)(2,1)} %reshape.512), calls=%async_computation | async-start | bytes 335872 | tf_op jit(solution)/shard_map/all_to_all | solution.py:174
  37.2 10.7 %all-to-all-done = bf16[8,2,5184]{2,1,0:T(2,128)(2,1)S(1)} async-done(((bf16[8,2,5184]{2,1,0:T(2,128)(2,1)}), bf16[8,2,5184]{2,1,0:T(2,128)(2,1)S(1)}, u32[]{:S(2)}, u32[]{:S(2)}) %all-to-all-start) | async-done | bytes 165920 | tf_op jit(solution)/shard_map/all_to_all | solution.py:174
  47.9 0.3 reshape.513
  48.4 2.0 %collective-permute-start.9 = (bf16[18,3,9,64]{3,1,2,0:T(4,128)(2,1)S(1)}, bf16[18,3,9,64]{3,1,2,0:T(4,128)(2,1)S(1)}, u32[]{:S(2)}, u32[]{:S(2)}) collective-permute-start(bf16[18,3,9,64]{3,1,2,0:T(4,128)(2,1)S(1)} %get-tuple-element.93), channel_id=1, source_target_pairs={{0,24},{8,0},{16,8},{24,16},{1,25},{9,1},{17,9},{25,17},{2,26},{10... | collective-permute-start | bytes 186632 | tf_op jit(solution)/shard_map/ppermute | solution.py:14
  50.5 4.6 %collective-permute-done.9 = bf16[18,3,9,64]{3,1,2,0:T(4,128)(2,1)S(1)} collective-permute-done((bf16[18,3,9,64]{3,1,2,0:T(4,128)(2,1)S(1)}, bf16[18,3,9,64]{3,1,2,0:T(4,128)(2,1)S(1)}, u32[]{:S(2)}, u32[]{:S(2)}) %collective-permute-start.9) | collective-permute-done | bytes 62240 | tf_op jit(solution)/shard_map/ppermute | solution.py:14
  55.2 2.6 %collective-permute-done.8 = bf16[18,3,9,64]{3,1,2,0:T(4,128)(2,1)S(1)} collective-permute-done((bf16[18,3,9,64]{3,1,2,0:T(4,128)(2,1)S(1)}, bf16[18,3,9,64]{3,1,2,0:T(4,128)(2,1)S(1)}, u32[]{:S(2)}, u32[]{:S(2)}) %collective-permute-start.8) | collective-permute-done | bytes 62240 | tf_op jit(solution)/shard_map/ppermute | solution.py:14
  57.8 1.0 convolution_bitcast_fusion
  58.8 0.3 copy_select_fusion
  59.2 0.3 copy_select_fusion.1
  59.5 1.0 copy-done
  60.5 0.3 pad_maximum_fusion.3
  60.8 1.9 %collective-permute-start.7 = (f32[12,6,21,128]{3,2,1,0:T(8,128)S(1)}, f32[12,6,21,128]{3,2,1,0:T(8,128)S(1)}, u32[]{:S(2)}, u32[]{:S(2)}) collective-permute-start(f32[12,6,21,128]{3,2,1,0:T(8,128)S(1)} %get-tuple-element.47), channel_id=1, source_target_pairs={{0,24},{8,0},{16,8},{24,16},{1,25},{9,1},{17,9},{25,17},{2,26},{10... | collective-permute-start | bytes 2322440 | tf_op jit(solution)/shard_map/ppermute | solution.py:14
  62.7 4.5 %fusion.2 = f32[18,32,64,17]{2,3,1,0:T(8,128)S(1)} fusion(f32[18,32,9,64]{3,1,2,0:T(8,128)S(1)} %convolution_bitcast_fusion, f32[9,3]{0,1:T(4,128)S(1)} %select_add_fusion.1, f32[9,3]{0,1:T(4,128)S(1)} %broadcast.1078), kind=kOutput, calls=%fused_computation.3 | convolution fusion | flops 33842528 | bytes 3834072 | tf_op jit(solution)/shard_map/gb,cfbz->cfgz/dot_general | solution.py:206
  67.2 0.5 collective-permute-start.6
  67.6 2.9 %fusion = f32[18,32,17,128]{3,2,1,0:T(8,128)S(1)} fusion(f32[18,32,64,17]{2,3,1,0:T(8,128)S(1)} %fusion.2, f32[128]{0:T(128)S(1)} %copy-done.8, s32[128]{0:T(128)S(1)} %get-tuple-element.164, f32[128]{0:T(128)S(1)} %copy-done.9, s32[128]{0:T(128)S(1)} %get-tuple-element.163), kind=kOutput, calls=%fused_computation | convolution fusion | flops 481337344 | bytes 7522304 | tf_op jit(solution)/shard_map/kz,cfgz->cfgk/dot_general | solution.py:207
  70.5 12.5 %collective-permute-done.7 = f32[12,6,21,128]{3,2,1,0:T(8,128)S(1)} collective-permute-done((f32[12,6,21,128]{3,2,1,0:T(8,128)S(1)}, f32[12,6,21,128]{3,2,1,0:T(8,128)S(1)}, u32[]{:S(2)}, u32[]{:S(2)}) %collective-permute-start.7) | collective-permute-done | bytes 774176 | tf_op jit(solution)/shard_map/ppermute | solution.py:14
  83.1 17.6 %collective-permute-done.6 = f32[12,6,21,128]{3,2,1,0:T(8,128)S(1)} collective-permute-done((f32[12,6,21,128]{3,2,1,0:T(8,128)S(1)}, f32[12,6,21,128]{3,2,1,0:T(8,128)S(1)}, u32[]{:S(2)}, u32[]{:S(2)}) %collective-permute-start.6) | collective-permute-done | bytes 774176 | tf_op jit(solution)/shard_map/ppermute | solution.py:14
  100.8 0.9 pad_maximum_fusion
  101.9 0.2 fusion.259
  102.1 0.3 fusion.257
  102.4 0.6 fusion.36
  103.1 0.2 slice_add_fusion
  103.5 0.2 fusion.262
  103.7 0.4 fusion.70
  104.1 0.2 fusion.63
  104.3 0.3 fusion.60
  104.6 0.2 fusion.57
  104.8 0.2 fusion.261
  105.0 0.3 slice_bitcast_fusion.6
  105.3 0.2 fusion.260
  105.5 0.3 fusion.43
  105.8 0.2 copy-done.4
  106.0 0.8 fusion.8
  107.3 0.4 fusion.85
  107.7 0.1 slice_add_fusion.1
  108.1 0.2 fusion.119
  108.5 0.2 fusion.109
  108.7 0.1 fusion.106
  108.9 0.2 slice_bitcast_fusion.18
  109.3 0.2 fusion.92
  109.5 0.8 fusion.13
  110.7 0.3 fusion.134
  111.4 0.2 fusion.168
  111.7 0.1 fusion.158
  112.1 0.2 slice_bitcast_fusion.30
  112.4 0.2 fusion.141
  112.6 0.2 copy-done.5
  112.8 0.6 fusion.16
  113.4 1.3 %copy.103 = f32[9,24,9,128]{3,1,2,0:T(8,128)} copy(f32[9,24,9,128]{3,2,1,0:T(8,128)S(1)} %fusion.16) | data formatting | bytes 1990656
  (119 shorter events, 5.0 us)
Async XLA Ops:
  2.2 26.5 %collective-permute-start.1 = (f32[10,1,24,64]{3,2,1,0:T(8,128)}, f32[10,1,24,64]{3,2,1,0:T(8,128)}, u32[]{:S(2)}, u32[]{:S(2)}) collective-permute-start(f32[10,1,24,64]{3,2,1,0:T(8,128)} %get-tuple-element.5), channel_id=1, source_target_pairs={{0,31},{1,0},{2,1},{3,2},{4,3},{5,4},{6,5},{7,6},{8,7},{9,8},{10,9... | collective-permute-start | bytes 184328 | tf_op jit(solution)/shard_map/ppermute | solution.py:14
  8.6 21.6 %collective-permute-start = (f32[10,1,24,64]{3,2,1,0:T(8,128)}, f32[10,1,24,64]{3,2,1,0:T(8,128)}, u32[]{:S(2)}, u32[]{:S(2)}) collective-permute-start(f32[10,1,24,64]{3,2,1,0:T(8,128)} %get-tuple-element.5), channel_id=1, source_target_pairs={{0,1},{1,2},{2,3},{3,4},{4,5},{5,6},{6,7},{7,8},{8,9},{9,10},{10,1... | collective-permute-start | bytes 184328 | tf_op jit(solution)/shard_map/ppermute | solution.py:14
  8.6 21.9 %collective-permute-start.3 = (f32[10,1,24,64]{3,2,1,0:T(8,128)}, f32[10,1,24,64]{3,2,1,0:T(8,128)S(1)}, u32[]{:S(2)}, u32[]{:S(2)}) collective-permute-start(f32[10,1,24,64]{3,2,1,0:T(8,128)} %get-tuple-element.5), channel_id=1, source_target_pairs={{0,2},{1,3},{2,4},{3,5},{4,6},{5,7},{6,8},{7,9},{8,10},{9,11},{10,... | collective-permute-start | bytes 184328 | tf_op jit(solution)/shard_map/ppermute | solution.py:14
  8.6 21.9 %collective-permute-start.2 = (f32[10,1,24,64]{3,2,1,0:T(8,128)}, f32[10,1,24,64]{3,2,1,0:T(8,128)S(1)}, u32[]{:S(2)}, u32[]{:S(2)}) collective-permute-start(f32[10,1,24,64]{3,2,1,0:T(8,128)} %get-tuple-element.5), channel_id=1, source_target_pairs={{0,30},{1,31},{2,0},{3,1},{4,2},{5,3},{6,4},{7,5},{8,6},{9,7},{10,... | collective-permute-start | bytes 184328 | tf_op jit(solution)/shard_map/ppermute | solution.py:14
  24.2 1.1 copy-start.2
  24.2 6.0 %copy-start.1 = (f32[10,1,24,64]{3,2,1,0:T(8,128)S(1)}, f32[10,1,24,64]{3,2,1,0:T(8,128)}, u32[]{:S(2)}) copy-start(f32[10,1,24,64]{3,2,1,0:T(8,128)} %get-tuple-element.5) | copy-start | bytes 184324
  25.3 33.5 %collective-permute-start.5 = (f32[12,24,6,128]{3,1,2,0:T(8,128)}, f32[12,24,6,128]{3,1,2,0:T(8,128)S(1)}, u32[]{:S(2)}, u32[]{:S(2)}) collective-permute-start(f32[12,24,6,128]{3,1,2,0:T(8,128)} %copy.83), channel_id=1, source_target_pairs={{0,7},{1,0},{2,1},{3,2},{4,3},{5,4},{6,5},{7,6},{8,15},{9,8},{10,9... | collective-permute-start | bytes 2654216 | tf_op jit(solution)/shard_map/ppermute | solution.py:14
  28.7 30.4 %collective-permute-start.4 = (f32[12,24,6,128]{3,1,2,0:T(8,128)}, f32[12,24,6,128]{3,1,2,0:T(8,128)S(1)}, u32[]{:S(2)}, u32[]{:S(2)}) collective-permute-start(f32[12,24,6,128]{3,1,2,0:T(8,128)} %copy.81), channel_id=1, source_target_pairs={{0,1},{1,2},{2,3},{3,4},{4,5},{5,6},{6,7},{7,0},{8,9},{9,10},{10,1... | collective-permute-start | bytes 2654216 | tf_op jit(solution)/shard_map/ppermute | solution.py:14
  30.5 0.7 copy-start.3
  30.5 0.7 copy-start.6
  32.8 15.1 %all-to-all-start = ((bf16[8,2,5184]{2,1,0:T(2,128)(2,1)}), bf16[8,2,5184]{2,1,0:T(2,128)(2,1)S(1)}, u32[]{:S(2)}, u32[]{:S(2)}) async-start(bf16[8,2,5184]{2,1,0:T(2,128)(2,1)} %reshape.512), calls=%async_computation | async-start | bytes 335872 | tf_op jit(solution)/shard_map/all_to_all | solution.py:174
  48.4 6.7 %collective-permute-start.9 = (bf16[18,3,9,64]{3,1,2,0:T(4,128)(2,1)S(1)}, bf16[18,3,9,64]{3,1,2,0:T(4,128)(2,1)S(1)}, u32[]{:S(2)}, u32[]{:S(2)}) collective-permute-start(bf16[18,3,9,64]{3,1,2,0:T(4,128)(2,1)S(1)} %get-tuple-element.93), channel_id=1, source_target_pairs={{0,24},{8,0},{16,8},{24,16},{1,25},{9,1},{17,9},{25,17},{2,26},{10... | collective-permute-start | bytes 186632 | tf_op jit(solution)/shard_map/ppermute | solution.py:14
  50.4 8.8 %copy-start.7 = (f32[9,1,24,64]{3,2,1,0:T(8,128)}, f32[9,1,24,64]{3,2,1,0:T(8,128)S(1)}, u32[]{:S(2)}) copy-start(f32[9,1,24,64]{3,2,1,0:T(8,128)S(1)} %constant_dynamic-update-slice_fusion) | copy-start | bytes 165892
  50.4 7.4 %collective-permute-start.8 = (bf16[18,3,9,64]{3,1,2,0:T(4,128)(2,1)S(1)}, bf16[18,3,9,64]{3,1,2,0:T(4,128)(2,1)S(1)}, u32[]{:S(2)}, u32[]{:S(2)}) collective-permute-start(bf16[18,3,9,64]{3,1,2,0:T(4,128)(2,1)S(1)} %get-tuple-element.92), channel_id=1, source_target_pairs={{0,8},{8,16},{16,24},{24,0},{1,9},{9,17},{17,25},{25,1},{2,10},{10... | collective-permute-start | bytes 186632 | tf_op jit(solution)/shard_map/ppermute | solution.py:14
  58.8 1.7 %copy-start = (f32[12,24,9,128]{3,2,1,0:T(8,128)S(1)}, f32[12,24,9,128]{3,2,1,0:T(8,128)}, u32[]{:S(2)}) copy-start(f32[12,24,9,128]{3,2,1,0:T(8,128)} %shard_map.69) | copy-start | bytes 3981316
  60.8 22.2 %collective-permute-start.7 = (f32[12,6,21,128]{3,2,1,0:T(8,128)S(1)}, f32[12,6,21,128]{3,2,1,0:T(8,128)S(1)}, u32[]{:S(2)}, u32[]{:S(2)}) collective-permute-start(f32[12,6,21,128]{3,2,1,0:T(8,128)S(1)} %get-tuple-element.47), channel_id=1, source_target_pairs={{0,24},{8,0},{16,8},{24,16},{1,25},{9,1},{17,9},{25,17},{2,26},{10... | collective-permute-start | bytes 2322440 | tf_op jit(solution)/shard_map/ppermute | solution.py:14
  62.7 4.9 %copy-start.8 = (f32[128]{0:T(128)S(1)}, f32[128]{0:T(128)}, u32[]{:S(2)}) copy-start(f32[128]{0:T(128)} %get-tuple-element.161) | copy-start | bytes 1540
  62.7 4.9 %copy-start.9 = (f32[128]{0:T(128)S(1)}, f32[128]{0:T(128)}, u32[]{:S(2)}) copy-start(f32[128]{0:T(128)} %get-tuple-element.162) | copy-start | bytes 1540
  67.2 33.5 %collective-permute-start.6 = (f32[12,6,21,128]{3,2,1,0:T(8,128)S(1)}, f32[12,6,21,128]{3,2,1,0:T(8,128)S(1)}, u32[]{:S(2)}, u32[]{:S(2)}) collective-permute-start(f32[12,6,21,128]{3,2,1,0:T(8,128)S(1)} %get-tuple-element.46), channel_id=1, source_target_pairs={{0,8},{8,16},{16,24},{24,0},{1,9},{9,17},{17,25},{25,1},{2,10},{10... | collective-permute-start | bytes 2322440 | tf_op jit(solution)/shard_map/ppermute | solution.py:14
  105.3 0.7 copy-start.4
  112.1 0.7 copy-start.5

commit v9 on v5

--- a/solution.py
+++ b/solution.py
@@ -17,30 +17,30 @@
     return jnp.concatenate([from_left, field, from_right], axis=1)
 
 
-def lookup_kernel(step, idx_ref, tab_ref, coef_ref, lam_ref, mu_ref):
-    idx = idx_ref[...]
-    rho = jnp.zeros(idx.shape, jnp.float32)
-    lam = jnp.zeros(idx.shape, jnp.float32)
-    shear = jnp.zeros(idx.shape, jnp.float32)
+def props_kernel(step, code_ref, tab_ref, coef_ref, lam_ref, mu_ref):
+    code = code_ref[...]
+    rho = jnp.ones(code.shape, jnp.float32)
+    lam = jnp.zeros(code.shape, jnp.float32)
+    shear = jnp.zeros(code.shape, jnp.float32)
     for material in range(tab_ref.shape[1]):
-        match = idx == material
+        match = code == material + 1.0
         rho = jnp.where(match, tab_ref[0, material], rho)
         lam = jnp.where(match, tab_ref[1, material], lam)
         shear = jnp.where(match, tab_ref[2, material], shear)
-    coef_ref[...] = step / rho
+    coef_ref[...] = jnp.where(code > 0.5, step / rho, 0.0)
     lam_ref[...] = lam
     mu_ref[...] = shear
 
 
-def lookup(index, table, step):
-    out = jax.ShapeDtypeStruct(index.shape, jnp.float32)
+def props(code, table, step):
+    cell = jax.ShapeDtypeStruct(code.shape, jnp.float32)
     vmem = pl.BlockSpec(memory_space=pltpu.VMEM)
     return pl.pallas_call(
-        lambda *refs: lookup_kernel(step, *refs),
-        out_shape=(out, out, out),
+        lambda *refs: props_kernel(step, *refs),
+        out_shape=(cell, cell, cell),
         in_specs=[vmem, pl.BlockSpec(memory_space=pltpu.SMEM)],
         out_specs=(vmem, vmem, vmem),
-    )(index, table)
+    )(code, table)
 
 
 def along(f, axis):
@@ -132,11 +132,11 @@
     rows_each = reg_y // count_y
     reach_y = 6
 
-    coef_r, lam_r, mu_r = lookup(region_material, material_table, 0.6)
-    coef_f, lam_f, mu_f = lookup(fine_material, material_table, 0.2)
-
-    region_pay = jnp.concatenate([region_state, coef_r[None]], 0)
-    fine_pay = jnp.concatenate([fine_state, coef_f[None], lam_f[None], mu_f[None]], 0)
+    region_pay = jnp.concatenate(
+        [region_state, (region_material + 1).astype(jnp.float32)[None]], 0
+    )
+    fine_pay = jnp.concatenate([fine_state, (fine_material + 1).astype(jnp.float32)[None]], 0)
+
     fine_lo = lax.ppermute(fine_pay[:, :, -reach_y:], "gy", shifted(count_y, 1))
     fine_hi = lax.ppermute(fine_pay[:, :, :reach_y], "gy", shifted(count_y, -1))
     reg_lo = lax.ppermute(region_pay, flat, shifted(n_flat, 1))
@@ -148,8 +148,9 @@
     reg_ext = jnp.concatenate(
         [jnp.concatenate(lows, 1)[:, -2:], region_pay, jnp.concatenate(highs, 1)[:, :2]], 1
     )
+    coef_r, lam_r, mu_r = props(reg_ext[9, 1:-1], material_table, 0.6)
     region_next = step_wide(
-        reg_ext, reg_ext[9, 1:-1], region_state[3:], lam_r, mu_r, 0.6, 3.0, True
+        reg_ext, coef_r, region_state[3:], lam_r[1:-1], mu_r[1:-1], 0.6, 3.0, True
     )
 
     both = jnp.concatenate([region_state, region_next], 0).astype(jnp.bfloat16)
@@ -159,7 +160,7 @@
     )
     band = lax.all_to_all(send, "gy", 2, 1, tiled=True).astype(jnp.float32)
     columns = band.shape[1]
-    high = lax.Precision.HIGHEST
+    high = lax.Precision.HIGH
     along_y_w = interp_matrix(fine_y, rows_each)
     zeros_w = jnp.zeros_like(along_y_w)
     tiles_w = jnp.concatenate(
@@ -180,13 +181,13 @@
     relax = (0.1 + 0.4 * jnp.maximum(along_x[:, None], along_y[None, :]))[:, :, None]
 
     wide = jnp.concatenate([fine_lo, fine_pay, fine_hi], axis=2)
-    lam_w, mu_w = wide[10], wide[11]
     state = wide[:9]
     coef_w = None
     for sub in range(1, 4):
         if sub == 1:
-            ext = x_halo(wide[:10], 2)
-            coef_w = ext[9, 1:-1]
+            ext = x_halo(wide, 2)
+            coef_w, lam_w, mu_w = props(ext[9, 1:-1], material_table, 0.2)
+            lam_w, mu_w = lam_w[1:-1], mu_w[1:-1]
             ext = ext[:9]
         else:
             ext = x_halo(state, 2)

time: 109 us -> 111 us (1.018)
  matrix products: 9.97 us -> 7.07 us
  local copies, waits for them, and re-layouts: 22 us -> 24.6 us
    all_to_all x1, waiting for transfers between devices: 2.82 us -> 5.89 us  [local(): band = lax.all_to_all(send, 'gy', 2, 1, tiled=True).astype(jnp.float32)]
    ppermute x0 -> x2, local copies, waits for them, and re-layouts: none -> 2.61 us  [the longest x1 1.3 us: local(): fine_hi = lax.ppermute(fine_pay[:, :, :reach_y], 'gy', shifted(count_y, -1))]
    dot_general x1, matrix products: 4.99 us -> 2.42 us  [local(): second = jnp.einsum('gb,cfbz->cfgz', tiles_w, first, precision=high)]
    unnamed x57 -> x81, local copies, waits for them, and re-layouts: 12.7 us -> 10.2 us
    slice x27, local copies, waits for them, and re-layouts: 2.42 us -> 4.6 us  [along(): lax.slice_in_dim(f, 1, n, axis=axis)]
    squeeze x1 -> x3, local copies, waits for them, and re-layouts: 0.03 us -> 1.82 us  [the longest x2 1.07 us: step_wide(): dz = lambda c: along(mid_s[c], 2) * scale]
    ppermute x3, waiting for transfers between devices: 2.82 us -> 1.47 us  [x_halo(): from_right = lax.ppermute(field[:, :width], 'gx', shifted(nx, -1))]
    another operation x12 -> x11, other arithmetic: 3.89 us -> 2.92 us  [step_wide(): vel = vel_old + coef[None] * jnp.stack([acc_x, acc_y, acc_z])]
  transfers between devices with their start and end apart: 13 -> 13, of which waited for: 7 -> 6; matrix products, arithmetic and copies ran while one was open for 33% -> 23% of each run, Pallas kernels for 2% -> 1%
where the time goes in v9:
time: 111 us; the launch traced here: 110 us
  starting transfers between devices  41.6 us (37%)
  local copies, waits for them, and re-layouts  24.6 us (22%)
  other arithmetic  20.2 us (18%)
  waiting for transfers between devices  10.9 us (10%)
  matrix products  7.07 us (6%)
  Pallas kernels  3.7 us (3%)
  between operations  1.6 us (1%)
    ppermute x3, starting transfers between devices, x_halo(): from_left = lax.ppermute(field[:, -width:], 'gx', shifted(nx, 1))  15.9 us
    unnamed x81, local copies, waits for them, and re-layouts  10.2 us
    all_to_all x1, waiting for transfers between devices, local(): band = lax.all_to_all(send, 'gy', 2, 1, tiled=True).astype(jnp.float32)  5.89 us
    ppermute x1, starting transfers between devices, local(): fine_lo = lax.ppermute(fine_pay[:, :, -reach_y:], 'gy', shifted(count_y, 1))  5.09 us
    all_to_all x1, starting transfers between devices, local(): band = lax.all_to_all(send, 'gy', 2, 1, tiled=True).astype(jnp.float32)  5.02 us
    ppermute x1, starting transfers between devices, local(): lows.insert(0, lax.ppermute(region_pay, flat, shifted(n_flat, d)))  4.85 us
    slice x27, local copies, waits for them, and re-layouts, along(): lax.slice_in_dim(f, 1, n, axis=axis)  4.6 us
    dot_general x1, matrix products, local(): jnp.einsum('kz,cfgz->cfgk', interp_matrix(fine_z, band.shape[3]), second,...  3.94 us
  transfers between devices with their start and end apart: 13, of which 6 were waited for; matrix products, arithmetic and copies ran while one was open for 23% of the time, Pallas kernels for 1%

profile of v9, /device:TPU:0, one launch (start us, length us, event | category | flops | bytes accessed | tf_op | source)
XLA Modules:
  0.0 109.7 jit_solution(16945980901331721808)
XLA Ops:
  0.6 0.7 convert_bitcast_fusion
  1.4 1.6 %pad_maximum_fusion.22 = f32[10,1,24,64]{3,2,1,0:T(8,128)} fusion(f32[1,1,24,64]{3,2,1,0:T(8,128)S(1)} %convert_bitcast_fusion, f32[9,1,24,64]{3,2,1,0:T(8,128)} %param.5), kind=kLoop, calls=%fused_computation.293 | loop fusion | flops 15360 | bytes 122880 | tf_op jit(solution)/shard_map/concatenate | solution.py:135
  2.9 1.3 %collective-permute-start.1 = (f32[10,1,24,64]{3,2,1,0:T(8,128)}, f32[10,1,24,64]{3,2,1,0:T(8,128)S(1)}, u32[]{:S(2)}, u32[]{:S(2)}) collective-permute-start(f32[10,1,24,64]{3,2,1,0:T(8,128)} %pad_maximum_fusion.22), channel_id=1, source_target_pairs={{1,0},{2,1},{3,2},{4,3},{5,4},{6,5},{7,6},{8,7},{9,8},{10,9},{11,1... | collective-permute-start | bytes 184328 | tf_op jit(solution)/shard_map/ppermute | solution.py:143
  4.2 3.0 %collective-permute-start = (f32[10,1,24,64]{3,2,1,0:T(8,128)}, f32[10,1,24,64]{3,2,1,0:T(8,128)S(1)}, u32[]{:S(2)}, u32[]{:S(2)}) collective-permute-start(f32[10,1,24,64]{3,2,1,0:T(8,128)} %pad_maximum_fusion.22), channel_id=1, source_target_pairs={{0,1},{1,2},{2,3},{3,4},{4,5},{5,6},{6,7},{7,8},{8,9},{9,10},{10,1... | collective-permute-start | bytes 184328 | tf_op jit(solution)/shard_map/ppermute | solution.py:142
  7.3 4.8 %collective-permute-start.3 = (f32[10,1,24,64]{3,2,1,0:T(8,128)}, f32[10,1,24,64]{3,2,1,0:T(8,128)S(1)}, u32[]{:S(2)}, u32[]{:S(2)}) collective-permute-start(f32[10,1,24,64]{3,2,1,0:T(8,128)} %pad_maximum_fusion.22), channel_id=1, source_target_pairs={{0,2},{1,3},{2,4},{3,5},{4,6},{5,7},{6,8},{7,9},{8,10},{9,11},{10,... | collective-permute-start | bytes 184328 | tf_op jit(solution)/shard_map/ppermute | solution.py:146
  12.1 1.3 %collective-permute-start.2 = (f32[10,1,24,64]{3,2,1,0:T(8,128)}, f32[10,1,24,64]{3,2,1,0:T(8,128)S(1)}, u32[]{:S(2)}, u32[]{:S(2)}) collective-permute-start(f32[10,1,24,64]{3,2,1,0:T(8,128)} %pad_maximum_fusion.22), channel_id=1, source_target_pairs={{2,0},{3,1},{4,2},{5,3},{6,4},{7,5},{8,6},{9,7},{10,8},{11,9},{12,... | collective-permute-start | bytes 184328 | tf_op jit(solution)/shard_map/ppermute | solution.py:147
  13.4 1.5 %copy.76 = f32[9,24,9,128]{3,2,1,0:T(8,128)S(1)} copy(f32[9,24,9,128]{3,1,2,0:T(8,128)} %param.7) | data formatting | bytes 1990656 | tf_op args[2]
  15.2 1.0 copy.78
  16.2 1.3 %collective-permute-start.5 = (f32[10,24,6,128]{3,1,2,0:T(8,128)}, f32[10,24,6,128]{3,1,2,0:T(8,128)}, u32[]{:S(2)}, u32[]{:S(2)}) collective-permute-start(f32[10,24,6,128]{3,1,2,0:T(8,128)} %copy.78), channel_id=1, source_target_pairs={{1,0},{2,1},{3,2},{4,3},{5,4},{6,5},{7,6},{9,8},{10,9},{11,10},{12... | collective-permute-start | bytes 2211848 | tf_op jit(solution)/shard_map/ppermute | solution.py:141
  17.5 0.6 constant_dynamic-update-slice_fusion.14
  18.1 0.6 compare_select_fusion.8
  18.7 0.5 compare_select_fusion.9
  19.2 0.5 compare_select_fusion.4
  19.8 0.5 compare_select_fusion.5
  20.3 0.6 compare_select_fusion
  20.9 0.7 multiply_add_fusion.1
  21.6 0.7 slice_bitcast_fusion.29
  22.3 0.7 slice_bitcast_fusion.28
  23.0 1.0 copy.77
  24.0 0.6 select_add_fusion
  24.6 0.5 compare_select_fusion.1
  25.2 5.1 %collective-permute-start.4 = (f32[10,24,6,128]{3,1,2,0:T(8,128)}, f32[10,24,6,128]{3,1,2,0:T(8,128)}, u32[]{:S(2)}, u32[]{:S(2)}) collective-permute-start(f32[10,24,6,128]{3,1,2,0:T(8,128)} %copy.77), channel_id=1, source_target_pairs={{0,1},{1,2},{2,3},{3,4},{4,5},{5,6},{6,7},{8,9},{9,10},{10,11},{11... | collective-permute-start | bytes 2211848 | tf_op jit(solution)/shard_map/ppermute | solution.py:140
  30.4 0.6 maximum_bitcast_fusion.13
  31.1 1.5 %shard_map.68 = (f32[3,24,64]{2,1,0:T(8,128)}, f32[3,24,64]{2,1,0:T(8,128)}, f32[3,24,64]{2,1,0:T(8,128)}) custom-call(f32[3,24,64]{2,1,0:T(8,128)} %get-tuple-element.74.refs_0_, f32[3,8]{1,0:T(4,128)} %refs_1_.3), custom_call_target="tpu_custom_call" | custom-call | tf_op jit(solution)/shard_map/pallas_call | solution.py:38
  32.6 0.8 pad_maximum_fusion.4
  34.1 0.8 constant_dynamic-update-slice_fusion.12
  35.4 0.9 reshape.513
  36.3 5.0 %all-to-all-start = ((bf16[8,2,5184]{2,1,0:T(2,128)(2,1)}), bf16[8,2,5184]{2,1,0:T(2,128)(2,1)S(1)}, u32[]{:S(2)}, u32[]{:S(2)}) async-start(bf16[8,2,5184]{2,1,0:T(2,128)(2,1)} %reshape.513), calls=%async_computation | async-start | bytes 335872 | tf_op jit(solution)/shard_map/all_to_all | solution.py:161
  41.4 5.9 %all-to-all-done = bf16[8,2,5184]{2,1,0:T(2,128)(2,1)S(1)} async-done(((bf16[8,2,5184]{2,1,0:T(2,128)(2,1)}), bf16[8,2,5184]{2,1,0:T(2,128)(2,1)S(1)}, u32[]{:S(2)}, u32[]{:S(2)}) %all-to-all-start) | async-done | bytes 165920 | tf_op jit(solution)/shard_map/all_to_all | solution.py:161
  47.6 0.7 convolution_bitcast_fusion
  48.4 2.4 %fusion.2 = f32[18,24,64,17]{2,3,1,0:T(8,128)S(1)} fusion(f32[18,24,9,64]{3,1,2,0:T(8,128)S(1)} %convolution_bitcast_fusion, f32[9,3]{0,1:T(4,128)S(1)} %select_add_fusion, f32[9,3]{0,1:T(4,128)S(1)} %broadcast.1089), kind=kOutput, calls=%fused_computation.2 | convolution fusion | flops 25382240 | bytes 2875608 | tf_op jit(solution)/shard_map/gb,cfbz->cfgz/dot_general | solution.py:175
  50.8 1.3 %copy.80 = f32[10,24,6,128]{3,2,1,0:T(8,128)S(1)} copy(f32[10,24,6,128]{3,1,2,0:T(8,128)} %collective-permute-done.5) | data formatting | bytes 1474560 | tf_op jit(solution)/shard_map/ppermute | solution.py:141
  52.1 1.3 %copy.79 = f32[10,24,6,128]{3,2,1,0:T(8,128)S(1)} copy(f32[10,24,6,128]{3,1,2,0:T(8,128)} %collective-permute-done.4) | data formatting | bytes 1474560 | tf_op jit(solution)/shard_map/ppermute | solution.py:140
  53.6 1.3 %collective-permute-start.7 = (f32[10,2,21,128]{3,2,1,0:T(8,128)S(1)}, f32[10,2,21,128]{3,2,1,0:T(8,128)S(1)}, u32[]{:S(2)}, u32[]{:S(2)}) collective-permute-start(f32[10,2,21,128]{3,2,1,0:T(8,128)S(1)} %get-tuple-element.46), channel_id=1, source_target_pairs={{8,0},{16,8},{24,16},{9,1},{17,9},{25,17},{10,2},{18,10},{26,18},{... | collective-permute-start | bytes 645128 | tf_op jit(solution)/shard_map/ppermute | solution.py:16
  54.9 5.6 %collective-permute-start.6 = (f32[10,2,21,128]{3,2,1,0:T(8,128)S(1)}, f32[10,2,21,128]{3,2,1,0:T(8,128)S(1)}, u32[]{:S(2)}, u32[]{:S(2)}) collective-permute-start(f32[10,2,21,128]{3,2,1,0:T(8,128)S(1)} %get-tuple-element.45), channel_id=1, source_target_pairs={{0,8},{8,16},{16,24},{1,9},{9,17},{17,25},{2,10},{10,18},{18,26},{... | collective-permute-start | bytes 645128 | tf_op jit(solution)/shard_map/ppermute | solution.py:15
  60.6 3.9 %fusion = f32[18,24,17,128]{3,2,1,0:T(8,128)} fusion(f32[18,24,64,17]{2,3,1,0:T(8,128)S(1)} %fusion.2, f32[128]{0:T(128)S(1)} %copy-done.21, s32[128]{0:T(128)S(1)} %copy-done.23, f32[128]{0:T(128)S(1)} %copy-done.22, s32[128]{0:T(128)S(1)} %get-tuple-element.159), kind=kOutput, calls=%fused_computation | convolution fusion | flops 361013248 | bytes 5642240 | tf_op jit(solution)/shard_map/kz,cfgz->cfgk/dot_general | solution.py:176
  64.5 0.8 collective-permute-done.6
  65.3 0.6 pad_maximum_fusion
  66.0 1.0 slice_bitcast_fusion.2
  67.0 1.0 copy-done.3
  68.0 0.7 slice_bitcast_fusion.3.refs_0_
  68.7 0.9 fusion.259
  69.6 2.2 %shard_map.69 = (f32[26,21,128]{2,1,0:T(8,128)}, f32[26,21,128]{2,1,0:T(8,128)}, f32[26,21,128]{2,1,0:T(8,128)}) custom-call(f32[26,21,128]{2,1,0:T(8,128)} %slice_bitcast_fusion.3.refs_0_, f32[3,8]{1,0:T(4,128)} %refs_1_.3), custom_call_target="tpu_custom_call" | custom-call | tf_op jit(solution)/shard_map/pallas_call | solution.py:38
  71.8 1.1 %slice.943 = f32[26,19,128]{2,1,0:T(8,128)S(1)} slice(f32[26,21,128]{2,1,0:T(8,128)} %get-tuple-element.11), slice={[0:26], [1:20], [0:128]} | slice | bytes 505856 | tf_op jit(solution)/shard_map/slice | solution.py:198
  73.0 1.5 %fusion.257 = (f32[26,19,127]{2,1,0:T(8,128)S(1)}, f32[26,19,127]{2,1,0:T(8,128)S(1)}, f32[26,19,127]{2,1,0:T(8,128)S(1)}, f32[26,19,127]{2,1,0:T(8,128)S(1)}) fusion(f32[26,19,128]{2,1,0:T(8,128)} %get-tuple-element.47, f32[26,19,128]{2,1,0:T(8,128)} %get-tuple-element.48), kind=kLoop, calls=%fused_computation.493 | loop fusion | bytes 2007616 | tf_op jit(solution)/shard_map/slice | solution.py:49
  74.5 1.4 %fusion.23 = f32[1,26,19,128]{3,2,1,0:T(8,128)S(1)} fusion(f32[10,28,21,128]{3,2,1,0:T(8,128)} %copy-done.3, f32[10,2,21,128]{3,2,1,0:T(8,128)S(1)} %collective-permute-done.6, f32[10,24,6,128]{3,2,1,0:T(8,128)S(1)} %copy.80, f32[10,24,6,128]{3,2,1,0:T(8,128)S(1)} %copy-done.1, f32[1,24,9,128]{3,2,1,0:T(8,128)S(1)} %fusion.171, ...), kind=kLoop, calls=%fused_computation.45 | loop fusion | flops 885248 | bytes 4271248 | tf_op jit(solution)/shard_map/stack | solution.py:72
  75.9 0.7 copy-done.4
  77.6 0.7 copy-done.2
  78.3 0.4 fusion.69
  80.2 1.4 %slice-done = s8[4194304]{0:T(1024)(128)(4,1)S(1)} async-done(((s8[5308416]{0:T(1024)(128)(4,1)}), s8[4194304]{0:T(1024)(128)(4,1)S(1)}, s32[]{:S(2)}) %slice-start) | async-done | bytes 4194328
  81.9 0.6 fusion.8
  82.6 1.3 %collective-permute-start.9 = (f32[9,2,17,128]{3,2,1,0:T(8,128)S(1)}, f32[9,2,17,128]{3,2,1,0:T(8,128)S(1)}, u32[]{:S(2)}, u32[]{:S(2)}) collective-permute-start(f32[9,2,17,128]{3,2,1,0:T(8,128)S(1)} %get-tuple-element.54), channel_id=1, source_target_pairs={{8,0},{16,8},{24,16},{9,1},{17,9},{25,17},{10,2},{18,10},{26,18},{... | collective-permute-start | bytes 470024 | tf_op jit(solution)/shard_map/ppermute | solution.py:16
  83.9 5.0 %collective-permute-start.8 = (f32[9,2,17,128]{3,2,1,0:T(8,128)S(1)}, f32[9,2,17,128]{3,2,1,0:T(8,128)S(1)}, u32[]{:S(2)}, u32[]{:S(2)}) collective-permute-start(f32[9,2,17,128]{3,2,1,0:T(8,128)S(1)} %get-tuple-element.53), channel_id=1, source_target_pairs={{0,8},{8,16},{16,24},{1,9},{9,17},{17,25},{2,10},{10,18},{18,26},{... | collective-permute-start | bytes 470024 | tf_op jit(solution)/shard_map/ppermute | solution.py:15
  88.9 0.6 constant_dynamic-update-slice_fusion.2
  89.5 0.6 constant_dynamic-update-slice_fusion.1
  90.1 1.1 %collective-permute-done.9 = f32[9,2,17,128]{3,2,1,0:T(8,128)S(1)} collective-permute-done((f32[9,2,17,128]{3,2,1,0:T(8,128)S(1)}, f32[9,2,17,128]{3,2,1,0:T(8,128)S(1)}, u32[]{:S(2)}, u32[]{:S(2)}) %collective-permute-start.9) | collective-permute-done | bytes 156704 | tf_op jit(solution)/shard_map/ppermute | solution.py:16
  91.3 1.2 %collective-permute-done.8 = f32[9,2,17,128]{3,2,1,0:T(8,128)S(1)} collective-permute-done((f32[9,2,17,128]{3,2,1,0:T(8,128)S(1)}, f32[9,2,17,128]{3,2,1,0:T(8,128)S(1)}, u32[]{:S(2)}, u32[]{:S(2)}) %collective-permute-start.8) | collective-permute-done | bytes 156704 | tf_op jit(solution)/shard_map/ppermute | solution.py:15
  95.4 0.6 fusion.16
  96.0 1.3 %collective-permute-start.11 = (f32[9,2,13,128]{3,2,1,0:T(8,128)S(1)}, f32[9,2,13,128]{3,2,1,0:T(8,128)S(1)}, u32[]{:S(2)}, u32[]{:S(2)}) collective-permute-start(f32[9,2,13,128]{3,2,1,0:T(8,128)S(1)} %get-tuple-element.61), channel_id=1, source_target_pairs={{8,0},{16,8},{24,16},{9,1},{17,9},{25,17},{10,2},{18,10},{26,18},{... | collective-permute-start | bytes 359432 | tf_op jit(solution)/shard_map/ppermute | solution.py:16
  97.3 5.2 %collective-permute-start.10 = (f32[9,2,13,128]{3,2,1,0:T(8,128)S(1)}, f32[9,2,13,128]{3,2,1,0:T(8,128)S(1)}, u32[]{:S(2)}, u32[]{:S(2)}) collective-permute-start(f32[9,2,13,128]{3,2,1,0:T(8,128)S(1)} %get-tuple-element.60), channel_id=1, source_target_pairs={{0,8},{8,16},{16,24},{1,9},{9,17},{17,25},{2,10},{10,18},{18,26},{... | collective-permute-start | bytes 359432 | tf_op jit(solution)/shard_map/ppermute | solution.py:15
  102.6 0.6 constant_dynamic-update-slice_fusion
  103.5 1.5 %collective-permute-done.10 = f32[9,2,13,128]{3,2,1,0:T(8,128)S(1)} collective-permute-done((f32[9,2,13,128]{3,2,1,0:T(8,128)S(1)}, f32[9,2,13,128]{3,2,1,0:T(8,128)S(1)}, u32[]{:S(2)}, u32[]{:S(2)}) %collective-permute-start.10) | collective-permute-done | bytes 119840 | tf_op jit(solution)/shard_map/ppermute | solution.py:15
  107.8 0.6 fusion.11
  108.4 1.3 %copy.97 = f32[9,24,9,128]{3,1,2,0:T(8,128)} copy(f32[9,24,9,128]{3,2,1,0:T(8,128)S(1)} %fusion.11) | data formatting | bytes 1990656
  (164 shorter events, 10.8 us)
Async XLA Ops:
  0.6 14.3 %copy-start.15 = (s32[24,9,128]{2,0,1:T(8,128)S(1)}, s32[24,9,128]{2,0,1:T(8,128)}, u32[]{:S(2)}) copy-start(s32[24,9,128]{2,0,1:T(8,128)} %param.8) | copy-start | bytes 331780
  1.4 10.7 %copy-start.10 = (f32[1,1,24,64]{3,2,1,0:T(8,128)}, f32[1,1,24,64]{3,2,1,0:T(8,128)S(1)}, u32[]{:S(2)}) copy-start(f32[1,1,24,64]{3,2,1,0:T(8,128)S(1)} %convert_bitcast_fusion) | copy-start | bytes 18436
  2.9 22.2 %collective-permute-start.1 = (f32[10,1,24,64]{3,2,1,0:T(8,128)}, f32[10,1,24,64]{3,2,1,0:T(8,128)S(1)}, u32[]{:S(2)}, u32[]{:S(2)}) collective-permute-start(f32[10,1,24,64]{3,2,1,0:T(8,128)} %pad_maximum_fusion.22), channel_id=1, source_target_pairs={{1,0},{2,1},{3,2},{4,3},{5,4},{6,5},{7,6},{8,7},{9,8},{10,9},{11,1... | collective-permute-start | bytes 184328 | tf_op jit(solution)/shard_map/ppermute | solution.py:143
  4.2 26.1 %collective-permute-start = (f32[10,1,24,64]{3,2,1,0:T(8,128)}, f32[10,1,24,64]{3,2,1,0:T(8,128)S(1)}, u32[]{:S(2)}, u32[]{:S(2)}) collective-permute-start(f32[10,1,24,64]{3,2,1,0:T(8,128)} %pad_maximum_fusion.22), channel_id=1, source_target_pairs={{0,1},{1,2},{2,3},{3,4},{4,5},{5,6},{6,7},{7,8},{8,9},{9,10},{10,1... | collective-permute-start | bytes 184328 | tf_op jit(solution)/shard_map/ppermute | solution.py:142
  7.3 26.1 %collective-permute-start.3 = (f32[10,1,24,64]{3,2,1,0:T(8,128)}, f32[10,1,24,64]{3,2,1,0:T(8,128)S(1)}, u32[]{:S(2)}, u32[]{:S(2)}) collective-permute-start(f32[10,1,24,64]{3,2,1,0:T(8,128)} %pad_maximum_fusion.22), channel_id=1, source_target_pairs={{0,2},{1,3},{2,4},{3,5},{4,6},{5,7},{6,8},{7,9},{8,10},{9,11},{10,... | collective-permute-start | bytes 184328 | tf_op jit(solution)/shard_map/ppermute | solution.py:146
  12.1 21.3 %collective-permute-start.2 = (f32[10,1,24,64]{3,2,1,0:T(8,128)}, f32[10,1,24,64]{3,2,1,0:T(8,128)S(1)}, u32[]{:S(2)}, u32[]{:S(2)}) collective-permute-start(f32[10,1,24,64]{3,2,1,0:T(8,128)} %pad_maximum_fusion.22), channel_id=1, source_target_pairs={{2,0},{3,1},{4,2},{5,3},{6,4},{7,5},{8,6},{9,7},{10,8},{11,9},{12,... | collective-permute-start | bytes 184328 | tf_op jit(solution)/shard_map/ppermute | solution.py:147
  15.0 2.5 %copy-start.5 = (f32[9,1,24,64]{3,2,1,0:T(8,128)S(1)}, f32[9,1,24,64]{3,2,1,0:T(8,128)}, u32[]{:S(2)}) copy-start(f32[9,1,24,64]{3,2,1,0:T(8,128)} %param.5) | copy-start | bytes 165892
  16.2 34.6 %collective-permute-start.5 = (f32[10,24,6,128]{3,1,2,0:T(8,128)}, f32[10,24,6,128]{3,1,2,0:T(8,128)}, u32[]{:S(2)}, u32[]{:S(2)}) collective-permute-start(f32[10,24,6,128]{3,1,2,0:T(8,128)} %copy.78), channel_id=1, source_target_pairs={{1,0},{2,1},{3,2},{4,3},{5,4},{6,5},{7,6},{9,8},{10,9},{11,10},{12... | collective-permute-start | bytes 2211848 | tf_op jit(solution)/shard_map/ppermute | solution.py:141
  20.9 9.5 %copy-start.11 = (f32[1,1,24,64]{3,2,1,0:T(8,128)S(1)}, f32[1,1,24,64]{3,2,1,0:T(8,128)}, u32[]{:S(2)}) copy-start(f32[1,1,24,64]{3,2,1,0:T(8,128)} %copy-done.10) | copy-start | bytes 18436
  24.0 9.4 %copy-start.12 = (f32[1,1,24,64]{3,2,1,0:T(8,128)S(1)}, f32[1,1,24,64]{3,2,1,0:T(8,128)}, u32[]{:S(2)}) copy-start(f32[1,1,24,64]{3,2,1,0:T(8,128)} %copy-done.10) | copy-start | bytes 18436
  25.2 26.9 %collective-permute-start.4 = (f32[10,24,6,128]{3,1,2,0:T(8,128)}, f32[10,24,6,128]{3,1,2,0:T(8,128)}, u32[]{:S(2)}, u32[]{:S(2)}) collective-permute-start(f32[10,24,6,128]{3,1,2,0:T(8,128)} %copy.77), channel_id=1, source_target_pairs={{0,1},{1,2},{2,3},{3,4},{4,5},{5,6},{6,7},{8,9},{9,10},{10,11},{11... | collective-permute-start | bytes 2211848 | tf_op jit(solution)/shard_map/ppermute | solution.py:140
  32.6 1.1 copy-start.19
  32.6 1.4 %copy-start.13 = (bf16[18,1,24,64]{3,2,1,0:T(8,128)(2,1)S(1)}, bf16[18,1,24,64]{3,2,1,0:T(8,128)(2,1)}, u32[]{:S(2)}) copy-start(bf16[18,1,24,64]{3,2,1,0:T(8,128)(2,1)} %constant_dynamic-update-slice_fusion.14) | copy-start | bytes 165892
  32.6 1.4 %copy-start.14 = (f32[3,24,64]{2,1,0:T(8,128)S(1)}, f32[3,24,64]{2,1,0:T(8,128)}, u32[]{:S(2)}) copy-start(f32[3,24,64]{2,1,0:T(8,128)} %get-tuple-element.10) | copy-start | bytes 55300
  33.7 13.8 %copy-start.24 = (f32[24]{0:T(128)S(1)}, f32[24]{0:T(128)}, u32[]{:S(2)}) copy-start(f32[24]{0:T(128)} %get-tuple-element.149) | copy-start | bytes 292
  33.8 13.8 %copy-start.25 = (f32[24]{0:T(128)S(1)}, f32[24]{0:T(128)}, u32[]{:S(2)}) copy-start(f32[24]{0:T(128)} %get-tuple-element.150) | copy-start | bytes 292
  33.8 13.8 %copy-start.26 = (s32[24]{0:T(128)S(1)}, s32[24]{0:T(128)}, u32[]{:S(2)}) copy-start(s32[24]{0:T(128)} %get-tuple-element.151) | copy-start | bytes 292
  33.8 13.8 %copy-start.27 = (s32[24]{0:T(128)S(1)}, s32[24]{0:T(128)}, u32[]{:S(2)}) copy-start(s32[24]{0:T(128)} %get-tuple-element.152) | copy-start | bytes 292
  36.3 11.0 %all-to-all-start = ((bf16[8,2,5184]{2,1,0:T(2,128)(2,1)}), bf16[8,2,5184]{2,1,0:T(2,128)(2,1)S(1)}, u32[]{:S(2)}, u32[]{:S(2)}) async-start(bf16[8,2,5184]{2,1,0:T(2,128)(2,1)} %reshape.513), calls=%async_computation | async-start | bytes 335872 | tf_op jit(solution)/shard_map/all_to_all | solution.py:161
  41.4 9.4 %copy-start.20 = (f32[9,1,24,64]{3,2,1,0:T(8,128)}, f32[9,1,24,64]{3,2,1,0:T(8,128)S(1)}, u32[]{:S(2)}) copy-start(f32[9,1,24,64]{3,2,1,0:T(8,128)S(1)} %constant_dynamic-update-slice_fusion.3) | copy-start | bytes 165892
  53.4 11.9 %copy-start = (f32[10,24,6,128]{3,2,1,0:T(8,128)}, f32[10,24,6,128]{3,2,1,0:T(8,128)S(1)}, u32[]{:S(2)}) copy-start(f32[10,24,6,128]{3,2,1,0:T(8,128)S(1)} %copy.79) | copy-start | bytes 2211844
  53.5 7.1 %copy-start.21 = (f32[128]{0:T(128)S(1)}, f32[128]{0:T(128)}, u32[]{:S(2)}) copy-start(f32[128]{0:T(128)} %get-tuple-element.157) | copy-start | bytes 1540
  53.5 7.1 %copy-start.22 = (f32[128]{0:T(128)S(1)}, f32[128]{0:T(128)}, u32[]{:S(2)}) copy-start(f32[128]{0:T(128)} %get-tuple-element.158) | copy-start | bytes 1540
  53.5 7.1 %copy-start.23 = (s32[128]{0:T(128)S(1)}, s32[128]{0:T(128)}, u32[]{:S(2)}) copy-start(s32[128]{0:T(128)} %get-tuple-element.160) | copy-start | bytes 1540
  53.6 10.9 %collective-permute-start.7 = (f32[10,2,21,128]{3,2,1,0:T(8,128)S(1)}, f32[10,2,21,128]{3,2,1,0:T(8,128)S(1)}, u32[]{:S(2)}, u32[]{:S(2)}) collective-permute-start(f32[10,2,21,128]{3,2,1,0:T(8,128)S(1)} %get-tuple-element.46), channel_id=1, source_target_pairs={{8,0},{16,8},{24,16},{9,1},{17,9},{25,17},{10,2},{18,10},{26,18},{... | collective-permute-start | bytes 645128 | tf_op jit(solution)/shard_map/ppermute | solution.py:16
  54.9 10.4 %collective-permute-start.6 = (f32[10,2,21,128]{3,2,1,0:T(8,128)S(1)}, f32[10,2,21,128]{3,2,1,0:T(8,128)S(1)}, u32[]{:S(2)}, u32[]{:S(2)}) collective-permute-start(f32[10,2,21,128]{3,2,1,0:T(8,128)S(1)} %get-tuple-element.45), channel_id=1, source_target_pairs={{0,8},{8,16},{16,24},{1,9},{9,17},{17,25},{2,10},{10,18},{18,26},{... | collective-permute-start | bytes 645128 | tf_op jit(solution)/shard_map/ppermute | solution.py:15
  66.0 2.0 %copy-start.3 = (f32[10,28,21,128]{3,2,1,0:T(8,128)}, f32[10,28,21,128]{3,2,1,0:T(8,128)S(1)}, u32[]{:S(2)}) copy-start(f32[10,28,21,128]{3,2,1,0:T(8,128)S(1)} %pad_maximum_fusion) | copy-start | bytes 9031684
  71.8 2.6 %copy-start.1 = (f32[10,24,6,128]{3,2,1,0:T(8,128)S(1)}, f32[10,24,6,128]{3,2,1,0:T(8,128)}, u32[]{:S(2)}) copy-start(f32[10,24,6,128]{3,2,1,0:T(8,128)} %copy-done) | copy-start | bytes 2211844
  71.8 2.6 %copy-start.8 = (f32[26,19,127]{2,1,0:T(8,128)S(1)}, f32[26,19,127]{2,1,0:T(8,128)}, u32[]{:S(2)}) copy-start(f32[26,19,127]{2,1,0:T(8,128)} %get-tuple-element.84) | copy-start | bytes 752860
  71.8 2.6 %copy-start.9 = (f32[26,19,127]{2,1,0:T(8,128)S(1)}, f32[26,19,127]{2,1,0:T(8,128)}, u32[]{:S(2)}) copy-start(f32[26,19,127]{2,1,0:T(8,128)} %get-tuple-element.85) | copy-start | bytes 752860
  74.5 2.2 %copy-start.4 = (f32[10,28,21,128]{3,2,1,0:T(8,128)S(1)}, f32[10,28,21,128]{3,2,1,0:T(8,128)}, u32[]{:S(2)}) copy-start(f32[10,28,21,128]{3,2,1,0:T(8,128)} %copy-done.3) | copy-start | bytes 9031684
  77.3 1.0 copy-start.2
  77.3 1.1 copy-start.7
  79.3 2.2 %slice-start = ((s8[5308416]{0:T(1024)(128)(4,1)}), s8[4194304]{0:T(1024)(128)(4,1)S(1)}, s32[]{:S(2)}) async-start(s8[5308416]{0:T(1024)(128)(4,1)} %bitcast.617), calls=%async_computation.1 | async-start | bytes 8388608
  79.5 2.4 %slice-start.1 = ((s8[5308416]{0:T(1024)(128)(4,1)}), s8[1114112]{0:T(1024)(128)(4,1)S(1)}, s32[]{:S(2)}) async-start(s8[5308416]{0:T(1024)(128)(4,1)} %bitcast.617), calls=%async_computation.2 | async-start | bytes 2228224
  79.9 2.0 %copy-start.16 = (f32[24,17]{1,0:T(8,128)S(1)}, f32[24,17]{1,0:T(8,128)}, u32[]{:S(2)}) copy-start(f32[24,17]{1,0:T(8,128)} %multiply_add_fusion.1) | copy-start | bytes 4900
  81.9 8.2 %copy-start.6 = (f32[26,21,128]{2,1,0:T(8,128)S(1)}, f32[26,21,128]{2,1,0:T(8,128)}, u32[]{:S(2)}) copy-start(f32[26,21,128]{2,1,0:T(8,128)} %get-tuple-element.11) | copy-start | bytes 838660
  82.6 8.7 %collective-permute-start.9 = (f32[9,2,17,128]{3,2,1,0:T(8,128)S(1)}, f32[9,2,17,128]{3,2,1,0:T(8,128)S(1)}, u32[]{:S(2)}, u32[]{:S(2)}) collective-permute-start(f32[9,2,17,128]{3,2,1,0:T(8,128)S(1)} %get-tuple-element.54), channel_id=1, source_target_pairs={{8,0},{16,8},{24,16},{9,1},{17,9},{25,17},{10,2},{18,10},{26,18},{... | collective-permute-start | bytes 470024 | tf_op jit(solution)/shard_map/ppermute | solution.py:16
  83.9 8.6 %collective-permute-start.8 = (f32[9,2,17,128]{3,2,1,0:T(8,128)S(1)}, f32[9,2,17,128]{3,2,1,0:T(8,128)S(1)}, u32[]{:S(2)}, u32[]{:S(2)}) collective-permute-start(f32[9,2,17,128]{3,2,1,0:T(8,128)S(1)} %get-tuple-element.53), channel_id=1, source_target_pairs={{0,8},{8,16},{16,24},{1,9},{9,17},{17,25},{2,10},{10,18},{18,26},{... | collective-permute-start | bytes 470024 | tf_op jit(solution)/shard_map/ppermute | solution.py:15
  94.7 0.7 copy-start.18
  96.0 7.5 %collective-permute-start.11 = (f32[9,2,13,128]{3,2,1,0:T(8,128)S(1)}, f32[9,2,13,128]{3,2,1,0:T(8,128)S(1)}, u32[]{:S(2)}, u32[]{:S(2)}) collective-permute-start(f32[9,2,13,128]{3,2,1,0:T(8,128)S(1)} %get-tuple-element.61), channel_id=1, source_target_pairs={{8,0},{16,8},{24,16},{9,1},{17,9},{25,17},{10,2},{18,10},{26,18},{... | collective-permute-start | bytes 359432 | tf_op jit(solution)/shard_map/ppermute | solution.py:16
  97.3 7.7 %collective-permute-start.10 = (f32[9,2,13,128]{3,2,1,0:T(8,128)S(1)}, f32[9,2,13,128]{3,2,1,0:T(8,128)S(1)}, u32[]{:S(2)}, u32[]{:S(2)}) collective-permute-start(f32[9,2,13,128]{3,2,1,0:T(8,128)S(1)} %get-tuple-element.60), channel_id=1, source_target_pairs={{0,8},{8,16},{16,24},{1,9},{9,17},{17,25},{2,10},{10,18},{18,26},{... | collective-permute-start | bytes 359432 | tf_op jit(solution)/shard_map/ppermute | solution.py:15
  107.1 0.7 copy-start.17

commit v10 on v6

--- a/solution.py
+++ b/solution.py
@@ -12,9 +12,9 @@
 
 def x_halo(field, width):
     nx = lax.axis_size("gx")
-    from_left = lax.ppermute(field[:, -width:], "gx", shifted(nx, 1))
-    from_right = lax.ppermute(field[:, :width], "gx", shifted(nx, -1))
-    return jnp.concatenate([from_left, field, from_right], axis=1)
+    from_left = lax.ppermute(field[:, :, -width:], "gx", shifted(nx, 1))
+    from_right = lax.ppermute(field[:, :, :width], "gx", shifted(nx, -1))
+    return jnp.concatenate([from_left, field, from_right], axis=2)
 
 
 def lookup_kernel(step, extra, idx_ref, tab_ref, state_ref, pay_ref, *rest):
@@ -60,7 +60,7 @@
     return up - down
 
 
-def step_wide(ext, coef, stress0, lam, shear, step, spacing, y_local):
+def step_wide(ext, coef, stress0, lam, shear, step, spacing, y_local, swap=False):
     scale = 0.5 / spacing
     s = ext[3:9]
     if y_local:
@@ -73,6 +73,8 @@
         mid_s = s[:, 1:-1, 1:-1]
         dx = lambda c: (s[c, 2:, 1:-1] - s[c, :-2, 1:-1]) * scale
         dy = lambda c: (s[c, 1:-1, 2:] - s[c, 1:-1, :-2]) * scale
+        if swap:
+            dx, dy = dy, dx
         dz = lambda c: along(mid_s[c], 2) * scale
         vel_old = ext[0:3, 1:-1, 1:-1]
     acc_x = dx(0) + dy(3) + dz(4)
@@ -88,6 +90,8 @@
         inner = vel[:, 1:-1, 1:-1]
         gx = lambda c: (vel[c, 2:, 1:-1] - vel[c, :-2, 1:-1]) * scale
         gy = lambda c: (vel[c, 1:-1, 2:] - vel[c, 1:-1, :-2]) * scale
+        if swap:
+            gx, gy = gy, gx
         gz = lambda c: along(inner[c], 2) * scale
     g_x0, g_y1, g_z2 = gx(0), gy(1), gz(2)
     spread = g_x0 + g_y1 + g_z2
@@ -142,10 +146,16 @@
     reach_y = 6
 
     region_pay, lam_r, mu_r = lookup(region_material, material_table, region_state, 0.6, False)
-    (fine_pay,) = lookup(fine_material, material_table, fine_state, 0.2, True)
-
-    fine_lo = lax.ppermute(fine_pay[:, :, -reach_y:], "gy", shifted(count_y, 1))
-    fine_hi = lax.ppermute(fine_pay[:, :, :reach_y], "gy", shifted(count_y, -1))
+    (fine_pay,) = lookup(
+        jnp.transpose(fine_material, (1, 0, 2)),
+        material_table,
+        jnp.transpose(fine_state, (0, 2, 1, 3)),
+        0.2,
+        True,
+    )
+
+    fine_lo = lax.ppermute(fine_pay[:, -reach_y:], "gy", shifted(count_y, 1))
+    fine_hi = lax.ppermute(fine_pay[:, :reach_y], "gy", shifted(count_y, -1))
     reg_lo = lax.ppermute(region_pay, flat, shifted(n_flat, 1))
     reg_hi = lax.ppermute(region_pay, flat, shifted(n_flat, -1))
     lows, highs = [reg_lo], [reg_hi]
@@ -178,43 +188,44 @@
         0,
     )[fine_y - 4: 2 * fine_y + 4]
     first = jnp.einsum("fa,cabz->cfbz", interp_matrix(fine_x, columns), band, precision=high)
-    second = jnp.einsum("gb,cfbz->cfgz", tiles_w, first, precision=high)
+    second = jnp.einsum("gb,cfbz->cgfz", tiles_w, first, precision=high)
     background = jnp.einsum(
-        "kz,cfgz->cfgk", interp_matrix(fine_z, band.shape[3]), second, precision=high
+        "kz,cgfz->cgfk", interp_matrix(fine_z, band.shape[3]), second, precision=high
     )
     along_x = ramp(lax.axis_index("gx") * fine_x, fine_x, count_x * fine_x, fine_x)
     along_y = ramp(me_y * fine_y - 4, fine_y + 8, count_y * fine_y, fine_y)
-    relax = (0.1 + 0.4 * jnp.maximum(along_x[:, None], along_y[None, :]))[:, :, None]
-
-    wide = jnp.concatenate([fine_lo, fine_pay, fine_hi], axis=2)
+    relax = (0.1 + 0.4 * jnp.maximum(along_y[:, None], along_x[None, :]))[:, :, None]
+
+    wide = jnp.concatenate([fine_lo, fine_pay, fine_hi], axis=1)
     lam_w, mu_w = wide[10], wide[11]
     state = wide[:9]
     coef_w = None
     for sub in range(1, 4):
         if sub == 1:
             ext = x_halo(wide[:10], 2)
-            coef_w = ext[9, 1:-1]
+            coef_w = ext[9, :, 1:-1]
             ext = ext[:9]
         else:
             ext = x_halo(state, 2)
         off = 2 * (sub - 1)
-        rows = state.shape[2]
+        rows = state.shape[1]
         state = step_wide(
             ext,
-            coef_w[:, off + 1: off + rows - 1],
-            state[3:, :, 2:-2],
-            lam_w[:, off + 2: off + rows - 2],
-            mu_w[:, off + 2: off + rows - 2],
+            coef_w[off + 1: off + rows - 1],
+            state[3:, 2:-2],
+            lam_w[off + 2: off + rows - 2],
+            mu_w[off + 2: off + rows - 2],
             0.2,
             1.0,
             False,
+            swap=True,
         )
         share = sub / 3.0
-        target = background[:9, :, off: off + rows - 4] + share * (
-            background[9:, :, off: off + rows - 4] - background[:9, :, off: off + rows - 4]
+        target = background[:9, off: off + rows - 4] + share * (
+            background[9:, off: off + rows - 4] - background[:9, off: off + rows - 4]
         )
-        state = state + relax[None, :, off: off + rows - 4] * (target - state)
-    return (region_next, state)
+        state = state + relax[None, off: off + rows - 4] * (target - state)
+    return (region_next, jnp.transpose(state, (0, 2, 1, 3)))
 
 
 def solution(mesh):

time: 104 us -> 95.4 us (0.917); the launches traced: 102 us -> 94.8 us
  waiting for transfers between devices: 17.1 us -> 29.9 us
  local copies, waits for them, and re-layouts: 18.6 us -> 7.3 us
  starting transfers between devices: 41.7 us -> 37.5 us
  other arithmetic: 12.1 us -> 9.03 us
    unnamed x62 -> x35, local copies, waits for them, and re-layouts: 8.86 us -> 1.68 us
    all_to_all x1, waiting for transfers between devices: 7.57 us -> 14.5 us  [local(): band = lax.all_to_all(send, 'gy', 2, 1, tiled=True).astype(jnp.float32)]
    ppermute x8, starting transfers between devices: 26.6 us -> 20.4 us  [the longest x3 10.5 us: x_halo(): from_left = lax.ppermute(field[:, :, -width:], 'gx', shifted(nx, 1))]
    ppermute x8, waiting for transfers between devices: 9.47 us -> 15.3 us  [the longest x3 12.9 us: x_halo(): from_right = lax.ppermute(field[:, :, :width], 'gx', shifted(nx, -1))]
    all_to_all x1, starting transfers between devices: 5.54 us -> 8.21 us  [local(): band = lax.all_to_all(send, 'gy', 2, 1, tiled=True).astype(jnp.float32)]
    select_n x3, other arithmetic: 1.79 us -> 0.05 us  [interp_matrix(): frac = jnp.where(above, 1.0, frac)]
    ppermute x2 -> x0, local copies, waits for them, and re-layouts: 1.74 us -> none  [the longest x1 1.52 us: local(): fine_lo = lax.ppermute(fine_pay[:, :, -reach_y:], 'gy', shifted(count_y, 1))]
    mul x2 -> x0, local copies, waits for them, and re-layouts: 1.35 us -> none  [local(): state = state + relax[None, :, off:off + rows - 4] * (target - state)]
  transfers between devices with their start and end apart: 13 -> 13, of which waited for: 7 -> 6; matrix products, arithmetic and copies ran while one was open for 22% -> 12% of each run, Pallas kernels for 3% -> 3%
where the time goes in v10:
time: 95.4 us; the launch traced here: 94.8 us
  starting transfers between devices  37.5 us (39%)
  waiting for transfers between devices  29.9 us (31%)
  other arithmetic  9.03 us (9%)
  local copies, waits for them, and re-layouts  7.3 us (8%)
  matrix products  5.3 us (6%)
  Pallas kernels  4.21 us (4%)
  between operations  1.54 us (2%)
    all_to_all x1, waiting for transfers between devices, local(): band = lax.all_to_all(send, 'gy', 2, 1, tiled=True).astype(jnp.float32)  14.5 us
    ppermute x3, waiting for transfers between devices, x_halo(): from_right = lax.ppermute(field[:, :, :width], 'gx', shifted(nx, -1))  12.9 us
    ppermute x3, starting transfers between devices, x_halo(): from_left = lax.ppermute(field[:, :, -width:], 'gx', shifted(nx, 1))  10.5 us
    all_to_all x1, starting transfers between devices, local(): band = lax.all_to_all(send, 'gy', 2, 1, tiled=True).astype(jnp.float32)  8.21 us
    ppermute x1, starting transfers between devices, local(): lows.insert(0, lax.ppermute(region_pay, flat, shifted(n_flat, d)))  4.84 us
    ppermute x1, starting transfers between devices, local(): fine_lo = lax.ppermute(fine_pay[:, -reach_y:], 'gy', shifted(count_y, 1))  4.62 us
    pallas_call x2, Pallas kernels, lookup(): pl.pallas_call(lambda *refs: lookup_kernel(step, extra, *refs), out_shape...  4.21 us
    ppermute x3, starting transfers between devices, x_halo(): from_right = lax.ppermute(field[:, :, :width], 'gx', shifted(nx, -1))  4.06 us
  transfers between devices with their start and end apart: 13, of which 6 were waited for; matrix products, arithmetic and copies ran while one was open for 12% of the time, Pallas kernels for 3%

profile of v10, /device:TPU:0, one launch (start us, length us, event | category | flops | bytes accessed | tf_op | source)
XLA Modules:
  0.0 94.8 jit_solution(7937836039074558597)
XLA Ops:
  0.6 1.6 %shard_map.68 = (f32[10,1,24,64]{3,2,1,0:T(8,128)}, f32[1,24,64]{2,1,0:T(8,128)}, f32[1,24,64]{2,1,0:T(8,128)}) custom-call(s32[1,24,64]{2,1,0:T(8,128)} %refs_0_.1, f32[3,8]{1,0:T(4,128)} %refs_1_.3, f32[9,1,24,64]{3,2,1,0:T(8,128)} %refs_2_.1), custom_call_target="tpu_custom_call" | custom-call | tf_op jit(solution)/shard_map/pallas_call | solution.py:47
  2.2 4.8 %collective-permute-start.3 = (f32[10,1,24,64]{3,2,1,0:T(8,128)}, f32[10,1,24,64]{3,2,1,0:T(8,128)S(1)}, u32[]{:S(2)}, u32[]{:S(2)}) collective-permute-start(f32[10,1,24,64]{3,2,1,0:T(8,128)} %get-tuple-element.5), channel_id=1, source_target_pairs={{0,2},{1,3},{2,4},{3,5},{4,6},{5,7},{6,8},{7,9},{8,10},{9,11},{10,... | collective-permute-start | bytes 184328 | tf_op jit(solution)/shard_map/ppermute | solution.py:163
  7.1 1.5 %collective-permute-start = (f32[10,1,24,64]{3,2,1,0:T(8,128)}, f32[10,1,24,64]{3,2,1,0:T(8,128)S(1)}, u32[]{:S(2)}, u32[]{:S(2)}) collective-permute-start(f32[10,1,24,64]{3,2,1,0:T(8,128)} %get-tuple-element.5), channel_id=1, source_target_pairs={{0,1},{1,2},{2,3},{3,4},{4,5},{5,6},{6,7},{7,8},{8,9},{9,10},{10,1... | collective-permute-start | bytes 184328 | tf_op jit(solution)/shard_map/ppermute | solution.py:159
  8.5 1.3 %collective-permute-start.1 = (f32[10,1,24,64]{3,2,1,0:T(8,128)}, f32[10,1,24,64]{3,2,1,0:T(8,128)S(1)}, u32[]{:S(2)}, u32[]{:S(2)}) collective-permute-start(f32[10,1,24,64]{3,2,1,0:T(8,128)} %get-tuple-element.5), channel_id=1, source_target_pairs={{1,0},{2,1},{3,2},{4,3},{5,4},{6,5},{7,6},{8,7},{9,8},{10,9},{11,1... | collective-permute-start | bytes 184328 | tf_op jit(solution)/shard_map/ppermute | solution.py:160
  9.8 1.3 %collective-permute-start.2 = (f32[10,1,24,64]{3,2,1,0:T(8,128)}, f32[10,1,24,64]{3,2,1,0:T(8,128)S(1)}, u32[]{:S(2)}, u32[]{:S(2)}) collective-permute-start(f32[10,1,24,64]{3,2,1,0:T(8,128)} %get-tuple-element.5), channel_id=1, source_target_pairs={{2,0},{3,1},{4,2},{5,3},{6,4},{7,5},{8,6},{9,7},{10,8},{11,9},{12,... | collective-permute-start | bytes 184328 | tf_op jit(solution)/shard_map/ppermute | solution.py:164
  11.1 2.6 %shard_map.69 = f32[12,9,24,128]{3,2,1,0:T(8,128)} custom-call(s32[9,24,128]{2,1,0:T(8,128)} %bitcast.662, f32[3,8]{1,0:T(4,128)} %refs_1_.3, f32[9,9,24,128]{3,2,1,0:T(8,128)} %bitcast.660), custom_call_target="tpu_custom_call" | custom-call | tf_op jit(solution)/shard_map/pallas_call | solution.py:47
  13.8 2.5 %fusion.273 = (f32[12,6,24,128]{3,2,1,0:T(8,128)}, f32[12,6,24,128]{3,2,1,0:T(8,128)S(1)}) fusion(f32[12,9,24,128]{3,2,1,0:T(8,128)} %shard_map.69), kind=kLoop, calls=%fused_computation.497 | loop fusion | bytes 3538944 | tf_op jit(solution)/shard_map/slice | solution.py:157
  16.3 4.6 %collective-permute-start.4 = (f32[12,6,24,128]{3,2,1,0:T(8,128)}, f32[12,6,24,128]{3,2,1,0:T(8,128)S(1)}, u32[]{:S(2)}, u32[]{:S(2)}) collective-permute-start(f32[12,6,24,128]{3,2,1,0:T(8,128)} %get-tuple-element.44), channel_id=1, source_target_pairs={{0,1},{1,2},{2,3},{3,4},{4,5},{5,6},{6,7},{8,9},{9,10},{10,11},{11... | collective-permute-start | bytes 2654216 | tf_op jit(solution)/shard_map/ppermute | solution.py:157
  21.2 1.3 %collective-permute-start.5 = (f32[12,6,24,128]{3,2,1,0:T(8,128)S(1)}, f32[12,6,24,128]{3,2,1,0:T(8,128)S(1)}, u32[]{:S(2)}, u32[]{:S(2)}) collective-permute-start(f32[12,6,24,128]{3,2,1,0:T(8,128)S(1)} %get-tuple-element.45), channel_id=1, source_target_pairs={{1,0},{2,1},{3,2},{4,3},{5,4},{6,5},{7,6},{9,8},{10,9},{11,10},{12... | collective-permute-start | bytes 2654216 | tf_op jit(solution)/shard_map/ppermute | solution.py:158
  24.0 1.0 %reshape.473 = bf16[8,2,5184]{2,1,0:T(2,128)(2,1)} reshape(bf16[72,1,18,64]{3,2,1,0:T(8,128)(2,1)S(1)} %bitcast.661) | data formatting | bytes 331776
  24.9 8.2 %all-to-all-start = ((bf16[8,2,5184]{2,1,0:T(2,128)(2,1)}), bf16[8,2,5184]{2,1,0:T(2,128)(2,1)S(1)}, u32[]{:S(2)}, u32[]{:S(2)}) async-start(bf16[8,2,5184]{2,1,0:T(2,128)(2,1)} %reshape.473), calls=%async_computation | async-start | bytes 335872 | tf_op jit(solution)/shard_map/all_to_all | solution.py:177
  33.2 14.5 %all-to-all-done = bf16[8,2,5184]{2,1,0:T(2,128)(2,1)S(1)} async-done(((bf16[8,2,5184]{2,1,0:T(2,128)(2,1)}), bf16[8,2,5184]{2,1,0:T(2,128)(2,1)S(1)}, u32[]{:S(2)}, u32[]{:S(2)}) %all-to-all-start) | async-done | bytes 165920 | tf_op jit(solution)/shard_map/all_to_all | solution.py:177
  47.7 0.3 reshape.474
  48.0 0.7 convolution_bitcast_fusion
  48.8 2.4 %fusion.4 = f32[18,17,24,64]{3,1,2,0:T(8,128)S(1)} fusion(f32[18,24,9,64]{3,1,2,0:T(8,128)S(1)} %convolution_bitcast_fusion, f32[9,3]{0,1:T(4,128)S(1)} %select_add_fusion, f32[9,3]{0,1:T(4,128)S(1)} %broadcast.1055), kind=kOutput, calls=%fused_computation.7 | convolution fusion | flops 25382240 | bytes 2875608 | tf_op jit(solution)/shard_map/gb,cfbz->cgfz/dot_general | solution.py:191
  51.2 0.2 pad_maximum_fusion.9
  51.4 3.5 %collective-permute-start.6 = (f32[10,21,2,128]{3,2,1,0:T(2,128)S(1)}, f32[10,21,2,128]{3,2,1,0:T(2,128)S(1)}, u32[]{:S(2)}, u32[]{:S(2)}) collective-permute-start(f32[10,21,2,128]{3,2,1,0:T(2,128)S(1)} %get-tuple-element.32), channel_id=1, source_target_pairs={{0,8},{8,16},{16,24},{1,9},{9,17},{17,25},{2,10},{10,18},{18,26},{... | collective-permute-start | bytes 645128 | tf_op jit(solution)/shard_map/ppermute | solution.py:15
  54.9 1.5 %collective-permute-start.7 = (f32[10,21,2,128]{3,2,1,0:T(2,128)S(1)}, f32[10,21,2,128]{3,2,1,0:T(2,128)S(1)}, u32[]{:S(2)}, u32[]{:S(2)}) collective-permute-start(f32[10,21,2,128]{3,2,1,0:T(2,128)S(1)} %get-tuple-element.33), channel_id=1, source_target_pairs={{8,0},{16,8},{24,16},{9,1},{17,9},{25,17},{10,2},{18,10},{26,18},{... | collective-permute-start | bytes 645128 | tf_op jit(solution)/shard_map/ppermute | solution.py:16
  56.4 2.2 %fusion = f32[18,17,24,128]{3,2,1,0:T(8,128)S(1)} fusion(f32[18,17,24,64]{3,1,2,0:T(8,128)S(1)} %fusion.4, f32[128]{0:T(128)S(1)} %get-tuple-element.150, s32[128]{0:T(128)S(1)} %get-tuple-element.153, f32[128]{0:T(128)S(1)} %get-tuple-element.151, s32[128]{0:T(128)S(1)} %get-tuple-element.152), kind=kOutput, calls=%fused_computation | convolution fusion | flops 361013248 | bytes 5642240 | tf_op jit(solution)/shard_map/kz,cgfz->cgfk/dot_general | solution.py:192
  58.5 0.2 pad_maximum_fusion.1
  58.7 0.2 slice.1191
  58.9 4.1 %collective-permute-done.7 = f32[10,21,2,128]{3,2,1,0:T(2,128)S(1)} collective-permute-done((f32[10,21,2,128]{3,2,1,0:T(2,128)S(1)}, f32[10,21,2,128]{3,2,1,0:T(2,128)S(1)}, u32[]{:S(2)}, u32[]{:S(2)}) %collective-permute-start.7) | collective-permute-done | bytes 215072 | tf_op jit(solution)/shard_map/ppermute | solution.py:16
  63.1 0.6 pad_maximum_fusion
  63.7 0.2 slice_bitcast_fusion.3
  63.8 0.2 fusion.276
  64.0 0.2 fusion.274
  64.2 0.2 fusion.26
  64.4 0.4 fusion.37
  64.8 0.2 slice_add_fusion
  65.2 0.2 fusion.86
  65.4 0.2 slice_bitcast_fusion.4
  65.8 0.1 fusion.280
  65.9 0.2 fusion.75
  66.2 0.1 fusion.67
  66.3 0.1 fusion.60
  66.5 0.5 fusion.11
  67.1 3.5 %collective-permute-start.8 = (f32[9,17,2,128]{3,2,1,0:T(2,128)S(1)}, f32[9,17,2,128]{3,2,1,0:T(2,128)S(1)}, u32[]{:S(2)}, u32[]{:S(2)}) collective-permute-start(f32[9,17,2,128]{3,2,1,0:T(2,128)S(1)} %get-tuple-element.37), channel_id=1, source_target_pairs={{0,8},{8,16},{16,24},{1,9},{9,17},{17,25},{2,10},{10,18},{18,26},{... | collective-permute-start | bytes 470024 | tf_op jit(solution)/shard_map/ppermute | solution.py:15
  70.6 1.3 %collective-permute-start.9 = (f32[9,17,2,128]{3,2,1,0:T(2,128)S(1)}, f32[9,17,2,128]{3,2,1,0:T(2,128)S(1)}, u32[]{:S(2)}, u32[]{:S(2)}) collective-permute-start(f32[9,17,2,128]{3,2,1,0:T(2,128)S(1)} %get-tuple-element.38), channel_id=1, source_target_pairs={{8,0},{16,8},{24,16},{9,1},{17,9},{25,17},{10,2},{18,10},{26,18},{... | collective-permute-start | bytes 470024 | tf_op jit(solution)/shard_map/ppermute | solution.py:16
  72.0 1.4 %collective-permute-done.8 = f32[9,17,2,128]{3,2,1,0:T(2,128)S(1)} collective-permute-done((f32[9,17,2,128]{3,2,1,0:T(2,128)S(1)}, f32[9,17,2,128]{3,2,1,0:T(2,128)S(1)}, u32[]{:S(2)}, u32[]{:S(2)}) %collective-permute-start.8) | collective-permute-done | bytes 156704 | tf_op jit(solution)/shard_map/ppermute | solution.py:15
  73.3 4.4 %collective-permute-done.9 = f32[9,17,2,128]{3,2,1,0:T(2,128)S(1)} collective-permute-done((f32[9,17,2,128]{3,2,1,0:T(2,128)S(1)}, f32[9,17,2,128]{3,2,1,0:T(2,128)S(1)}, u32[]{:S(2)}, u32[]{:S(2)}) %collective-permute-start.9) | collective-permute-done | bytes 156704 | tf_op jit(solution)/shard_map/ppermute | solution.py:16
  77.7 0.1 maximum_bitcast_fusion.2
  77.9 0.1 fusion.277
  78.0 0.1 fusion.278
  78.1 0.1 fusion.279
  78.3 0.4 pad_maximum_fusion.2
  78.7 0.2 fusion.53
  78.9 0.2 fusion.48
  79.1 0.2 fusion.42
  79.2 0.2 slice_add_fusion.1
  79.6 0.1 fusion.142
  79.8 0.1 fusion.131
  80.1 0.1 slice_bitcast_fusion.7
  80.4 0.1 fusion.116
  80.5 0.4 fusion.16
  81.0 3.5 %collective-permute-start.10 = (f32[9,13,2,128]{3,2,1,0:T(2,128)S(1)}, f32[9,13,2,128]{3,2,1,0:T(2,128)S(1)}, u32[]{:S(2)}, u32[]{:S(2)}) collective-permute-start(f32[9,13,2,128]{3,2,1,0:T(2,128)S(1)} %get-tuple-element.42), channel_id=1, source_target_pairs={{0,8},{8,16},{16,24},{1,9},{9,17},{17,25},{2,10},{10,18},{18,26},{... | collective-permute-start | bytes 359432 | tf_op jit(solution)/shard_map/ppermute | solution.py:15
  84.5 1.3 %collective-permute-start.11 = (f32[9,13,2,128]{3,2,1,0:T(2,128)S(1)}, f32[9,13,2,128]{3,2,1,0:T(2,128)S(1)}, u32[]{:S(2)}, u32[]{:S(2)}) collective-permute-start(f32[9,13,2,128]{3,2,1,0:T(2,128)S(1)} %get-tuple-element.43), channel_id=1, source_target_pairs={{8,0},{16,8},{24,16},{9,1},{17,9},{25,17},{10,2},{18,10},{26,18},{... | collective-permute-start | bytes 359432 | tf_op jit(solution)/shard_map/ppermute | solution.py:16
  85.9 1.0 %collective-permute-done.10 = f32[9,13,2,128]{3,2,1,0:T(2,128)S(1)} collective-permute-done((f32[9,13,2,128]{3,2,1,0:T(2,128)S(1)}, f32[9,13,2,128]{3,2,1,0:T(2,128)S(1)}, u32[]{:S(2)}, u32[]{:S(2)}) %collective-permute-start.10) | collective-permute-done | bytes 119840 | tf_op jit(solution)/shard_map/ppermute | solution.py:15
  86.9 4.3 %collective-permute-done.11 = f32[9,13,2,128]{3,2,1,0:T(2,128)S(1)} collective-permute-done((f32[9,13,2,128]{3,2,1,0:T(2,128)S(1)}, f32[9,13,2,128]{3,2,1,0:T(2,128)S(1)}, u32[]{:S(2)}, u32[]{:S(2)}) %collective-permute-start.11) | collective-permute-done | bytes 119840 | tf_op jit(solution)/shard_map/ppermute | solution.py:16
  91.7 0.3 pad_maximum_fusion.3
  92.1 0.1 fusion.109
  92.2 0.1 fusion.104
  92.3 0.1 fusion.98
  92.4 0.1 slice_add_fusion.2
  93.5 1.2 %fusion.20 = f32[9,24,9,128]{3,1,2,0:T(8,128)} fusion(f32[9,9,24,128]{3,2,1,0:T(8,128)S(1)} %fusion.155, f32[18,17,24,128]{3,2,1,0:T(8,128)S(1)} %fusion, f32[9,24]{1,0:T(8,128)S(1)} %slice.1318), kind=kLoop, calls=%fused_computation.26 | loop fusion | flops 1244160 | bytes 3982176 | tf_op jit(solution)/shard_map/transpose | solution.py:228
  (106 shorter events, 4.1 us)
Async XLA Ops:
  2.2 19.0 %collective-permute-start.3 = (f32[10,1,24,64]{3,2,1,0:T(8,128)}, f32[10,1,24,64]{3,2,1,0:T(8,128)S(1)}, u32[]{:S(2)}, u32[]{:S(2)}) collective-permute-start(f32[10,1,24,64]{3,2,1,0:T(8,128)} %get-tuple-element.5), channel_id=1, source_target_pairs={{0,2},{1,3},{2,4},{3,5},{4,6},{5,7},{6,8},{7,9},{8,10},{9,11},{10,... | collective-permute-start | bytes 184328 | tf_op jit(solution)/shard_map/ppermute | solution.py:163
  7.1 15.5 %collective-permute-start = (f32[10,1,24,64]{3,2,1,0:T(8,128)}, f32[10,1,24,64]{3,2,1,0:T(8,128)S(1)}, u32[]{:S(2)}, u32[]{:S(2)}) collective-permute-start(f32[10,1,24,64]{3,2,1,0:T(8,128)} %get-tuple-element.5), channel_id=1, source_target_pairs={{0,1},{1,2},{2,3},{3,4},{4,5},{5,6},{6,7},{7,8},{8,9},{9,10},{10,1... | collective-permute-start | bytes 184328 | tf_op jit(solution)/shard_map/ppermute | solution.py:159
  8.5 14.1 %collective-permute-start.1 = (f32[10,1,24,64]{3,2,1,0:T(8,128)}, f32[10,1,24,64]{3,2,1,0:T(8,128)S(1)}, u32[]{:S(2)}, u32[]{:S(2)}) collective-permute-start(f32[10,1,24,64]{3,2,1,0:T(8,128)} %get-tuple-element.5), channel_id=1, source_target_pairs={{1,0},{2,1},{3,2},{4,3},{5,4},{6,5},{7,6},{8,7},{9,8},{10,9},{11,1... | collective-permute-start | bytes 184328 | tf_op jit(solution)/shard_map/ppermute | solution.py:160
  9.8 13.0 %collective-permute-start.2 = (f32[10,1,24,64]{3,2,1,0:T(8,128)}, f32[10,1,24,64]{3,2,1,0:T(8,128)S(1)}, u32[]{:S(2)}, u32[]{:S(2)}) collective-permute-start(f32[10,1,24,64]{3,2,1,0:T(8,128)} %get-tuple-element.5), channel_id=1, source_target_pairs={{2,0},{3,1},{4,2},{5,3},{6,4},{7,5},{8,6},{9,7},{10,8},{11,9},{12,... | collective-permute-start | bytes 184328 | tf_op jit(solution)/shard_map/ppermute | solution.py:164
  13.8 7.1 %copy-start.1 = (f32[9,1,24,64]{3,2,1,0:T(8,128)S(1)}, f32[9,1,24,64]{3,2,1,0:T(8,128)}, u32[]{:S(2)}) copy-start(f32[9,1,24,64]{3,2,1,0:T(8,128)} %refs_2_.1) | copy-start | bytes 165892
  13.8 8.8 %copy-start.3 = (f32[10,1,24,64]{3,2,1,0:T(8,128)S(1)}, f32[10,1,24,64]{3,2,1,0:T(8,128)}, u32[]{:S(2)}) copy-start(f32[10,1,24,64]{3,2,1,0:T(8,128)} %get-tuple-element.5) | copy-start | bytes 184324
  16.3 34.9 %collective-permute-start.4 = (f32[12,6,24,128]{3,2,1,0:T(8,128)}, f32[12,6,24,128]{3,2,1,0:T(8,128)S(1)}, u32[]{:S(2)}, u32[]{:S(2)}) collective-permute-start(f32[12,6,24,128]{3,2,1,0:T(8,128)} %get-tuple-element.44), channel_id=1, source_target_pairs={{0,1},{1,2},{2,3},{3,4},{4,5},{5,6},{6,7},{8,9},{9,10},{10,11},{11... | collective-permute-start | bytes 2654216 | tf_op jit(solution)/shard_map/ppermute | solution.py:157
  21.2 30.0 %collective-permute-start.5 = (f32[12,6,24,128]{3,2,1,0:T(8,128)S(1)}, f32[12,6,24,128]{3,2,1,0:T(8,128)S(1)}, u32[]{:S(2)}, u32[]{:S(2)}) collective-permute-start(f32[12,6,24,128]{3,2,1,0:T(8,128)S(1)} %get-tuple-element.45), channel_id=1, source_target_pairs={{1,0},{2,1},{3,2},{4,3},{5,4},{6,5},{7,6},{9,8},{10,9},{11,10},{12... | collective-permute-start | bytes 2654216 | tf_op jit(solution)/shard_map/ppermute | solution.py:158
  22.6 0.7 copy-start.2
  22.6 0.7 copy-start.4
  24.9 22.8 %all-to-all-start = ((bf16[8,2,5184]{2,1,0:T(2,128)(2,1)}), bf16[8,2,5184]{2,1,0:T(2,128)(2,1)S(1)}, u32[]{:S(2)}, u32[]{:S(2)}) async-start(bf16[8,2,5184]{2,1,0:T(2,128)(2,1)} %reshape.473), calls=%async_computation | async-start | bytes 335872 | tf_op jit(solution)/shard_map/all_to_all | solution.py:177
  48.8 2.5 %copy-start = (f32[12,9,24,128]{3,2,1,0:T(8,128)S(1)}, f32[12,9,24,128]{3,2,1,0:T(8,128)}, u32[]{:S(2)}) copy-start(f32[12,9,24,128]{3,2,1,0:T(8,128)} %shard_map.69) | copy-start | bytes 3981316
  51.4 7.6 %collective-permute-start.6 = (f32[10,21,2,128]{3,2,1,0:T(2,128)S(1)}, f32[10,21,2,128]{3,2,1,0:T(2,128)S(1)}, u32[]{:S(2)}, u32[]{:S(2)}) collective-permute-start(f32[10,21,2,128]{3,2,1,0:T(2,128)S(1)} %get-tuple-element.32), channel_id=1, source_target_pairs={{0,8},{8,16},{16,24},{1,9},{9,17},{17,25},{2,10},{10,18},{18,26},{... | collective-permute-start | bytes 645128 | tf_op jit(solution)/shard_map/ppermute | solution.py:15
  54.9 8.2 %collective-permute-start.7 = (f32[10,21,2,128]{3,2,1,0:T(2,128)S(1)}, f32[10,21,2,128]{3,2,1,0:T(2,128)S(1)}, u32[]{:S(2)}, u32[]{:S(2)}) collective-permute-start(f32[10,21,2,128]{3,2,1,0:T(2,128)S(1)} %get-tuple-element.33), channel_id=1, source_target_pairs={{8,0},{16,8},{24,16},{9,1},{17,9},{25,17},{10,2},{18,10},{26,18},{... | collective-permute-start | bytes 645128 | tf_op jit(solution)/shard_map/ppermute | solution.py:16
  67.1 6.2 %collective-permute-start.8 = (f32[9,17,2,128]{3,2,1,0:T(2,128)S(1)}, f32[9,17,2,128]{3,2,1,0:T(2,128)S(1)}, u32[]{:S(2)}, u32[]{:S(2)}) collective-permute-start(f32[9,17,2,128]{3,2,1,0:T(2,128)S(1)} %get-tuple-element.37), channel_id=1, source_target_pairs={{0,8},{8,16},{16,24},{1,9},{9,17},{17,25},{2,10},{10,18},{18,26},{... | collective-permute-start | bytes 470024 | tf_op jit(solution)/shard_map/ppermute | solution.py:15
  70.6 7.1 %collective-permute-start.9 = (f32[9,17,2,128]{3,2,1,0:T(2,128)S(1)}, f32[9,17,2,128]{3,2,1,0:T(2,128)S(1)}, u32[]{:S(2)}, u32[]{:S(2)}) collective-permute-start(f32[9,17,2,128]{3,2,1,0:T(2,128)S(1)} %get-tuple-element.38), channel_id=1, source_target_pairs={{8,0},{16,8},{24,16},{9,1},{17,9},{25,17},{10,2},{18,10},{26,18},{... | collective-permute-start | bytes 470024 | tf_op jit(solution)/shard_map/ppermute | solution.py:16
  81.0 5.9 %collective-permute-start.10 = (f32[9,13,2,128]{3,2,1,0:T(2,128)S(1)}, f32[9,13,2,128]{3,2,1,0:T(2,128)S(1)}, u32[]{:S(2)}, u32[]{:S(2)}) collective-permute-start(f32[9,13,2,128]{3,2,1,0:T(2,128)S(1)} %get-tuple-element.42), channel_id=1, source_target_pairs={{0,8},{8,16},{16,24},{1,9},{9,17},{17,25},{2,10},{10,18},{18,26},{... | collective-permute-start | bytes 359432 | tf_op jit(solution)/shard_map/ppermute | solution.py:15
  84.5 6.7 %collective-permute-start.11 = (f32[9,13,2,128]{3,2,1,0:T(2,128)S(1)}, f32[9,13,2,128]{3,2,1,0:T(2,128)S(1)}, u32[]{:S(2)}, u32[]{:S(2)}) collective-permute-start(f32[9,13,2,128]{3,2,1,0:T(2,128)S(1)} %get-tuple-element.43), channel_id=1, source_target_pairs={{8,0},{16,8},{24,16},{9,1},{17,9},{25,17},{10,2},{18,10},{26,18},{... | collective-permute-start | bytes 359432 | tf_op jit(solution)/shard_map/ppermute | solution.py:16
  85.8 5.5 %copy-start.5 = (f32[9,1,24,64]{3,2,1,0:T(8,128)}, f32[9,1,24,64]{3,2,1,0:T(8,128)S(1)}, u32[]{:S(2)}) copy-start(f32[9,1,24,64]{3,2,1,0:T(8,128)S(1)} %constant_dynamic-update-slice_fusion.9) | copy-start | bytes 165892

commit v11 on v10

--- a/solution.py
+++ b/solution.py
@@ -171,10 +171,15 @@
 
     both = jnp.concatenate([region_state, region_next], 0).astype(jnp.bfloat16)
     both = jnp.pad(both, ((0, 0), (0, 0), (rows_each, rows_each), (0, 0)))
-    send = jnp.concatenate(
-        [both[:, :, rows_each * d: rows_each * (d + 3)] for d in range(count_y)], 2
-    )
-    band = lax.all_to_all(send, "gy", 2, 1, tiled=True).astype(jnp.float32)
+    chunks = []
+    for shift in range(count_y):
+        dest = (me_y + shift) % count_y
+        piece = lax.dynamic_slice_in_dim(both, dest * rows_each, 3 * rows_each, axis=2)
+        if shift:
+            cycle = [(i, (i + shift) % count_y) for i in range(count_y)]
+            piece = lax.ppermute(piece, "gy", cycle)
+        chunks.append(piece)
+    band = jnp.concatenate(chunks, 1).astype(jnp.float32)
     columns = band.shape[1]
     high = lax.Precision.HIGH
     along_y_w = interp_matrix(fine_y, rows_each)
@@ -187,7 +192,10 @@
         ],
         0,
     )[fine_y - 4: 2 * fine_y + 4]
-    first = jnp.einsum("fa,cabz->cfbz", interp_matrix(fine_x, columns), band, precision=high)
+    source = (me_y - jnp.arange(count_y)) % count_y
+    order = (source[:, None] * own + jnp.arange(own)[None, :]).reshape(-1)
+    along_x_w = jnp.take(interp_matrix(fine_x, columns), order, axis=1)
+    first = jnp.einsum("fa,cabz->cfbz", along_x_w, band, precision=high)
     second = jnp.einsum("gb,cfbz->cgfz", tiles_w, first, precision=high)
     background = jnp.einsum(
         "kz,cgfz->cgfk", interp_matrix(fine_z, band.shape[3]), second, precision=high

time: 95.4 us -> 102 us (1.069)
  starting transfers between devices: 37.5 us -> 49.5 us
  waiting for transfers between devices: 29.9 us -> 22.8 us
  other arithmetic: 9.03 us -> 12.1 us
  local copies, waits for them, and re-layouts: 7.3 us -> 6.01 us
    ppermute x0 -> x7, starting transfers between devices: none -> 20.1 us  [local(): piece = lax.ppermute(piece, 'gy', cycle)]
    all_to_all x1 -> x0, waiting for transfers between devices: 14.5 us -> none  [local(): band = lax.all_to_all(send, 'gy', 2, 1, tiled=True).astype(jnp.float32)]
    all_to_all x1 -> x0, starting transfers between devices: 8.21 us -> none  [local(): band = lax.all_to_all(send, 'gy', 2, 1, tiled=True).astype(jnp.float32)]
    ppermute x0 -> x7, waiting for transfers between devices: none -> 5.25 us  [local(): piece = lax.ppermute(piece, 'gy', cycle)]
    ppermute x3, waiting for transfers between devices: 2.44 us -> 4.45 us  [x_halo(): from_left = lax.ppermute(field[:, :, -width:], 'gx', shifted(nx, 1))]
    add x1 -> x2, other arithmetic: 0.01 us -> 1.41 us  [interp_matrix(): return (1.0 - frac)[:, None] * low_hit + frac[:, None] * high_hit]
    unnamed x35 -> x32, local copies, waits for them, and re-layouts: 1.68 us -> 0.38 us
    select_n x3, other arithmetic: 0.05 us -> 1.18 us  [interp_matrix(): lower = jnp.where(above, n_coarse - 2, lower)]
  transfers between devices with their start and end apart: 13 -> 19, of which waited for: 6 -> 9; matrix products, arithmetic and copies ran while one was open for 12% -> 13% of each run, Pallas kernels for 3% -> 3%
where the time goes in v11:
time: 102 us
  starting transfers between devices  49.5 us (49%)
  waiting for transfers between devices  22.8 us (22%)
  other arithmetic  12.1 us (12%)
  local copies, waits for them, and re-layouts  6.01 us (6%)
  matrix products  5.4 us (5%)
  Pallas kernels  4.2 us (4%)
  between operations  1.67 us (2%)
    ppermute x7, starting transfers between devices, local(): piece = lax.ppermute(piece, 'gy', cycle)  20.1 us
    ppermute x3, waiting for transfers between devices, x_halo(): from_right = lax.ppermute(field[:, :, :width], 'gx', shifted(nx, -1))  13.1 us
    ppermute x3, starting transfers between devices, x_halo(): from_left = lax.ppermute(field[:, :, -width:], 'gx', shifted(nx, 1))  10.5 us
    ppermute x7, waiting for transfers between devices, local(): piece = lax.ppermute(piece, 'gy', cycle)  5.25 us
    ppermute x1, starting transfers between devices, local(): lows.insert(0, lax.ppermute(region_pay, flat, shifted(n_flat, d)))  4.84 us
    ppermute x1, starting transfers between devices, local(): fine_lo = lax.ppermute(fine_pay[:, -reach_y:], 'gy', shifted(count_y, 1))  4.63 us
    ppermute x3, waiting for transfers between devices, x_halo(): from_left = lax.ppermute(field[:, :, -width:], 'gx', shifted(nx, 1))  4.45 us
    pallas_call x2, Pallas kernels, lookup(): pl.pallas_call(lambda *refs: lookup_kernel(step, extra, *refs), out_shape...  4.2 us
  transfers between devices with their start and end apart: 19, of which 9 were waited for; matrix products, arithmetic and copies ran while one was open for 13% of the time, Pallas kernels for 3%

profile of v11, /device:TPU:0, one launch (start us, length us, event | category | flops | bytes accessed | tf_op | source)
XLA Modules:
  0.0 101.6 jit_solution(10011274982190087838)
XLA Ops:
  0.6 1.6 %shard_map.68 = (f32[10,1,24,64]{3,2,1,0:T(8,128)}, f32[1,24,64]{2,1,0:T(8,128)}, f32[1,24,64]{2,1,0:T(8,128)}) custom-call(s32[1,24,64]{2,1,0:T(8,128)} %refs_0_.1, f32[3,8]{1,0:T(4,128)} %refs_1_.3, f32[9,1,24,64]{3,2,1,0:T(8,128)} %refs_2_.1), custom_call_target="tpu_custom_call" | custom-call | tf_op jit(solution)/shard_map/pallas_call | solution.py:47
  2.2 4.8 %collective-permute-start.3 = (f32[10,1,24,64]{3,2,1,0:T(8,128)}, f32[10,1,24,64]{3,2,1,0:T(8,128)S(1)}, u32[]{:S(2)}, u32[]{:S(2)}) collective-permute-start(f32[10,1,24,64]{3,2,1,0:T(8,128)} %get-tuple-element.5), channel_id=1, source_target_pairs={{0,2},{1,3},{2,4},{3,5},{4,6},{5,7},{6,8},{7,9},{8,10},{9,11},{10,... | collective-permute-start | bytes 184328 | tf_op jit(solution)/shard_map/ppermute | solution.py:163
  7.1 1.5 %collective-permute-start = (f32[10,1,24,64]{3,2,1,0:T(8,128)}, f32[10,1,24,64]{3,2,1,0:T(8,128)S(1)}, u32[]{:S(2)}, u32[]{:S(2)}) collective-permute-start(f32[10,1,24,64]{3,2,1,0:T(8,128)} %get-tuple-element.5), channel_id=1, source_target_pairs={{0,1},{1,2},{2,3},{3,4},{4,5},{5,6},{6,7},{7,8},{8,9},{9,10},{10,1... | collective-permute-start | bytes 184328 | tf_op jit(solution)/shard_map/ppermute | solution.py:159
  8.5 1.3 %collective-permute-start.1 = (f32[10,1,24,64]{3,2,1,0:T(8,128)}, f32[10,1,24,64]{3,2,1,0:T(8,128)S(1)}, u32[]{:S(2)}, u32[]{:S(2)}) collective-permute-start(f32[10,1,24,64]{3,2,1,0:T(8,128)} %get-tuple-element.5), channel_id=1, source_target_pairs={{1,0},{2,1},{3,2},{4,3},{5,4},{6,5},{7,6},{8,7},{9,8},{10,9},{11,1... | collective-permute-start | bytes 184328 | tf_op jit(solution)/shard_map/ppermute | solution.py:160
  9.8 1.3 %collective-permute-start.2 = (f32[10,1,24,64]{3,2,1,0:T(8,128)}, f32[10,1,24,64]{3,2,1,0:T(8,128)S(1)}, u32[]{:S(2)}, u32[]{:S(2)}) collective-permute-start(f32[10,1,24,64]{3,2,1,0:T(8,128)} %get-tuple-element.5), channel_id=1, source_target_pairs={{2,0},{3,1},{4,2},{5,3},{6,4},{7,5},{8,6},{9,7},{10,8},{11,9},{12,... | collective-permute-start | bytes 184328 | tf_op jit(solution)/shard_map/ppermute | solution.py:164
  11.1 2.6 %shard_map.69 = f32[12,9,24,128]{3,2,1,0:T(8,128)} custom-call(s32[9,24,128]{2,1,0:T(8,128)} %bitcast.660, f32[3,8]{1,0:T(4,128)} %refs_1_.3, f32[9,9,24,128]{3,2,1,0:T(8,128)} %bitcast.659), custom_call_target="tpu_custom_call" | custom-call | tf_op jit(solution)/shard_map/pallas_call | solution.py:47
  13.8 1.6 %fusion.269 = (f32[12,6,24,128]{3,2,1,0:T(8,128)S(1)}, f32[12,6,24,128]{3,2,1,0:T(8,128)S(1)}) fusion(f32[12,9,24,128]{3,2,1,0:T(8,128)} %shard_map.69), kind=kLoop, calls=%fused_computation.513 | loop fusion | bytes 3538944 | tf_op jit(solution)/shard_map/slice | solution.py:157
  15.3 4.6 %collective-permute-start.4 = (f32[12,6,24,128]{3,2,1,0:T(8,128)S(1)}, f32[12,6,24,128]{3,2,1,0:T(8,128)S(1)}, u32[]{:S(2)}, u32[]{:S(2)}) collective-permute-start(f32[12,6,24,128]{3,2,1,0:T(8,128)S(1)} %get-tuple-element.44), channel_id=1, source_target_pairs={{0,1},{1,2},{2,3},{3,4},{4,5},{5,6},{6,7},{8,9},{9,10},{10,11},{11... | collective-permute-start | bytes 2654216 | tf_op jit(solution)/shard_map/ppermute | solution.py:157
  20.1 0.5 compare_select_fusion.12
  20.7 0.6 compare_select_fusion.13
  21.3 0.6 compare_select_fusion.7
  22.1 0.7 select_add_fusion.1
  22.8 0.6 gather_fusion
  23.3 0.7 select_add_fusion
  24.1 1.3 %collective-permute-start.5 = (f32[12,6,24,128]{3,2,1,0:T(8,128)S(1)}, f32[12,6,24,128]{3,2,1,0:T(8,128)S(1)}, u32[]{:S(2)}, u32[]{:S(2)}) collective-permute-start(f32[12,6,24,128]{3,2,1,0:T(8,128)S(1)} %get-tuple-element.45), channel_id=1, source_target_pairs={{1,0},{2,1},{3,2},{4,3},{5,4},{6,5},{7,6},{9,8},{10,9},{11,10},{12... | collective-permute-start | bytes 2654216 | tf_op jit(solution)/shard_map/ppermute | solution.py:158
  26.6 0.4 pad_dynamic-slice_fusion
  27.0 3.0 %collective-permute-start.8 = (bf16[18,1,9,64]{3,2,1,0:T(8,128)(2,1)S(1)}, bf16[18,1,9,64]{3,2,1,0:T(8,128)(2,1)S(1)}, u32[]{:S(2)}, u32[]{:S(2)}) collective-permute-start(bf16[18,1,9,64]{3,2,1,0:T(8,128)(2,1)S(1)} %get-tuple-element.110), channel_id=1, source_target_pairs={{0,1},{1,2},{2,3},{3,4},{4,5},{5,6},{6,7},{7,0},{8,9},{9,10},{10,1... | collective-permute-start | bytes 62216 | tf_op jit(solution)/shard_map/ppermute | solution.py:180
  30.0 2.9 %collective-permute-start.9 = (bf16[18,1,9,64]{3,2,1,0:T(8,128)(2,1)S(1)}, bf16[18,1,9,64]{3,2,1,0:T(8,128)(2,1)S(1)}, u32[]{:S(2)}, u32[]{:S(2)}) collective-permute-start(bf16[18,1,9,64]{3,2,1,0:T(8,128)(2,1)S(1)} %get-tuple-element.111), channel_id=1, source_target_pairs={{0,2},{1,3},{2,4},{3,5},{4,6},{5,7},{6,0},{7,1},{8,10},{9,11},{10,... | collective-permute-start | bytes 62216 | tf_op jit(solution)/shard_map/ppermute | solution.py:180
  32.9 2.6 %collective-permute-start.10 = (bf16[18,1,9,64]{3,2,1,0:T(8,128)(2,1)S(1)}, bf16[18,1,9,64]{3,2,1,0:T(8,128)(2,1)S(1)}, u32[]{:S(2)}, u32[]{:S(2)}) collective-permute-start(bf16[18,1,9,64]{3,2,1,0:T(8,128)(2,1)S(1)} %get-tuple-element.112), channel_id=1, source_target_pairs={{0,3},{1,4},{2,5},{3,6},{4,7},{5,0},{6,1},{7,2},{8,11},{9,12},{10,... | collective-permute-start | bytes 62216 | tf_op jit(solution)/shard_map/ppermute | solution.py:180
  35.5 7.0 %collective-permute-start.11 = (bf16[18,1,9,64]{3,2,1,0:T(8,128)(2,1)S(1)}, bf16[18,1,9,64]{3,2,1,0:T(8,128)(2,1)S(1)}, u32[]{:S(2)}, u32[]{:S(2)}) collective-permute-start(bf16[18,1,9,64]{3,2,1,0:T(8,128)(2,1)S(1)} %get-tuple-element.113), channel_id=1, source_target_pairs={{0,4},{1,5},{2,6},{3,7},{4,0},{5,1},{6,2},{7,3},{8,12},{9,13},{10,... | collective-permute-start | bytes 62216 | tf_op jit(solution)/shard_map/ppermute | solution.py:180
  42.6 3.1 %collective-permute-done.9 = bf16[18,1,9,64]{3,2,1,0:T(8,128)(2,1)S(1)} collective-permute-done((bf16[18,1,9,64]{3,2,1,0:T(8,128)(2,1)S(1)}, bf16[18,1,9,64]{3,2,1,0:T(8,128)(2,1)S(1)}, u32[]{:S(2)}, u32[]{:S(2)}) %collective-permute-start.9) | collective-permute-done | bytes 20768 | tf_op jit(solution)/shard_map/ppermute | solution.py:180
  45.7 3.3 %collective-permute-start.13 = (bf16[18,1,9,64]{3,2,1,0:T(8,128)(2,1)S(1)}, bf16[18,1,9,64]{3,2,1,0:T(8,128)(2,1)S(1)}, u32[]{:S(2)}, u32[]{:S(2)}) collective-permute-start(bf16[18,1,9,64]{3,2,1,0:T(8,128)(2,1)S(1)} %get-tuple-element.115), channel_id=1, source_target_pairs={{0,6},{1,7},{2,0},{3,1},{4,2},{5,3},{6,4},{7,5},{8,14},{9,15},{10,... | collective-permute-start | bytes 62216 | tf_op jit(solution)/shard_map/ppermute | solution.py:180
  49.0 1.3 %collective-permute-start.14 = (bf16[18,1,9,64]{3,2,1,0:T(8,128)(2,1)S(1)}, bf16[18,1,9,64]{3,2,1,0:T(8,128)(2,1)S(1)}, u32[]{:S(2)}, u32[]{:S(2)}) collective-permute-start(bf16[18,1,9,64]{3,2,1,0:T(8,128)(2,1)S(1)} %get-tuple-element.109), channel_id=1, source_target_pairs={{0,7},{1,0},{2,1},{3,2},{4,3},{5,4},{6,5},{7,6},{8,15},{9,8},{10,9... | collective-permute-start | bytes 62216 | tf_op jit(solution)/shard_map/ppermute | solution.py:180
  50.4 1.1 %collective-permute-done.13 = bf16[18,1,9,64]{3,2,1,0:T(8,128)(2,1)S(1)} collective-permute-done((bf16[18,1,9,64]{3,2,1,0:T(8,128)(2,1)S(1)}, bf16[18,1,9,64]{3,2,1,0:T(8,128)(2,1)S(1)}, u32[]{:S(2)}, u32[]{:S(2)}) %collective-permute-start.13) | collective-permute-done | bytes 20768 | tf_op jit(solution)/shard_map/ppermute | solution.py:180
  51.5 1.1 %collective-permute-done.14 = bf16[18,1,9,64]{3,2,1,0:T(8,128)(2,1)S(1)} collective-permute-done((bf16[18,1,9,64]{3,2,1,0:T(8,128)(2,1)S(1)}, bf16[18,1,9,64]{3,2,1,0:T(8,128)(2,1)S(1)}, u32[]{:S(2)}, u32[]{:S(2)}) %collective-permute-start.14) | collective-permute-done | bytes 20768 | tf_op jit(solution)/shard_map/ppermute | solution.py:180
  52.6 0.8 convolution_bitcast_fusion
  53.4 2.5 %fusion.3 = f32[18,24,64,17]{2,3,1,0:T(8,128)S(1)} fusion(f32[18,24,9,64]{3,1,2,0:T(8,128)S(1)} %convolution_bitcast_fusion, f32[9,3]{1,0:T(8,128)S(1)} %select_add_fusion, f32[9,3]{1,0:T(8,128)S(1)} %broadcast.1158), kind=kOutput, calls=%fused_computation.4 | convolution fusion | flops 25382240 | bytes 2875608 | tf_op jit(solution)/shard_map/gb,cfbz->cgfz/dot_general | solution.py:199
  55.9 0.2 pad_maximum_fusion.9
  56.1 3.5 %collective-permute-start.6 = (f32[10,21,2,128]{3,2,1,0:T(2,128)S(1)}, f32[10,21,2,128]{3,2,1,0:T(2,128)S(1)}, u32[]{:S(2)}, u32[]{:S(2)}) collective-permute-start(f32[10,21,2,128]{3,2,1,0:T(2,128)S(1)} %get-tuple-element.32), channel_id=1, source_target_pairs={{0,8},{8,16},{16,24},{1,9},{9,17},{17,25},{2,10},{10,18},{18,26},{... | collective-permute-start | bytes 645128 | tf_op jit(solution)/shard_map/ppermute | solution.py:15
  59.6 1.5 %collective-permute-start.7 = (f32[10,21,2,128]{3,2,1,0:T(2,128)S(1)}, f32[10,21,2,128]{3,2,1,0:T(2,128)S(1)}, u32[]{:S(2)}, u32[]{:S(2)}) collective-permute-start(f32[10,21,2,128]{3,2,1,0:T(2,128)S(1)} %get-tuple-element.33), channel_id=1, source_target_pairs={{8,0},{16,8},{24,16},{9,1},{17,9},{25,17},{10,2},{18,10},{26,18},{... | collective-permute-start | bytes 645128 | tf_op jit(solution)/shard_map/ppermute | solution.py:16
  61.1 2.1 %fusion = f32[18,17,24,128]{3,2,1,0:T(8,128)S(1)} fusion(f32[18,24,64,17]{2,3,1,0:T(8,128)S(1)} %fusion.3, f32[128]{0:T(128)S(1)} %get-tuple-element.150, s32[128]{0:T(128)S(1)} %get-tuple-element.153, f32[128]{0:T(128)S(1)} %get-tuple-element.151, s32[128]{0:T(128)S(1)} %get-tuple-element.152), kind=kOutput, calls=%fused_computation.1 | convolution fusion | flops 361013248 | bytes 5642240 | tf_op jit(solution)/shard_map/kz,cgfz->cgfk/dot_general | solution.py:200
  63.2 0.2 pad_maximum_fusion.1
  63.4 0.2 slice.1155
  63.6 1.2 %collective-permute-done.6 = f32[10,21,2,128]{3,2,1,0:T(2,128)S(1)} collective-permute-done((f32[10,21,2,128]{3,2,1,0:T(2,128)S(1)}, f32[10,21,2,128]{3,2,1,0:T(2,128)S(1)}, u32[]{:S(2)}, u32[]{:S(2)}) %collective-permute-start.6) | collective-permute-done | bytes 215072 | tf_op jit(solution)/shard_map/ppermute | solution.py:15
  64.8 4.6 %collective-permute-done.7 = f32[10,21,2,128]{3,2,1,0:T(2,128)S(1)} collective-permute-done((f32[10,21,2,128]{3,2,1,0:T(2,128)S(1)}, f32[10,21,2,128]{3,2,1,0:T(2,128)S(1)}, u32[]{:S(2)}, u32[]{:S(2)}) %collective-permute-start.7) | collective-permute-done | bytes 215072 | tf_op jit(solution)/shard_map/ppermute | solution.py:16
  69.4 0.6 pad_maximum_fusion
  70.0 0.2 slice_bitcast_fusion.3
  70.2 0.2 fusion.272
  70.3 0.2 fusion.270
  70.6 0.2 fusion.24
  70.8 0.4 fusion.35
  71.2 0.2 slice_add_fusion
  71.6 0.2 fusion.84
  71.8 0.2 slice_bitcast_fusion.4
  72.3 0.2 fusion.73
  72.7 0.1 fusion.58
  72.9 0.5 fusion.9
  73.5 3.5 %collective-permute-start.15 = (f32[9,17,2,128]{3,2,1,0:T(2,128)S(1)}, f32[9,17,2,128]{3,2,1,0:T(2,128)S(1)}, u32[]{:S(2)}, u32[]{:S(2)}) collective-permute-start(f32[9,17,2,128]{3,2,1,0:T(2,128)S(1)} %get-tuple-element.37), channel_id=1, source_target_pairs={{0,8},{8,16},{16,24},{1,9},{9,17},{17,25},{2,10},{10,18},{18,26},{... | collective-permute-start | bytes 470024 | tf_op jit(solution)/shard_map/ppermute | solution.py:15
  77.0 1.3 %collective-permute-start.16 = (f32[9,17,2,128]{3,2,1,0:T(2,128)S(1)}, f32[9,17,2,128]{3,2,1,0:T(2,128)S(1)}, u32[]{:S(2)}, u32[]{:S(2)}) collective-permute-start(f32[9,17,2,128]{3,2,1,0:T(2,128)S(1)} %get-tuple-element.38), channel_id=1, source_target_pairs={{8,0},{16,8},{24,16},{9,1},{17,9},{25,17},{10,2},{18,10},{26,18},{... | collective-permute-start | bytes 470024 | tf_op jit(solution)/shard_map/ppermute | solution.py:16
  78.3 2.2 %collective-permute-done.15 = f32[9,17,2,128]{3,2,1,0:T(2,128)S(1)} collective-permute-done((f32[9,17,2,128]{3,2,1,0:T(2,128)S(1)}, f32[9,17,2,128]{3,2,1,0:T(2,128)S(1)}, u32[]{:S(2)}, u32[]{:S(2)}) %collective-permute-start.15) | collective-permute-done | bytes 156704 | tf_op jit(solution)/shard_map/ppermute | solution.py:15
  80.5 4.1 %collective-permute-done.16 = f32[9,17,2,128]{3,2,1,0:T(2,128)S(1)} collective-permute-done((f32[9,17,2,128]{3,2,1,0:T(2,128)S(1)}, f32[9,17,2,128]{3,2,1,0:T(2,128)S(1)}, u32[]{:S(2)}, u32[]{:S(2)}) %collective-permute-start.16) | collective-permute-done | bytes 156704 | tf_op jit(solution)/shard_map/ppermute | solution.py:16
  85.2 0.4 pad_maximum_fusion.2
  85.7 0.2 fusion.51
  85.8 0.2 fusion.46
  86.0 0.2 fusion.40
  86.1 0.2 slice_add_fusion.1
  86.5 0.1 fusion.140
  87.4 0.4 fusion.14
  87.9 3.5 %collective-permute-start.17 = (f32[9,13,2,128]{3,2,1,0:T(2,128)S(1)}, f32[9,13,2,128]{3,2,1,0:T(2,128)S(1)}, u32[]{:S(2)}, u32[]{:S(2)}) collective-permute-start(f32[9,13,2,128]{3,2,1,0:T(2,128)S(1)} %get-tuple-element.42), channel_id=1, source_target_pairs={{0,8},{8,16},{16,24},{1,9},{9,17},{17,25},{2,10},{10,18},{18,26},{... | collective-permute-start | bytes 359432 | tf_op jit(solution)/shard_map/ppermute | solution.py:15
  91.4 1.3 %collective-permute-start.18 = (f32[9,13,2,128]{3,2,1,0:T(2,128)S(1)}, f32[9,13,2,128]{3,2,1,0:T(2,128)S(1)}, u32[]{:S(2)}, u32[]{:S(2)}) collective-permute-start(f32[9,13,2,128]{3,2,1,0:T(2,128)S(1)} %get-tuple-element.43), channel_id=1, source_target_pairs={{8,0},{16,8},{24,16},{9,1},{17,9},{25,17},{10,2},{18,10},{26,18},{... | collective-permute-start | bytes 359432 | tf_op jit(solution)/shard_map/ppermute | solution.py:16
  92.8 1.0 %collective-permute-done.17 = f32[9,13,2,128]{3,2,1,0:T(2,128)S(1)} collective-permute-done((f32[9,13,2,128]{3,2,1,0:T(2,128)S(1)}, f32[9,13,2,128]{3,2,1,0:T(2,128)S(1)}, u32[]{:S(2)}, u32[]{:S(2)}) %collective-permute-start.17) | collective-permute-done | bytes 119840 | tf_op jit(solution)/shard_map/ppermute | solution.py:15
  93.8 4.3 %collective-permute-done.18 = f32[9,13,2,128]{3,2,1,0:T(2,128)S(1)} collective-permute-done((f32[9,13,2,128]{3,2,1,0:T(2,128)S(1)}, f32[9,13,2,128]{3,2,1,0:T(2,128)S(1)}, u32[]{:S(2)}, u32[]{:S(2)}) %collective-permute-start.18) | collective-permute-done | bytes 119840 | tf_op jit(solution)/shard_map/ppermute | solution.py:16
  98.6 0.4 pad_maximum_fusion.3
  100.4 1.2 %fusion.18 = f32[9,24,9,128]{3,1,2,0:T(8,128)} fusion(f32[9,9,24,128]{3,2,1,0:T(8,128)S(1)} %fusion.153, f32[18,17,24,128]{3,2,1,0:T(8,128)S(1)} %fusion, f32[9,24]{1,0:T(8,128)S(1)} %slice.1276), kind=kLoop, calls=%fused_computation.27 | loop fusion | flops 1244160 | bytes 3982176 | tf_op jit(solution)/shard_map/transpose | solution.py:236
  (120 shorter events, 5.6 us)
Async XLA Ops:
  2.2 21.8 %collective-permute-start.3 = (f32[10,1,24,64]{3,2,1,0:T(8,128)}, f32[10,1,24,64]{3,2,1,0:T(8,128)S(1)}, u32[]{:S(2)}, u32[]{:S(2)}) collective-permute-start(f32[10,1,24,64]{3,2,1,0:T(8,128)} %get-tuple-element.5), channel_id=1, source_target_pairs={{0,2},{1,3},{2,4},{3,5},{4,6},{5,7},{6,8},{7,9},{8,10},{9,11},{10,... | collective-permute-start | bytes 184328 | tf_op jit(solution)/shard_map/ppermute | solution.py:163
  7.1 18.3 %collective-permute-start = (f32[10,1,24,64]{3,2,1,0:T(8,128)}, f32[10,1,24,64]{3,2,1,0:T(8,128)S(1)}, u32[]{:S(2)}, u32[]{:S(2)}) collective-permute-start(f32[10,1,24,64]{3,2,1,0:T(8,128)} %get-tuple-element.5), channel_id=1, source_target_pairs={{0,1},{1,2},{2,3},{3,4},{4,5},{5,6},{6,7},{7,8},{8,9},{9,10},{10,1... | collective-permute-start | bytes 184328 | tf_op jit(solution)/shard_map/ppermute | solution.py:159
  8.5 17.0 %collective-permute-start.1 = (f32[10,1,24,64]{3,2,1,0:T(8,128)}, f32[10,1,24,64]{3,2,1,0:T(8,128)S(1)}, u32[]{:S(2)}, u32[]{:S(2)}) collective-permute-start(f32[10,1,24,64]{3,2,1,0:T(8,128)} %get-tuple-element.5), channel_id=1, source_target_pairs={{1,0},{2,1},{3,2},{4,3},{5,4},{6,5},{7,6},{8,7},{9,8},{10,9},{11,1... | collective-permute-start | bytes 184328 | tf_op jit(solution)/shard_map/ppermute | solution.py:160
  9.8 15.9 %collective-permute-start.2 = (f32[10,1,24,64]{3,2,1,0:T(8,128)}, f32[10,1,24,64]{3,2,1,0:T(8,128)S(1)}, u32[]{:S(2)}, u32[]{:S(2)}) collective-permute-start(f32[10,1,24,64]{3,2,1,0:T(8,128)} %get-tuple-element.5), channel_id=1, source_target_pairs={{2,0},{3,1},{4,2},{5,3},{6,4},{7,5},{8,6},{9,7},{10,8},{11,9},{12,... | collective-permute-start | bytes 184328 | tf_op jit(solution)/shard_map/ppermute | solution.py:164
  13.7 6.2 %copy-start.1 = (f32[9,1,24,64]{3,2,1,0:T(8,128)S(1)}, f32[9,1,24,64]{3,2,1,0:T(8,128)}, u32[]{:S(2)}) copy-start(f32[9,1,24,64]{3,2,1,0:T(8,128)} %refs_2_.1) | copy-start | bytes 165892
  13.7 11.7 %copy-start.3 = (f32[10,1,24,64]{3,2,1,0:T(8,128)S(1)}, f32[10,1,24,64]{3,2,1,0:T(8,128)}, u32[]{:S(2)}) copy-start(f32[10,1,24,64]{3,2,1,0:T(8,128)} %get-tuple-element.5) | copy-start | bytes 184324
  15.3 40.6 %collective-permute-start.4 = (f32[12,6,24,128]{3,2,1,0:T(8,128)S(1)}, f32[12,6,24,128]{3,2,1,0:T(8,128)S(1)}, u32[]{:S(2)}, u32[]{:S(2)}) collective-permute-start(f32[12,6,24,128]{3,2,1,0:T(8,128)S(1)} %get-tuple-element.44), channel_id=1, source_target_pairs={{0,1},{1,2},{2,3},{3,4},{4,5},{5,6},{6,7},{8,9},{9,10},{10,11},{11... | collective-permute-start | bytes 2654216 | tf_op jit(solution)/shard_map/ppermute | solution.py:157
  24.1 31.8 %collective-permute-start.5 = (f32[12,6,24,128]{3,2,1,0:T(8,128)S(1)}, f32[12,6,24,128]{3,2,1,0:T(8,128)S(1)}, u32[]{:S(2)}, u32[]{:S(2)}) collective-permute-start(f32[12,6,24,128]{3,2,1,0:T(8,128)S(1)} %get-tuple-element.45), channel_id=1, source_target_pairs={{1,0},{2,1},{3,2},{4,3},{5,4},{6,5},{7,6},{9,8},{10,9},{11,10},{12... | collective-permute-start | bytes 2654216 | tf_op jit(solution)/shard_map/ppermute | solution.py:158
  25.5 0.7 copy-start.2
  25.5 0.7 copy-start.4
  27.0 8.5 %collective-permute-start.8 = (bf16[18,1,9,64]{3,2,1,0:T(8,128)(2,1)S(1)}, bf16[18,1,9,64]{3,2,1,0:T(8,128)(2,1)S(1)}, u32[]{:S(2)}, u32[]{:S(2)}) collective-permute-start(bf16[18,1,9,64]{3,2,1,0:T(8,128)(2,1)S(1)} %get-tuple-element.110), channel_id=1, source_target_pairs={{0,1},{1,2},{2,3},{3,4},{4,5},{5,6},{6,7},{7,0},{8,9},{9,10},{10,1... | collective-permute-start | bytes 62216 | tf_op jit(solution)/shard_map/ppermute | solution.py:180
  30.0 15.6 %collective-permute-start.9 = (bf16[18,1,9,64]{3,2,1,0:T(8,128)(2,1)S(1)}, bf16[18,1,9,64]{3,2,1,0:T(8,128)(2,1)S(1)}, u32[]{:S(2)}, u32[]{:S(2)}) collective-permute-start(bf16[18,1,9,64]{3,2,1,0:T(8,128)(2,1)S(1)} %get-tuple-element.111), channel_id=1, source_target_pairs={{0,2},{1,3},{2,4},{3,5},{4,6},{5,7},{6,0},{7,1},{8,10},{9,11},{10,... | collective-permute-start | bytes 62216 | tf_op jit(solution)/shard_map/ppermute | solution.py:180
  32.9 12.7 %collective-permute-start.10 = (bf16[18,1,9,64]{3,2,1,0:T(8,128)(2,1)S(1)}, bf16[18,1,9,64]{3,2,1,0:T(8,128)(2,1)S(1)}, u32[]{:S(2)}, u32[]{:S(2)}) collective-permute-start(bf16[18,1,9,64]{3,2,1,0:T(8,128)(2,1)S(1)} %get-tuple-element.112), channel_id=1, source_target_pairs={{0,3},{1,4},{2,5},{3,6},{4,7},{5,0},{6,1},{7,2},{8,11},{9,12},{10,... | collective-permute-start | bytes 62216 | tf_op jit(solution)/shard_map/ppermute | solution.py:180
  35.5 13.5 %collective-permute-start.11 = (bf16[18,1,9,64]{3,2,1,0:T(8,128)(2,1)S(1)}, bf16[18,1,9,64]{3,2,1,0:T(8,128)(2,1)S(1)}, u32[]{:S(2)}, u32[]{:S(2)}) collective-permute-start(bf16[18,1,9,64]{3,2,1,0:T(8,128)(2,1)S(1)} %get-tuple-element.113), channel_id=1, source_target_pairs={{0,4},{1,5},{2,6},{3,7},{4,0},{5,1},{6,2},{7,3},{8,12},{9,13},{10,... | collective-permute-start | bytes 62216 | tf_op jit(solution)/shard_map/ppermute | solution.py:180
  45.6 4.7 %collective-permute-start.12 = (bf16[18,1,9,64]{3,2,1,0:T(8,128)(2,1)S(1)}, bf16[18,1,9,64]{3,2,1,0:T(8,128)(2,1)S(1)}, u32[]{:S(2)}, u32[]{:S(2)}) collective-permute-start(bf16[18,1,9,64]{3,2,1,0:T(8,128)(2,1)S(1)} %get-tuple-element.114), channel_id=1, source_target_pairs={{0,5},{1,6},{2,7},{3,0},{4,1},{5,2},{6,3},{7,4},{8,13},{9,14},{10,... | collective-permute-start | bytes 62216 | tf_op jit(solution)/shard_map/ppermute | solution.py:180
  45.7 5.8 %collective-permute-start.13 = (bf16[18,1,9,64]{3,2,1,0:T(8,128)(2,1)S(1)}, bf16[18,1,9,64]{3,2,1,0:T(8,128)(2,1)S(1)}, u32[]{:S(2)}, u32[]{:S(2)}) collective-permute-start(bf16[18,1,9,64]{3,2,1,0:T(8,128)(2,1)S(1)} %get-tuple-element.115), channel_id=1, source_target_pairs={{0,6},{1,7},{2,0},{3,1},{4,2},{5,3},{6,4},{7,5},{8,14},{9,15},{10,... | collective-permute-start | bytes 62216 | tf_op jit(solution)/shard_map/ppermute | solution.py:180
  49.0 3.6 %collective-permute-start.14 = (bf16[18,1,9,64]{3,2,1,0:T(8,128)(2,1)S(1)}, bf16[18,1,9,64]{3,2,1,0:T(8,128)(2,1)S(1)}, u32[]{:S(2)}, u32[]{:S(2)}) collective-permute-start(bf16[18,1,9,64]{3,2,1,0:T(8,128)(2,1)S(1)} %get-tuple-element.109), channel_id=1, source_target_pairs={{0,7},{1,0},{2,1},{3,2},{4,3},{5,4},{6,5},{7,6},{8,15},{9,8},{10,9... | collective-permute-start | bytes 62216 | tf_op jit(solution)/shard_map/ppermute | solution.py:180
  53.4 2.5 %copy-start = (f32[12,9,24,128]{3,2,1,0:T(8,128)S(1)}, f32[12,9,24,128]{3,2,1,0:T(8,128)}, u32[]{:S(2)}) copy-start(f32[12,9,24,128]{3,2,1,0:T(8,128)} %shard_map.69) | copy-start | bytes 3981316
  56.1 8.7 %collective-permute-start.6 = (f32[10,21,2,128]{3,2,1,0:T(2,128)S(1)}, f32[10,21,2,128]{3,2,1,0:T(2,128)S(1)}, u32[]{:S(2)}, u32[]{:S(2)}) collective-permute-start(f32[10,21,2,128]{3,2,1,0:T(2,128)S(1)} %get-tuple-element.32), channel_id=1, source_target_pairs={{0,8},{8,16},{16,24},{1,9},{9,17},{17,25},{2,10},{10,18},{18,26},{... | collective-permute-start | bytes 645128 | tf_op jit(solution)/shard_map/ppermute | solution.py:15
  59.6 9.8 %collective-permute-start.7 = (f32[10,21,2,128]{3,2,1,0:T(2,128)S(1)}, f32[10,21,2,128]{3,2,1,0:T(2,128)S(1)}, u32[]{:S(2)}, u32[]{:S(2)}) collective-permute-start(f32[10,21,2,128]{3,2,1,0:T(2,128)S(1)} %get-tuple-element.33), channel_id=1, source_target_pairs={{8,0},{16,8},{24,16},{9,1},{17,9},{25,17},{10,2},{18,10},{26,18},{... | collective-permute-start | bytes 645128 | tf_op jit(solution)/shard_map/ppermute | solution.py:16
  73.5 7.0 %collective-permute-start.15 = (f32[9,17,2,128]{3,2,1,0:T(2,128)S(1)}, f32[9,17,2,128]{3,2,1,0:T(2,128)S(1)}, u32[]{:S(2)}, u32[]{:S(2)}) collective-permute-start(f32[9,17,2,128]{3,2,1,0:T(2,128)S(1)} %get-tuple-element.37), channel_id=1, source_target_pairs={{0,8},{8,16},{16,24},{1,9},{9,17},{17,25},{2,10},{10,18},{18,26},{... | collective-permute-start | bytes 470024 | tf_op jit(solution)/shard_map/ppermute | solution.py:15
  77.0 7.7 %collective-permute-start.16 = (f32[9,17,2,128]{3,2,1,0:T(2,128)S(1)}, f32[9,17,2,128]{3,2,1,0:T(2,128)S(1)}, u32[]{:S(2)}, u32[]{:S(2)}) collective-permute-start(f32[9,17,2,128]{3,2,1,0:T(2,128)S(1)} %get-tuple-element.38), channel_id=1, source_target_pairs={{8,0},{16,8},{24,16},{9,1},{17,9},{25,17},{10,2},{18,10},{26,18},{... | collective-permute-start | bytes 470024 | tf_op jit(solution)/shard_map/ppermute | solution.py:16
  87.9 5.9 %collective-permute-start.17 = (f32[9,13,2,128]{3,2,1,0:T(2,128)S(1)}, f32[9,13,2,128]{3,2,1,0:T(2,128)S(1)}, u32[]{:S(2)}, u32[]{:S(2)}) collective-permute-start(f32[9,13,2,128]{3,2,1,0:T(2,128)S(1)} %get-tuple-element.42), channel_id=1, source_target_pairs={{0,8},{8,16},{16,24},{1,9},{9,17},{17,25},{2,10},{10,18},{18,26},{... | collective-permute-start | bytes 359432 | tf_op jit(solution)/shard_map/ppermute | solution.py:15
  91.4 6.7 %collective-permute-start.18 = (f32[9,13,2,128]{3,2,1,0:T(2,128)S(1)}, f32[9,13,2,128]{3,2,1,0:T(2,128)S(1)}, u32[]{:S(2)}, u32[]{:S(2)}) collective-permute-start(f32[9,13,2,128]{3,2,1,0:T(2,128)S(1)} %get-tuple-element.43), channel_id=1, source_target_pairs={{8,0},{16,8},{24,16},{9,1},{17,9},{25,17},{10,2},{18,10},{26,18},{... | collective-permute-start | bytes 359432 | tf_op jit(solution)/shard_map/ppermute | solution.py:16
  92.7 5.5 %copy-start.5 = (f32[9,1,24,64]{3,2,1,0:T(8,128)}, f32[9,1,24,64]{3,2,1,0:T(8,128)S(1)}, u32[]{:S(2)}) copy-start(f32[9,1,24,64]{3,2,1,0:T(8,128)S(1)} %constant_dynamic-update-slice_fusion.9) | copy-start | bytes 165892

commit v12 on v10

--- a/solution.py
+++ b/solution.py
@@ -1,3 +1,4 @@
+import numpy as np
 import jax
 import jax.numpy as jnp
 from jax import lax
@@ -124,6 +125,23 @@
     return (1.0 - frac)[:, None] * low_hit + frac[:, None] * high_hit
 
 
+def interp_np(n_fine, n_coarse):
+    fine_pos = np.arange(n_fine)
+    whole = fine_pos // 3
+    rest = fine_pos - 3 * whole
+    lower = np.where(rest == 0, whole - 1, whole)
+    frac = np.where(rest == 0, 2.0 / 3.0, np.where(rest == 1, 0.0, 1.0 / 3.0))
+    frac = np.where(lower < 0, 0.0, frac)
+    lower = np.where(lower < 0, 0, lower)
+    above = lower >= n_coarse - 1
+    lower = np.where(above, n_coarse - 2, lower)
+    frac = np.where(above, 1.0, frac)
+    out = np.zeros((n_fine, n_coarse))
+    out[fine_pos, lower] += 1.0 - frac
+    out[fine_pos, lower + 1] += frac
+    return out
+
+
 def ramp(first, count, total, tile):
     place = first + jnp.arange(count, dtype=jnp.int32)
     margin = jnp.minimum(place, total - 1 - place).astype(jnp.float32) + 0.5
@@ -170,9 +188,13 @@
     )
 
     both = jnp.concatenate([region_state, region_next], 0).astype(jnp.bfloat16)
+    tile_np = interp_np(fine_y, rows_each)
+    blocks_np = np.kron(np.eye(3), tile_np)[fine_y - 4: 2 * fine_y + 4]
+    used = np.nonzero(np.any(blocks_np != 0.0, axis=0))[0]
+    lo, hi = int(used[0]), int(used[-1]) + 1
     both = jnp.pad(both, ((0, 0), (0, 0), (rows_each, rows_each), (0, 0)))
     send = jnp.concatenate(
-        [both[:, :, rows_each * d: rows_each * (d + 3)] for d in range(count_y)], 2
+        [both[:, :, rows_each * d + lo: rows_each * d + hi] for d in range(count_y)], 2
     )
     band = lax.all_to_all(send, "gy", 2, 1, tiled=True).astype(jnp.float32)
     columns = band.shape[1]
@@ -186,7 +208,7 @@
             jnp.concatenate([zeros_w, zeros_w, along_y_w], 1),
         ],
         0,
-    )[fine_y - 4: 2 * fine_y + 4]
+    )[fine_y - 4: 2 * fine_y + 4, lo:hi]
     first = jnp.einsum("fa,cabz->cfbz", interp_matrix(fine_x, columns), band, precision=high)
     second = jnp.einsum("gb,cfbz->cgfz", tiles_w, first, precision=high)
     background = jnp.einsum(

time: 95.4 us -> 93.4 us (0.979)
  waiting for transfers between devices: 29.9 us -> 23.9 us
  local copies, waits for them, and re-layouts: 7.3 us -> 10.1 us
    all_to_all x1, waiting for transfers between devices: 14.5 us -> 8.53 us  [local(): band = lax.all_to_all(send, 'gy', 2, 1, tiled=True).astype(jnp.float32)]
    ppermute x1, starting transfers between devices: 1.47 us -> 3.68 us  [local(): reg_lo = lax.ppermute(region_pay, flat, shifted(n_flat, 1))]
    all_to_all x1, starting transfers between devices: 8.21 us -> 6.55 us  [local(): band = lax.all_to_all(send, 'gy', 2, 1, tiled=True).astype(jnp.float32)]
    unnamed x35 -> x32, local copies, waits for them, and re-layouts: 1.68 us -> 3.24 us
    concatenate x2, local copies, waits for them, and re-layouts: 0.05 us -> 1.18 us  [local(): jnp.concatenate([both[:, :, rows_each * d + lo:rows_each * d + hi] for d...]
    select_n x3, other arithmetic: 0.05 us -> 1.14 us  [interp_matrix(): frac = jnp.where(above, 1.0, frac)]
  transfers between devices with their start and end apart: 13 -> 13, of which waited for: 6 -> 7; matrix products, arithmetic and copies ran while one was open for 12% -> 16% of each run, Pallas kernels for 3% -> 3%
where the time goes in v12:
time: 93.4 us; the launch traced here: 92.8 us
  starting transfers between devices  37.9 us (41%)
  waiting for transfers between devices  23.9 us (26%)
  local copies, waits for them, and re-layouts  10.1 us (11%)
  other arithmetic  9.94 us (11%)
  matrix products  5.16 us (6%)
  Pallas kernels  4.21 us (5%)
  between operations  1.51 us (2%)
    ppermute x3, waiting for transfers between devices, x_halo(): from_right = lax.ppermute(field[:, :, :width], 'gx', shifted(nx, -1))  12.9 us
    ppermute x3, starting transfers between devices, x_halo(): from_left = lax.ppermute(field[:, :, -width:], 'gx', shifted(nx, 1))  10.5 us
    all_to_all x1, waiting for transfers between devices, local(): band = lax.all_to_all(send, 'gy', 2, 1, tiled=True).astype(jnp.float32)  8.53 us
    all_to_all x1, starting transfers between devices, local(): band = lax.all_to_all(send, 'gy', 2, 1, tiled=True).astype(jnp.float32)  6.55 us
    ppermute x1, starting transfers between devices, local(): lows.insert(0, lax.ppermute(region_pay, flat, shifted(n_flat, d)))  5.48 us
    pallas_call x2, Pallas kernels, lookup(): pl.pallas_call(lambda *refs: lookup_kernel(step, extra, *refs), out_shape...  4.21 us
    ppermute x3, starting transfers between devices, x_halo(): from_right = lax.ppermute(field[:, :, :width], 'gx', shifted(nx, -1))  4.06 us
    ppermute x1, starting transfers between devices, local(): fine_lo = lax.ppermute(fine_pay[:, -reach_y:], 'gy', shifted(count_y, 1))  3.84 us
  transfers between devices with their start and end apart: 13, of which 7 were waited for; matrix products, arithmetic and copies ran while one was open for 16% of the time, Pallas kernels for 3%

profile of v12, /device:TPU:0, one launch (start us, length us, event | category | flops | bytes accessed | tf_op | source)
XLA Modules:
  0.0 92.8 jit_solution(5607851998572959970)
XLA Ops:
  0.6 1.6 %shard_map.68 = (f32[10,1,24,64]{3,2,1,0:T(8,128)}, f32[1,24,64]{2,1,0:T(8,128)}, f32[1,24,64]{2,1,0:T(8,128)}) custom-call(s32[1,24,64]{2,1,0:T(8,128)} %refs_0_.1, f32[3,8]{1,0:T(4,128)} %refs_1_.3, f32[9,1,24,64]{3,2,1,0:T(8,128)} %refs_2_.1), custom_call_target="tpu_custom_call" | custom-call | tf_op jit(solution)/shard_map/pallas_call | solution.py:48
  2.2 1.3 %collective-permute-start.2 = (f32[10,1,24,64]{3,2,1,0:T(8,128)}, f32[10,1,24,64]{3,2,1,0:T(8,128)S(1)}, u32[]{:S(2)}, u32[]{:S(2)}) collective-permute-start(f32[10,1,24,64]{3,2,1,0:T(8,128)} %get-tuple-element.5), channel_id=1, source_target_pairs={{2,0},{3,1},{4,2},{5,3},{6,4},{7,5},{8,6},{9,7},{10,8},{11,9},{12,... | collective-permute-start | bytes 184328 | tf_op jit(solution)/shard_map/ppermute | solution.py:182
  3.5 5.5 %collective-permute-start.3 = (f32[10,1,24,64]{3,2,1,0:T(8,128)}, f32[10,1,24,64]{3,2,1,0:T(8,128)S(1)}, u32[]{:S(2)}, u32[]{:S(2)}) collective-permute-start(f32[10,1,24,64]{3,2,1,0:T(8,128)} %get-tuple-element.5), channel_id=1, source_target_pairs={{0,2},{1,3},{2,4},{3,5},{4,6},{5,7},{6,8},{7,9},{8,10},{9,11},{10,... | collective-permute-start | bytes 184328 | tf_op jit(solution)/shard_map/ppermute | solution.py:181
  9.0 1.3 %collective-permute-start.1 = (f32[10,1,24,64]{3,2,1,0:T(8,128)}, f32[10,1,24,64]{3,2,1,0:T(8,128)S(1)}, u32[]{:S(2)}, u32[]{:S(2)}) collective-permute-start(f32[10,1,24,64]{3,2,1,0:T(8,128)} %get-tuple-element.5), channel_id=1, source_target_pairs={{1,0},{2,1},{3,2},{4,3},{5,4},{6,5},{7,6},{8,7},{9,8},{10,9},{11,1... | collective-permute-start | bytes 184328 | tf_op jit(solution)/shard_map/ppermute | solution.py:178
  10.3 3.7 %collective-permute-start = (f32[10,1,24,64]{3,2,1,0:T(8,128)}, f32[10,1,24,64]{3,2,1,0:T(8,128)}, u32[]{:S(2)}, u32[]{:S(2)}) collective-permute-start(f32[10,1,24,64]{3,2,1,0:T(8,128)} %get-tuple-element.5), channel_id=1, source_target_pairs={{0,1},{1,2},{2,3},{3,4},{4,5},{5,6},{6,7},{7,8},{8,9},{9,10},{10,1... | collective-permute-start | bytes 184328 | tf_op jit(solution)/shard_map/ppermute | solution.py:177
  14.0 2.6 %shard_map.69 = f32[12,9,24,128]{3,2,1,0:T(8,128)} custom-call(s32[9,24,128]{2,1,0:T(8,128)} %bitcast.664, f32[3,8]{1,0:T(4,128)} %refs_1_.3, f32[9,9,24,128]{3,2,1,0:T(8,128)} %bitcast.663), custom_call_target="tpu_custom_call" | custom-call | tf_op jit(solution)/shard_map/pallas_call | solution.py:48
  16.6 2.5 %fusion.269 = (f32[12,6,24,128]{3,2,1,0:T(8,128)}, f32[12,6,24,128]{3,2,1,0:T(8,128)S(1)}) fusion(f32[12,9,24,128]{3,2,1,0:T(8,128)} %shard_map.69), kind=kLoop, calls=%fused_computation.488 | loop fusion | bytes 3538944 | tf_op jit(solution)/shard_map/slice | solution.py:175
  19.1 3.8 %collective-permute-start.4 = (f32[12,6,24,128]{3,2,1,0:T(8,128)}, f32[12,6,24,128]{3,2,1,0:T(8,128)S(1)}, u32[]{:S(2)}, u32[]{:S(2)}) collective-permute-start(f32[12,6,24,128]{3,2,1,0:T(8,128)} %get-tuple-element.44), channel_id=1, source_target_pairs={{0,1},{1,2},{2,3},{3,4},{4,5},{5,6},{6,7},{8,9},{9,10},{10,11},{11... | collective-permute-start | bytes 2654216 | tf_op jit(solution)/shard_map/ppermute | solution.py:175
  23.0 0.6 compare_select_fusion.8
  23.8 0.5 compare_select_fusion
  24.3 1.3 %collective-permute-start.5 = (f32[12,6,24,128]{3,2,1,0:T(8,128)S(1)}, f32[12,6,24,128]{3,2,1,0:T(8,128)S(1)}, u32[]{:S(2)}, u32[]{:S(2)}) collective-permute-start(f32[12,6,24,128]{3,2,1,0:T(8,128)S(1)} %get-tuple-element.45), channel_id=1, source_target_pairs={{1,0},{2,1},{3,2},{4,3},{5,4},{6,5},{7,6},{9,8},{10,9},{11,10},{12... | collective-permute-start | bytes 2654216 | tf_op jit(solution)/shard_map/ppermute | solution.py:176
  25.6 0.9 constant_dynamic-update-slice_fusion.7
  26.6 0.9 %constant_dynamic-update-slice_fusion.5 = (f32[10,3,24,64]{3,2,1,0:T(8,128)S(1)}, f32[10,3,24,64]{3,2,1,0:T(8,128)S(1)}, f32[10,3,24,64]{3,2,1,0:T(8,128)S(1)}) fusion(f32[10,1,24,64]{3,2,1,0:T(8,128)} %get-tuple-element.5, f32[10,3,24,64]{3,2,1,0:T(8,128)S(1)} %get-tuple-element.101, f32[10,3,24,64]{3,2,1,0:T(8,128)S(1)} %get-tuple-element.102), kind=kLoop, calls=%fused_computation.307 | loop fusion | bytes 430080
  28.7 1.1 %concatenate.325 = bf16[18,1,56,64]{3,2,1,0:T(8,128)(2,1)S(1)} concatenate(bf16[18,1,7,64]{3,2,1,0:T(8,128)(2,1)S(1)} %get-tuple-element.116, bf16[18,1,7,64]{3,2,1,0:T(8,128)(2,1)S(1)} %get-tuple-element.115, bf16[18,1,7,64]{3,2,1,0:T(8,128)(2,1)S(1)} %get-tuple-element.114, bf16[18,1,7,64]{3,2,1,0:T(8,128)(2,1)S(1)} %get-tuple-element.113, ...), dimensions={2} | concatenate | bytes 258048 | tf_op jit(solution)/shard_map/concatenate | solution.py:196
  29.9 0.9 reshape.473
  30.8 6.6 %all-to-all-start = ((bf16[8,2,4032]{2,1,0:T(2,128)(2,1)}), bf16[8,2,4032]{2,1,0:T(2,128)(2,1)S(1)}, u32[]{:S(2)}, u32[]{:S(2)}) async-start(bf16[8,2,4032]{2,1,0:T(2,128)(2,1)} %reshape.473), calls=%async_computation | async-start | bytes 262144 | tf_op jit(solution)/shard_map/all_to_all | solution.py:199
  37.4 8.5 %all-to-all-done = bf16[8,2,4032]{2,1,0:T(2,128)(2,1)S(1)} async-done(((bf16[8,2,4032]{2,1,0:T(2,128)(2,1)}), bf16[8,2,4032]{2,1,0:T(2,128)(2,1)S(1)}, u32[]{:S(2)}, u32[]{:S(2)}) %all-to-all-start) | async-done | bytes 129056 | tf_op jit(solution)/shard_map/all_to_all | solution.py:199
  45.9 0.2 reshape.474
  46.2 0.6 convolution_bitcast_fusion.1
  46.8 2.4 %convolution_bitcast_fusion = f32[18,17,24,64]{3,1,2,0:T(8,128)S(1)} fusion(f32[18,24,7,64]{3,1,2,0:T(8,128)S(1)} %convolution_bitcast_fusion.1, f32[9,3]{0,1:T(4,128)S(1)} %select_add_fusion, f32[9,3]{0,1:T(4,128)S(1)} %broadcast.1055), kind=kOutput, calls=%fused_computation.5 | convolution fusion | flops 19741744 | bytes 2654424 | tf_op jit(solution)/shard_map/gb,cfbz->cgfz/dot_general | solution.py:213
  49.3 0.2 pad_maximum_fusion.9
  49.4 3.5 %collective-permute-start.6 = (f32[10,21,2,128]{3,2,1,0:T(2,128)S(1)}, f32[10,21,2,128]{3,2,1,0:T(2,128)S(1)}, u32[]{:S(2)}, u32[]{:S(2)}) collective-permute-start(f32[10,21,2,128]{3,2,1,0:T(2,128)S(1)} %get-tuple-element.32), channel_id=1, source_target_pairs={{0,8},{8,16},{16,24},{1,9},{9,17},{17,25},{2,10},{10,18},{18,26},{... | collective-permute-start | bytes 645128 | tf_op jit(solution)/shard_map/ppermute | solution.py:16
  52.9 1.5 %collective-permute-start.7 = (f32[10,21,2,128]{3,2,1,0:T(2,128)S(1)}, f32[10,21,2,128]{3,2,1,0:T(2,128)S(1)}, u32[]{:S(2)}, u32[]{:S(2)}) collective-permute-start(f32[10,21,2,128]{3,2,1,0:T(2,128)S(1)} %get-tuple-element.33), channel_id=1, source_target_pairs={{8,0},{16,8},{24,16},{9,1},{17,9},{25,17},{10,2},{18,10},{26,18},{... | collective-permute-start | bytes 645128 | tf_op jit(solution)/shard_map/ppermute | solution.py:17
  54.4 2.2 %fusion = f32[18,17,24,128]{3,2,1,0:T(8,128)S(1)} fusion(f32[18,17,24,64]{3,1,2,0:T(8,128)S(1)} %convolution_bitcast_fusion, f32[128]{0:T(128)S(1)} %copy-done.6, s32[128]{0:T(128)S(1)} %get-tuple-element.161, f32[128]{0:T(128)S(1)} %copy-done.7, s32[128]{0:T(128)S(1)} %get-tuple-element.160), kind=kOutput, calls=%fused_computation | convolution fusion | flops 361013248 | bytes 5642240 | tf_op jit(solution)/shard_map/kz,cgfz->cgfk/dot_general | solution.py:214
  56.6 0.2 pad_maximum_fusion.1
  56.8 0.2 slice.1191
  57.1 4.1 %collective-permute-done.7 = f32[10,21,2,128]{3,2,1,0:T(2,128)S(1)} collective-permute-done((f32[10,21,2,128]{3,2,1,0:T(2,128)S(1)}, f32[10,21,2,128]{3,2,1,0:T(2,128)S(1)}, u32[]{:S(2)}, u32[]{:S(2)}) %collective-permute-start.7) | collective-permute-done | bytes 215072 | tf_op jit(solution)/shard_map/ppermute | solution.py:17
  61.2 0.6 pad_maximum_fusion
  61.8 0.2 slice_bitcast_fusion.3
  62.0 0.2 fusion.272
  62.1 0.2 fusion.270
  62.4 0.2 fusion.21
  62.6 0.3 fusion.32
  62.9 0.2 slice_add_fusion
  63.3 0.2 fusion.82
  63.5 0.2 slice_bitcast_fusion.4
  64.0 0.2 fusion.71
  64.3 0.1 fusion.63
  64.4 0.1 fusion.56
  64.6 0.5 fusion.6
  65.2 3.5 %collective-permute-start.8 = (f32[9,17,2,128]{3,2,1,0:T(2,128)S(1)}, f32[9,17,2,128]{3,2,1,0:T(2,128)S(1)}, u32[]{:S(2)}, u32[]{:S(2)}) collective-permute-start(f32[9,17,2,128]{3,2,1,0:T(2,128)S(1)} %get-tuple-element.37), channel_id=1, source_target_pairs={{0,8},{8,16},{16,24},{1,9},{9,17},{17,25},{2,10},{10,18},{18,26},{... | collective-permute-start | bytes 470024 | tf_op jit(solution)/shard_map/ppermute | solution.py:16
  68.6 1.3 %collective-permute-start.9 = (f32[9,17,2,128]{3,2,1,0:T(2,128)S(1)}, f32[9,17,2,128]{3,2,1,0:T(2,128)S(1)}, u32[]{:S(2)}, u32[]{:S(2)}) collective-permute-start(f32[9,17,2,128]{3,2,1,0:T(2,128)S(1)} %get-tuple-element.38), channel_id=1, source_target_pairs={{8,0},{16,8},{24,16},{9,1},{17,9},{25,17},{10,2},{18,10},{26,18},{... | collective-permute-start | bytes 470024 | tf_op jit(solution)/shard_map/ppermute | solution.py:17
  70.0 1.4 %collective-permute-done.8 = f32[9,17,2,128]{3,2,1,0:T(2,128)S(1)} collective-permute-done((f32[9,17,2,128]{3,2,1,0:T(2,128)S(1)}, f32[9,17,2,128]{3,2,1,0:T(2,128)S(1)}, u32[]{:S(2)}, u32[]{:S(2)}) %collective-permute-start.8) | collective-permute-done | bytes 156704 | tf_op jit(solution)/shard_map/ppermute | solution.py:16
  71.4 4.4 %collective-permute-done.9 = f32[9,17,2,128]{3,2,1,0:T(2,128)S(1)} collective-permute-done((f32[9,17,2,128]{3,2,1,0:T(2,128)S(1)}, f32[9,17,2,128]{3,2,1,0:T(2,128)S(1)}, u32[]{:S(2)}, u32[]{:S(2)}) %collective-permute-start.9) | collective-permute-done | bytes 156704 | tf_op jit(solution)/shard_map/ppermute | solution.py:17
  75.9 0.1 fusion.273
  76.1 0.1 fusion.274
  76.2 0.1 fusion.275
  76.3 0.4 pad_maximum_fusion.2
  76.8 0.2 fusion.49
  76.9 0.2 fusion.44
  77.1 0.2 fusion.38
  77.3 0.2 slice_add_fusion.1
  77.7 0.1 fusion.138
  78.4 0.1 fusion.112
  78.5 0.4 fusion.12
  79.0 3.5 %collective-permute-start.10 = (f32[9,13,2,128]{3,2,1,0:T(2,128)S(1)}, f32[9,13,2,128]{3,2,1,0:T(2,128)S(1)}, u32[]{:S(2)}, u32[]{:S(2)}) collective-permute-start(f32[9,13,2,128]{3,2,1,0:T(2,128)S(1)} %get-tuple-element.42), channel_id=1, source_target_pairs={{0,8},{8,16},{16,24},{1,9},{9,17},{17,25},{2,10},{10,18},{18,26},{... | collective-permute-start | bytes 359432 | tf_op jit(solution)/shard_map/ppermute | solution.py:16
  82.5 1.3 %collective-permute-start.11 = (f32[9,13,2,128]{3,2,1,0:T(2,128)S(1)}, f32[9,13,2,128]{3,2,1,0:T(2,128)S(1)}, u32[]{:S(2)}, u32[]{:S(2)}) collective-permute-start(f32[9,13,2,128]{3,2,1,0:T(2,128)S(1)} %get-tuple-element.43), channel_id=1, source_target_pairs={{8,0},{16,8},{24,16},{9,1},{17,9},{25,17},{10,2},{18,10},{26,18},{... | collective-permute-start | bytes 359432 | tf_op jit(solution)/shard_map/ppermute | solution.py:17
  83.9 1.0 %collective-permute-done.10 = f32[9,13,2,128]{3,2,1,0:T(2,128)S(1)} collective-permute-done((f32[9,13,2,128]{3,2,1,0:T(2,128)S(1)}, f32[9,13,2,128]{3,2,1,0:T(2,128)S(1)}, u32[]{:S(2)}, u32[]{:S(2)}) %collective-permute-start.10) | collective-permute-done | bytes 119840 | tf_op jit(solution)/shard_map/ppermute | solution.py:16
  84.9 4.3 %collective-permute-done.11 = f32[9,13,2,128]{3,2,1,0:T(2,128)S(1)} collective-permute-done((f32[9,13,2,128]{3,2,1,0:T(2,128)S(1)}, f32[9,13,2,128]{3,2,1,0:T(2,128)S(1)}, u32[]{:S(2)}, u32[]{:S(2)}) %collective-permute-start.11) | collective-permute-done | bytes 119840 | tf_op jit(solution)/shard_map/ppermute | solution.py:17
  89.7 0.4 pad_maximum_fusion.3
  90.1 0.1 fusion.105
  90.2 0.1 fusion.100
  90.3 0.1 fusion.94
  91.5 1.2 %fusion.16 = f32[9,24,9,128]{3,1,2,0:T(8,128)} fusion(f32[9,9,24,128]{3,2,1,0:T(8,128)S(1)} %fusion.151, f32[18,17,24,128]{3,2,1,0:T(8,128)S(1)} %fusion, f32[9,24]{1,0:T(8,128)S(1)} %slice.1318), kind=kLoop, calls=%fused_computation.25 | loop fusion | flops 1244160 | bytes 3982176 | tf_op jit(solution)/shard_map/transpose | solution.py:250
  (104 shorter events, 4.6 us)
Async XLA Ops:
  2.2 25.5 %collective-permute-start.2 = (f32[10,1,24,64]{3,2,1,0:T(8,128)}, f32[10,1,24,64]{3,2,1,0:T(8,128)S(1)}, u32[]{:S(2)}, u32[]{:S(2)}) collective-permute-start(f32[10,1,24,64]{3,2,1,0:T(8,128)} %get-tuple-element.5), channel_id=1, source_target_pairs={{2,0},{3,1},{4,2},{5,3},{6,4},{7,5},{8,6},{9,7},{10,8},{11,9},{12,... | collective-permute-start | bytes 184328 | tf_op jit(solution)/shard_map/ppermute | solution.py:182
  3.5 20.8 %collective-permute-start.3 = (f32[10,1,24,64]{3,2,1,0:T(8,128)}, f32[10,1,24,64]{3,2,1,0:T(8,128)S(1)}, u32[]{:S(2)}, u32[]{:S(2)}) collective-permute-start(f32[10,1,24,64]{3,2,1,0:T(8,128)} %get-tuple-element.5), channel_id=1, source_target_pairs={{0,2},{1,3},{2,4},{3,5},{4,6},{5,7},{6,8},{7,9},{8,10},{9,11},{10,... | collective-permute-start | bytes 184328 | tf_op jit(solution)/shard_map/ppermute | solution.py:181
  9.0 18.5 %collective-permute-start.1 = (f32[10,1,24,64]{3,2,1,0:T(8,128)}, f32[10,1,24,64]{3,2,1,0:T(8,128)S(1)}, u32[]{:S(2)}, u32[]{:S(2)}) collective-permute-start(f32[10,1,24,64]{3,2,1,0:T(8,128)} %get-tuple-element.5), channel_id=1, source_target_pairs={{1,0},{2,1},{3,2},{4,3},{5,4},{6,5},{7,6},{8,7},{9,8},{10,9},{11,1... | collective-permute-start | bytes 184328 | tf_op jit(solution)/shard_map/ppermute | solution.py:178
  10.3 15.3 %collective-permute-start = (f32[10,1,24,64]{3,2,1,0:T(8,128)}, f32[10,1,24,64]{3,2,1,0:T(8,128)}, u32[]{:S(2)}, u32[]{:S(2)}) collective-permute-start(f32[10,1,24,64]{3,2,1,0:T(8,128)} %get-tuple-element.5), channel_id=1, source_target_pairs={{0,1},{1,2},{2,3},{3,4},{4,5},{5,6},{6,7},{7,8},{8,9},{9,10},{10,1... | collective-permute-start | bytes 184328 | tf_op jit(solution)/shard_map/ppermute | solution.py:177
  16.6 7.1 %copy-start.1 = (f32[9,1,24,64]{3,2,1,0:T(8,128)S(1)}, f32[9,1,24,64]{3,2,1,0:T(8,128)}, u32[]{:S(2)}) copy-start(f32[9,1,24,64]{3,2,1,0:T(8,128)} %refs_2_.1) | copy-start | bytes 165892
  19.1 30.2 %collective-permute-start.4 = (f32[12,6,24,128]{3,2,1,0:T(8,128)}, f32[12,6,24,128]{3,2,1,0:T(8,128)S(1)}, u32[]{:S(2)}, u32[]{:S(2)}) collective-permute-start(f32[12,6,24,128]{3,2,1,0:T(8,128)} %get-tuple-element.44), channel_id=1, source_target_pairs={{0,1},{1,2},{2,3},{3,4},{4,5},{5,6},{6,7},{8,9},{9,10},{10,11},{11... | collective-permute-start | bytes 2654216 | tf_op jit(solution)/shard_map/ppermute | solution.py:175
  24.3 24.9 %collective-permute-start.5 = (f32[12,6,24,128]{3,2,1,0:T(8,128)S(1)}, f32[12,6,24,128]{3,2,1,0:T(8,128)S(1)}, u32[]{:S(2)}, u32[]{:S(2)}) collective-permute-start(f32[12,6,24,128]{3,2,1,0:T(8,128)S(1)} %get-tuple-element.45), channel_id=1, source_target_pairs={{1,0},{2,1},{3,2},{4,3},{5,4},{6,5},{7,6},{9,8},{10,9},{11,10},{12... | collective-permute-start | bytes 2654216 | tf_op jit(solution)/shard_map/ppermute | solution.py:176
  27.5 0.7 copy-start.2
  27.5 0.7 copy-start.3
  28.2 18.0 %copy-start.5 = (f32[24]{0:T(128)S(1)}, f32[24]{0:T(128)}, u32[]{:S(2)}) copy-start(f32[24]{0:T(128)} %get-tuple-element.151) | copy-start | bytes 292
  30.8 15.1 %all-to-all-start = ((bf16[8,2,4032]{2,1,0:T(2,128)(2,1)}), bf16[8,2,4032]{2,1,0:T(2,128)(2,1)S(1)}, u32[]{:S(2)}, u32[]{:S(2)}) async-start(bf16[8,2,4032]{2,1,0:T(2,128)(2,1)} %reshape.473), calls=%async_computation | async-start | bytes 262144 | tf_op jit(solution)/shard_map/all_to_all | solution.py:199
  46.8 2.5 %copy-start = (f32[12,9,24,128]{3,2,1,0:T(8,128)S(1)}, f32[12,9,24,128]{3,2,1,0:T(8,128)}, u32[]{:S(2)}) copy-start(f32[12,9,24,128]{3,2,1,0:T(8,128)} %shard_map.69) | copy-start | bytes 3981316
  49.2 5.2 %copy-start.6 = (f32[128]{0:T(128)S(1)}, f32[128]{0:T(128)}, u32[]{:S(2)}) copy-start(f32[128]{0:T(128)} %get-tuple-element.158) | copy-start | bytes 1540
  49.2 5.2 %copy-start.7 = (f32[128]{0:T(128)S(1)}, f32[128]{0:T(128)}, u32[]{:S(2)}) copy-start(f32[128]{0:T(128)} %get-tuple-element.159) | copy-start | bytes 1540
  49.4 7.7 %collective-permute-start.6 = (f32[10,21,2,128]{3,2,1,0:T(2,128)S(1)}, f32[10,21,2,128]{3,2,1,0:T(2,128)S(1)}, u32[]{:S(2)}, u32[]{:S(2)}) collective-permute-start(f32[10,21,2,128]{3,2,1,0:T(2,128)S(1)} %get-tuple-element.32), channel_id=1, source_target_pairs={{0,8},{8,16},{16,24},{1,9},{9,17},{17,25},{2,10},{10,18},{18,26},{... | collective-permute-start | bytes 645128 | tf_op jit(solution)/shard_map/ppermute | solution.py:16
  52.9 8.3 %collective-permute-start.7 = (f32[10,21,2,128]{3,2,1,0:T(2,128)S(1)}, f32[10,21,2,128]{3,2,1,0:T(2,128)S(1)}, u32[]{:S(2)}, u32[]{:S(2)}) collective-permute-start(f32[10,21,2,128]{3,2,1,0:T(2,128)S(1)} %get-tuple-element.33), channel_id=1, source_target_pairs={{8,0},{16,8},{24,16},{9,1},{17,9},{25,17},{10,2},{18,10},{26,18},{... | collective-permute-start | bytes 645128 | tf_op jit(solution)/shard_map/ppermute | solution.py:17
  65.2 6.2 %collective-permute-start.8 = (f32[9,17,2,128]{3,2,1,0:T(2,128)S(1)}, f32[9,17,2,128]{3,2,1,0:T(2,128)S(1)}, u32[]{:S(2)}, u32[]{:S(2)}) collective-permute-start(f32[9,17,2,128]{3,2,1,0:T(2,128)S(1)} %get-tuple-element.37), channel_id=1, source_target_pairs={{0,8},{8,16},{16,24},{1,9},{9,17},{17,25},{2,10},{10,18},{18,26},{... | collective-permute-start | bytes 470024 | tf_op jit(solution)/shard_map/ppermute | solution.py:16
  68.6 7.1 %collective-permute-start.9 = (f32[9,17,2,128]{3,2,1,0:T(2,128)S(1)}, f32[9,17,2,128]{3,2,1,0:T(2,128)S(1)}, u32[]{:S(2)}, u32[]{:S(2)}) collective-permute-start(f32[9,17,2,128]{3,2,1,0:T(2,128)S(1)} %get-tuple-element.38), channel_id=1, source_target_pairs={{8,0},{16,8},{24,16},{9,1},{17,9},{25,17},{10,2},{18,10},{26,18},{... | collective-permute-start | bytes 470024 | tf_op jit(solution)/shard_map/ppermute | solution.py:17
  79.0 5.9 %collective-permute-start.10 = (f32[9,13,2,128]{3,2,1,0:T(2,128)S(1)}, f32[9,13,2,128]{3,2,1,0:T(2,128)S(1)}, u32[]{:S(2)}, u32[]{:S(2)}) collective-permute-start(f32[9,13,2,128]{3,2,1,0:T(2,128)S(1)} %get-tuple-element.42), channel_id=1, source_target_pairs={{0,8},{8,16},{16,24},{1,9},{9,17},{17,25},{2,10},{10,18},{18,26},{... | collective-permute-start | bytes 359432 | tf_op jit(solution)/shard_map/ppermute | solution.py:16
  82.5 6.7 %collective-permute-start.11 = (f32[9,13,2,128]{3,2,1,0:T(2,128)S(1)}, f32[9,13,2,128]{3,2,1,0:T(2,128)S(1)}, u32[]{:S(2)}, u32[]{:S(2)}) collective-permute-start(f32[9,13,2,128]{3,2,1,0:T(2,128)S(1)} %get-tuple-element.43), channel_id=1, source_target_pairs={{8,0},{16,8},{24,16},{9,1},{17,9},{25,17},{10,2},{18,10},{26,18},{... | collective-permute-start | bytes 359432 | tf_op jit(solution)/shard_map/ppermute | solution.py:17
  83.8 5.5 %copy-start.4 = (f32[9,1,24,64]{3,2,1,0:T(8,128)}, f32[9,1,24,64]{3,2,1,0:T(8,128)S(1)}, u32[]{:S(2)}) copy-start(f32[9,1,24,64]{3,2,1,0:T(8,128)S(1)} %constant_dynamic-update-slice_fusion.9) | copy-start | bytes 165892

commit v13 on v12

--- a/solution.py
+++ b/solution.py
@@ -187,17 +187,10 @@
         reg_ext, reg_ext[9, 1:-1], region_state[3:], lam_r, mu_r, 0.6, 3.0, True
     )
 
-    both = jnp.concatenate([region_state, region_next], 0).astype(jnp.bfloat16)
     tile_np = interp_np(fine_y, rows_each)
     blocks_np = np.kron(np.eye(3), tile_np)[fine_y - 4: 2 * fine_y + 4]
     used = np.nonzero(np.any(blocks_np != 0.0, axis=0))[0]
     lo, hi = int(used[0]), int(used[-1]) + 1
-    both = jnp.pad(both, ((0, 0), (0, 0), (rows_each, rows_each), (0, 0)))
-    send = jnp.concatenate(
-        [both[:, :, rows_each * d + lo: rows_each * d + hi] for d in range(count_y)], 2
-    )
-    band = lax.all_to_all(send, "gy", 2, 1, tiled=True).astype(jnp.float32)
-    columns = band.shape[1]
     high = lax.Precision.HIGH
     along_y_w = interp_matrix(fine_y, rows_each)
     zeros_w = jnp.zeros_like(along_y_w)
@@ -209,10 +202,25 @@
         ],
         0,
     )[fine_y - 4: 2 * fine_y + 4, lo:hi]
-    first = jnp.einsum("fa,cabz->cfbz", interp_matrix(fine_x, columns), band, precision=high)
-    second = jnp.einsum("gb,cfbz->cgfz", tiles_w, first, precision=high)
-    background = jnp.einsum(
-        "kz,cgfz->cgfk", interp_matrix(fine_z, band.shape[3]), second, precision=high
+
+    def background_of(part):
+        part = jnp.pad(
+            part.astype(jnp.bfloat16), ((0, 0), (0, 0), (rows_each, rows_each), (0, 0))
+        )
+        send = jnp.concatenate(
+            [part[:, :, rows_each * d + lo: rows_each * d + hi] for d in range(count_y)], 2
+        )
+        band = lax.all_to_all(send, "gy", 2, 1, tiled=True).astype(jnp.float32)
+        first = jnp.einsum(
+            "fa,cabz->cfbz", interp_matrix(fine_x, band.shape[1]), band, precision=high
+        )
+        second = jnp.einsum("gb,cfbz->cgfz", tiles_w, first, precision=high)
+        return jnp.einsum(
+            "kz,cgfz->cgfk", interp_matrix(fine_z, band.shape[3]), second, precision=high
+        )
+
+    background = jnp.concatenate(
+        [background_of(region_state), background_of(region_next)], 0
     )
     along_x = ramp(lax.axis_index("gx") * fine_x, fine_x, count_x * fine_x, fine_x)
     along_y = ramp(me_y * fine_y - 4, fine_y + 8, count_y * fine_y, fine_y)

time: 93.4 us -> 104 us (1.11)
  waiting for transfers between devices: 23.9 us -> 29.3 us
  matrix products: 5.16 us -> 8.18 us
  starting transfers between devices: 37.9 us -> 40.1 us
  local copies, waits for them, and re-layouts: 10.1 us -> 11.6 us
  other arithmetic: 9.94 us -> 8.46 us
    all_to_all x1 -> x2, waiting for transfers between devices: 8.53 us -> 13.1 us  [background_of(): band = lax.all_to_all(send, 'gy', 2, 1, tiled=True).astype(jnp.float32)]
    all_to_all x1 -> x2, starting transfers between devices: 6.55 us -> 10.6 us  [background_of(): band = lax.all_to_all(send, 'gy', 2, 1, tiled=True).astype(jnp.float32)]
    dot_general x3 -> x6, matrix products: 5.16 us -> 8.18 us  [the longest x2 4.11 us: background_of(): second = jnp.einsum('gb,cfbz->cgfz', tiles_w, first, precision=high)]
    ppermute x1, starting transfers between devices: 3.68 us -> 1.47 us  [local(): reg_lo = lax.ppermute(region_pay, flat, shifted(n_flat, 1))]
    select_n x3, other arithmetic: 1.14 us -> 0.05 us  [interp_matrix(): frac = jnp.where(above, 1.0, frac)]
    unnamed x32 -> x26, local copies, waits for them, and re-layouts: 3.24 us -> 3.84 us
  transfers between devices with their start and end apart: 13 -> 14, of which waited for: 7 -> 8; matrix products, arithmetic and copies ran while one was open for 16% -> 14% of each run, Pallas kernels for 3% -> 3%
where the time goes in v13:
time: 104 us; the launch traced here: 103 us
  starting transfers between devices  40.1 us (39%)
  waiting for transfers between devices  29.3 us (28%)
  local copies, waits for them, and re-layouts  11.6 us (11%)
  other arithmetic  8.46 us (8%)
  matrix products  8.18 us (8%)
  Pallas kernels  4.22 us (4%)
  between operations  1.48 us (1%)
    all_to_all x2, waiting for transfers between devices, background_of(): band = lax.all_to_all(send, 'gy', 2, 1, tiled=True).astype(jnp.float32)  13.1 us
    ppermute x3, waiting for transfers between devices, x_halo(): from_right = lax.ppermute(field[:, :, :width], 'gx', shifted(nx, -1))  12.9 us
    all_to_all x2, starting transfers between devices, background_of(): band = lax.all_to_all(send, 'gy', 2, 1, tiled=True).astype(jnp.float32)  10.6 us
    ppermute x3, starting transfers between devices, x_halo(): from_left = lax.ppermute(field[:, :, -width:], 'gx', shifted(nx, 1))  10.5 us
    ppermute x1, starting transfers between devices, local(): lows.insert(0, lax.ppermute(region_pay, flat, shifted(n_flat, d)))  4.84 us
    ppermute x1, starting transfers between devices, local(): fine_lo = lax.ppermute(fine_pay[:, -reach_y:], 'gy', shifted(count_y, 1))  4.75 us
    pallas_call x2, Pallas kernels, lookup(): pl.pallas_call(lambda *refs: lookup_kernel(step, extra, *refs), out_shape...  4.22 us
    dot_general x2, matrix products, background_of(): second = jnp.einsum('gb,cfbz->cgfz', tiles_w, first, precision=high)  4.11 us
  transfers between devices with their start and end apart: 14, of which 8 were waited for; matrix products, arithmetic and copies ran while one was open for 14% of the time, Pallas kernels for 3%

profile of v13, /device:TPU:0, one launch (start us, length us, event | category | flops | bytes accessed | tf_op | source)
XLA Modules:
  0.0 103.3 jit_solution(18290999015271644490)
XLA Ops:
  0.6 1.6 %shard_map.68 = (f32[10,1,24,64]{3,2,1,0:T(8,128)}, f32[1,24,64]{2,1,0:T(8,128)}, f32[1,24,64]{2,1,0:T(8,128)}) custom-call(s32[1,24,64]{2,1,0:T(8,128)} %refs_0_.1, f32[3,8]{1,0:T(4,128)} %refs_1_.3, f32[9,1,24,64]{3,2,1,0:T(8,128)} %refs_2_.1), custom_call_target="tpu_custom_call" | custom-call | tf_op jit(solution)/shard_map/pallas_call | solution.py:48
  2.2 4.8 %collective-permute-start.3 = (f32[10,1,24,64]{3,2,1,0:T(8,128)}, f32[10,1,24,64]{3,2,1,0:T(8,128)S(1)}, u32[]{:S(2)}, u32[]{:S(2)}) collective-permute-start(f32[10,1,24,64]{3,2,1,0:T(8,128)} %get-tuple-element.5), channel_id=1, source_target_pairs={{0,2},{1,3},{2,4},{3,5},{4,6},{5,7},{6,8},{7,9},{8,10},{9,11},{10,... | collective-permute-start | bytes 184328 | tf_op jit(solution)/shard_map/ppermute | solution.py:181
  7.1 1.5 %collective-permute-start = (f32[10,1,24,64]{3,2,1,0:T(8,128)}, f32[10,1,24,64]{3,2,1,0:T(8,128)S(1)}, u32[]{:S(2)}, u32[]{:S(2)}) collective-permute-start(f32[10,1,24,64]{3,2,1,0:T(8,128)} %get-tuple-element.5), channel_id=1, source_target_pairs={{0,1},{1,2},{2,3},{3,4},{4,5},{5,6},{6,7},{7,8},{8,9},{9,10},{10,1... | collective-permute-start | bytes 184328 | tf_op jit(solution)/shard_map/ppermute | solution.py:177
  8.6 1.3 %collective-permute-start.1 = (f32[10,1,24,64]{3,2,1,0:T(8,128)}, f32[10,1,24,64]{3,2,1,0:T(8,128)S(1)}, u32[]{:S(2)}, u32[]{:S(2)}) collective-permute-start(f32[10,1,24,64]{3,2,1,0:T(8,128)} %get-tuple-element.5), channel_id=1, source_target_pairs={{1,0},{2,1},{3,2},{4,3},{5,4},{6,5},{7,6},{8,7},{9,8},{10,9},{11,1... | collective-permute-start | bytes 184328 | tf_op jit(solution)/shard_map/ppermute | solution.py:178
  9.9 1.3 %collective-permute-start.2 = (f32[10,1,24,64]{3,2,1,0:T(8,128)}, f32[10,1,24,64]{3,2,1,0:T(8,128)S(1)}, u32[]{:S(2)}, u32[]{:S(2)}) collective-permute-start(f32[10,1,24,64]{3,2,1,0:T(8,128)} %get-tuple-element.5), channel_id=1, source_target_pairs={{2,0},{3,1},{4,2},{5,3},{6,4},{7,5},{8,6},{9,7},{10,8},{11,9},{12,... | collective-permute-start | bytes 184328 | tf_op jit(solution)/shard_map/ppermute | solution.py:182
  11.2 2.6 %shard_map.69 = f32[12,9,24,128]{3,2,1,0:T(8,128)} custom-call(s32[9,24,128]{2,1,0:T(8,128)} %bitcast.675, f32[3,8]{1,0:T(4,128)} %refs_1_.3, f32[9,9,24,128]{3,2,1,0:T(8,128)} %bitcast.670), custom_call_target="tpu_custom_call" | custom-call | tf_op jit(solution)/shard_map/pallas_call | solution.py:48
  13.8 2.8 %fusion.279 = (f32[12,6,24,128]{3,2,1,0:T(8,128)}, f32[12,6,24,128]{3,2,1,0:T(8,128)}) fusion(f32[12,9,24,128]{3,2,1,0:T(8,128)} %shard_map.69), kind=kLoop, calls=%fused_computation.495 | loop fusion | bytes 3538944 | tf_op jit(solution)/shard_map/slice | solution.py:175
  16.6 4.8 %collective-permute-start.4 = (f32[12,6,24,128]{3,2,1,0:T(8,128)}, f32[12,6,24,128]{3,2,1,0:T(8,128)S(1)}, u32[]{:S(2)}, u32[]{:S(2)}) collective-permute-start(f32[12,6,24,128]{3,2,1,0:T(8,128)} %get-tuple-element.33), channel_id=1, source_target_pairs={{0,1},{1,2},{2,3},{3,4},{4,5},{5,6},{6,7},{8,9},{9,10},{10,11},{11... | collective-permute-start | bytes 2654216 | tf_op jit(solution)/shard_map/ppermute | solution.py:175
  21.4 0.9 concatenate.322
  22.3 0.8 reshape.464
  23.1 6.1 %all-to-all-start = ((bf16[8,2,2016]{2,1,0:T(2,128)(2,1)}), bf16[8,2,2016]{2,1,0:T(2,128)(2,1)S(1)}, u32[]{:S(2)}, u32[]{:S(2)}) async-start(bf16[8,2,2016]{2,1,0:T(2,128)(2,1)} %reshape.464), calls=%async_computation | async-start | bytes 131072 | tf_op jit(solution)/shard_map/all_to_all | solution.py:213
  29.5 8.2 %all-to-all-done = bf16[8,2,2016]{2,1,0:T(2,128)(2,1)S(1)} async-done(((bf16[8,2,2016]{2,1,0:T(2,128)(2,1)}), bf16[8,2,2016]{2,1,0:T(2,128)(2,1)S(1)}, u32[]{:S(2)}, u32[]{:S(2)}) %all-to-all-start) | async-done | bytes 64544 | tf_op jit(solution)/shard_map/all_to_all | solution.py:213
  37.7 0.2 reshape.465
  37.9 0.4 convolution_bitcast_fusion.3
  38.3 1.3 %collective-permute-start.5 = (f32[12,6,24,128]{3,2,1,0:T(8,128)}, f32[12,6,24,128]{3,2,1,0:T(8,128)S(1)}, u32[]{:S(2)}, u32[]{:S(2)}) collective-permute-start(f32[12,6,24,128]{3,2,1,0:T(8,128)} %get-tuple-element.34), channel_id=1, source_target_pairs={{1,0},{2,1},{3,2},{4,3},{5,4},{6,5},{7,6},{9,8},{10,9},{11,10},{12... | collective-permute-start | bytes 2654216 | tf_op jit(solution)/shard_map/ppermute | solution.py:176
  40.9 0.9 concatenate.327
  41.8 0.8 reshape.466
  42.6 4.5 %all-to-all-start.1 = ((bf16[8,2,2016]{2,1,0:T(2,128)(2,1)}), bf16[8,2,2016]{2,1,0:T(2,128)(2,1)S(1)}, u32[]{:S(2)}, u32[]{:S(2)}) async-start(bf16[8,2,2016]{2,1,0:T(2,128)(2,1)} %reshape.466), calls=%async_computation.1 | async-start | bytes 131072 | tf_op jit(solution)/shard_map/all_to_all | solution.py:213
  47.1 2.8 %convolution_bitcast_fusion.1 = f32[9,17,24,64]{3,1,2,0:T(8,128)} fusion(f32[9,24,7,64]{3,1,2,0:T(8,128)S(1)} %convolution_bitcast_fusion.3, f32[9,3]{0,1:T(4,128)S(1)} %select_add_fusion.6, f32[9,3]{0,1:T(4,128)S(1)} %broadcast.1067), kind=kOutput, calls=%fused_computation.10 | convolution fusion | flops 9871407 | bytes 1327320 | tf_op jit(solution)/shard_map/gb,cfbz->cgfz/dot_general | solution.py:217
  49.9 4.9 %all-to-all-done.1 = bf16[8,2,2016]{2,1,0:T(2,128)(2,1)S(1)} async-done(((bf16[8,2,2016]{2,1,0:T(2,128)(2,1)}), bf16[8,2,2016]{2,1,0:T(2,128)(2,1)S(1)}, u32[]{:S(2)}, u32[]{:S(2)}) %all-to-all-start.1) | async-done | bytes 64544 | tf_op jit(solution)/shard_map/all_to_all | solution.py:213
  54.8 0.2 reshape.467
  55.0 0.4 convolution_bitcast_fusion.2
  55.4 1.3 %convolution_bitcast_fusion = f32[9,17,24,64]{3,1,2,0:T(8,128)S(1)} fusion(f32[9,24,7,64]{3,1,2,0:T(8,128)S(1)} %convolution_bitcast_fusion.2, f32[9,3]{0,1:T(4,128)S(1)} %select_add_fusion.6, f32[9,3]{0,1:T(4,128)S(1)} %broadcast.1067), kind=kOutput, calls=%fused_computation.9 | convolution fusion | flops 9871407 | bytes 1327320 | tf_op jit(solution)/shard_map/gb,cfbz->cgfz/dot_general | solution.py:217
  56.8 0.2 pad_maximum_fusion.9
  56.9 3.5 %collective-permute-start.6 = (f32[10,21,2,128]{3,2,1,0:T(2,128)S(1)}, f32[10,21,2,128]{3,2,1,0:T(2,128)S(1)}, u32[]{:S(2)}, u32[]{:S(2)}) collective-permute-start(f32[10,21,2,128]{3,2,1,0:T(2,128)S(1)} %get-tuple-element.21), channel_id=1, source_target_pairs={{0,8},{8,16},{16,24},{1,9},{9,17},{17,25},{2,10},{10,18},{18,26},{... | collective-permute-start | bytes 645128 | tf_op jit(solution)/shard_map/ppermute | solution.py:16
  60.4 1.5 %collective-permute-start.7 = (f32[10,21,2,128]{3,2,1,0:T(2,128)S(1)}, f32[10,21,2,128]{3,2,1,0:T(2,128)S(1)}, u32[]{:S(2)}, u32[]{:S(2)}) collective-permute-start(f32[10,21,2,128]{3,2,1,0:T(2,128)S(1)} %get-tuple-element.22), channel_id=1, source_target_pairs={{8,0},{16,8},{24,16},{9,1},{17,9},{25,17},{10,2},{18,10},{26,18},{... | collective-permute-start | bytes 645128 | tf_op jit(solution)/shard_map/ppermute | solution.py:17
  61.9 1.6 %fusion = f32[9,17,24,128]{3,2,1,0:T(8,128)S(1)} fusion(f32[9,17,24,64]{3,1,2,0:T(8,128)S(1)} %convolution_bitcast_fusion, f32[128]{0:T(128)S(1)} %get-tuple-element.157, s32[128]{0:T(128)S(1)} %get-tuple-element.160, f32[128]{0:T(128)S(1)} %get-tuple-element.158, s32[128]{0:T(128)S(1)} %get-tuple-element.159), kind=kOutput, calls=%fused_computation.4 | convolution fusion | flops 180527104 | bytes 2822144 | tf_op jit(solution)/shard_map/kz,cgfz->cgfk/dot_general | solution.py:218
  63.5 0.2 pad_maximum_fusion.1
  63.8 0.2 slice.1220
  63.9 0.8 collective-permute-done.6
  64.8 4.1 %collective-permute-done.7 = f32[10,21,2,128]{3,2,1,0:T(2,128)S(1)} collective-permute-done((f32[10,21,2,128]{3,2,1,0:T(2,128)S(1)}, f32[10,21,2,128]{3,2,1,0:T(2,128)S(1)}, u32[]{:S(2)}, u32[]{:S(2)}) %collective-permute-start.7) | collective-permute-done | bytes 215072 | tf_op jit(solution)/shard_map/ppermute | solution.py:17
  68.9 0.6 pad_maximum_fusion
  69.5 0.2 slice_bitcast_fusion.3
  69.7 0.2 fusion.282
  69.9 0.2 fusion.280
  70.1 0.2 fusion.19
  70.3 0.4 fusion.30
  70.7 0.2 slice_add_fusion
  71.1 0.2 fusion.79
  71.3 0.2 slice_bitcast_fusion.4
  71.8 0.2 fusion.68
  72.1 0.1 fusion.60
  72.2 0.1 fusion.53
  72.4 1.6 %copy-done.1 = f32[9,17,24,64]{3,1,2,0:T(8,128)S(1)} copy-done((f32[9,17,24,64]{3,1,2,0:T(8,128)S(1)}, f32[9,17,24,64]{3,1,2,0:T(8,128)}, u32[]{:S(2)}) %copy-start.1) | copy-done | bytes 940056
  74.0 1.6 %multiply_add_fusion = (f32[9,17,24,128]{3,2,1,0:T(8,128)S(1)}, f32[9,17,24,128]{3,2,1,0:T(8,128)S(1)}) fusion(f32[9,17,24,128]{3,2,1,0:T(8,128)S(1)} %fusion.53, f32[9,17,24,128]{3,2,1,0:T(8,128)S(1)} %fusion, f32[17,24]{1,0:T(8,128)S(1)} %multiply_add_fusion.1, f32[128]{0:T(128)S(1)} %get-tuple-element.157, s32[128]{0:T(128)S(1)} %get-tuple-element.160, ...), kind=kOutput, calls=%fused_computation.8 | convolution fusion | flops 183347200 | bytes 8463968 | tf_op jit(solution)/shard_map/kz,cgfz->cgfk/dot_general | solution.py:218
  75.7 3.5 %collective-permute-start.8 = (f32[9,17,2,128]{3,2,1,0:T(2,128)S(1)}, f32[9,17,2,128]{3,2,1,0:T(2,128)S(1)}, u32[]{:S(2)}, u32[]{:S(2)}) collective-permute-start(f32[9,17,2,128]{3,2,1,0:T(2,128)S(1)} %get-tuple-element.26), channel_id=1, source_target_pairs={{0,8},{8,16},{16,24},{1,9},{9,17},{17,25},{2,10},{10,18},{18,26},{... | collective-permute-start | bytes 470024 | tf_op jit(solution)/shard_map/ppermute | solution.py:16
  79.2 1.3 %collective-permute-start.9 = (f32[9,17,2,128]{3,2,1,0:T(2,128)S(1)}, f32[9,17,2,128]{3,2,1,0:T(2,128)S(1)}, u32[]{:S(2)}, u32[]{:S(2)}) collective-permute-start(f32[9,17,2,128]{3,2,1,0:T(2,128)S(1)} %get-tuple-element.27), channel_id=1, source_target_pairs={{8,0},{16,8},{24,16},{9,1},{17,9},{25,17},{10,2},{18,10},{26,18},{... | collective-permute-start | bytes 470024 | tf_op jit(solution)/shard_map/ppermute | solution.py:17
  80.6 1.4 %collective-permute-done.8 = f32[9,17,2,128]{3,2,1,0:T(2,128)S(1)} collective-permute-done((f32[9,17,2,128]{3,2,1,0:T(2,128)S(1)}, f32[9,17,2,128]{3,2,1,0:T(2,128)S(1)}, u32[]{:S(2)}, u32[]{:S(2)}) %collective-permute-start.8) | collective-permute-done | bytes 156704 | tf_op jit(solution)/shard_map/ppermute | solution.py:16
  81.9 4.4 %collective-permute-done.9 = f32[9,17,2,128]{3,2,1,0:T(2,128)S(1)} collective-permute-done((f32[9,17,2,128]{3,2,1,0:T(2,128)S(1)}, f32[9,17,2,128]{3,2,1,0:T(2,128)S(1)}, u32[]{:S(2)}, u32[]{:S(2)}) %collective-permute-start.9) | collective-permute-done | bytes 156704 | tf_op jit(solution)/shard_map/ppermute | solution.py:17
  86.6 0.1 fusion.284
  86.8 0.1 fusion.285
  86.9 0.4 pad_maximum_fusion.2
  87.3 0.2 fusion.46
  87.5 0.2 fusion.41
  87.7 0.2 fusion.35
  87.8 0.2 slice_add_fusion.1
  88.2 0.2 fusion.135
  89.1 0.4 fusion.8
  89.6 3.5 %collective-permute-start.10 = (f32[9,13,2,128]{3,2,1,0:T(2,128)S(1)}, f32[9,13,2,128]{3,2,1,0:T(2,128)S(1)}, u32[]{:S(2)}, u32[]{:S(2)}) collective-permute-start(f32[9,13,2,128]{3,2,1,0:T(2,128)S(1)} %get-tuple-element.31), channel_id=1, source_target_pairs={{0,8},{8,16},{16,24},{1,9},{9,17},{17,25},{2,10},{10,18},{18,26},{... | collective-permute-start | bytes 359432 | tf_op jit(solution)/shard_map/ppermute | solution.py:16
  93.1 1.3 %collective-permute-start.11 = (f32[9,13,2,128]{3,2,1,0:T(2,128)S(1)}, f32[9,13,2,128]{3,2,1,0:T(2,128)S(1)}, u32[]{:S(2)}, u32[]{:S(2)}) collective-permute-start(f32[9,13,2,128]{3,2,1,0:T(2,128)S(1)} %get-tuple-element.32), channel_id=1, source_target_pairs={{8,0},{16,8},{24,16},{9,1},{17,9},{25,17},{10,2},{18,10},{26,18},{... | collective-permute-start | bytes 359432 | tf_op jit(solution)/shard_map/ppermute | solution.py:17
  94.5 1.0 %collective-permute-done.10 = f32[9,13,2,128]{3,2,1,0:T(2,128)S(1)} collective-permute-done((f32[9,13,2,128]{3,2,1,0:T(2,128)S(1)}, f32[9,13,2,128]{3,2,1,0:T(2,128)S(1)}, u32[]{:S(2)}, u32[]{:S(2)}) %collective-permute-start.10) | collective-permute-done | bytes 119840 | tf_op jit(solution)/shard_map/ppermute | solution.py:16
  95.5 4.3 %collective-permute-done.11 = f32[9,13,2,128]{3,2,1,0:T(2,128)S(1)} collective-permute-done((f32[9,13,2,128]{3,2,1,0:T(2,128)S(1)}, f32[9,13,2,128]{3,2,1,0:T(2,128)S(1)}, u32[]{:S(2)}, u32[]{:S(2)}) %collective-permute-start.11) | collective-permute-done | bytes 119840 | tf_op jit(solution)/shard_map/ppermute | solution.py:17
  100.3 0.4 pad_maximum_fusion.3
  102.1 1.2 %fusion.12 = f32[9,24,9,128]{3,1,2,0:T(8,128)} fusion(f32[9,9,24,128]{3,2,1,0:T(8,128)S(1)} %fusion.150, f32[9,17,24,128]{3,2,1,0:T(8,128)S(1)} %fusion, f32[9,17,24,128]{3,2,1,0:T(8,128)S(1)} %get-tuple-element.142, f32[9,24]{1,0:T(8,128)S(1)} %slice.1351), kind=kLoop, calls=%fused_computation.23 | loop fusion | flops 1244160 | bytes 3982176 | tf_op jit(solution)/shard_map/transpose | solution.py:258
  (105 shorter events, 5.2 us)
Async XLA Ops:
  2.2 36.1 %collective-permute-start.3 = (f32[10,1,24,64]{3,2,1,0:T(8,128)}, f32[10,1,24,64]{3,2,1,0:T(8,128)S(1)}, u32[]{:S(2)}, u32[]{:S(2)}) collective-permute-start(f32[10,1,24,64]{3,2,1,0:T(8,128)} %get-tuple-element.5), channel_id=1, source_target_pairs={{0,2},{1,3},{2,4},{3,5},{4,6},{5,7},{6,8},{7,9},{8,10},{9,11},{10,... | collective-permute-start | bytes 184328 | tf_op jit(solution)/shard_map/ppermute | solution.py:181
  7.1 32.6 %collective-permute-start = (f32[10,1,24,64]{3,2,1,0:T(8,128)}, f32[10,1,24,64]{3,2,1,0:T(8,128)S(1)}, u32[]{:S(2)}, u32[]{:S(2)}) collective-permute-start(f32[10,1,24,64]{3,2,1,0:T(8,128)} %get-tuple-element.5), channel_id=1, source_target_pairs={{0,1},{1,2},{2,3},{3,4},{4,5},{5,6},{6,7},{7,8},{8,9},{9,10},{10,1... | collective-permute-start | bytes 184328 | tf_op jit(solution)/shard_map/ppermute | solution.py:177
  8.6 31.2 %collective-permute-start.1 = (f32[10,1,24,64]{3,2,1,0:T(8,128)}, f32[10,1,24,64]{3,2,1,0:T(8,128)S(1)}, u32[]{:S(2)}, u32[]{:S(2)}) collective-permute-start(f32[10,1,24,64]{3,2,1,0:T(8,128)} %get-tuple-element.5), channel_id=1, source_target_pairs={{1,0},{2,1},{3,2},{4,3},{5,4},{6,5},{7,6},{8,7},{9,8},{10,9},{11,1... | collective-permute-start | bytes 184328 | tf_op jit(solution)/shard_map/ppermute | solution.py:178
  9.9 30.2 %collective-permute-start.2 = (f32[10,1,24,64]{3,2,1,0:T(8,128)}, f32[10,1,24,64]{3,2,1,0:T(8,128)S(1)}, u32[]{:S(2)}, u32[]{:S(2)}) collective-permute-start(f32[10,1,24,64]{3,2,1,0:T(8,128)} %get-tuple-element.5), channel_id=1, source_target_pairs={{2,0},{3,1},{4,2},{5,3},{6,4},{7,5},{8,6},{9,7},{10,8},{11,9},{12,... | collective-permute-start | bytes 184328 | tf_op jit(solution)/shard_map/ppermute | solution.py:182
  13.8 7.6 %copy-start.2 = (f32[9,1,24,64]{3,2,1,0:T(8,128)S(1)}, f32[9,1,24,64]{3,2,1,0:T(8,128)}, u32[]{:S(2)}) copy-start(f32[9,1,24,64]{3,2,1,0:T(8,128)} %refs_2_.1) | copy-start | bytes 165892
  16.6 23.1 %copy-start.5 = (f32[10,1,24,64]{3,2,1,0:T(8,128)S(1)}, f32[10,1,24,64]{3,2,1,0:T(8,128)}, u32[]{:S(2)}) copy-start(f32[10,1,24,64]{3,2,1,0:T(8,128)} %get-tuple-element.5) | copy-start | bytes 184324
  16.6 40.2 %collective-permute-start.4 = (f32[12,6,24,128]{3,2,1,0:T(8,128)}, f32[12,6,24,128]{3,2,1,0:T(8,128)S(1)}, u32[]{:S(2)}, u32[]{:S(2)}) collective-permute-start(f32[12,6,24,128]{3,2,1,0:T(8,128)} %get-tuple-element.33), channel_id=1, source_target_pairs={{0,1},{1,2},{2,3},{3,4},{4,5},{5,6},{6,7},{8,9},{9,10},{10,11},{11... | collective-permute-start | bytes 2654216 | tf_op jit(solution)/shard_map/ppermute | solution.py:175
  23.1 14.6 %all-to-all-start = ((bf16[8,2,2016]{2,1,0:T(2,128)(2,1)}), bf16[8,2,2016]{2,1,0:T(2,128)(2,1)S(1)}, u32[]{:S(2)}, u32[]{:S(2)}) async-start(bf16[8,2,2016]{2,1,0:T(2,128)(2,1)} %reshape.464), calls=%async_computation | async-start | bytes 131072 | tf_op jit(solution)/shard_map/all_to_all | solution.py:213
  38.3 18.4 %collective-permute-start.5 = (f32[12,6,24,128]{3,2,1,0:T(8,128)}, f32[12,6,24,128]{3,2,1,0:T(8,128)S(1)}, u32[]{:S(2)}, u32[]{:S(2)}) collective-permute-start(f32[12,6,24,128]{3,2,1,0:T(8,128)} %get-tuple-element.34), channel_id=1, source_target_pairs={{1,0},{2,1},{3,2},{4,3},{5,4},{6,5},{7,6},{9,8},{10,9},{11,10},{12... | collective-permute-start | bytes 2654216 | tf_op jit(solution)/shard_map/ppermute | solution.py:176
  39.7 0.7 copy-start.3
  39.8 0.7 copy-start.6
  40.8 9.1 %copy-start.4 = (f32[9,1,24,64]{3,2,1,0:T(8,128)}, f32[9,1,24,64]{3,2,1,0:T(8,128)S(1)}, u32[]{:S(2)}) copy-start(f32[9,1,24,64]{3,2,1,0:T(8,128)S(1)} %constant_dynamic-update-slice_fusion.9) | copy-start | bytes 165892
  42.6 12.2 %all-to-all-start.1 = ((bf16[8,2,2016]{2,1,0:T(2,128)(2,1)}), bf16[8,2,2016]{2,1,0:T(2,128)(2,1)S(1)}, u32[]{:S(2)}, u32[]{:S(2)}) async-start(bf16[8,2,2016]{2,1,0:T(2,128)(2,1)} %reshape.466), calls=%async_computation.1 | async-start | bytes 131072 | tf_op jit(solution)/shard_map/all_to_all | solution.py:213
  55.4 1.4 %copy-start = (f32[12,9,24,128]{3,2,1,0:T(8,128)S(1)}, f32[12,9,24,128]{3,2,1,0:T(8,128)}, u32[]{:S(2)}) copy-start(f32[12,9,24,128]{3,2,1,0:T(8,128)} %shard_map.69) | copy-start | bytes 3981316
  56.9 7.9 %collective-permute-start.6 = (f32[10,21,2,128]{3,2,1,0:T(2,128)S(1)}, f32[10,21,2,128]{3,2,1,0:T(2,128)S(1)}, u32[]{:S(2)}, u32[]{:S(2)}) collective-permute-start(f32[10,21,2,128]{3,2,1,0:T(2,128)S(1)} %get-tuple-element.21), channel_id=1, source_target_pairs={{0,8},{8,16},{16,24},{1,9},{9,17},{17,25},{2,10},{10,18},{18,26},{... | collective-permute-start | bytes 645128 | tf_op jit(solution)/shard_map/ppermute | solution.py:16
  60.4 8.5 %collective-permute-start.7 = (f32[10,21,2,128]{3,2,1,0:T(2,128)S(1)}, f32[10,21,2,128]{3,2,1,0:T(2,128)S(1)}, u32[]{:S(2)}, u32[]{:S(2)}) collective-permute-start(f32[10,21,2,128]{3,2,1,0:T(2,128)S(1)} %get-tuple-element.22), channel_id=1, source_target_pairs={{8,0},{16,8},{24,16},{9,1},{17,9},{25,17},{10,2},{18,10},{26,18},{... | collective-permute-start | bytes 645128 | tf_op jit(solution)/shard_map/ppermute | solution.py:17
  72.2 1.8 %copy-start.1 = (f32[9,17,24,64]{3,1,2,0:T(8,128)S(1)}, f32[9,17,24,64]{3,1,2,0:T(8,128)}, u32[]{:S(2)}) copy-start(f32[9,17,24,64]{3,1,2,0:T(8,128)} %convolution_bitcast_fusion.1) | copy-start | bytes 2820100
  75.7 6.2 %collective-permute-start.8 = (f32[9,17,2,128]{3,2,1,0:T(2,128)S(1)}, f32[9,17,2,128]{3,2,1,0:T(2,128)S(1)}, u32[]{:S(2)}, u32[]{:S(2)}) collective-permute-start(f32[9,17,2,128]{3,2,1,0:T(2,128)S(1)} %get-tuple-element.26), channel_id=1, source_target_pairs={{0,8},{8,16},{16,24},{1,9},{9,17},{17,25},{2,10},{10,18},{18,26},{... | collective-permute-start | bytes 470024 | tf_op jit(solution)/shard_map/ppermute | solution.py:16
  79.2 7.1 %collective-permute-start.9 = (f32[9,17,2,128]{3,2,1,0:T(2,128)S(1)}, f32[9,17,2,128]{3,2,1,0:T(2,128)S(1)}, u32[]{:S(2)}, u32[]{:S(2)}) collective-permute-start(f32[9,17,2,128]{3,2,1,0:T(2,128)S(1)} %get-tuple-element.27), channel_id=1, source_target_pairs={{8,0},{16,8},{24,16},{9,1},{17,9},{25,17},{10,2},{18,10},{26,18},{... | collective-permute-start | bytes 470024 | tf_op jit(solution)/shard_map/ppermute | solution.py:17
  89.6 5.9 %collective-permute-start.10 = (f32[9,13,2,128]{3,2,1,0:T(2,128)S(1)}, f32[9,13,2,128]{3,2,1,0:T(2,128)S(1)}, u32[]{:S(2)}, u32[]{:S(2)}) collective-permute-start(f32[9,13,2,128]{3,2,1,0:T(2,128)S(1)} %get-tuple-element.31), channel_id=1, source_target_pairs={{0,8},{8,16},{16,24},{1,9},{9,17},{17,25},{2,10},{10,18},{18,26},{... | collective-permute-start | bytes 359432 | tf_op jit(solution)/shard_map/ppermute | solution.py:16
  93.1 6.7 %collective-permute-start.11 = (f32[9,13,2,128]{3,2,1,0:T(2,128)S(1)}, f32[9,13,2,128]{3,2,1,0:T(2,128)S(1)}, u32[]{:S(2)}, u32[]{:S(2)}) collective-permute-start(f32[9,13,2,128]{3,2,1,0:T(2,128)S(1)} %get-tuple-element.32), channel_id=1, source_target_pairs={{8,0},{16,8},{24,16},{9,1},{17,9},{25,17},{10,2},{18,10},{26,18},{... | collective-permute-start | bytes 359432 | tf_op jit(solution)/shard_map/ppermute | solution.py:17

commit v14 on v12

--- a/solution.py
+++ b/solution.py
@@ -13,8 +13,13 @@
 
 def x_halo(field, width):
     nx = lax.axis_size("gx")
-    from_left = lax.ppermute(field[:, :, -width:], "gx", shifted(nx, 1))
-    from_right = lax.ppermute(field[:, :, :width], "gx", shifted(nx, -1))
+    me = lax.axis_index("gx")
+    cycle = [(i, (i + 1) % nx) for i in range(nx)]
+    back = [(j, i) for i, j in cycle]
+    from_left = lax.ppermute(field[:, :, -width:], "gx", cycle)
+    from_right = lax.ppermute(field[:, :, :width], "gx", back)
+    from_left = jnp.where(me > 0, from_left, 0.0)
+    from_right = jnp.where(me < nx - 1, from_right, 0.0)
     return jnp.concatenate([from_left, field, from_right], axis=2)
 
 

time: 93.4 us -> 92.1 us (0.986)
  starting transfers between devices: 37.9 us -> 35.3 us
  local copies, waits for them, and re-layouts: 10.1 us -> 12.5 us
    ppermute x6, starting transfers between devices: 14.5 us -> 11.9 us  [the longest x3 9.34 us: x_halo(): from_right = lax.ppermute(field[:, :, :width], 'gx', back)]
    unnamed x32 -> x26, local copies, waits for them, and re-layouts: 3.24 us -> 5.02 us
    select_n x3, other arithmetic: 1.14 us -> 0.05 us  [interp_matrix(): frac = jnp.where(above, 1.0, frac)]
  transfers between devices with their start and end apart: 13 -> 13, of which waited for: 7 -> 7; matrix products, arithmetic and copies ran while one was open for 16% -> 18% of each run, Pallas kernels for 3% -> 3%
where the time goes in v14:
time: 92.1 us; the launch traced here: 91.6 us
  starting transfers between devices  35.3 us (38%)
  waiting for transfers between devices  23.6 us (26%)
  local copies, waits for them, and re-layouts  12.5 us (14%)
  other arithmetic  9.53 us (10%)
  matrix products  5.11 us (6%)
  Pallas kernels  4.22 us (5%)
  between operations  1.43 us (2%)
    ppermute x3, starting transfers between devices, x_halo(): from_right = lax.ppermute(field[:, :, :width], 'gx', back)  9.34 us
    ppermute x3, waiting for transfers between devices, x_halo(): from_left = lax.ppermute(field[:, :, -width:], 'gx', cycle)  9.31 us
    all_to_all x1, waiting for transfers between devices, local(): band = lax.all_to_all(send, 'gy', 2, 1, tiled=True).astype(jnp.float32)  8.42 us
    all_to_all x1, starting transfers between devices, local(): band = lax.all_to_all(send, 'gy', 2, 1, tiled=True).astype(jnp.float32)  6.55 us
    ppermute x3, waiting for transfers between devices, x_halo(): from_right = lax.ppermute(field[:, :, :width], 'gx', back)  5.83 us
    ppermute x1, starting transfers between devices, local(): lows.insert(0, lax.ppermute(region_pay, flat, shifted(n_flat, d)))  5.48 us
    unnamed x26, local copies, waits for them, and re-layouts  5.02 us
    ppermute x1, starting transfers between devices, local(): fine_lo = lax.ppermute(fine_pay[:, -reach_y:], 'gy', shifted(count_y, 1))  4.47 us
  transfers between devices with their start and end apart: 13, of which 7 were waited for; matrix products, arithmetic and copies ran while one was open for 18% of the time, Pallas kernels for 3%

profile of v14, /device:TPU:0, one launch (start us, length us, event | category | flops | bytes accessed | tf_op | source)
XLA Modules:
  0.0 91.6 jit_solution(14240328672971550212)
XLA Ops:
  0.6 1.6 %shard_map.68 = (f32[10,1,24,64]{3,2,1,0:T(8,128)}, f32[1,24,64]{2,1,0:T(8,128)}, f32[1,24,64]{2,1,0:T(8,128)}) custom-call(s32[1,24,64]{2,1,0:T(8,128)} %refs_0_.1, f32[3,8]{1,0:T(4,128)} %refs_1_.3, f32[9,1,24,64]{3,2,1,0:T(8,128)} %refs_2_.1), custom_call_target="tpu_custom_call" | custom-call | tf_op jit(solution)/shard_map/pallas_call | solution.py:53
  2.2 1.3 %collective-permute-start.2 = (f32[10,1,24,64]{3,2,1,0:T(8,128)}, f32[10,1,24,64]{3,2,1,0:T(8,128)S(1)}, u32[]{:S(2)}, u32[]{:S(2)}) collective-permute-start(f32[10,1,24,64]{3,2,1,0:T(8,128)} %get-tuple-element.5), channel_id=1, source_target_pairs={{2,0},{3,1},{4,2},{5,3},{6,4},{7,5},{8,6},{9,7},{10,8},{11,9},{12,... | collective-permute-start | bytes 184328 | tf_op jit(solution)/shard_map/ppermute | solution.py:187
  3.5 5.5 %collective-permute-start.3 = (f32[10,1,24,64]{3,2,1,0:T(8,128)}, f32[10,1,24,64]{3,2,1,0:T(8,128)S(1)}, u32[]{:S(2)}, u32[]{:S(2)}) collective-permute-start(f32[10,1,24,64]{3,2,1,0:T(8,128)} %get-tuple-element.5), channel_id=1, source_target_pairs={{0,2},{1,3},{2,4},{3,5},{4,6},{5,7},{6,8},{7,9},{8,10},{9,11},{10,... | collective-permute-start | bytes 184328 | tf_op jit(solution)/shard_map/ppermute | solution.py:186
  9.0 1.3 %collective-permute-start.1 = (f32[10,1,24,64]{3,2,1,0:T(8,128)}, f32[10,1,24,64]{3,2,1,0:T(8,128)S(1)}, u32[]{:S(2)}, u32[]{:S(2)}) collective-permute-start(f32[10,1,24,64]{3,2,1,0:T(8,128)} %get-tuple-element.5), channel_id=1, source_target_pairs={{1,0},{2,1},{3,2},{4,3},{5,4},{6,5},{7,6},{8,7},{9,8},{10,9},{11,1... | collective-permute-start | bytes 184328 | tf_op jit(solution)/shard_map/ppermute | solution.py:183
  10.3 3.0 %collective-permute-start = (f32[10,1,24,64]{3,2,1,0:T(8,128)}, f32[10,1,24,64]{3,2,1,0:T(8,128)S(1)}, u32[]{:S(2)}, u32[]{:S(2)}) collective-permute-start(f32[10,1,24,64]{3,2,1,0:T(8,128)} %get-tuple-element.5), channel_id=1, source_target_pairs={{0,1},{1,2},{2,3},{3,4},{4,5},{5,6},{6,7},{7,8},{8,9},{9,10},{10,1... | collective-permute-start | bytes 184328 | tf_op jit(solution)/shard_map/ppermute | solution.py:182
  13.3 2.6 %shard_map.69 = f32[12,9,24,128]{3,2,1,0:T(8,128)} custom-call(s32[9,24,128]{2,1,0:T(8,128)} %bitcast.664, f32[3,8]{1,0:T(4,128)} %refs_1_.3, f32[9,9,24,128]{3,2,1,0:T(8,128)} %bitcast.663), custom_call_target="tpu_custom_call" | custom-call | tf_op jit(solution)/shard_map/pallas_call | solution.py:53
  16.0 2.5 %fusion.269 = (f32[12,6,24,128]{3,2,1,0:T(8,128)}, f32[12,6,24,128]{3,2,1,0:T(8,128)S(1)}) fusion(f32[12,9,24,128]{3,2,1,0:T(8,128)} %shard_map.69), kind=kLoop, calls=%fused_computation.494 | loop fusion | bytes 3538944 | tf_op jit(solution)/shard_map/slice | solution.py:180
  18.5 4.5 %collective-permute-start.4 = (f32[12,6,24,128]{3,2,1,0:T(8,128)}, f32[12,6,24,128]{3,2,1,0:T(8,128)S(1)}, u32[]{:S(2)}, u32[]{:S(2)}) collective-permute-start(f32[12,6,24,128]{3,2,1,0:T(8,128)} %get-tuple-element.44), channel_id=1, source_target_pairs={{0,1},{1,2},{2,3},{3,4},{4,5},{5,6},{6,7},{8,9},{9,10},{10,11},{11... | collective-permute-start | bytes 2654216 | tf_op jit(solution)/shard_map/ppermute | solution.py:180
  23.3 1.3 %collective-permute-start.5 = (f32[12,6,24,128]{3,2,1,0:T(8,128)S(1)}, f32[12,6,24,128]{3,2,1,0:T(8,128)S(1)}, u32[]{:S(2)}, u32[]{:S(2)}) collective-permute-start(f32[12,6,24,128]{3,2,1,0:T(8,128)S(1)} %get-tuple-element.45), channel_id=1, source_target_pairs={{1,0},{2,1},{3,2},{4,3},{5,4},{6,5},{7,6},{9,8},{10,9},{11,10},{12... | collective-permute-start | bytes 2654216 | tf_op jit(solution)/shard_map/ppermute | solution.py:181
  25.4 0.6 constant_dynamic-update-slice_fusion.15
  26.5 1.1 %concatenate.325 = bf16[18,1,56,64]{3,2,1,0:T(8,128)(2,1)S(1)} concatenate(bf16[18,1,7,64]{3,2,1,0:T(8,128)(2,1)S(1)} %get-tuple-element.116, bf16[18,1,7,64]{3,2,1,0:T(8,128)(2,1)S(1)} %get-tuple-element.115, bf16[18,1,7,64]{3,2,1,0:T(8,128)(2,1)S(1)} %get-tuple-element.114, bf16[18,1,7,64]{3,2,1,0:T(8,128)(2,1)S(1)} %get-tuple-element.113, ...), dimensions={2} | concatenate | bytes 258048 | tf_op jit(solution)/shard_map/concatenate | solution.py:201
  27.7 0.9 reshape.473
  28.6 6.6 %all-to-all-start = ((bf16[8,2,4032]{2,1,0:T(2,128)(2,1)}), bf16[8,2,4032]{2,1,0:T(2,128)(2,1)S(1)}, u32[]{:S(2)}, u32[]{:S(2)}) async-start(bf16[8,2,4032]{2,1,0:T(2,128)(2,1)} %reshape.473), calls=%async_computation | async-start | bytes 262144 | tf_op jit(solution)/shard_map/all_to_all | solution.py:204
  35.1 0.6 constant_dynamic-update-slice_fusion.14
  35.7 0.6 constant_dynamic-update-slice_fusion.13
  36.3 0.6 constant_dynamic-update-slice_fusion.12
  36.9 0.6 constant_dynamic-update-slice_fusion.11
  37.5 8.4 %all-to-all-done = bf16[8,2,4032]{2,1,0:T(2,128)(2,1)S(1)} async-done(((bf16[8,2,4032]{2,1,0:T(2,128)(2,1)}), bf16[8,2,4032]{2,1,0:T(2,128)(2,1)S(1)}, u32[]{:S(2)}, u32[]{:S(2)}) %all-to-all-start) | async-done | bytes 129056 | tf_op jit(solution)/shard_map/all_to_all | solution.py:204
  45.9 0.2 reshape.474
  46.2 0.6 convolution_bitcast_fusion.1
  46.8 2.3 %convolution_bitcast_fusion = f32[18,17,24,64]{3,1,2,0:T(8,128)S(1)} fusion(f32[18,24,7,64]{3,1,2,0:T(8,128)S(1)} %convolution_bitcast_fusion.1, f32[9,3]{0,1:T(4,128)S(1)} %select_add_fusion, f32[9,3]{0,1:T(4,128)S(1)} %broadcast.1055), kind=kOutput, calls=%fused_computation.5 | convolution fusion | flops 19741744 | bytes 2654424 | tf_op jit(solution)/shard_map/gb,cfbz->cgfz/dot_general | solution.py:218
  49.2 0.2 pad_maximum_fusion.9
  49.4 1.6 %collective-permute-start.6 = (f32[10,21,2,128]{3,2,1,0:T(2,128)S(1)}, f32[10,21,2,128]{3,2,1,0:T(2,128)S(1)}, u32[]{:S(2)}, u32[]{:S(2)}) collective-permute-start(f32[10,21,2,128]{3,2,1,0:T(2,128)S(1)} %get-tuple-element.32), channel_id=1, source_target_pairs={{0,8},{8,16},{16,24},{24,0},{1,9},{9,17},{17,25},{25,1},{2,10},{10... | collective-permute-start | bytes 645128 | tf_op jit(solution)/shard_map/ppermute | solution.py:19
  51.0 2.2 %fusion = f32[18,17,24,128]{3,2,1,0:T(8,128)S(1)} fusion(f32[18,17,24,64]{3,1,2,0:T(8,128)S(1)} %convolution_bitcast_fusion, f32[128]{0:T(128)S(1)} %get-tuple-element.158, s32[128]{0:T(128)S(1)} %get-tuple-element.161, f32[128]{0:T(128)S(1)} %get-tuple-element.159, s32[128]{0:T(128)S(1)} %get-tuple-element.160), kind=kOutput, calls=%fused_computation | convolution fusion | flops 361013248 | bytes 5642240 | tf_op jit(solution)/shard_map/kz,cgfz->cgfk/dot_general | solution.py:219
  53.2 2.5 %collective-permute-start.7 = (f32[10,21,2,128]{3,2,1,0:T(2,128)S(1)}, f32[10,21,2,128]{3,2,1,0:T(2,128)S(1)}, u32[]{:S(2)}, u32[]{:S(2)}) collective-permute-start(f32[10,21,2,128]{3,2,1,0:T(2,128)S(1)} %get-tuple-element.33), channel_id=1, source_target_pairs={{8,0},{16,8},{24,16},{0,24},{9,1},{17,9},{25,17},{1,25},{10,2},{18... | collective-permute-start | bytes 645128 | tf_op jit(solution)/shard_map/ppermute | solution.py:20
  55.6 0.2 pad_maximum_fusion.1
  55.8 0.2 slice.1191
  56.0 2.6 %collective-permute-done.6 = f32[10,21,2,128]{3,2,1,0:T(2,128)S(1)} collective-permute-done((f32[10,21,2,128]{3,2,1,0:T(2,128)S(1)}, f32[10,21,2,128]{3,2,1,0:T(2,128)S(1)}, u32[]{:S(2)}, u32[]{:S(2)}) %collective-permute-start.6) | collective-permute-done | bytes 215072 | tf_op jit(solution)/shard_map/ppermute | solution.py:19
  58.7 3.8 %collective-permute-done.7 = f32[10,21,2,128]{3,2,1,0:T(2,128)S(1)} collective-permute-done((f32[10,21,2,128]{3,2,1,0:T(2,128)S(1)}, f32[10,21,2,128]{3,2,1,0:T(2,128)S(1)}, u32[]{:S(2)}, u32[]{:S(2)}) %collective-permute-start.7) | collective-permute-done | bytes 215072 | tf_op jit(solution)/shard_map/ppermute | solution.py:20
  62.7 0.6 pad_maximum_fusion
  63.3 0.2 slice_bitcast_fusion.3
  63.4 0.2 fusion.272
  63.6 0.2 fusion.21
  63.8 0.2 fusion.270
  64.0 0.4 fusion.32
  64.4 0.3 slice_add_fusion
  64.9 0.2 fusion.82
  65.1 0.2 slice_bitcast_fusion.4
  65.6 0.2 fusion.71
  65.9 0.1 fusion.63
  66.1 0.1 fusion.56
  66.2 0.5 fusion.6
  66.8 0.6 collective-permute-start.8
  67.4 0.6 constant_dynamic-update-slice_fusion.10
  68.0 3.3 %collective-permute-start.9 = (f32[9,17,2,128]{3,2,1,0:T(2,128)S(1)}, f32[9,17,2,128]{3,2,1,0:T(2,128)S(1)}, u32[]{:S(2)}, u32[]{:S(2)}) collective-permute-start(f32[9,17,2,128]{3,2,1,0:T(2,128)S(1)} %get-tuple-element.38), channel_id=1, source_target_pairs={{8,0},{16,8},{24,16},{0,24},{9,1},{17,9},{25,17},{1,25},{10,2},{18... | collective-permute-start | bytes 470024 | tf_op jit(solution)/shard_map/ppermute | solution.py:20
  71.4 4.3 %collective-permute-done.8 = f32[9,17,2,128]{3,2,1,0:T(2,128)S(1)} collective-permute-done((f32[9,17,2,128]{3,2,1,0:T(2,128)S(1)}, f32[9,17,2,128]{3,2,1,0:T(2,128)S(1)}, u32[]{:S(2)}, u32[]{:S(2)}) %collective-permute-start.8) | collective-permute-done | bytes 156704 | tf_op jit(solution)/shard_map/ppermute | solution.py:19
  75.7 1.1 %collective-permute-done.9 = f32[9,17,2,128]{3,2,1,0:T(2,128)S(1)} collective-permute-done((f32[9,17,2,128]{3,2,1,0:T(2,128)S(1)}, f32[9,17,2,128]{3,2,1,0:T(2,128)S(1)}, u32[]{:S(2)}, u32[]{:S(2)}) %collective-permute-start.9) | collective-permute-done | bytes 156704 | tf_op jit(solution)/shard_map/ppermute | solution.py:20
  77.0 0.4 pad_maximum_fusion.2
  77.6 0.1 fusion.274
  77.7 0.1 fusion.275
  77.9 0.2 fusion.49
  78.0 0.2 fusion.44
  78.2 0.2 fusion.38
  78.3 0.2 slice_add_fusion.1
  78.8 0.2 fusion.138
  79.5 0.1 fusion.112
  79.7 0.4 fusion.12
  80.2 0.3 collective-permute-start.10
  80.5 0.6 constant_dynamic-update-slice_fusion.9
  81.1 3.6 %collective-permute-start.11 = (f32[9,13,2,128]{3,2,1,0:T(2,128)S(1)}, f32[9,13,2,128]{3,2,1,0:T(2,128)S(1)}, u32[]{:S(2)}, u32[]{:S(2)}) collective-permute-start(f32[9,13,2,128]{3,2,1,0:T(2,128)S(1)} %get-tuple-element.43), channel_id=1, source_target_pairs={{8,0},{16,8},{24,16},{0,24},{9,1},{17,9},{25,17},{1,25},{10,2},{18... | collective-permute-start | bytes 359432 | tf_op jit(solution)/shard_map/ppermute | solution.py:20
  84.7 2.4 %collective-permute-done.10 = f32[9,13,2,128]{3,2,1,0:T(2,128)S(1)} collective-permute-done((f32[9,13,2,128]{3,2,1,0:T(2,128)S(1)}, f32[9,13,2,128]{3,2,1,0:T(2,128)S(1)}, u32[]{:S(2)}, u32[]{:S(2)}) %collective-permute-start.10) | collective-permute-done | bytes 119840 | tf_op jit(solution)/shard_map/ppermute | solution.py:19
  87.2 0.9 collective-permute-done.11
  88.3 0.3 pad_maximum_fusion.3
  90.4 1.2 %fusion.16 = f32[9,24,9,128]{3,1,2,0:T(8,128)} fusion(f32[9,9,24,128]{3,2,1,0:T(8,128)S(1)} %fusion.151, f32[18,17,24,128]{3,2,1,0:T(8,128)S(1)} %fusion, f32[9,24]{1,0:T(8,128)S(1)} %slice.1318), kind=kLoop, calls=%fused_computation.25 | loop fusion | flops 1244160 | bytes 3982176 | tf_op jit(solution)/shard_map/transpose | solution.py:255
  (104 shorter events, 5.5 us)
Async XLA Ops:
  2.2 22.7 %collective-permute-start.2 = (f32[10,1,24,64]{3,2,1,0:T(8,128)}, f32[10,1,24,64]{3,2,1,0:T(8,128)S(1)}, u32[]{:S(2)}, u32[]{:S(2)}) collective-permute-start(f32[10,1,24,64]{3,2,1,0:T(8,128)} %get-tuple-element.5), channel_id=1, source_target_pairs={{2,0},{3,1},{4,2},{5,3},{6,4},{7,5},{8,6},{9,7},{10,8},{11,9},{12,... | collective-permute-start | bytes 184328 | tf_op jit(solution)/shard_map/ppermute | solution.py:187
  3.5 19.7 %collective-permute-start.3 = (f32[10,1,24,64]{3,2,1,0:T(8,128)}, f32[10,1,24,64]{3,2,1,0:T(8,128)S(1)}, u32[]{:S(2)}, u32[]{:S(2)}) collective-permute-start(f32[10,1,24,64]{3,2,1,0:T(8,128)} %get-tuple-element.5), channel_id=1, source_target_pairs={{0,2},{1,3},{2,4},{3,5},{4,6},{5,7},{6,8},{7,9},{8,10},{9,11},{10,... | collective-permute-start | bytes 184328 | tf_op jit(solution)/shard_map/ppermute | solution.py:186
  9.0 15.7 %collective-permute-start.1 = (f32[10,1,24,64]{3,2,1,0:T(8,128)}, f32[10,1,24,64]{3,2,1,0:T(8,128)S(1)}, u32[]{:S(2)}, u32[]{:S(2)}) collective-permute-start(f32[10,1,24,64]{3,2,1,0:T(8,128)} %get-tuple-element.5), channel_id=1, source_target_pairs={{1,0},{2,1},{3,2},{4,3},{5,4},{6,5},{7,6},{8,7},{9,8},{10,9},{11,1... | collective-permute-start | bytes 184328 | tf_op jit(solution)/shard_map/ppermute | solution.py:183
  10.3 14.3 %collective-permute-start = (f32[10,1,24,64]{3,2,1,0:T(8,128)}, f32[10,1,24,64]{3,2,1,0:T(8,128)S(1)}, u32[]{:S(2)}, u32[]{:S(2)}) collective-permute-start(f32[10,1,24,64]{3,2,1,0:T(8,128)} %get-tuple-element.5), channel_id=1, source_target_pairs={{0,1},{1,2},{2,3},{3,4},{4,5},{5,6},{6,7},{7,8},{8,9},{9,10},{10,1... | collective-permute-start | bytes 184328 | tf_op jit(solution)/shard_map/ppermute | solution.py:182
  16.0 7.2 %copy-start.1 = (f32[9,1,24,64]{3,2,1,0:T(8,128)S(1)}, f32[9,1,24,64]{3,2,1,0:T(8,128)}, u32[]{:S(2)}) copy-start(f32[9,1,24,64]{3,2,1,0:T(8,128)} %refs_2_.1) | copy-start | bytes 165892
  16.0 8.7 %copy-start.3 = (f32[10,1,24,64]{3,2,1,0:T(8,128)S(1)}, f32[10,1,24,64]{3,2,1,0:T(8,128)}, u32[]{:S(2)}) copy-start(f32[10,1,24,64]{3,2,1,0:T(8,128)} %get-tuple-element.5) | copy-start | bytes 184324
  18.5 30.7 %collective-permute-start.4 = (f32[12,6,24,128]{3,2,1,0:T(8,128)}, f32[12,6,24,128]{3,2,1,0:T(8,128)S(1)}, u32[]{:S(2)}, u32[]{:S(2)}) collective-permute-start(f32[12,6,24,128]{3,2,1,0:T(8,128)} %get-tuple-element.44), channel_id=1, source_target_pairs={{0,1},{1,2},{2,3},{3,4},{4,5},{5,6},{6,7},{8,9},{9,10},{10,11},{11... | collective-permute-start | bytes 2654216 | tf_op jit(solution)/shard_map/ppermute | solution.py:180
  23.3 25.9 %collective-permute-start.5 = (f32[12,6,24,128]{3,2,1,0:T(8,128)S(1)}, f32[12,6,24,128]{3,2,1,0:T(8,128)S(1)}, u32[]{:S(2)}, u32[]{:S(2)}) collective-permute-start(f32[12,6,24,128]{3,2,1,0:T(8,128)S(1)} %get-tuple-element.45), channel_id=1, source_target_pairs={{1,0},{2,1},{3,2},{4,3},{5,4},{6,5},{7,6},{9,8},{10,9},{11,10},{12... | collective-permute-start | bytes 2654216 | tf_op jit(solution)/shard_map/ppermute | solution.py:181
  24.7 1.3 %copy-start.2 = (f32[1,24,64]{2,1,0:T(8,128)S(1)}, f32[1,24,64]{2,1,0:T(8,128)}, u32[]{:S(2)}) copy-start(f32[1,24,64]{2,1,0:T(8,128)} %get-tuple-element.7) | copy-start | bytes 18436
  24.7 1.3 %copy-start.4 = (f32[1,24,64]{2,1,0:T(8,128)S(1)}, f32[1,24,64]{2,1,0:T(8,128)}, u32[]{:S(2)}) copy-start(f32[1,24,64]{2,1,0:T(8,128)} %get-tuple-element.6) | copy-start | bytes 18436
  28.6 17.4 %all-to-all-start = ((bf16[8,2,4032]{2,1,0:T(2,128)(2,1)}), bf16[8,2,4032]{2,1,0:T(2,128)(2,1)S(1)}, u32[]{:S(2)}, u32[]{:S(2)}) async-start(bf16[8,2,4032]{2,1,0:T(2,128)(2,1)} %reshape.473), calls=%async_computation | async-start | bytes 262144 | tf_op jit(solution)/shard_map/all_to_all | solution.py:204
  46.8 2.4 %copy-start = (f32[12,9,24,128]{3,2,1,0:T(8,128)S(1)}, f32[12,9,24,128]{3,2,1,0:T(8,128)}, u32[]{:S(2)}) copy-start(f32[12,9,24,128]{3,2,1,0:T(8,128)} %shard_map.69) | copy-start | bytes 3981316
  49.4 9.3 %collective-permute-start.6 = (f32[10,21,2,128]{3,2,1,0:T(2,128)S(1)}, f32[10,21,2,128]{3,2,1,0:T(2,128)S(1)}, u32[]{:S(2)}, u32[]{:S(2)}) collective-permute-start(f32[10,21,2,128]{3,2,1,0:T(2,128)S(1)} %get-tuple-element.32), channel_id=1, source_target_pairs={{0,8},{8,16},{16,24},{24,0},{1,9},{9,17},{17,25},{25,1},{2,10},{10... | collective-permute-start | bytes 645128 | tf_op jit(solution)/shard_map/ppermute | solution.py:19
  53.2 9.4 %collective-permute-start.7 = (f32[10,21,2,128]{3,2,1,0:T(2,128)S(1)}, f32[10,21,2,128]{3,2,1,0:T(2,128)S(1)}, u32[]{:S(2)}, u32[]{:S(2)}) collective-permute-start(f32[10,21,2,128]{3,2,1,0:T(2,128)S(1)} %get-tuple-element.33), channel_id=1, source_target_pairs={{8,0},{16,8},{24,16},{0,24},{9,1},{17,9},{25,17},{1,25},{10,2},{18... | collective-permute-start | bytes 645128 | tf_op jit(solution)/shard_map/ppermute | solution.py:20
  66.8 8.8 %collective-permute-start.8 = (f32[9,17,2,128]{3,2,1,0:T(2,128)S(1)}, f32[9,17,2,128]{3,2,1,0:T(2,128)S(1)}, u32[]{:S(2)}, u32[]{:S(2)}) collective-permute-start(f32[9,17,2,128]{3,2,1,0:T(2,128)S(1)} %get-tuple-element.37), channel_id=1, source_target_pairs={{0,8},{8,16},{16,24},{24,0},{1,9},{9,17},{17,25},{25,1},{2,10},{10... | collective-permute-start | bytes 470024 | tf_op jit(solution)/shard_map/ppermute | solution.py:19
  68.0 8.8 %collective-permute-start.9 = (f32[9,17,2,128]{3,2,1,0:T(2,128)S(1)}, f32[9,17,2,128]{3,2,1,0:T(2,128)S(1)}, u32[]{:S(2)}, u32[]{:S(2)}) collective-permute-start(f32[9,17,2,128]{3,2,1,0:T(2,128)S(1)} %get-tuple-element.38), channel_id=1, source_target_pairs={{8,0},{16,8},{24,16},{0,24},{9,1},{17,9},{25,17},{1,25},{10,2},{18... | collective-permute-start | bytes 470024 | tf_op jit(solution)/shard_map/ppermute | solution.py:20
  80.2 7.0 %collective-permute-start.10 = (f32[9,13,2,128]{3,2,1,0:T(2,128)S(1)}, f32[9,13,2,128]{3,2,1,0:T(2,128)S(1)}, u32[]{:S(2)}, u32[]{:S(2)}) collective-permute-start(f32[9,13,2,128]{3,2,1,0:T(2,128)S(1)} %get-tuple-element.42), channel_id=1, source_target_pairs={{0,8},{8,16},{16,24},{24,0},{1,9},{9,17},{17,25},{25,1},{2,10},{10... | collective-permute-start | bytes 359432 | tf_op jit(solution)/shard_map/ppermute | solution.py:19
  81.1 7.0 %collective-permute-start.11 = (f32[9,13,2,128]{3,2,1,0:T(2,128)S(1)}, f32[9,13,2,128]{3,2,1,0:T(2,128)S(1)}, u32[]{:S(2)}, u32[]{:S(2)}) collective-permute-start(f32[9,13,2,128]{3,2,1,0:T(2,128)S(1)} %get-tuple-element.43), channel_id=1, source_target_pairs={{8,0},{16,8},{24,16},{0,24},{9,1},{17,9},{25,17},{1,25},{10,2},{18... | collective-permute-start | bytes 359432 | tf_op jit(solution)/shard_map/ppermute | solution.py:20

commit v15 on v14

--- a/solution.py
+++ b/solution.py
@@ -9,6 +9,11 @@
 
 def shifted(n, s):
     return [(i, i + s) for i in range(n) if 0 <= i + s < n]
+
+
+def from_cycle(field, axis, n, d, me):
+    got = lax.ppermute(field, axis, [(i, (i + d) % n) for i in range(n)])
+    return jnp.where((me - d >= 0) & (me - d < n), got, 0.0)
 
 
 def x_halo(field, width):
@@ -177,14 +182,15 @@
         True,
     )
 
-    fine_lo = lax.ppermute(fine_pay[:, -reach_y:], "gy", shifted(count_y, 1))
-    fine_hi = lax.ppermute(fine_pay[:, :reach_y], "gy", shifted(count_y, -1))
-    reg_lo = lax.ppermute(region_pay, flat, shifted(n_flat, 1))
-    reg_hi = lax.ppermute(region_pay, flat, shifted(n_flat, -1))
+    me_flat = lax.axis_index("gx") * count_y + me_y
+    fine_lo = from_cycle(fine_pay[:, -reach_y:], "gy", count_y, 1, me_y)
+    fine_hi = from_cycle(fine_pay[:, :reach_y], "gy", count_y, -1, me_y)
+    reg_lo = from_cycle(region_pay, flat, n_flat, 1, me_flat)
+    reg_hi = from_cycle(region_pay, flat, n_flat, -1, me_flat)
     lows, highs = [reg_lo], [reg_hi]
     for d in range(2, -(-2 // own) + 1):
-        lows.insert(0, lax.ppermute(region_pay, flat, shifted(n_flat, d)))
-        highs.append(lax.ppermute(region_pay, flat, shifted(n_flat, -d)))
+        lows.insert(0, from_cycle(region_pay, flat, n_flat, d, me_flat))
+        highs.append(from_cycle(region_pay, flat, n_flat, -d, me_flat))
     reg_ext = jnp.concatenate(
         [jnp.concatenate(lows, 1)[:, -2:], region_pay, jnp.concatenate(highs, 1)[:, :2]], 1
     )

time: 92.1 us -> 85.9 us (0.933)
  starting transfers between devices: 35.3 us -> 25.9 us
  waiting for transfers between devices: 23.6 us -> 26.2 us
  other arithmetic: 9.53 us -> 11.2 us
    ppermute x6, starting transfers between devices: 16.9 us -> 10.6 us  [from_cycle(): got = lax.ppermute(field, axis, [(i, (i + d) % n) for i in range(n)])]
    all_to_all x1, starting transfers between devices: 6.55 us -> 3.37 us  [local(): band = lax.all_to_all(send, 'gy', 2, 1, tiled=True).astype(jnp.float32)]
    all_to_all x1, waiting for transfers between devices: 8.42 us -> 10.5 us  [local(): band = lax.all_to_all(send, 'gy', 2, 1, tiled=True).astype(jnp.float32)]
    ppermute x3, starting transfers between devices: 2.57 us -> 1.11 us  [x_halo(): from_left = lax.ppermute(field[:, :, -width:], 'gx', cycle)]
    ppermute x3, starting transfers between devices: 9.34 us -> 10.8 us  [x_halo(): from_right = lax.ppermute(field[:, :, :width], 'gx', back)]
    select_n x0 -> x6, other arithmetic: none -> 1.44 us  [from_cycle(): return jnp.where((me - d >= 0) & (me - d < n), got, 0.0)]
    unnamed x26 -> x22, local copies, waits for them, and re-layouts: 5.02 us -> 5.11 us
  transfers between devices with their start and end apart: 13 -> 13, of which waited for: 7 -> 8; matrix products, arithmetic and copies ran while one was open for 18% -> 18% of each run, Pallas kernels for 3% -> 3%
where the time goes in v15:
time: 85.9 us; the launch traced here: 85.6 us
  waiting for transfers between devices  26.2 us (31%)
  starting transfers between devices  25.9 us (30%)
  local copies, waits for them, and re-layouts  11.6 us (14%)
  other arithmetic  11.2 us (13%)
  matrix products  5.14 us (6%)
  Pallas kernels  4.21 us (5%)
  between operations  1.39 us (2%)
    ppermute x3, starting transfers between devices, x_halo(): from_right = lax.ppermute(field[:, :, :width], 'gx', back)  10.8 us
    ppermute x6, starting transfers between devices, from_cycle(): got = lax.ppermute(field, axis, [(i, (i + d) % n) for i in range(n)])  10.6 us
    all_to_all x1, waiting for transfers between devices, local(): band = lax.all_to_all(send, 'gy', 2, 1, tiled=True).astype(jnp.float32)  10.5 us
    ppermute x3, waiting for transfers between devices, x_halo(): from_left = lax.ppermute(field[:, :, -width:], 'gx', cycle)  9.57 us
    ppermute x3, waiting for transfers between devices, x_halo(): from_right = lax.ppermute(field[:, :, :width], 'gx', back)  5.31 us
    unnamed x22, local copies, waits for them, and re-layouts  5.11 us
    pallas_call x2, Pallas kernels, lookup(): pl.pallas_call(lambda *refs: lookup_kernel(step, extra, *refs), out_shape...  4.21 us
    all_to_all x1, starting transfers between devices, local(): band = lax.all_to_all(send, 'gy', 2, 1, tiled=True).astype(jnp.float32)  3.37 us
  transfers between devices with their start and end apart: 13, of which 8 were waited for; matrix products, arithmetic and copies ran while one was open for 18% of the time, Pallas kernels for 3%

profile of v15, /device:TPU:0, one launch (start us, length us, event | category | flops | bytes accessed | tf_op | source)
XLA Modules:
  0.0 85.6 jit_solution(10040207977898478791)
XLA Ops:
  0.6 1.6 %shard_map.68 = (f32[10,1,24,64]{3,2,1,0:T(8,128)}, f32[1,24,64]{2,1,0:T(8,128)}, f32[1,24,64]{2,1,0:T(8,128)}) custom-call(s32[1,24,64]{2,1,0:T(8,128)} %refs_0_.1, f32[3,8]{1,0:T(4,128)} %refs_1_.3, f32[9,1,24,64]{3,2,1,0:T(8,128)} %refs_2_.1), custom_call_target="tpu_custom_call" | custom-call | tf_op jit(solution)/shard_map/pallas_call | solution.py:58
  2.2 2.9 %collective-permute-start.3 = (f32[10,1,24,64]{3,2,1,0:T(8,128)}, f32[10,1,24,64]{3,2,1,0:T(8,128)}, u32[]{:S(2)}, u32[]{:S(2)}) collective-permute-start(f32[10,1,24,64]{3,2,1,0:T(8,128)} %get-tuple-element.5), channel_id=1, source_target_pairs={{0,2},{1,3},{2,4},{3,5},{4,6},{5,7},{6,8},{7,9},{8,10},{9,11},{10,... | collective-permute-start | bytes 184328 | tf_op jit(solution)/shard_map/ppermute | solution.py:15
  5.2 4.0 %collective-permute-start.2 = (f32[10,1,24,64]{3,2,1,0:T(8,128)}, f32[10,1,24,64]{3,2,1,0:T(8,128)S(1)}, u32[]{:S(2)}, u32[]{:S(2)}) collective-permute-start(f32[10,1,24,64]{3,2,1,0:T(8,128)} %get-tuple-element.5), channel_id=1, source_target_pairs={{0,30},{1,31},{2,0},{3,1},{4,2},{5,3},{6,4},{7,5},{8,6},{9,7},{10,... | collective-permute-start | bytes 184328 | tf_op jit(solution)/shard_map/ppermute | solution.py:15
  9.2 0.9 %collective-permute-start.1 = (f32[10,1,24,64]{3,2,1,0:T(8,128)}, f32[10,1,24,64]{3,2,1,0:T(8,128)S(1)}, u32[]{:S(2)}, u32[]{:S(2)}) collective-permute-start(f32[10,1,24,64]{3,2,1,0:T(8,128)} %get-tuple-element.5), channel_id=1, source_target_pairs={{0,31},{1,0},{2,1},{3,2},{4,3},{5,4},{6,5},{7,6},{8,7},{9,8},{10,9... | collective-permute-start | bytes 184328 | tf_op jit(solution)/shard_map/ppermute | solution.py:15
  10.1 2.6 %shard_map.69 = f32[12,9,24,128]{3,2,1,0:T(8,128)} custom-call(s32[9,24,128]{2,1,0:T(8,128)} %bitcast.664, f32[3,8]{1,0:T(4,128)} %refs_1_.3, f32[9,9,24,128]{3,2,1,0:T(8,128)} %bitcast.663), custom_call_target="tpu_custom_call" | custom-call | tf_op jit(solution)/shard_map/pallas_call | solution.py:58
  12.7 1.6 %fusion.270 = (f32[12,6,24,128]{3,2,1,0:T(8,128)S(1)}, f32[12,6,24,128]{3,2,1,0:T(8,128)S(1)}) fusion(f32[12,9,24,128]{3,2,1,0:T(8,128)} %shard_map.69), kind=kLoop, calls=%fused_computation.496 | loop fusion | bytes 3538944 | tf_op jit(solution)/shard_map/slice | solution.py:186
  14.3 0.4 collective-permute-start.4
  15.1 2.3 %collective-permute-start.5 = (f32[12,6,24,128]{3,2,1,0:T(8,128)S(1)}, f32[12,6,24,128]{3,2,1,0:T(8,128)}, u32[]{:S(2)}, u32[]{:S(2)}) collective-permute-start(f32[12,6,24,128]{3,2,1,0:T(8,128)S(1)} %get-tuple-element.45), channel_id=1, source_target_pairs={{0,7},{1,0},{2,1},{3,2},{4,3},{5,4},{6,5},{7,6},{8,15},{9,8},{10,9... | collective-permute-start | bytes 2654216 | tf_op jit(solution)/shard_map/ppermute | solution.py:15
  17.4 0.8 collective-permute-done
  19.1 0.6 constant_dynamic-update-slice_fusion.6
  20.2 1.1 %concatenate.325 = bf16[18,1,56,64]{3,2,1,0:T(8,128)(2,1)S(1)} concatenate(bf16[18,1,7,64]{3,2,1,0:T(8,128)(2,1)S(1)} %get-tuple-element.106, bf16[18,1,7,64]{3,2,1,0:T(8,128)(2,1)S(1)} %get-tuple-element.105, bf16[18,1,7,64]{3,2,1,0:T(8,128)(2,1)S(1)} %get-tuple-element.104, bf16[18,1,7,64]{3,2,1,0:T(8,128)(2,1)S(1)} %get-tuple-element.103, ...), dimensions={2} | concatenate | bytes 258048 | tf_op jit(solution)/shard_map/concatenate | solution.py:207
  21.4 0.9 %reshape.473 = bf16[8,2,4032]{2,1,0:T(2,128)(2,1)} reshape(bf16[56,1,18,64]{3,2,1,0:T(8,128)(2,1)S(1)} %bitcast.661) | data formatting | bytes 258048
  22.3 3.4 %all-to-all-start = ((bf16[8,2,4032]{2,1,0:T(2,128)(2,1)}), bf16[8,2,4032]{2,1,0:T(2,128)(2,1)S(1)}, u32[]{:S(2)}, u32[]{:S(2)}) async-start(bf16[8,2,4032]{2,1,0:T(2,128)(2,1)} %reshape.473), calls=%async_computation | async-start | bytes 262144 | tf_op jit(solution)/shard_map/all_to_all | solution.py:210
  25.7 0.6 constant_dynamic-update-slice_fusion.5
  26.3 0.6 constant_dynamic-update-slice_fusion.4
  26.9 0.6 constant_dynamic-update-slice_fusion.3
  27.5 0.6 constant_dynamic-update-slice_fusion.2
  28.1 10.5 %all-to-all-done = bf16[8,2,4032]{2,1,0:T(2,128)(2,1)S(1)} async-done(((bf16[8,2,4032]{2,1,0:T(2,128)(2,1)}), bf16[8,2,4032]{2,1,0:T(2,128)(2,1)S(1)}, u32[]{:S(2)}, u32[]{:S(2)}) %all-to-all-start) | async-done | bytes 129056 | tf_op jit(solution)/shard_map/all_to_all | solution.py:210
  38.6 0.2 reshape.474
  38.8 0.6 convolution_bitcast_fusion.1
  39.4 2.4 %convolution_bitcast_fusion = f32[18,17,24,64]{3,1,2,0:T(8,128)S(1)} fusion(f32[18,24,7,64]{3,1,2,0:T(8,128)S(1)} %convolution_bitcast_fusion.1, f32[9,3]{0,1:T(4,128)S(1)} %select_add_fusion, f32[9,3]{0,1:T(4,128)S(1)} %broadcast.1055), kind=kOutput, calls=%fused_computation.5 | convolution fusion | flops 19741744 | bytes 2654424 | tf_op jit(solution)/shard_map/gb,cfbz->cgfz/dot_general | solution.py:224
  41.9 1.3 %broadcast_select_fusion = f32[12,6,24,128]{3,2,1,0:T(8,128)S(1)} fusion(f32[12,6,24,128]{3,2,1,0:T(8,128)} %collective-permute-done.5, pred[]{:T(512)S(6)} %and.80), kind=kLoop, calls=%fused_computation.34 | loop fusion | flops 221184 | bytes 1769473 | tf_op jit(solution)/shard_map/jit(_where)/select_n | solution.py:16
  43.3 0.2 copy-done
  43.4 0.1 pad_maximum_fusion.10
  43.7 2.2 %fusion = f32[18,17,24,128]{3,2,1,0:T(8,128)S(1)} fusion(f32[18,17,24,64]{3,1,2,0:T(8,128)S(1)} %convolution_bitcast_fusion, f32[128]{0:T(128)S(1)} %get-tuple-element.148, s32[128]{0:T(128)S(1)} %get-tuple-element.151, f32[128]{0:T(128)S(1)} %get-tuple-element.149, s32[128]{0:T(128)S(1)} %get-tuple-element.150), kind=kOutput, calls=%fused_computation | convolution fusion | flops 361013248 | bytes 5642240 | tf_op jit(solution)/shard_map/kz,cgfz->cgfk/dot_general | solution.py:225
  45.8 4.0 %collective-permute-start.7 = (f32[10,21,2,128]{3,2,1,0:T(2,128)S(1)}, f32[10,21,2,128]{3,2,1,0:T(2,128)S(1)}, u32[]{:S(2)}, u32[]{:S(2)}) collective-permute-start(f32[10,21,2,128]{3,2,1,0:T(2,128)S(1)} %get-tuple-element.33), channel_id=1, source_target_pairs={{8,0},{16,8},{24,16},{0,24},{9,1},{17,9},{25,17},{1,25},{10,2},{18... | collective-permute-start | bytes 645128 | tf_op jit(solution)/shard_map/ppermute | solution.py:25
  49.8 0.2 pad_maximum_fusion.1
  50.0 0.2 slice.1179
  50.2 2.3 %collective-permute-done.6 = f32[10,21,2,128]{3,2,1,0:T(2,128)S(1)} collective-permute-done((f32[10,21,2,128]{3,2,1,0:T(2,128)S(1)}, f32[10,21,2,128]{3,2,1,0:T(2,128)S(1)}, u32[]{:S(2)}, u32[]{:S(2)}) %collective-permute-start.6) | collective-permute-done | bytes 215072 | tf_op jit(solution)/shard_map/ppermute | solution.py:24
  52.6 3.8 %collective-permute-done.7 = f32[10,21,2,128]{3,2,1,0:T(2,128)S(1)} collective-permute-done((f32[10,21,2,128]{3,2,1,0:T(2,128)S(1)}, f32[10,21,2,128]{3,2,1,0:T(2,128)S(1)}, u32[]{:S(2)}, u32[]{:S(2)}) %collective-permute-start.7) | collective-permute-done | bytes 215072 | tf_op jit(solution)/shard_map/ppermute | solution.py:25
  56.5 0.6 pad_maximum_fusion
  57.2 0.2 slice_bitcast_fusion.3
  57.3 0.2 fusion.273
  57.5 0.2 fusion.21
  57.7 0.2 fusion.271
  57.9 0.4 fusion.32
  58.3 0.3 slice_add_fusion
  58.8 0.2 fusion.82
  59.0 0.2 slice_bitcast_fusion.4
  59.5 0.2 fusion.71
  59.8 0.1 fusion.63
  60.0 0.1 fusion.56
  60.1 0.5 fusion.6
  60.7 0.7 collective-permute-start.8
  61.4 0.6 constant_dynamic-update-slice_fusion.1
  62.0 3.2 %collective-permute-start.9 = (f32[9,17,2,128]{3,2,1,0:T(2,128)S(1)}, f32[9,17,2,128]{3,2,1,0:T(2,128)S(1)}, u32[]{:S(2)}, u32[]{:S(2)}) collective-permute-start(f32[9,17,2,128]{3,2,1,0:T(2,128)S(1)} %get-tuple-element.38), channel_id=1, source_target_pairs={{8,0},{16,8},{24,16},{0,24},{9,1},{17,9},{25,17},{1,25},{10,2},{18... | collective-permute-start | bytes 470024 | tf_op jit(solution)/shard_map/ppermute | solution.py:25
  65.2 4.3 %collective-permute-done.8 = f32[9,17,2,128]{3,2,1,0:T(2,128)S(1)} collective-permute-done((f32[9,17,2,128]{3,2,1,0:T(2,128)S(1)}, f32[9,17,2,128]{3,2,1,0:T(2,128)S(1)}, u32[]{:S(2)}, u32[]{:S(2)}) %collective-permute-start.8) | collective-permute-done | bytes 156704 | tf_op jit(solution)/shard_map/ppermute | solution.py:24
  69.6 1.4 %collective-permute-done.9 = f32[9,17,2,128]{3,2,1,0:T(2,128)S(1)} collective-permute-done((f32[9,17,2,128]{3,2,1,0:T(2,128)S(1)}, f32[9,17,2,128]{3,2,1,0:T(2,128)S(1)}, u32[]{:S(2)}, u32[]{:S(2)}) %collective-permute-start.9) | collective-permute-done | bytes 156704 | tf_op jit(solution)/shard_map/ppermute | solution.py:25
  71.2 0.4 pad_maximum_fusion.2
  71.8 0.1 fusion.275
  71.9 0.1 fusion.276
  72.1 0.2 fusion.49
  72.2 0.2 fusion.44
  72.4 0.2 fusion.38
  72.6 0.2 slice_add_fusion.1
  73.1 0.2 fusion.138
  73.7 0.1 fusion.112
  73.9 0.4 fusion.12
  74.4 0.3 collective-permute-start.10
  74.7 0.6 constant_dynamic-update-slice_fusion
  75.3 3.6 %collective-permute-start.11 = (f32[9,13,2,128]{3,2,1,0:T(2,128)S(1)}, f32[9,13,2,128]{3,2,1,0:T(2,128)S(1)}, u32[]{:S(2)}, u32[]{:S(2)}) collective-permute-start(f32[9,13,2,128]{3,2,1,0:T(2,128)S(1)} %get-tuple-element.43), channel_id=1, source_target_pairs={{8,0},{16,8},{24,16},{0,24},{9,1},{17,9},{25,17},{1,25},{10,2},{18... | collective-permute-start | bytes 359432 | tf_op jit(solution)/shard_map/ppermute | solution.py:25
  78.9 3.0 %collective-permute-done.10 = f32[9,13,2,128]{3,2,1,0:T(2,128)S(1)} collective-permute-done((f32[9,13,2,128]{3,2,1,0:T(2,128)S(1)}, f32[9,13,2,128]{3,2,1,0:T(2,128)S(1)}, u32[]{:S(2)}, u32[]{:S(2)}) %collective-permute-start.10) | collective-permute-done | bytes 119840 | tf_op jit(solution)/shard_map/ppermute | solution.py:24
  82.2 0.4 pad_maximum_fusion.3
  84.4 1.2 %fusion.16 = f32[9,24,9,128]{3,1,2,0:T(8,128)} fusion(f32[9,9,24,128]{3,2,1,0:T(8,128)S(1)} %fusion.151, f32[18,17,24,128]{3,2,1,0:T(8,128)S(1)} %fusion, f32[9,24]{1,0:T(8,128)S(1)} %slice.1306), kind=kLoop, calls=%fused_computation.25 | loop fusion | flops 1244160 | bytes 3982176 | tf_op jit(solution)/shard_map/transpose | solution.py:261
  (108 shorter events, 6.0 us)
Async XLA Ops:
  2.2 16.2 %collective-permute-start.3 = (f32[10,1,24,64]{3,2,1,0:T(8,128)}, f32[10,1,24,64]{3,2,1,0:T(8,128)}, u32[]{:S(2)}, u32[]{:S(2)}) collective-permute-start(f32[10,1,24,64]{3,2,1,0:T(8,128)} %get-tuple-element.5), channel_id=1, source_target_pairs={{0,2},{1,3},{2,4},{3,5},{4,6},{5,7},{6,8},{7,9},{8,10},{9,11},{10,... | collective-permute-start | bytes 184328 | tf_op jit(solution)/shard_map/ppermute | solution.py:15
  5.2 13.3 %collective-permute-start.2 = (f32[10,1,24,64]{3,2,1,0:T(8,128)}, f32[10,1,24,64]{3,2,1,0:T(8,128)S(1)}, u32[]{:S(2)}, u32[]{:S(2)}) collective-permute-start(f32[10,1,24,64]{3,2,1,0:T(8,128)} %get-tuple-element.5), channel_id=1, source_target_pairs={{0,30},{1,31},{2,0},{3,1},{4,2},{5,3},{6,4},{7,5},{8,6},{9,7},{10,... | collective-permute-start | bytes 184328 | tf_op jit(solution)/shard_map/ppermute | solution.py:15
  9.2 5.9 %collective-permute-start.1 = (f32[10,1,24,64]{3,2,1,0:T(8,128)}, f32[10,1,24,64]{3,2,1,0:T(8,128)S(1)}, u32[]{:S(2)}, u32[]{:S(2)}) collective-permute-start(f32[10,1,24,64]{3,2,1,0:T(8,128)} %get-tuple-element.5), channel_id=1, source_target_pairs={{0,31},{1,0},{2,1},{3,2},{4,3},{5,4},{6,5},{7,6},{8,7},{9,8},{10,9... | collective-permute-start | bytes 184328 | tf_op jit(solution)/shard_map/ppermute | solution.py:15
  10.1 8.1 %collective-permute-start = (f32[10,1,24,64]{3,2,1,0:T(8,128)}, f32[10,1,24,64]{3,2,1,0:T(8,128)S(1)}, u32[]{:S(2)}, u32[]{:S(2)}) collective-permute-start(f32[10,1,24,64]{3,2,1,0:T(8,128)} %get-tuple-element.5), channel_id=1, source_target_pairs={{0,1},{1,2},{2,3},{3,4},{4,5},{5,6},{6,7},{7,8},{8,9},{9,10},{10,1... | collective-permute-start | bytes 184328 | tf_op jit(solution)/shard_map/ppermute | solution.py:15
  12.7 2.3 %copy-start.2 = (f32[9,1,24,64]{3,2,1,0:T(8,128)S(1)}, f32[9,1,24,64]{3,2,1,0:T(8,128)}, u32[]{:S(2)}) copy-start(f32[9,1,24,64]{3,2,1,0:T(8,128)} %refs_2_.1) | copy-start | bytes 165892
  12.7 5.5 %copy-start.1 = (f32[10,1,24,64]{3,2,1,0:T(8,128)S(1)}, f32[10,1,24,64]{3,2,1,0:T(8,128)}, u32[]{:S(2)}) copy-start(f32[10,1,24,64]{3,2,1,0:T(8,128)} %get-tuple-element.5) | copy-start | bytes 184324
  14.3 27.6 %collective-permute-start.4 = (f32[12,6,24,128]{3,2,1,0:T(8,128)S(1)}, f32[12,6,24,128]{3,2,1,0:T(8,128)S(1)}, u32[]{:S(2)}, u32[]{:S(2)}) collective-permute-start(f32[12,6,24,128]{3,2,1,0:T(8,128)S(1)} %get-tuple-element.44), channel_id=1, source_target_pairs={{0,1},{1,2},{2,3},{3,4},{4,5},{5,6},{6,7},{7,0},{8,9},{9,10},{10,1... | collective-permute-start | bytes 2654216 | tf_op jit(solution)/shard_map/ppermute | solution.py:15
  15.1 26.9 %collective-permute-start.5 = (f32[12,6,24,128]{3,2,1,0:T(8,128)S(1)}, f32[12,6,24,128]{3,2,1,0:T(8,128)}, u32[]{:S(2)}, u32[]{:S(2)}) collective-permute-start(f32[12,6,24,128]{3,2,1,0:T(8,128)S(1)} %get-tuple-element.45), channel_id=1, source_target_pairs={{0,7},{1,0},{2,1},{3,2},{4,3},{5,4},{6,5},{7,6},{8,15},{9,8},{10,9... | collective-permute-start | bytes 2654216 | tf_op jit(solution)/shard_map/ppermute | solution.py:15
  18.5 1.2 %copy-start.3 = (f32[1,24,64]{2,1,0:T(8,128)S(1)}, f32[1,24,64]{2,1,0:T(8,128)}, u32[]{:S(2)}) copy-start(f32[1,24,64]{2,1,0:T(8,128)} %get-tuple-element.7) | copy-start | bytes 18436
  18.5 1.2 %copy-start.4 = (f32[1,24,64]{2,1,0:T(8,128)S(1)}, f32[1,24,64]{2,1,0:T(8,128)}, u32[]{:S(2)}) copy-start(f32[1,24,64]{2,1,0:T(8,128)} %get-tuple-element.6) | copy-start | bytes 18436
  22.3 16.3 %all-to-all-start = ((bf16[8,2,4032]{2,1,0:T(2,128)(2,1)}), bf16[8,2,4032]{2,1,0:T(2,128)(2,1)S(1)}, u32[]{:S(2)}, u32[]{:S(2)}) async-start(bf16[8,2,4032]{2,1,0:T(2,128)(2,1)} %reshape.473), calls=%async_computation | async-start | bytes 262144 | tf_op jit(solution)/shard_map/all_to_all | solution.py:210
  41.8 1.6 %copy-start = (f32[12,9,24,128]{3,2,1,0:T(8,128)S(1)}, f32[12,9,24,128]{3,2,1,0:T(8,128)}, u32[]{:S(2)}) copy-start(f32[12,9,24,128]{3,2,1,0:T(8,128)} %shard_map.69) | copy-start | bytes 3981316
  43.6 9.0 %collective-permute-start.6 = (f32[10,21,2,128]{3,2,1,0:T(2,128)S(1)}, f32[10,21,2,128]{3,2,1,0:T(2,128)S(1)}, u32[]{:S(2)}, u32[]{:S(2)}) collective-permute-start(f32[10,21,2,128]{3,2,1,0:T(2,128)S(1)} %get-tuple-element.32), channel_id=1, source_target_pairs={{0,8},{8,16},{16,24},{24,0},{1,9},{9,17},{17,25},{25,1},{2,10},{10... | collective-permute-start | bytes 645128 | tf_op jit(solution)/shard_map/ppermute | solution.py:24
  45.8 10.6 %collective-permute-start.7 = (f32[10,21,2,128]{3,2,1,0:T(2,128)S(1)}, f32[10,21,2,128]{3,2,1,0:T(2,128)S(1)}, u32[]{:S(2)}, u32[]{:S(2)}) collective-permute-start(f32[10,21,2,128]{3,2,1,0:T(2,128)S(1)} %get-tuple-element.33), channel_id=1, source_target_pairs={{8,0},{16,8},{24,16},{0,24},{9,1},{17,9},{25,17},{1,25},{10,2},{18... | collective-permute-start | bytes 645128 | tf_op jit(solution)/shard_map/ppermute | solution.py:25
  60.7 8.8 %collective-permute-start.8 = (f32[9,17,2,128]{3,2,1,0:T(2,128)S(1)}, f32[9,17,2,128]{3,2,1,0:T(2,128)S(1)}, u32[]{:S(2)}, u32[]{:S(2)}) collective-permute-start(f32[9,17,2,128]{3,2,1,0:T(2,128)S(1)} %get-tuple-element.37), channel_id=1, source_target_pairs={{0,8},{8,16},{16,24},{24,0},{1,9},{9,17},{17,25},{25,1},{2,10},{10... | collective-permute-start | bytes 470024 | tf_op jit(solution)/shard_map/ppermute | solution.py:24
  62.0 9.0 %collective-permute-start.9 = (f32[9,17,2,128]{3,2,1,0:T(2,128)S(1)}, f32[9,17,2,128]{3,2,1,0:T(2,128)S(1)}, u32[]{:S(2)}, u32[]{:S(2)}) collective-permute-start(f32[9,17,2,128]{3,2,1,0:T(2,128)S(1)} %get-tuple-element.38), channel_id=1, source_target_pairs={{8,0},{16,8},{24,16},{0,24},{9,1},{17,9},{25,17},{1,25},{10,2},{18... | collective-permute-start | bytes 470024 | tf_op jit(solution)/shard_map/ppermute | solution.py:25
  74.4 7.5 %collective-permute-start.10 = (f32[9,13,2,128]{3,2,1,0:T(2,128)S(1)}, f32[9,13,2,128]{3,2,1,0:T(2,128)S(1)}, u32[]{:S(2)}, u32[]{:S(2)}) collective-permute-start(f32[9,13,2,128]{3,2,1,0:T(2,128)S(1)} %get-tuple-element.42), channel_id=1, source_target_pairs={{0,8},{8,16},{16,24},{24,0},{1,9},{9,17},{17,25},{25,1},{2,10},{10... | collective-permute-start | bytes 359432 | tf_op jit(solution)/shard_map/ppermute | solution.py:24
  75.3 6.7 %collective-permute-start.11 = (f32[9,13,2,128]{3,2,1,0:T(2,128)S(1)}, f32[9,13,2,128]{3,2,1,0:T(2,128)S(1)}, u32[]{:S(2)}, u32[]{:S(2)}) collective-permute-start(f32[9,13,2,128]{3,2,1,0:T(2,128)S(1)} %get-tuple-element.43), channel_id=1, source_target_pairs={{8,0},{16,8},{24,16},{0,24},{9,1},{17,9},{25,17},{1,25},{10,2},{18... | collective-permute-start | bytes 359432 | tf_op jit(solution)/shard_map/ppermute | solution.py:25

commit v16 on v15

--- a/solution.py
+++ b/solution.py
@@ -183,8 +183,9 @@
     )
 
     me_flat = lax.axis_index("gx") * count_y + me_y
-    fine_lo = from_cycle(fine_pay[:, -reach_y:], "gy", count_y, 1, me_y)
-    fine_hi = from_cycle(fine_pay[:, :reach_y], "gy", count_y, -1, me_y)
+    fine_xw = x_halo(fine_pay, 2)
+    fine_lo = from_cycle(fine_xw[:, -reach_y:], "gy", count_y, 1, me_y)
+    fine_hi = from_cycle(fine_xw[:, :reach_y], "gy", count_y, -1, me_y)
     reg_lo = from_cycle(region_pay, flat, n_flat, 1, me_flat)
     reg_hi = from_cycle(region_pay, flat, n_flat, -1, me_flat)
     lows, highs = [reg_lo], [reg_hi]
@@ -229,15 +230,12 @@
     along_y = ramp(me_y * fine_y - 4, fine_y + 8, count_y * fine_y, fine_y)
     relax = (0.1 + 0.4 * jnp.maximum(along_y[:, None], along_x[None, :]))[:, :, None]
 
-    wide = jnp.concatenate([fine_lo, fine_pay, fine_hi], axis=1)
-    lam_w, mu_w = wide[10], wide[11]
-    state = wide[:9]
-    coef_w = None
+    wide = jnp.concatenate([fine_lo, fine_xw, fine_hi], axis=1)
+    coef_w, lam_w, mu_w = wide[9, :, 1:-1], wide[10, :, 2:-2], wide[11, :, 2:-2]
+    state = wide[:9, :, 2:-2]
     for sub in range(1, 4):
         if sub == 1:
-            ext = x_halo(wide[:10], 2)
-            coef_w = ext[9, :, 1:-1]
-            ext = ext[:9]
+            ext = wide[:9]
         else:
             ext = x_halo(state, 2)
         off = 2 * (sub - 1)

time: 85.9 us -> 86.9 us (1.012)
  local copies, waits for them, and re-layouts: 11.6 us -> 8.74 us
  starting transfers between devices: 25.9 us -> 28 us
  waiting for transfers between devices: 26.2 us -> 28 us
    ppermute x6, waiting for transfers between devices: 0.82 us -> 20.3 us  [from_cycle(): got = lax.ppermute(field, axis, [(i, (i + d) % n) for i in range(n)])]
    all_to_all x1, waiting for transfers between devices: 10.5 us -> 0.42 us  [local(): band = lax.all_to_all(send, 'gy', 2, 1, tiled=True).astype(jnp.float32)]
    ppermute x3, waiting for transfers between devices: 5.31 us -> 0.26 us  [x_halo(): from_right = lax.ppermute(field[:, :, :width], 'gx', back)]
    ppermute x6, starting transfers between devices: 10.6 us -> 14.6 us  [from_cycle(): got = lax.ppermute(field, axis, [(i, (i + d) % n) for i in range(n)])]
    ppermute x3, starting transfers between devices: 10.8 us -> 7.19 us  [x_halo(): from_right = lax.ppermute(field[:, :, :width], 'gx', back)]
    unnamed x22 -> x24, local copies, waits for them, and re-layouts: 5.11 us -> 1.6 us
    ppermute x3, waiting for transfers between devices: 9.57 us -> 6.98 us  [x_halo(): from_left = lax.ppermute(field[:, :, -width:], 'gx', cycle)]
    ppermute x3, starting transfers between devices: 1.11 us -> 2.75 us  [x_halo(): from_left = lax.ppermute(field[:, :, -width:], 'gx', cycle)]
  transfers between devices with their start and end apart: 13 -> 13, of which waited for: 8 -> 6; matrix products, arithmetic and copies ran while one was open for 18% -> 16% of each run, Pallas kernels for 3% -> 3%
where the time goes in v16:
time: 86.9 us; the launch traced here: 86.5 us
  starting transfers between devices  28 us (32%)
  waiting for transfers between devices  28 us (32%)
  other arithmetic  10.9 us (13%)
  local copies, waits for them, and re-layouts  8.74 us (10%)
  matrix products  5.12 us (6%)
  Pallas kernels  4.27 us (5%)
  between operations  1.49 us (2%)
    ppermute x6, waiting for transfers between devices, from_cycle(): got = lax.ppermute(field, axis, [(i, (i + d) % n) for i in range(n)])  20.3 us
    ppermute x6, starting transfers between devices, from_cycle(): got = lax.ppermute(field, axis, [(i, (i + d) % n) for i in range(n)])  14.6 us
    ppermute x3, starting transfers between devices, x_halo(): from_right = lax.ppermute(field[:, :, :width], 'gx', back)  7.19 us
    ppermute x3, waiting for transfers between devices, x_halo(): from_left = lax.ppermute(field[:, :, -width:], 'gx', cycle)  6.98 us
    pallas_call x2, Pallas kernels, lookup(): pl.pallas_call(lambda *refs: lookup_kernel(step, extra, *refs), out_shape...  4.27 us
    all_to_all x1, starting transfers between devices, local(): band = lax.all_to_all(send, 'gy', 2, 1, tiled=True).astype(jnp.float32)  3.37 us
    ppermute x3, starting transfers between devices, x_halo(): from_left = lax.ppermute(field[:, :, -width:], 'gx', cycle)  2.75 us
    slice x27, local copies, waits for them, and re-layouts, along(): lax.slice_in_dim(f, 1, n, axis=axis)  2.42 us
  transfers between devices with their start and end apart: 13, of which 6 were waited for; matrix products, arithmetic and copies ran while one was open for 16% of the time, Pallas kernels for 3%

profile of v16, /device:TPU:0, one launch (start us, length us, event | category | flops | bytes accessed | tf_op | source)
XLA Modules:
  0.0 86.5 jit_solution(10441592252588000601)
XLA Ops:
  0.6 1.6 %shard_map.68 = (f32[10,1,24,64]{3,2,1,0:T(8,128)}, f32[1,24,64]{2,1,0:T(8,128)}, f32[1,24,64]{2,1,0:T(8,128)}) custom-call(s32[1,24,64]{2,1,0:T(8,128)} %refs_0_.1, f32[3,8]{1,0:T(4,128)} %refs_1_.3, f32[9,1,24,64]{3,2,1,0:T(8,128)} %refs_2_.1), custom_call_target="tpu_custom_call" | custom-call | tf_op jit(solution)/shard_map/pallas_call | solution.py:58
  2.3 0.5 collective-permute-start
  2.7 6.0 %collective-permute-start.1 = (f32[10,1,24,64]{3,2,1,0:T(8,128)}, f32[10,1,24,64]{3,2,1,0:T(8,128)S(1)}, u32[]{:S(2)}, u32[]{:S(2)}) collective-permute-start(f32[10,1,24,64]{3,2,1,0:T(8,128)} %get-tuple-element.5), channel_id=1, source_target_pairs={{0,31},{1,0},{2,1},{3,2},{4,3},{5,4},{6,5},{7,6},{8,7},{9,8},{10,9... | collective-permute-start | bytes 184328 | tf_op jit(solution)/shard_map/ppermute | solution.py:15
  8.7 5.6 %collective-permute-start.2 = (f32[10,1,24,64]{3,2,1,0:T(8,128)}, f32[10,1,24,64]{3,2,1,0:T(8,128)S(1)}, u32[]{:S(2)}, u32[]{:S(2)}) collective-permute-start(f32[10,1,24,64]{3,2,1,0:T(8,128)} %get-tuple-element.5), channel_id=1, source_target_pairs={{0,30},{1,31},{2,0},{3,1},{4,2},{5,3},{6,4},{7,5},{8,6},{9,7},{10,... | collective-permute-start | bytes 184328 | tf_op jit(solution)/shard_map/ppermute | solution.py:15
  14.3 2.6 %shard_map.69 = f32[12,9,24,128]{3,2,1,0:T(8,128)} custom-call(s32[9,24,128]{2,1,0:T(8,128)} %bitcast.657, f32[3,8]{1,0:T(4,128)} %refs_1_.3, f32[9,9,24,128]{3,2,1,0:T(8,128)} %bitcast.656), custom_call_target="tpu_custom_call" | custom-call | tf_op jit(solution)/shard_map/pallas_call | solution.py:58
  17.0 1.2 %fusion.270 = (f32[12,9,2,128]{3,2,1,0:T(2,128)S(1)}, f32[12,9,2,128]{3,2,1,0:T(2,128)S(1)}) fusion(f32[12,9,24,128]{3,2,1,0:T(8,128)} %shard_map.69), kind=kLoop, calls=%fused_computation.494 | loop fusion | bytes 442368 | tf_op jit(solution)/shard_map/slice | solution.py:24
  18.2 0.4 collective-permute-start.5
  18.9 1.7 %collective-permute-start.4 = (f32[12,9,2,128]{3,2,1,0:T(2,128)S(1)}, f32[12,9,2,128]{3,2,1,0:T(2,128)S(1)}, u32[]{:S(2)}, u32[]{:S(2)}) collective-permute-start(f32[12,9,2,128]{3,2,1,0:T(2,128)S(1)} %get-tuple-element.46), channel_id=1, source_target_pairs={{0,8},{8,16},{16,24},{24,0},{1,9},{9,17},{17,25},{25,1},{2,10},{10... | collective-permute-start | bytes 331784 | tf_op jit(solution)/shard_map/ppermute | solution.py:24
  22.2 1.1 %concatenate.313 = bf16[18,1,56,64]{3,2,1,0:T(8,128)(2,1)S(1)} concatenate(bf16[18,1,7,64]{3,2,1,0:T(8,128)(2,1)S(1)} %get-tuple-element.109, bf16[18,1,7,64]{3,2,1,0:T(8,128)(2,1)S(1)} %get-tuple-element.108, bf16[18,1,7,64]{3,2,1,0:T(8,128)(2,1)S(1)} %get-tuple-element.107, bf16[18,1,7,64]{3,2,1,0:T(8,128)(2,1)S(1)} %get-tuple-element.106, ...), dimensions={2} | concatenate | bytes 258048 | tf_op jit(solution)/shard_map/concatenate | solution.py:208
  23.4 0.9 %reshape.473 = bf16[8,2,4032]{2,1,0:T(2,128)(2,1)} reshape(bf16[56,1,18,64]{3,2,1,0:T(8,128)(2,1)S(1)} %bitcast.654) | data formatting | bytes 258048
  24.3 3.4 %all-to-all-start = ((bf16[8,2,4032]{2,1,0:T(2,128)(2,1)}), bf16[8,2,4032]{2,1,0:T(2,128)(2,1)S(1)}, u32[]{:S(2)}, u32[]{:S(2)}) async-start(bf16[8,2,4032]{2,1,0:T(2,128)(2,1)} %reshape.473), calls=%async_computation | async-start | bytes 262144 | tf_op jit(solution)/shard_map/all_to_all | solution.py:211
  27.9 0.3 pad_maximum_fusion.3
  28.2 0.2 copy-done.5
  28.4 1.7 %fusion.268 = (f32[12,6,28,128]{3,2,1,0:T(8,128)}, f32[12,6,28,128]{3,2,1,0:T(8,128)}) fusion(f32[12,9,28,128]{3,2,1,0:T(8,128)S(1)} %pad_maximum_fusion.3), kind=kLoop, calls=%fused_computation.492 | loop fusion | bytes 4128768 | tf_op jit(solution)/shard_map/slice | solution.py:187
  30.1 2.6 %collective-permute-start.7 = (f32[12,6,28,128]{3,2,1,0:T(8,128)}, f32[12,6,28,128]{3,2,1,0:T(8,128)}, u32[]{:S(2)}, u32[]{:S(2)}) collective-permute-start(f32[12,6,28,128]{3,2,1,0:T(8,128)} %get-tuple-element.40), channel_id=1, source_target_pairs={{0,7},{1,0},{2,1},{3,2},{4,3},{5,4},{6,5},{7,6},{8,15},{9,8},{10,9... | collective-permute-start | bytes 3096584 | tf_op jit(solution)/shard_map/ppermute | solution.py:15
  32.7 0.4 all-to-all-done
  33.1 0.2 reshape.474
  33.4 0.6 convolution_bitcast_fusion.1
  34.0 2.4 %convolution_bitcast_fusion = f32[18,17,24,64]{3,1,2,0:T(8,128)S(1)} fusion(f32[18,24,7,64]{3,1,2,0:T(8,128)S(1)} %convolution_bitcast_fusion.1, f32[9,3]{0,1:T(4,128)S(1)} %select_add_fusion, f32[9,3]{0,1:T(4,128)S(1)} %broadcast.1055), kind=kOutput, calls=%fused_computation.4 | convolution fusion | flops 19741744 | bytes 2654424 | tf_op jit(solution)/shard_map/gb,cfbz->cgfz/dot_general | solution.py:225
  36.4 2.1 %fusion = f32[18,17,24,128]{3,2,1,0:T(8,128)S(1)} fusion(f32[18,17,24,64]{3,1,2,0:T(8,128)S(1)} %convolution_bitcast_fusion, f32[128]{0:T(128)S(1)} %get-tuple-element.151, s32[128]{0:T(128)S(1)} %get-tuple-element.154, f32[128]{0:T(128)S(1)} %get-tuple-element.152, s32[128]{0:T(128)S(1)} %get-tuple-element.153), kind=kOutput, calls=%fused_computation.1 | convolution fusion | flops 361013248 | bytes 5642240 | tf_op jit(solution)/shard_map/kz,cgfz->cgfk/dot_general | solution.py:226
  38.5 19.7 %collective-permute-done.7 = f32[12,6,28,128]{3,2,1,0:T(8,128)} collective-permute-done((f32[12,6,28,128]{3,2,1,0:T(8,128)}, f32[12,6,28,128]{3,2,1,0:T(8,128)}, u32[]{:S(2)}, u32[]{:S(2)}) %collective-permute-start.7) | collective-permute-done | bytes 1032224 | tf_op jit(solution)/shard_map/ppermute | solution.py:15
  58.2 1.4 %broadcast_select_fusion = f32[12,6,28,128]{3,2,1,0:T(8,128)S(1)} fusion(f32[12,6,28,128]{3,2,1,0:T(8,128)} %collective-permute-done.7, pred[]{:T(512)S(6)} %and.80), kind=kLoop, calls=%fused_computation.31 | loop fusion | flops 258048 | bytes 2064385 | tf_op jit(solution)/shard_map/jit(_where)/select_n | solution.py:16
  59.6 0.6 collective-permute-done.6
  60.3 0.1 broadcast_select_fusion.1
  60.4 0.6 pad_maximum_fusion
  61.0 0.2 slice_bitcast_fusion.3
  61.1 0.2 fusion.273
  61.3 0.2 fusion.271
  61.5 0.5 fusion.31
  62.1 0.2 slice_add_fusion
  62.4 0.1 fusion.279
  62.5 0.2 fusion.81
  62.9 0.2 fusion.70
  63.0 0.1 fusion.67
  63.2 0.1 fusion.278
  63.3 0.2 slice_bitcast_fusion.5
  63.6 0.2 fusion.55
  63.8 0.5 fusion.6
  64.5 3.8 %collective-permute-start.9 = (f32[9,17,2,128]{3,2,1,0:T(2,128)S(1)}, f32[9,17,2,128]{3,2,1,0:T(2,128)S(1)}, u32[]{:S(2)}, u32[]{:S(2)}) collective-permute-start(f32[9,17,2,128]{3,2,1,0:T(2,128)S(1)} %get-tuple-element.38), channel_id=1, source_target_pairs={{8,0},{16,8},{24,16},{0,24},{9,1},{17,9},{25,17},{1,25},{10,2},{18... | collective-permute-start | bytes 470024 | tf_op jit(solution)/shard_map/ppermute | solution.py:25
  68.3 4.1 %collective-permute-done.8 = f32[9,17,2,128]{3,2,1,0:T(2,128)S(1)} collective-permute-done((f32[9,17,2,128]{3,2,1,0:T(2,128)S(1)}, f32[9,17,2,128]{3,2,1,0:T(2,128)S(1)}, u32[]{:S(2)}, u32[]{:S(2)}) %collective-permute-start.8) | collective-permute-done | bytes 156704 | tf_op jit(solution)/shard_map/ppermute | solution.py:24
  72.6 0.1 maximum_bitcast_fusion.2
  72.7 0.4 pad_maximum_fusion.1
  73.1 0.1 fusion.274
  73.3 0.1 fusion.275
  73.4 0.1 fusion.276
  73.5 0.2 fusion.48
  73.7 0.2 fusion.43
  73.9 0.2 fusion.37
  74.0 0.1 slice_add_fusion.1
  74.4 0.2 fusion.136
  74.7 0.1 fusion.125
  75.0 0.1 slice_bitcast_fusion.15
  75.2 0.1 fusion.110
  75.4 0.3 fusion.12
  75.8 1.0 %collective-permute-start.10 = (f32[9,13,2,128]{3,2,1,0:T(2,128)S(1)}, f32[9,13,2,128]{3,2,1,0:T(2,128)S(1)}, u32[]{:S(2)}, u32[]{:S(2)}) collective-permute-start(f32[9,13,2,128]{3,2,1,0:T(2,128)S(1)} %get-tuple-element.44), channel_id=1, source_target_pairs={{0,8},{8,16},{16,24},{24,0},{1,9},{9,17},{17,25},{25,1},{2,10},{10... | collective-permute-start | bytes 359432 | tf_op jit(solution)/shard_map/ppermute | solution.py:24
  76.8 3.0 %collective-permute-start.11 = (f32[9,13,2,128]{3,2,1,0:T(2,128)S(1)}, f32[9,13,2,128]{3,2,1,0:T(2,128)S(1)}, u32[]{:S(2)}, u32[]{:S(2)}) collective-permute-start(f32[9,13,2,128]{3,2,1,0:T(2,128)S(1)} %get-tuple-element.45), channel_id=1, source_target_pairs={{8,0},{16,8},{24,16},{0,24},{9,1},{17,9},{25,17},{1,25},{10,2},{18... | collective-permute-start | bytes 359432 | tf_op jit(solution)/shard_map/ppermute | solution.py:25
  79.8 2.9 %collective-permute-done.10 = f32[9,13,2,128]{3,2,1,0:T(2,128)S(1)} collective-permute-done((f32[9,13,2,128]{3,2,1,0:T(2,128)S(1)}, f32[9,13,2,128]{3,2,1,0:T(2,128)S(1)}, u32[]{:S(2)}, u32[]{:S(2)}) %collective-permute-start.10) | collective-permute-done | bytes 119840 | tf_op jit(solution)/shard_map/ppermute | solution.py:24
  82.7 0.3 collective-permute-done.11
  83.1 0.4 pad_maximum_fusion.2
  83.8 0.1 fusion.103
  84.0 0.1 fusion.98
  84.1 0.1 fusion.92
  84.5 0.1 fusion.175
  85.3 1.2 %fusion.16 = f32[9,24,9,128]{3,1,2,0:T(8,128)} fusion(f32[9,9,24,128]{3,2,1,0:T(8,128)S(1)} %fusion.149, f32[18,17,24,128]{3,2,1,0:T(8,128)S(1)} %fusion, f32[9,24]{1,0:T(8,128)S(1)} %slice.1315), kind=kLoop, calls=%fused_computation.25 | loop fusion | flops 1244160 | bytes 3982176 | tf_op jit(solution)/shard_map/transpose | solution.py:259
  (108 shorter events, 4.6 us)
Async XLA Ops:
  0.6 18.0 %copy-start.2 = (f32[9,1,24,64]{3,2,1,0:T(8,128)S(1)}, f32[9,1,24,64]{3,2,1,0:T(8,128)}, u32[]{:S(2)}) copy-start(f32[9,1,24,64]{3,2,1,0:T(8,128)} %refs_2_.1) | copy-start | bytes 165892
  2.3 18.4 %copy-start.1 = (f32[10,1,24,64]{3,2,1,0:T(8,128)S(1)}, f32[10,1,24,64]{3,2,1,0:T(8,128)}, u32[]{:S(2)}) copy-start(f32[10,1,24,64]{3,2,1,0:T(8,128)} %get-tuple-element.5) | copy-start | bytes 184324
  2.3 16.7 %collective-permute-start = (f32[10,1,24,64]{3,2,1,0:T(8,128)}, f32[10,1,24,64]{3,2,1,0:T(8,128)S(1)}, u32[]{:S(2)}, u32[]{:S(2)}) collective-permute-start(f32[10,1,24,64]{3,2,1,0:T(8,128)} %get-tuple-element.5), channel_id=1, source_target_pairs={{0,1},{1,2},{2,3},{3,4},{4,5},{5,6},{6,7},{7,8},{8,9},{9,10},{10,1... | collective-permute-start | bytes 184328 | tf_op jit(solution)/shard_map/ppermute | solution.py:15
  2.7 17.9 %collective-permute-start.1 = (f32[10,1,24,64]{3,2,1,0:T(8,128)}, f32[10,1,24,64]{3,2,1,0:T(8,128)S(1)}, u32[]{:S(2)}, u32[]{:S(2)}) collective-permute-start(f32[10,1,24,64]{3,2,1,0:T(8,128)} %get-tuple-element.5), channel_id=1, source_target_pairs={{0,31},{1,0},{2,1},{3,2},{4,3},{5,4},{6,5},{7,6},{8,7},{9,8},{10,9... | collective-permute-start | bytes 184328 | tf_op jit(solution)/shard_map/ppermute | solution.py:15
  8.7 12.2 %collective-permute-start.3 = (f32[10,1,24,64]{3,2,1,0:T(8,128)}, f32[10,1,24,64]{3,2,1,0:T(8,128)S(1)}, u32[]{:S(2)}, u32[]{:S(2)}) collective-permute-start(f32[10,1,24,64]{3,2,1,0:T(8,128)} %get-tuple-element.5), channel_id=1, source_target_pairs={{0,2},{1,3},{2,4},{3,5},{4,6},{5,7},{6,8},{7,9},{8,10},{9,11},{10,... | collective-permute-start | bytes 184328 | tf_op jit(solution)/shard_map/ppermute | solution.py:15
  8.7 12.3 %collective-permute-start.2 = (f32[10,1,24,64]{3,2,1,0:T(8,128)}, f32[10,1,24,64]{3,2,1,0:T(8,128)S(1)}, u32[]{:S(2)}, u32[]{:S(2)}) collective-permute-start(f32[10,1,24,64]{3,2,1,0:T(8,128)} %get-tuple-element.5), channel_id=1, source_target_pairs={{0,30},{1,31},{2,0},{3,1},{4,2},{5,3},{6,4},{7,5},{8,6},{9,7},{10,... | collective-permute-start | bytes 184328 | tf_op jit(solution)/shard_map/ppermute | solution.py:15
  18.2 9.5 %collective-permute-start.5 = (f32[12,9,2,128]{3,2,1,0:T(2,128)S(1)}, f32[12,9,2,128]{3,2,1,0:T(2,128)S(1)}, u32[]{:S(2)}, u32[]{:S(2)}) collective-permute-start(f32[12,9,2,128]{3,2,1,0:T(2,128)S(1)} %get-tuple-element.47), channel_id=1, source_target_pairs={{8,0},{16,8},{24,16},{0,24},{9,1},{17,9},{25,17},{1,25},{10,2},{18... | collective-permute-start | bytes 331784 | tf_op jit(solution)/shard_map/ppermute | solution.py:25
  18.9 8.9 %collective-permute-start.4 = (f32[12,9,2,128]{3,2,1,0:T(2,128)S(1)}, f32[12,9,2,128]{3,2,1,0:T(2,128)S(1)}, u32[]{:S(2)}, u32[]{:S(2)}) collective-permute-start(f32[12,9,2,128]{3,2,1,0:T(2,128)S(1)} %get-tuple-element.46), channel_id=1, source_target_pairs={{0,8},{8,16},{16,24},{24,0},{1,9},{9,17},{17,25},{25,1},{2,10},{10... | collective-permute-start | bytes 331784 | tf_op jit(solution)/shard_map/ppermute | solution.py:24
  21.0 0.7 copy-start.3
  21.0 0.7 copy-start.4
  21.6 6.2 %copy-start = (f32[12,9,24,128]{3,2,1,0:T(8,128)S(1)}, f32[12,9,24,128]{3,2,1,0:T(8,128)}, u32[]{:S(2)}) copy-start(f32[12,9,24,128]{3,2,1,0:T(8,128)} %shard_map.69) | copy-start | bytes 3981316
  24.3 8.8 %all-to-all-start = ((bf16[8,2,4032]{2,1,0:T(2,128)(2,1)}), bf16[8,2,4032]{2,1,0:T(2,128)(2,1)S(1)}, u32[]{:S(2)}, u32[]{:S(2)}) async-start(bf16[8,2,4032]{2,1,0:T(2,128)(2,1)} %reshape.473), calls=%async_computation | async-start | bytes 262144 | tf_op jit(solution)/shard_map/all_to_all | solution.py:211
  27.7 0.6 copy-start.5
  30.1 28.1 %collective-permute-start.7 = (f32[12,6,28,128]{3,2,1,0:T(8,128)}, f32[12,6,28,128]{3,2,1,0:T(8,128)}, u32[]{:S(2)}, u32[]{:S(2)}) collective-permute-start(f32[12,6,28,128]{3,2,1,0:T(8,128)} %get-tuple-element.40), channel_id=1, source_target_pairs={{0,7},{1,0},{2,1},{3,2},{4,3},{5,4},{6,5},{7,6},{8,15},{9,8},{10,9... | collective-permute-start | bytes 3096584 | tf_op jit(solution)/shard_map/ppermute | solution.py:15
  32.7 27.6 %collective-permute-start.6 = (f32[12,6,28,128]{3,2,1,0:T(8,128)}, f32[12,6,28,128]{3,2,1,0:T(8,128)S(1)}, u32[]{:S(2)}, u32[]{:S(2)}) collective-permute-start(f32[12,6,28,128]{3,2,1,0:T(8,128)} %get-tuple-element.39), channel_id=1, source_target_pairs={{0,1},{1,2},{2,3},{3,4},{4,5},{5,6},{6,7},{7,0},{8,9},{9,10},{10,1... | collective-permute-start | bytes 3096584 | tf_op jit(solution)/shard_map/ppermute | solution.py:15
  64.4 8.0 %collective-permute-start.8 = (f32[9,17,2,128]{3,2,1,0:T(2,128)S(1)}, f32[9,17,2,128]{3,2,1,0:T(2,128)S(1)}, u32[]{:S(2)}, u32[]{:S(2)}) collective-permute-start(f32[9,17,2,128]{3,2,1,0:T(2,128)S(1)} %get-tuple-element.37), channel_id=1, source_target_pairs={{0,8},{8,16},{16,24},{24,0},{1,9},{9,17},{17,25},{25,1},{2,10},{10... | collective-permute-start | bytes 470024 | tf_op jit(solution)/shard_map/ppermute | solution.py:24
  64.5 8.0 %collective-permute-start.9 = (f32[9,17,2,128]{3,2,1,0:T(2,128)S(1)}, f32[9,17,2,128]{3,2,1,0:T(2,128)S(1)}, u32[]{:S(2)}, u32[]{:S(2)}) collective-permute-start(f32[9,17,2,128]{3,2,1,0:T(2,128)S(1)} %get-tuple-element.38), channel_id=1, source_target_pairs={{8,0},{16,8},{24,16},{0,24},{9,1},{17,9},{25,17},{1,25},{10,2},{18... | collective-permute-start | bytes 470024 | tf_op jit(solution)/shard_map/ppermute | solution.py:25
  75.8 6.9 %collective-permute-start.10 = (f32[9,13,2,128]{3,2,1,0:T(2,128)S(1)}, f32[9,13,2,128]{3,2,1,0:T(2,128)S(1)}, u32[]{:S(2)}, u32[]{:S(2)}) collective-permute-start(f32[9,13,2,128]{3,2,1,0:T(2,128)S(1)} %get-tuple-element.44), channel_id=1, source_target_pairs={{0,8},{8,16},{16,24},{24,0},{1,9},{9,17},{17,25},{25,1},{2,10},{10... | collective-permute-start | bytes 359432 | tf_op jit(solution)/shard_map/ppermute | solution.py:24
  76.8 6.2 %collective-permute-start.11 = (f32[9,13,2,128]{3,2,1,0:T(2,128)S(1)}, f32[9,13,2,128]{3,2,1,0:T(2,128)S(1)}, u32[]{:S(2)}, u32[]{:S(2)}) collective-permute-start(f32[9,13,2,128]{3,2,1,0:T(2,128)S(1)} %get-tuple-element.45), channel_id=1, source_target_pairs={{8,0},{16,8},{24,16},{0,24},{9,1},{17,9},{25,17},{1,25},{10,2},{18... | collective-permute-start | bytes 359432 | tf_op jit(solution)/shard_map/ppermute | solution.py:25

commit v17 on v15

--- a/solution.py
+++ b/solution.py
@@ -189,8 +189,11 @@
     reg_hi = from_cycle(region_pay, flat, n_flat, -1, me_flat)
     lows, highs = [reg_lo], [reg_hi]
     for d in range(2, -(-2 // own) + 1):
-        lows.insert(0, from_cycle(region_pay, flat, n_flat, d, me_flat))
-        highs.append(from_cycle(region_pay, flat, n_flat, -d, me_flat))
+        outer = jnp.concatenate([region_pay[3:4], region_pay[6:8]], 0)
+        lo_far = from_cycle(outer, flat, n_flat, d, me_flat)
+        hi_far = from_cycle(outer, flat, n_flat, -d, me_flat)
+        lows.insert(0, jnp.zeros_like(region_pay).at[jnp.array([3, 6, 7])].set(lo_far))
+        highs.append(jnp.zeros_like(region_pay).at[jnp.array([3, 6, 7])].set(hi_far))
     reg_ext = jnp.concatenate(
         [jnp.concatenate(lows, 1)[:, -2:], region_pay, jnp.concatenate(highs, 1)[:, :2]], 1
     )

time: 85.9 us -> 87.8 us (1.022)
  other arithmetic: 11.2 us -> 13.2 us
  waiting for transfers between devices: 26.2 us -> 25.3 us
    unnamed x22 -> x46, local copies, waits for them, and re-layouts: 5.11 us -> 2.49 us
    slice x0 -> x2, local copies, waits for them, and re-layouts: none -> 1.45 us  [local(): outer = jnp.concatenate([region_pay[3:4], region_pay[6:8]], 0)]
    scatter x0 -> x2, local copies, waits for them, and re-layouts: none -> 1.28 us  [the longest x1 0.64 us: local(): jnp.zeros_like(region_pay).at[jnp.array([3, 6, 7])].set(lo_far)]
    slice x2, local copies, waits for them, and re-layouts: 0.01 us -> 1.2 us  [local(): state = state + relax[None, off:off + rows - 4] * (target - state)]
    select_n x3, other arithmetic: 0.05 us -> 1.23 us  [interp_matrix(): frac = jnp.where(above, 1.0, frac)]
    select_n x3, other arithmetic: 0.05 us -> 1.14 us  [interp_matrix(): lower = jnp.where(above, n_coarse - 2, lower)]
    ppermute x3, waiting for transfers between devices: 9.57 us -> 10.5 us  [x_halo(): from_left = lax.ppermute(field[:, :, -width:], 'gx', cycle)]
    all_to_all x1, waiting for transfers between devices: 10.5 us -> 9.55 us  [local(): band = lax.all_to_all(send, 'gy', 2, 1, tiled=True).astype(jnp.float32)]
  transfers between devices with their start and end apart: 13 -> 13, of which waited for: 8 -> 7; matrix products, arithmetic and copies ran while one was open for 18% -> 18% of each run, Pallas kernels for 3% -> 3%
where the time goes in v17:
time: 87.8 us; the launch traced here: 87.2 us
  starting transfers between devices  25.4 us (29%)
  waiting for transfers between devices  25.3 us (29%)
  other arithmetic  13.2 us (15%)
  local copies, waits for them, and re-layouts  12.3 us (14%)
  matrix products  5.16 us (6%)
  Pallas kernels  4.21 us (5%)
  between operations  1.51 us (2%)
    ppermute x6, starting transfers between devices, from_cycle(): got = lax.ppermute(field, axis, [(i, (i + d) % n) for i in range(n)])  10.6 us
    ppermute x3, waiting for transfers between devices, x_halo(): from_left = lax.ppermute(field[:, :, -width:], 'gx', cycle)  10.5 us
    ppermute x3, starting transfers between devices, x_halo(): from_right = lax.ppermute(field[:, :, :width], 'gx', back)  10.4 us
    all_to_all x1, waiting for transfers between devices, local(): band = lax.all_to_all(send, 'gy', 2, 1, tiled=True).astype(jnp.float32)  9.55 us
    ppermute x3, waiting for transfers between devices, x_halo(): from_right = lax.ppermute(field[:, :, :width], 'gx', back)  5.17 us
    pallas_call x2, Pallas kernels, lookup(): pl.pallas_call(lambda *refs: lookup_kernel(step, extra, *refs), out_shape...  4.21 us
    all_to_all x1, starting transfers between devices, local(): band = lax.all_to_all(send, 'gy', 2, 1, tiled=True).astype(jnp.float32)  3.37 us
    unnamed x46, local copies, waits for them, and re-layouts  2.49 us
  transfers between devices with their start and end apart: 13, of which 7 were waited for; matrix products, arithmetic and copies ran while one was open for 18% of the time, Pallas kernels for 3%

profile of v17, /device:TPU:0, one launch (start us, length us, event | category | flops | bytes accessed | tf_op | source)
XLA Modules:
  0.0 87.2 jit_solution(3714571288639095014)
XLA Ops:
  0.6 1.6 %shard_map.86 = (f32[10,1,24,64]{3,2,1,0:T(8,128)}, f32[1,24,64]{2,1,0:T(8,128)}, f32[1,24,64]{2,1,0:T(8,128)}) custom-call(s32[1,24,64]{2,1,0:T(8,128)} %refs_0_.1, f32[3,8]{1,0:T(4,128)} %refs_1_.3, f32[9,1,24,64]{3,2,1,0:T(8,128)} %refs_2_.1), custom_call_target="tpu_custom_call" | custom-call | tf_op jit(solution)/shard_map/pallas_call | solution.py:58
  2.2 0.7 slice.1151
  2.9 0.7 slice.1152
  3.7 3.0 %collective-permute-start.3 = (f32[3,1,24,64]{3,2,0,1:T(8,128)S(1)}, f32[3,1,24,64]{3,2,0,1:T(8,128)S(1)}, u32[]{:S(2)}, u32[]{:S(2)}) collective-permute-start(f32[3,1,24,64]{3,2,0,1:T(8,128)S(1)} %pad_maximum_fusion.19), channel_id=1, source_target_pairs={{0,2},{1,3},{2,4},{3,5},{4,6},{5,7},{6,8},{7,9},{8,10},{9,11},{10,... | collective-permute-start | bytes 55304 | tf_op jit(solution)/shard_map/ppermute | solution.py:15
  6.7 4.1 %collective-permute-start.2 = (f32[3,1,24,64]{3,2,0,1:T(8,128)S(1)}, f32[3,1,24,64]{3,2,0,1:T(8,128)S(1)}, u32[]{:S(2)}, u32[]{:S(2)}) collective-permute-start(f32[3,1,24,64]{3,2,0,1:T(8,128)S(1)} %pad_maximum_fusion.19), channel_id=1, source_target_pairs={{0,30},{1,31},{2,0},{3,1},{4,2},{5,3},{6,4},{7,5},{8,6},{9,7},{10,... | collective-permute-start | bytes 55304 | tf_op jit(solution)/shard_map/ppermute | solution.py:15
  10.7 0.8 collective-permute-start.1
  11.6 2.6 %shard_map.87 = f32[12,9,24,128]{3,2,1,0:T(8,128)} custom-call(s32[9,24,128]{2,1,0:T(8,128)} %bitcast.684, f32[3,8]{1,0:T(4,128)} %refs_1_.3, f32[9,9,24,128]{3,2,1,0:T(8,128)} %bitcast.683), custom_call_target="tpu_custom_call" | custom-call | tf_op jit(solution)/shard_map/pallas_call | solution.py:58
  14.2 1.6 %fusion.270 = (f32[12,6,24,128]{3,2,1,0:T(8,128)S(1)}, f32[12,6,24,128]{3,2,1,0:T(8,128)S(1)}) fusion(f32[12,9,24,128]{3,2,1,0:T(8,128)} %shard_map.87), kind=kLoop, calls=%fused_computation.499 | loop fusion | bytes 3538944 | tf_op jit(solution)/shard_map/slice | solution.py:186
  15.8 0.5 collective-permute-start.4
  16.3 0.5 compare_select_fusion.9
  16.8 0.6 compare_select_fusion.8
  17.5 0.6 compare_select_fusion.1
  18.2 0.6 compare_select_fusion
  18.8 0.6 slice.1316
  19.4 0.6 slice.1274
  20.0 2.2 %collective-permute-start.5 = (f32[12,6,24,128]{3,2,1,0:T(8,128)S(1)}, f32[12,6,24,128]{3,2,1,0:T(8,128)}, u32[]{:S(2)}, u32[]{:S(2)}) collective-permute-start(f32[12,6,24,128]{3,2,1,0:T(8,128)S(1)} %get-tuple-element.45), channel_id=1, source_target_pairs={{0,7},{1,0},{2,1},{3,2},{4,3},{5,4},{6,5},{7,6},{8,15},{9,8},{10,9... | collective-permute-start | bytes 2654216 | tf_op jit(solution)/shard_map/ppermute | solution.py:15
  22.3 0.6 scatter_fusion.1
  22.9 0.6 scatter_fusion
  25.1 1.1 %concatenate.329 = bf16[18,1,56,64]{3,2,1,0:T(8,128)(2,1)S(1)} concatenate(bf16[18,1,7,64]{3,2,1,0:T(8,128)(2,1)S(1)} %get-tuple-element.106, bf16[18,1,7,64]{3,2,1,0:T(8,128)(2,1)S(1)} %get-tuple-element.105, bf16[18,1,7,64]{3,2,1,0:T(8,128)(2,1)S(1)} %get-tuple-element.104, bf16[18,1,7,64]{3,2,1,0:T(8,128)(2,1)S(1)} %get-tuple-element.103, ...), dimensions={2} | concatenate | bytes 258048 | tf_op jit(solution)/shard_map/concatenate | solution.py:210
  26.2 0.9 %reshape.493 = bf16[8,2,4032]{2,1,0:T(2,128)(2,1)} reshape(bf16[56,1,18,64]{3,2,1,0:T(8,128)(2,1)S(1)} %bitcast.681) | data formatting | bytes 258048
  27.1 3.4 %all-to-all-start = ((bf16[8,2,4032]{2,1,0:T(2,128)(2,1)}), bf16[8,2,4032]{2,1,0:T(2,128)(2,1)S(1)}, u32[]{:S(2)}, u32[]{:S(2)}) async-start(bf16[8,2,4032]{2,1,0:T(2,128)(2,1)} %reshape.493), calls=%async_computation | async-start | bytes 262144 | tf_op jit(solution)/shard_map/all_to_all | solution.py:213
  30.5 9.5 %all-to-all-done = bf16[8,2,4032]{2,1,0:T(2,128)(2,1)S(1)} async-done(((bf16[8,2,4032]{2,1,0:T(2,128)(2,1)}), bf16[8,2,4032]{2,1,0:T(2,128)(2,1)S(1)}, u32[]{:S(2)}, u32[]{:S(2)}) %all-to-all-start) | async-done | bytes 129056 | tf_op jit(solution)/shard_map/all_to_all | solution.py:213
  40.1 0.2 reshape.494
  40.4 0.6 convolution_bitcast_fusion.1
  41.0 2.4 %convolution_bitcast_fusion = f32[18,17,24,64]{3,1,2,0:T(8,128)S(1)} fusion(f32[18,24,7,64]{3,1,2,0:T(8,128)S(1)} %convolution_bitcast_fusion.1, f32[9,3]{0,1:T(4,128)S(1)} %select_add_fusion, f32[9,3]{0,1:T(4,128)S(1)} %broadcast.1067), kind=kOutput, calls=%fused_computation.7 | convolution fusion | flops 19741744 | bytes 2654424 | tf_op jit(solution)/shard_map/gb,cfbz->cgfz/dot_general | solution.py:227
  43.5 1.3 %broadcast_select_fusion = f32[12,6,24,128]{3,2,1,0:T(8,128)S(1)} fusion(f32[12,6,24,128]{3,2,1,0:T(8,128)} %collective-permute-done.5, pred[]{:T(512)S(6)} %and.80), kind=kLoop, calls=%fused_computation.36 | loop fusion | flops 221184 | bytes 1769473 | tf_op jit(solution)/shard_map/jit(_where)/select_n | solution.py:16
  44.9 0.2 copy-done
  45.0 0.2 pad_maximum_fusion.10
  45.3 0.4 copy-done.9
  45.7 2.2 %fusion = f32[18,17,24,128]{3,2,1,0:T(8,128)S(1)} fusion(f32[18,17,24,64]{3,1,2,0:T(8,128)S(1)} %convolution_bitcast_fusion, f32[128]{0:T(128)S(1)} %copy-done.15, s32[128]{0:T(128)S(1)} %copy-done.10, f32[128]{0:T(128)S(1)} %copy-done.16, s32[128]{0:T(128)S(1)} %copy-done.9), kind=kOutput, calls=%fused_computation.2 | convolution fusion | flops 361013248 | bytes 5642240 | tf_op jit(solution)/shard_map/kz,cgfz->cgfk/dot_general | solution.py:228
  47.9 3.6 %collective-permute-start.7 = (f32[10,21,2,128]{3,2,1,0:T(2,128)S(1)}, f32[10,21,2,128]{3,2,1,0:T(2,128)S(1)}, u32[]{:S(2)}, u32[]{:S(2)}) collective-permute-start(f32[10,21,2,128]{3,2,1,0:T(2,128)S(1)} %get-tuple-element.33), channel_id=1, source_target_pairs={{8,0},{16,8},{24,16},{0,24},{9,1},{17,9},{25,17},{1,25},{10,2},{18... | collective-permute-start | bytes 645128 | tf_op jit(solution)/shard_map/ppermute | solution.py:25
  51.5 0.2 pad_maximum_fusion.1
  51.7 0.2 slice.1189
  51.8 2.8 %collective-permute-done.6 = f32[10,21,2,128]{3,2,1,0:T(2,128)S(1)} collective-permute-done((f32[10,21,2,128]{3,2,1,0:T(2,128)S(1)}, f32[10,21,2,128]{3,2,1,0:T(2,128)S(1)}, u32[]{:S(2)}, u32[]{:S(2)}) %collective-permute-start.6) | collective-permute-done | bytes 215072 | tf_op jit(solution)/shard_map/ppermute | solution.py:24
  54.7 3.6 %collective-permute-done.7 = f32[10,21,2,128]{3,2,1,0:T(2,128)S(1)} collective-permute-done((f32[10,21,2,128]{3,2,1,0:T(2,128)S(1)}, f32[10,21,2,128]{3,2,1,0:T(2,128)S(1)}, u32[]{:S(2)}, u32[]{:S(2)}) %collective-permute-start.7) | collective-permute-done | bytes 215072 | tf_op jit(solution)/shard_map/ppermute | solution.py:25
  58.4 0.6 pad_maximum_fusion
  59.0 0.2 slice_bitcast_fusion.3
  59.2 0.2 fusion.273
  59.4 0.2 fusion.21
  59.6 0.2 fusion.271
  59.8 0.4 fusion.32
  60.1 0.2 slice_add_fusion
  60.6 0.2 fusion.82
  60.8 0.2 slice_bitcast_fusion.4
  61.2 0.2 fusion.71
  61.8 0.5 fusion.6
  62.4 0.6 collective-permute-start.8
  63.0 3.3 %collective-permute-start.9 = (f32[9,17,2,128]{3,2,1,0:T(2,128)S(1)}, f32[9,17,2,128]{3,2,1,0:T(2,128)S(1)}, u32[]{:S(2)}, u32[]{:S(2)}) collective-permute-start(f32[9,17,2,128]{3,2,1,0:T(2,128)S(1)} %get-tuple-element.38), channel_id=1, source_target_pairs={{8,0},{16,8},{24,16},{0,24},{9,1},{17,9},{25,17},{1,25},{10,2},{18... | collective-permute-start | bytes 470024 | tf_op jit(solution)/shard_map/ppermute | solution.py:25
  66.3 4.9 %collective-permute-done.8 = f32[9,17,2,128]{3,2,1,0:T(2,128)S(1)} collective-permute-done((f32[9,17,2,128]{3,2,1,0:T(2,128)S(1)}, f32[9,17,2,128]{3,2,1,0:T(2,128)S(1)}, u32[]{:S(2)}, u32[]{:S(2)}) %collective-permute-start.8) | collective-permute-done | bytes 156704 | tf_op jit(solution)/shard_map/ppermute | solution.py:24
  71.3 0.8 collective-permute-done.9
  72.3 0.4 pad_maximum_fusion.2
  73.1 0.2 fusion.49
  73.3 0.2 fusion.44
  73.4 0.2 fusion.38
  73.6 0.1 slice_add_fusion.1
  74.9 0.3 copy-done.5
  75.2 0.4 fusion.12
  75.7 0.4 collective-permute-start.10
  76.2 3.5 %collective-permute-start.11 = (f32[9,13,2,128]{3,2,1,0:T(2,128)S(1)}, f32[9,13,2,128]{3,2,1,0:T(2,128)S(1)}, u32[]{:S(2)}, u32[]{:S(2)}) collective-permute-start(f32[9,13,2,128]{3,2,1,0:T(2,128)S(1)} %get-tuple-element.43), channel_id=1, source_target_pairs={{8,0},{16,8},{24,16},{0,24},{9,1},{17,9},{25,17},{1,25},{10,2},{18... | collective-permute-start | bytes 359432 | tf_op jit(solution)/shard_map/ppermute | solution.py:25
  79.7 2.9 %collective-permute-done.10 = f32[9,13,2,128]{3,2,1,0:T(2,128)S(1)} collective-permute-done((f32[9,13,2,128]{3,2,1,0:T(2,128)S(1)}, f32[9,13,2,128]{3,2,1,0:T(2,128)S(1)}, u32[]{:S(2)}, u32[]{:S(2)}) %collective-permute-start.10) | collective-permute-done | bytes 119840 | tf_op jit(solution)/shard_map/ppermute | solution.py:24
  82.6 0.8 collective-permute-done.11
  83.6 0.4 pad_maximum_fusion.3
  85.8 0.2 copy-done.4
  86.0 1.2 %fusion.16 = f32[9,24,9,128]{3,1,2,0:T(8,128)} fusion(f32[9,9,24,128]{3,2,1,0:T(8,128)S(1)} %fusion.151, f32[18,17,24,128]{3,2,1,0:T(8,128)S(1)} %fusion, f32[9,24]{1,0:T(8,128)S(1)} %copy-done.4), kind=kLoop, calls=%fused_computation.27 | loop fusion | flops 1244160 | bytes 3982176 | tf_op jit(solution)/shard_map/transpose | solution.py:264
  (139 shorter events, 6.6 us)
Async XLA Ops:
  3.7 16.3 %collective-permute-start.3 = (f32[3,1,24,64]{3,2,0,1:T(8,128)S(1)}, f32[3,1,24,64]{3,2,0,1:T(8,128)S(1)}, u32[]{:S(2)}, u32[]{:S(2)}) collective-permute-start(f32[3,1,24,64]{3,2,0,1:T(8,128)S(1)} %pad_maximum_fusion.19), channel_id=1, source_target_pairs={{0,2},{1,3},{2,4},{3,5},{4,6},{5,7},{6,8},{7,9},{8,10},{9,11},{10,... | collective-permute-start | bytes 55304 | tf_op jit(solution)/shard_map/ppermute | solution.py:15
  6.7 15.5 %collective-permute-start.2 = (f32[3,1,24,64]{3,2,0,1:T(8,128)S(1)}, f32[3,1,24,64]{3,2,0,1:T(8,128)S(1)}, u32[]{:S(2)}, u32[]{:S(2)}) collective-permute-start(f32[3,1,24,64]{3,2,0,1:T(8,128)S(1)} %pad_maximum_fusion.19), channel_id=1, source_target_pairs={{0,30},{1,31},{2,0},{3,1},{4,2},{5,3},{6,4},{7,5},{8,6},{9,7},{10,... | collective-permute-start | bytes 55304 | tf_op jit(solution)/shard_map/ppermute | solution.py:15
  10.7 12.9 %collective-permute-start.1 = (f32[10,1,24,64]{3,2,1,0:T(8,128)}, f32[10,1,24,64]{3,2,1,0:T(8,128)S(1)}, u32[]{:S(2)}, u32[]{:S(2)}) collective-permute-start(f32[10,1,24,64]{3,2,1,0:T(8,128)} %get-tuple-element.5), channel_id=1, source_target_pairs={{0,31},{1,0},{2,1},{3,2},{4,3},{5,4},{6,5},{7,6},{8,7},{9,8},{10,9... | collective-permute-start | bytes 184328 | tf_op jit(solution)/shard_map/ppermute | solution.py:15
  11.6 12.0 %collective-permute-start = (f32[10,1,24,64]{3,2,1,0:T(8,128)}, f32[10,1,24,64]{3,2,1,0:T(8,128)S(1)}, u32[]{:S(2)}, u32[]{:S(2)}) collective-permute-start(f32[10,1,24,64]{3,2,1,0:T(8,128)} %get-tuple-element.5), channel_id=1, source_target_pairs={{0,1},{1,2},{2,3},{3,4},{4,5},{5,6},{6,7},{7,8},{8,9},{9,10},{10,1... | collective-permute-start | bytes 184328 | tf_op jit(solution)/shard_map/ppermute | solution.py:15
  14.2 3.9 %copy-start.2 = (f32[9,1,24,64]{3,2,1,0:T(8,128)S(1)}, f32[9,1,24,64]{3,2,1,0:T(8,128)}, u32[]{:S(2)}) copy-start(f32[9,1,24,64]{3,2,1,0:T(8,128)} %refs_2_.1) | copy-start | bytes 165892
  14.2 8.1 %copy-start.8 = (s32[3]{0:T(128)S(1)}, s32[3]{0:T(128)}, u32[]{:S(2)}) copy-start(s32[3]{0:T(128)} %constant.291) | copy-start | bytes 40
  14.2 9.5 %copy-start.1 = (f32[10,1,24,64]{3,2,1,0:T(8,128)S(1)}, f32[10,1,24,64]{3,2,1,0:T(8,128)}, u32[]{:S(2)}) copy-start(f32[10,1,24,64]{3,2,1,0:T(8,128)} %get-tuple-element.5) | copy-start | bytes 184324
  15.8 27.6 %collective-permute-start.4 = (f32[12,6,24,128]{3,2,1,0:T(8,128)S(1)}, f32[12,6,24,128]{3,2,1,0:T(8,128)S(1)}, u32[]{:S(2)}, u32[]{:S(2)}) collective-permute-start(f32[12,6,24,128]{3,2,1,0:T(8,128)S(1)} %get-tuple-element.44), channel_id=1, source_target_pairs={{0,1},{1,2},{2,3},{3,4},{4,5},{5,6},{6,7},{7,0},{8,9},{9,10},{10,1... | collective-permute-start | bytes 2654216 | tf_op jit(solution)/shard_map/ppermute | solution.py:15
  20.0 23.5 %collective-permute-start.5 = (f32[12,6,24,128]{3,2,1,0:T(8,128)S(1)}, f32[12,6,24,128]{3,2,1,0:T(8,128)}, u32[]{:S(2)}, u32[]{:S(2)}) collective-permute-start(f32[12,6,24,128]{3,2,1,0:T(8,128)S(1)} %get-tuple-element.45), channel_id=1, source_target_pairs={{0,7},{1,0},{2,1},{3,2},{4,3},{5,4},{6,5},{7,6},{8,15},{9,8},{10,9... | collective-permute-start | bytes 2654216 | tf_op jit(solution)/shard_map/ppermute | solution.py:15
  23.8 0.7 copy-start.3
  23.8 0.7 copy-start.6
  24.5 15.8 %copy-start.11 = (s32[24]{0:T(128)S(1)}, s32[24]{0:T(128)}, u32[]{:S(2)}) copy-start(s32[24]{0:T(128)} %get-tuple-element.142) | copy-start | bytes 292
  24.5 15.8 %copy-start.12 = (s32[24]{0:T(128)S(1)}, s32[24]{0:T(128)}, u32[]{:S(2)}) copy-start(s32[24]{0:T(128)} %get-tuple-element.143) | copy-start | bytes 292
  24.5 15.8 %copy-start.13 = (f32[24]{0:T(128)S(1)}, f32[24]{0:T(128)}, u32[]{:S(2)}) copy-start(f32[24]{0:T(128)} %get-tuple-element.140) | copy-start | bytes 292
  24.5 15.8 %copy-start.14 = (f32[24]{0:T(128)S(1)}, f32[24]{0:T(128)}, u32[]{:S(2)}) copy-start(f32[24]{0:T(128)} %get-tuple-element.141) | copy-start | bytes 292
  27.1 13.0 %all-to-all-start = ((bf16[8,2,4032]{2,1,0:T(2,128)(2,1)}), bf16[8,2,4032]{2,1,0:T(2,128)(2,1)S(1)}, u32[]{:S(2)}, u32[]{:S(2)}) async-start(bf16[8,2,4032]{2,1,0:T(2,128)(2,1)} %reshape.493), calls=%async_computation | async-start | bytes 262144 | tf_op jit(solution)/shard_map/all_to_all | solution.py:213
  43.4 1.6 %copy-start = (f32[12,9,24,128]{3,2,1,0:T(8,128)S(1)}, f32[12,9,24,128]{3,2,1,0:T(8,128)}, u32[]{:S(2)}) copy-start(f32[12,9,24,128]{3,2,1,0:T(8,128)} %shard_map.87) | copy-start | bytes 3981316
  45.0 0.7 copy-start.9
  45.0 0.7 copy-start.10
  45.0 0.7 copy-start.15
  45.0 0.7 copy-start.16
  45.2 9.5 %collective-permute-start.6 = (f32[10,21,2,128]{3,2,1,0:T(2,128)S(1)}, f32[10,21,2,128]{3,2,1,0:T(2,128)S(1)}, u32[]{:S(2)}, u32[]{:S(2)}) collective-permute-start(f32[10,21,2,128]{3,2,1,0:T(2,128)S(1)} %get-tuple-element.32), channel_id=1, source_target_pairs={{0,8},{8,16},{16,24},{24,0},{1,9},{9,17},{17,25},{25,1},{2,10},{10... | collective-permute-start | bytes 645128 | tf_op jit(solution)/shard_map/ppermute | solution.py:24
  47.9 10.4 %collective-permute-start.7 = (f32[10,21,2,128]{3,2,1,0:T(2,128)S(1)}, f32[10,21,2,128]{3,2,1,0:T(2,128)S(1)}, u32[]{:S(2)}, u32[]{:S(2)}) collective-permute-start(f32[10,21,2,128]{3,2,1,0:T(2,128)S(1)} %get-tuple-element.33), channel_id=1, source_target_pairs={{8,0},{16,8},{24,16},{0,24},{9,1},{17,9},{25,17},{1,25},{10,2},{18... | collective-permute-start | bytes 645128 | tf_op jit(solution)/shard_map/ppermute | solution.py:25
  62.4 8.8 %collective-permute-start.8 = (f32[9,17,2,128]{3,2,1,0:T(2,128)S(1)}, f32[9,17,2,128]{3,2,1,0:T(2,128)S(1)}, u32[]{:S(2)}, u32[]{:S(2)}) collective-permute-start(f32[9,17,2,128]{3,2,1,0:T(2,128)S(1)} %get-tuple-element.37), channel_id=1, source_target_pairs={{0,8},{8,16},{16,24},{24,0},{1,9},{9,17},{17,25},{25,1},{2,10},{10... | collective-permute-start | bytes 470024 | tf_op jit(solution)/shard_map/ppermute | solution.py:24
  63.0 9.0 %collective-permute-start.9 = (f32[9,17,2,128]{3,2,1,0:T(2,128)S(1)}, f32[9,17,2,128]{3,2,1,0:T(2,128)S(1)}, u32[]{:S(2)}, u32[]{:S(2)}) collective-permute-start(f32[9,17,2,128]{3,2,1,0:T(2,128)S(1)} %get-tuple-element.38), channel_id=1, source_target_pairs={{8,0},{16,8},{24,16},{0,24},{9,1},{17,9},{25,17},{1,25},{10,2},{18... | collective-permute-start | bytes 470024 | tf_op jit(solution)/shard_map/ppermute | solution.py:25
  74.5 0.7 copy-start.5
  75.7 6.8 %collective-permute-start.10 = (f32[9,13,2,128]{3,2,1,0:T(2,128)S(1)}, f32[9,13,2,128]{3,2,1,0:T(2,128)S(1)}, u32[]{:S(2)}, u32[]{:S(2)}) collective-permute-start(f32[9,13,2,128]{3,2,1,0:T(2,128)S(1)} %get-tuple-element.42), channel_id=1, source_target_pairs={{0,8},{8,16},{16,24},{24,0},{1,9},{9,17},{17,25},{25,1},{2,10},{10... | collective-permute-start | bytes 359432 | tf_op jit(solution)/shard_map/ppermute | solution.py:24
  76.1 7.5 %copy-start.7 = (f32[9,1,24,64]{3,2,1,0:T(8,128)}, f32[9,1,24,64]{3,2,1,0:T(8,128)S(1)}, u32[]{:S(2)}) copy-start(f32[9,1,24,64]{3,2,1,0:T(8,128)S(1)} %constant_dynamic-update-slice_fusion) | copy-start | bytes 165892
  76.2 7.3 %collective-permute-start.11 = (f32[9,13,2,128]{3,2,1,0:T(2,128)S(1)}, f32[9,13,2,128]{3,2,1,0:T(2,128)S(1)}, u32[]{:S(2)}, u32[]{:S(2)}) collective-permute-start(f32[9,13,2,128]{3,2,1,0:T(2,128)S(1)} %get-tuple-element.43), channel_id=1, source_target_pairs={{8,0},{16,8},{24,16},{0,24},{9,1},{17,9},{25,17},{1,25},{10,2},{18... | collective-permute-start | bytes 359432 | tf_op jit(solution)/shard_map/ppermute | solution.py:25
  85.3 0.7 copy-start.4

commit v18 on v15

--- a/solution.py
+++ b/solution.py
@@ -204,8 +204,10 @@
     used = np.nonzero(np.any(blocks_np != 0.0, axis=0))[0]
     lo, hi = int(used[0]), int(used[-1]) + 1
     both = jnp.pad(both, ((0, 0), (0, 0), (rows_each, rows_each), (0, 0)))
+    depth_np = interp_np(fine_z, both.shape[3])
+    deep = int(np.nonzero(np.any(depth_np != 0.0, axis=0))[0][-1]) + 1
     send = jnp.concatenate(
-        [both[:, :, rows_each * d + lo: rows_each * d + hi] for d in range(count_y)], 2
+        [both[:, :, rows_each * d + lo: rows_each * d + hi, :deep] for d in range(count_y)], 2
     )
     band = lax.all_to_all(send, "gy", 2, 1, tiled=True).astype(jnp.float32)
     columns = band.shape[1]
@@ -223,7 +225,7 @@
     first = jnp.einsum("fa,cabz->cfbz", interp_matrix(fine_x, columns), band, precision=high)
     second = jnp.einsum("gb,cfbz->cgfz", tiles_w, first, precision=high)
     background = jnp.einsum(
-        "kz,cgfz->cgfk", interp_matrix(fine_z, band.shape[3]), second, precision=high
+        "kz,cgfz->cgfk", interp_matrix(fine_z, both.shape[3])[:, :deep], second, precision=high
     )
     along_x = ramp(lax.axis_index("gx") * fine_x, fine_x, count_x * fine_x, fine_x)
     along_y = ramp(me_y * fine_y - 4, fine_y + 8, count_y * fine_y, fine_y)

time: 85.9 us -> 85.2 us (level)
  local copies, waits for them, and re-layouts: 11.6 us -> 6.7 us
  waiting for transfers between devices: 26.2 us -> 29.5 us
    all_to_all x1, waiting for transfers between devices: 10.5 us -> 13.8 us  [local(): band = lax.all_to_all(send, 'gy', 2, 1, tiled=True).astype(jnp.float32)]
    unnamed x22 -> x31, local copies, waits for them, and re-layouts: 5.11 us -> 2 us
    concatenate x2, local copies, waits for them, and re-layouts: 1.18 us -> 0.05 us  [the longest x1 0.02 us: local(): both = jnp.concatenate([region_state, region_next], 0).astype(jnp.bfloat16)]
    select_n x6, other arithmetic: 1.44 us -> 2.34 us  [from_cycle(): return jnp.where((me - d >= 0) & (me - d < n), got, 0.0)]
  transfers between devices with their start and end apart: 13 -> 13, of which waited for: 8 -> 7; matrix products, arithmetic and copies ran while one was open for 18% -> 13% of each run, Pallas kernels for 3% -> 3%
where the time goes in v18:
time: 85.2 us; the launch traced here: 84.7 us
  waiting for transfers between devices  29.5 us (35%)
  starting transfers between devices  25.9 us (30%)
  other arithmetic  11.9 us (14%)
  local copies, waits for them, and re-layouts  6.7 us (8%)
  matrix products  5.15 us (6%)
  Pallas kernels  4.21 us (5%)
  between operations  1.47 us (2%)
    all_to_all x1, waiting for transfers between devices, local(): band = lax.all_to_all(send, 'gy', 2, 1, tiled=True).astype(jnp.float32)  13.8 us
    ppermute x3, starting transfers between devices, x_halo(): from_right = lax.ppermute(field[:, :, :width], 'gx', back)  10.8 us
    ppermute x6, starting transfers between devices, from_cycle(): got = lax.ppermute(field, axis, [(i, (i + d) % n) for i in range(n)])  10.6 us
    ppermute x3, waiting for transfers between devices, x_halo(): from_left = lax.ppermute(field[:, :, -width:], 'gx', cycle)  10.4 us
    ppermute x3, waiting for transfers between devices, x_halo(): from_right = lax.ppermute(field[:, :, :width], 'gx', back)  5.22 us
    pallas_call x2, Pallas kernels, lookup(): pl.pallas_call(lambda *refs: lookup_kernel(step, extra, *refs), out_shape...  4.21 us
    all_to_all x1, starting transfers between devices, local(): band = lax.all_to_all(send, 'gy', 2, 1, tiled=True).astype(jnp.float32)  3.36 us
    slice x27, local copies, waits for them, and re-layouts, along(): lax.slice_in_dim(f, 1, n, axis=axis)  2.43 us
  transfers between devices with their start and end apart: 13, of which 7 were waited for; matrix products, arithmetic and copies ran while one was open for 13% of the time, Pallas kernels for 3%

profile of v18, /device:TPU:0, one launch (start us, length us, event | category | flops | bytes accessed | tf_op | source)
XLA Modules:
  0.0 84.7 jit_solution(6792420429149869647)
XLA Ops:
  0.6 1.6 %shard_map.68 = (f32[10,1,24,64]{3,2,1,0:T(8,128)}, f32[1,24,64]{2,1,0:T(8,128)}, f32[1,24,64]{2,1,0:T(8,128)}) custom-call(s32[1,24,64]{2,1,0:T(8,128)} %refs_0_.1, f32[3,8]{1,0:T(4,128)} %refs_1_.3, f32[9,1,24,64]{3,2,1,0:T(8,128)} %refs_2_.1), custom_call_target="tpu_custom_call" | custom-call | tf_op jit(solution)/shard_map/pallas_call | solution.py:58
  2.2 2.9 %collective-permute-start.3 = (f32[10,1,24,64]{3,2,1,0:T(8,128)}, f32[10,1,24,64]{3,2,1,0:T(8,128)S(1)}, u32[]{:S(2)}, u32[]{:S(2)}) collective-permute-start(f32[10,1,24,64]{3,2,1,0:T(8,128)} %get-tuple-element.5), channel_id=1, source_target_pairs={{0,2},{1,3},{2,4},{3,5},{4,6},{5,7},{6,8},{7,9},{8,10},{9,11},{10,... | collective-permute-start | bytes 184328 | tf_op jit(solution)/shard_map/ppermute | solution.py:15
  5.2 4.0 %collective-permute-start.2 = (f32[10,1,24,64]{3,2,1,0:T(8,128)}, f32[10,1,24,64]{3,2,1,0:T(8,128)S(1)}, u32[]{:S(2)}, u32[]{:S(2)}) collective-permute-start(f32[10,1,24,64]{3,2,1,0:T(8,128)} %get-tuple-element.5), channel_id=1, source_target_pairs={{0,30},{1,31},{2,0},{3,1},{4,2},{5,3},{6,4},{7,5},{8,6},{9,7},{10,... | collective-permute-start | bytes 184328 | tf_op jit(solution)/shard_map/ppermute | solution.py:15
  9.2 0.9 %collective-permute-start.1 = (f32[10,1,24,64]{3,2,1,0:T(8,128)}, f32[10,1,24,64]{3,2,1,0:T(8,128)}, u32[]{:S(2)}, u32[]{:S(2)}) collective-permute-start(f32[10,1,24,64]{3,2,1,0:T(8,128)} %get-tuple-element.5), channel_id=1, source_target_pairs={{0,31},{1,0},{2,1},{3,2},{4,3},{5,4},{6,5},{7,6},{8,7},{9,8},{10,9... | collective-permute-start | bytes 184328 | tf_op jit(solution)/shard_map/ppermute | solution.py:15
  10.1 2.6 %shard_map.69 = f32[12,9,24,128]{3,2,1,0:T(8,128)} custom-call(s32[9,24,128]{2,1,0:T(8,128)} %bitcast.662, f32[3,8]{1,0:T(4,128)} %refs_1_.3, f32[9,9,24,128]{3,2,1,0:T(8,128)} %bitcast.660), custom_call_target="tpu_custom_call" | custom-call | tf_op jit(solution)/shard_map/pallas_call | solution.py:58
  12.7 1.6 %fusion.275 = (f32[12,6,24,128]{3,2,1,0:T(8,128)S(1)}, f32[12,6,24,128]{3,2,1,0:T(8,128)S(1)}) fusion(f32[12,9,24,128]{3,2,1,0:T(8,128)} %shard_map.69), kind=kLoop, calls=%fused_computation.506 | loop fusion | bytes 3538944 | tf_op jit(solution)/shard_map/slice | solution.py:186
  14.3 0.4 collective-permute-start.4
  15.1 2.3 %collective-permute-start.5 = (f32[12,6,24,128]{3,2,1,0:T(8,128)S(1)}, f32[12,6,24,128]{3,2,1,0:T(8,128)}, u32[]{:S(2)}, u32[]{:S(2)}) collective-permute-start(f32[12,6,24,128]{3,2,1,0:T(8,128)S(1)} %get-tuple-element.45), channel_id=1, source_target_pairs={{0,7},{1,0},{2,1},{3,2},{4,3},{5,4},{6,5},{7,6},{8,15},{9,8},{10,9... | collective-permute-start | bytes 2654216 | tf_op jit(solution)/shard_map/ppermute | solution.py:15
  17.4 0.9 %broadcast_select_fusion.10 = f32[10,1,24,64]{3,2,1,0:T(8,128)S(1)} fusion(f32[10,1,24,64]{3,2,1,0:T(8,128)} %collective-permute-done.1, pred[]{:T(512)S(6)} %and.76), kind=kLoop, calls=%fused_computation.336 | loop fusion | flops 15360 | bytes 122881 | tf_op jit(solution)/shard_map/jit(_where)/select_n | solution.py:16
  19.9 1.0 %reshape.473 = bf16[8,2,2709]{2,1,0:T(2,128)(2,1)} reshape(bf16[56,1,18,43]{3,2,1,0:T(8,128)(2,1)S(1)} %bitcast.661) | data formatting | bytes 173376
  20.9 3.4 %all-to-all-start = ((bf16[8,2,2709]{2,1,0:T(2,128)(2,1)}), bf16[8,2,2709]{2,1,0:T(2,128)(2,1)S(1)}, u32[]{:S(2)}, u32[]{:S(2)}) async-start(bf16[8,2,2709]{2,1,0:T(2,128)(2,1)} %reshape.473), calls=%async_computation | async-start | bytes 180224 | tf_op jit(solution)/shard_map/all_to_all | solution.py:212
  24.3 13.8 %all-to-all-done = bf16[8,2,2709]{2,1,0:T(2,128)(2,1)S(1)} async-done(((bf16[8,2,2709]{2,1,0:T(2,128)(2,1)}), bf16[8,2,2709]{2,1,0:T(2,128)(2,1)S(1)}, u32[]{:S(2)}, u32[]{:S(2)}) %all-to-all-start) | async-done | bytes 86720 | tf_op jit(solution)/shard_map/all_to_all | solution.py:212
  38.1 0.4 reshape.474
  38.6 0.6 convolution_bitcast_fusion.1
  39.2 2.4 %convolution_bitcast_fusion = f32[18,17,24,43]{3,1,2,0:T(8,128)S(1)} fusion(f32[18,24,7,43]{3,1,2,0:T(8,128)S(1)} %convolution_bitcast_fusion.1, f32[9,3]{0,1:T(4,128)S(1)} %select_add_fusion, f32[9,3]{0,1:T(4,128)S(1)} %broadcast.1055), kind=kOutput, calls=%fused_computation.5 | convolution fusion | flops 13264335 | bytes 1783512 | tf_op jit(solution)/shard_map/gb,cfbz->cgfz/dot_general | solution.py:226
  41.7 1.3 %broadcast_select_fusion = f32[12,6,24,128]{3,2,1,0:T(8,128)S(1)} fusion(f32[12,6,24,128]{3,2,1,0:T(8,128)} %collective-permute-done.5, pred[]{:T(512)S(6)} %and.80), kind=kLoop, calls=%fused_computation.34 | loop fusion | flops 221184 | bytes 1769473 | tf_op jit(solution)/shard_map/jit(_where)/select_n | solution.py:16
  43.0 0.2 copy-done
  43.2 0.1 pad_maximum_fusion.10
  43.4 2.1 %fusion = f32[18,17,24,128]{3,2,1,0:T(8,128)S(1)} fusion(f32[18,17,24,43]{3,1,2,0:T(8,128)S(1)} %convolution_bitcast_fusion, f32[128]{0:T(128)S(1)} %get-tuple-element.140, f32[128]{0:T(128)S(1)} %get-tuple-element.141, s32[128]{0:T(128)S(1)} %get-tuple-element.143, s32[128]{0:T(128)S(1)} %get-tuple-element.142), kind=kOutput, calls=%fused_computation | convolution fusion | flops 242561280 | bytes 5025344 | tf_op jit(solution)/shard_map/kz,cgfz->cgfk/dot_general | solution.py:227
  45.6 4.0 %collective-permute-start.7 = (f32[10,21,2,128]{3,2,1,0:T(2,128)S(1)}, f32[10,21,2,128]{3,2,1,0:T(2,128)S(1)}, u32[]{:S(2)}, u32[]{:S(2)}) collective-permute-start(f32[10,21,2,128]{3,2,1,0:T(2,128)S(1)} %get-tuple-element.33), channel_id=1, source_target_pairs={{8,0},{16,8},{24,16},{0,24},{9,1},{17,9},{25,17},{1,25},{10,2},{18... | collective-permute-start | bytes 645128 | tf_op jit(solution)/shard_map/ppermute | solution.py:25
  49.6 0.2 pad_maximum_fusion.1
  49.8 0.2 slice.1183
  50.0 2.6 %collective-permute-done.6 = f32[10,21,2,128]{3,2,1,0:T(2,128)S(1)} collective-permute-done((f32[10,21,2,128]{3,2,1,0:T(2,128)S(1)}, f32[10,21,2,128]{3,2,1,0:T(2,128)S(1)}, u32[]{:S(2)}, u32[]{:S(2)}) %collective-permute-start.6) | collective-permute-done | bytes 215072 | tf_op jit(solution)/shard_map/ppermute | solution.py:24
  52.7 3.7 %collective-permute-done.7 = f32[10,21,2,128]{3,2,1,0:T(2,128)S(1)} collective-permute-done((f32[10,21,2,128]{3,2,1,0:T(2,128)S(1)}, f32[10,21,2,128]{3,2,1,0:T(2,128)S(1)}, u32[]{:S(2)}, u32[]{:S(2)}) %collective-permute-start.7) | collective-permute-done | bytes 215072 | tf_op jit(solution)/shard_map/ppermute | solution.py:25
  56.5 0.6 pad_maximum_fusion
  57.1 0.2 slice_bitcast_fusion.3
  57.3 0.2 fusion.278
  57.4 0.2 fusion.21
  57.6 0.2 fusion.276
  57.9 0.4 fusion.32
  58.2 0.2 slice_add_fusion
  58.7 0.2 fusion.82
  58.8 0.2 slice_bitcast_fusion.4
  59.3 0.2 fusion.71
  59.6 0.1 fusion.63
  59.8 0.1 fusion.56
  59.9 0.5 fusion.6
  60.5 0.7 collective-permute-start.8
  61.2 3.2 %collective-permute-start.9 = (f32[9,17,2,128]{3,2,1,0:T(2,128)S(1)}, f32[9,17,2,128]{3,2,1,0:T(2,128)S(1)}, u32[]{:S(2)}, u32[]{:S(2)}) collective-permute-start(f32[9,17,2,128]{3,2,1,0:T(2,128)S(1)} %get-tuple-element.38), channel_id=1, source_target_pairs={{8,0},{16,8},{24,16},{0,24},{9,1},{17,9},{25,17},{1,25},{10,2},{18... | collective-permute-start | bytes 470024 | tf_op jit(solution)/shard_map/ppermute | solution.py:25
  64.4 4.9 %collective-permute-done.8 = f32[9,17,2,128]{3,2,1,0:T(2,128)S(1)} collective-permute-done((f32[9,17,2,128]{3,2,1,0:T(2,128)S(1)}, f32[9,17,2,128]{3,2,1,0:T(2,128)S(1)}, u32[]{:S(2)}, u32[]{:S(2)}) %collective-permute-start.8) | collective-permute-done | bytes 156704 | tf_op jit(solution)/shard_map/ppermute | solution.py:24
  69.4 0.8 collective-permute-done.9
  70.3 0.1 maximum_bitcast_fusion.2
  70.4 0.4 pad_maximum_fusion.2
  70.8 0.1 fusion.279
  71.0 0.1 fusion.280
  71.1 0.1 fusion.281
  71.3 0.2 fusion.49
  71.4 0.2 fusion.44
  71.6 0.2 fusion.38
  71.7 0.1 slice_add_fusion.1
  72.2 0.1 fusion.138
  72.4 0.1 fusion.127
  72.6 0.1 slice_bitcast_fusion.7
  72.9 0.1 fusion.112
  73.0 0.4 fusion.12
  73.5 0.4 collective-permute-start.10
  74.0 3.5 %collective-permute-start.11 = (f32[9,13,2,128]{3,2,1,0:T(2,128)S(1)}, f32[9,13,2,128]{3,2,1,0:T(2,128)S(1)}, u32[]{:S(2)}, u32[]{:S(2)}) collective-permute-start(f32[9,13,2,128]{3,2,1,0:T(2,128)S(1)} %get-tuple-element.43), channel_id=1, source_target_pairs={{8,0},{16,8},{24,16},{0,24},{9,1},{17,9},{25,17},{1,25},{10,2},{18... | collective-permute-start | bytes 359432 | tf_op jit(solution)/shard_map/ppermute | solution.py:25
  77.5 3.0 %collective-permute-done.10 = f32[9,13,2,128]{3,2,1,0:T(2,128)S(1)} collective-permute-done((f32[9,13,2,128]{3,2,1,0:T(2,128)S(1)}, f32[9,13,2,128]{3,2,1,0:T(2,128)S(1)}, u32[]{:S(2)}, u32[]{:S(2)}) %collective-permute-start.10) | collective-permute-done | bytes 119840 | tf_op jit(solution)/shard_map/ppermute | solution.py:24
  80.5 0.7 collective-permute-done.11
  81.3 0.4 pad_maximum_fusion.3
  82.1 0.1 fusion.105
  82.2 0.1 fusion.100
  82.3 0.1 fusion.94
  83.5 1.2 %fusion.16 = f32[9,24,9,128]{3,1,2,0:T(8,128)} fusion(f32[9,9,24,128]{3,2,1,0:T(8,128)S(1)} %fusion.151, f32[18,17,24,128]{3,2,1,0:T(8,128)S(1)} %fusion, f32[9,24]{1,0:T(8,128)S(1)} %slice.1310), kind=kLoop, calls=%fused_computation.25 | loop fusion | flops 1244160 | bytes 3982176 | tf_op jit(solution)/shard_map/transpose | solution.py:263
  (116 shorter events, 5.1 us)
Async XLA Ops:
  2.2 16.3 %collective-permute-start.3 = (f32[10,1,24,64]{3,2,1,0:T(8,128)}, f32[10,1,24,64]{3,2,1,0:T(8,128)S(1)}, u32[]{:S(2)}, u32[]{:S(2)}) collective-permute-start(f32[10,1,24,64]{3,2,1,0:T(8,128)} %get-tuple-element.5), channel_id=1, source_target_pairs={{0,2},{1,3},{2,4},{3,5},{4,6},{5,7},{6,8},{7,9},{8,10},{9,11},{10,... | collective-permute-start | bytes 184328 | tf_op jit(solution)/shard_map/ppermute | solution.py:15
  5.2 13.5 %collective-permute-start.2 = (f32[10,1,24,64]{3,2,1,0:T(8,128)}, f32[10,1,24,64]{3,2,1,0:T(8,128)S(1)}, u32[]{:S(2)}, u32[]{:S(2)}) collective-permute-start(f32[10,1,24,64]{3,2,1,0:T(8,128)} %get-tuple-element.5), channel_id=1, source_target_pairs={{0,30},{1,31},{2,0},{3,1},{4,2},{5,3},{6,4},{7,5},{8,6},{9,7},{10,... | collective-permute-start | bytes 184328 | tf_op jit(solution)/shard_map/ppermute | solution.py:15
  9.2 5.9 %collective-permute-start.1 = (f32[10,1,24,64]{3,2,1,0:T(8,128)}, f32[10,1,24,64]{3,2,1,0:T(8,128)}, u32[]{:S(2)}, u32[]{:S(2)}) collective-permute-start(f32[10,1,24,64]{3,2,1,0:T(8,128)} %get-tuple-element.5), channel_id=1, source_target_pairs={{0,31},{1,0},{2,1},{3,2},{4,3},{5,4},{6,5},{7,6},{8,7},{9,8},{10,9... | collective-permute-start | bytes 184328 | tf_op jit(solution)/shard_map/ppermute | solution.py:15
  10.1 8.2 %collective-permute-start = (f32[10,1,24,64]{3,2,1,0:T(8,128)}, f32[10,1,24,64]{3,2,1,0:T(8,128)S(1)}, u32[]{:S(2)}, u32[]{:S(2)}) collective-permute-start(f32[10,1,24,64]{3,2,1,0:T(8,128)} %get-tuple-element.5), channel_id=1, source_target_pairs={{0,1},{1,2},{2,3},{3,4},{4,5},{5,6},{6,7},{7,8},{8,9},{9,10},{10,1... | collective-permute-start | bytes 184328 | tf_op jit(solution)/shard_map/ppermute | solution.py:15
  12.7 2.3 %copy-start.2 = (f32[9,1,24,64]{3,2,1,0:T(8,128)S(1)}, f32[9,1,24,64]{3,2,1,0:T(8,128)}, u32[]{:S(2)}) copy-start(f32[9,1,24,64]{3,2,1,0:T(8,128)} %refs_2_.1) | copy-start | bytes 165892
  12.7 5.6 %copy-start.1 = (f32[10,1,24,64]{3,2,1,0:T(8,128)S(1)}, f32[10,1,24,64]{3,2,1,0:T(8,128)}, u32[]{:S(2)}) copy-start(f32[10,1,24,64]{3,2,1,0:T(8,128)} %get-tuple-element.5) | copy-start | bytes 184324
  14.3 27.3 %collective-permute-start.4 = (f32[12,6,24,128]{3,2,1,0:T(8,128)S(1)}, f32[12,6,24,128]{3,2,1,0:T(8,128)S(1)}, u32[]{:S(2)}, u32[]{:S(2)}) collective-permute-start(f32[12,6,24,128]{3,2,1,0:T(8,128)S(1)} %get-tuple-element.44), channel_id=1, source_target_pairs={{0,1},{1,2},{2,3},{3,4},{4,5},{5,6},{6,7},{7,0},{8,9},{9,10},{10,1... | collective-permute-start | bytes 2654216 | tf_op jit(solution)/shard_map/ppermute | solution.py:15
  15.1 26.6 %collective-permute-start.5 = (f32[12,6,24,128]{3,2,1,0:T(8,128)S(1)}, f32[12,6,24,128]{3,2,1,0:T(8,128)}, u32[]{:S(2)}, u32[]{:S(2)}) collective-permute-start(f32[12,6,24,128]{3,2,1,0:T(8,128)S(1)} %get-tuple-element.45), channel_id=1, source_target_pairs={{0,7},{1,0},{2,1},{3,2},{4,3},{5,4},{6,5},{7,6},{8,15},{9,8},{10,9... | collective-permute-start | bytes 2654216 | tf_op jit(solution)/shard_map/ppermute | solution.py:15
  18.6 0.7 copy-start.3
  18.6 0.7 copy-start.4
  20.9 17.2 %all-to-all-start = ((bf16[8,2,2709]{2,1,0:T(2,128)(2,1)}), bf16[8,2,2709]{2,1,0:T(2,128)(2,1)S(1)}, u32[]{:S(2)}, u32[]{:S(2)}) async-start(bf16[8,2,2709]{2,1,0:T(2,128)(2,1)} %reshape.473), calls=%async_computation | async-start | bytes 180224 | tf_op jit(solution)/shard_map/all_to_all | solution.py:212
  41.6 1.6 %copy-start = (f32[12,9,24,128]{3,2,1,0:T(8,128)S(1)}, f32[12,9,24,128]{3,2,1,0:T(8,128)}, u32[]{:S(2)}) copy-start(f32[12,9,24,128]{3,2,1,0:T(8,128)} %shard_map.69) | copy-start | bytes 3981316
  43.3 9.2 %collective-permute-start.6 = (f32[10,21,2,128]{3,2,1,0:T(2,128)S(1)}, f32[10,21,2,128]{3,2,1,0:T(2,128)S(1)}, u32[]{:S(2)}, u32[]{:S(2)}) collective-permute-start(f32[10,21,2,128]{3,2,1,0:T(2,128)S(1)} %get-tuple-element.32), channel_id=1, source_target_pairs={{0,8},{8,16},{16,24},{24,0},{1,9},{9,17},{17,25},{25,1},{2,10},{10... | collective-permute-start | bytes 645128 | tf_op jit(solution)/shard_map/ppermute | solution.py:24
  45.6 10.8 %collective-permute-start.7 = (f32[10,21,2,128]{3,2,1,0:T(2,128)S(1)}, f32[10,21,2,128]{3,2,1,0:T(2,128)S(1)}, u32[]{:S(2)}, u32[]{:S(2)}) collective-permute-start(f32[10,21,2,128]{3,2,1,0:T(2,128)S(1)} %get-tuple-element.33), channel_id=1, source_target_pairs={{8,0},{16,8},{24,16},{0,24},{9,1},{17,9},{25,17},{1,25},{10,2},{18... | collective-permute-start | bytes 645128 | tf_op jit(solution)/shard_map/ppermute | solution.py:25
  60.5 8.8 %collective-permute-start.8 = (f32[9,17,2,128]{3,2,1,0:T(2,128)S(1)}, f32[9,17,2,128]{3,2,1,0:T(2,128)S(1)}, u32[]{:S(2)}, u32[]{:S(2)}) collective-permute-start(f32[9,17,2,128]{3,2,1,0:T(2,128)S(1)} %get-tuple-element.37), channel_id=1, source_target_pairs={{0,8},{8,16},{16,24},{24,0},{1,9},{9,17},{17,25},{25,1},{2,10},{10... | collective-permute-start | bytes 470024 | tf_op jit(solution)/shard_map/ppermute | solution.py:24
  61.2 9.0 %collective-permute-start.9 = (f32[9,17,2,128]{3,2,1,0:T(2,128)S(1)}, f32[9,17,2,128]{3,2,1,0:T(2,128)S(1)}, u32[]{:S(2)}, u32[]{:S(2)}) collective-permute-start(f32[9,17,2,128]{3,2,1,0:T(2,128)S(1)} %get-tuple-element.38), channel_id=1, source_target_pairs={{8,0},{16,8},{24,16},{0,24},{9,1},{17,9},{25,17},{1,25},{10,2},{18... | collective-permute-start | bytes 470024 | tf_op jit(solution)/shard_map/ppermute | solution.py:25
  73.5 6.9 %collective-permute-start.10 = (f32[9,13,2,128]{3,2,1,0:T(2,128)S(1)}, f32[9,13,2,128]{3,2,1,0:T(2,128)S(1)}, u32[]{:S(2)}, u32[]{:S(2)}) collective-permute-start(f32[9,13,2,128]{3,2,1,0:T(2,128)S(1)} %get-tuple-element.42), channel_id=1, source_target_pairs={{0,8},{8,16},{16,24},{24,0},{1,9},{9,17},{17,25},{25,1},{2,10},{10... | collective-permute-start | bytes 359432 | tf_op jit(solution)/shard_map/ppermute | solution.py:24
  73.9 7.4 %copy-start.5 = (f32[9,1,24,64]{3,2,1,0:T(8,128)}, f32[9,1,24,64]{3,2,1,0:T(8,128)S(1)}, u32[]{:S(2)}) copy-start(f32[9,1,24,64]{3,2,1,0:T(8,128)S(1)} %constant_dynamic-update-slice_fusion) | copy-start | bytes 165892
  74.0 7.2 %collective-permute-start.11 = (f32[9,13,2,128]{3,2,1,0:T(2,128)S(1)}, f32[9,13,2,128]{3,2,1,0:T(2,128)S(1)}, u32[]{:S(2)}, u32[]{:S(2)}) collective-permute-start(f32[9,13,2,128]{3,2,1,0:T(2,128)S(1)} %get-tuple-element.43), channel_id=1, source_target_pairs={{8,0},{16,8},{24,16},{0,24},{9,1},{17,9},{25,17},{1,25},{10,2},{18... | collective-permute-start | bytes 359432 | tf_op jit(solution)/shard_map/ppermute | solution.py:25

commit v19 on v18

--- a/solution.py
+++ b/solution.py
@@ -174,17 +174,8 @@
     reach_y = 6
 
     region_pay, lam_r, mu_r = lookup(region_material, material_table, region_state, 0.6, False)
-    (fine_pay,) = lookup(
-        jnp.transpose(fine_material, (1, 0, 2)),
-        material_table,
-        jnp.transpose(fine_state, (0, 2, 1, 3)),
-        0.2,
-        True,
-    )
 
     me_flat = lax.axis_index("gx") * count_y + me_y
-    fine_lo = from_cycle(fine_pay[:, -reach_y:], "gy", count_y, 1, me_y)
-    fine_hi = from_cycle(fine_pay[:, :reach_y], "gy", count_y, -1, me_y)
     reg_lo = from_cycle(region_pay, flat, n_flat, 1, me_flat)
     reg_hi = from_cycle(region_pay, flat, n_flat, -1, me_flat)
     lows, highs = [reg_lo], [reg_hi]
@@ -209,7 +200,17 @@
     send = jnp.concatenate(
         [both[:, :, rows_each * d + lo: rows_each * d + hi, :deep] for d in range(count_y)], 2
     )
+    send, fine_mat, fine_in = lax.optimization_barrier((send, fine_material, fine_state))
     band = lax.all_to_all(send, "gy", 2, 1, tiled=True).astype(jnp.float32)
+    (fine_pay,) = lookup(
+        jnp.transpose(fine_mat, (1, 0, 2)),
+        material_table,
+        jnp.transpose(fine_in, (0, 2, 1, 3)),
+        0.2,
+        True,
+    )
+    fine_lo = from_cycle(fine_pay[:, -reach_y:], "gy", count_y, 1, me_y)
+    fine_hi = from_cycle(fine_pay[:, :reach_y], "gy", count_y, -1, me_y)
     columns = band.shape[1]
     high = lax.Precision.HIGH
     along_y_w = interp_matrix(fine_y, rows_each)

time: 85.2 us -> 97.9 us (1.15)
  waiting for transfers between devices: 29.5 us -> 39.5 us
  local copies, waits for them, and re-layouts: 6.7 us -> 9.87 us
    ppermute x6, waiting for transfers between devices: 0.02 us -> 22.1 us  [from_cycle(): got = lax.ppermute(field, axis, [(i, (i + d) % n) for i in range(n)])]
    all_to_all x1, waiting for transfers between devices: 13.8 us -> 0.01 us  [local(): band = lax.all_to_all(send, 'gy', 2, 1, tiled=True).astype(jnp.float32)]
    slice x0 -> x9, local copies, waits for them, and re-layouts: none -> 2.18 us  [local(): both[:, :, rows_each * d + lo:rows_each * d + hi, :deep]]
    select_n x6, other arithmetic: 2.34 us -> 0.17 us  [from_cycle(): return jnp.where((me - d >= 0) & (me - d < n), got, 0.0)]
    slice x27 -> x28, local copies, waits for them, and re-layouts: 2.43 us -> 2.52 us  [along(): lax.slice_in_dim(f, 1, n, axis=axis)]
    unnamed x31 -> x24, local copies, waits for them, and re-layouts: 2 us -> 1.91 us
  transfers between devices with their start and end apart: 13 -> 13, of which waited for: 7 -> 10; matrix products, arithmetic and copies ran while one was open for 13% -> 10% of each run, Pallas kernels for 3% -> 3%
where the time goes in v19:
time: 97.9 us; the launch traced here: 97.4 us
  waiting for transfers between devices  39.5 us (40%)
  starting transfers between devices  25.8 us (26%)
  other arithmetic  11.4 us (12%)
  local copies, waits for them, and re-layouts  9.87 us (10%)
  matrix products  5.16 us (5%)
  Pallas kernels  4.21 us (4%)
  between operations  1.42 us (1%)
    ppermute x6, waiting for transfers between devices, from_cycle(): got = lax.ppermute(field, axis, [(i, (i + d) % n) for i in range(n)])  22.1 us
    ppermute x3, waiting for transfers between devices, x_halo(): from_left = lax.ppermute(field[:, :, -width:], 'gx', cycle)  11.4 us
    ppermute x3, starting transfers between devices, x_halo(): from_right = lax.ppermute(field[:, :, :width], 'gx', back)  11.2 us
    ppermute x6, starting transfers between devices, from_cycle(): got = lax.ppermute(field, axis, [(i, (i + d) % n) for i in range(n)])  10.6 us
    ppermute x3, waiting for transfers between devices, x_halo(): from_right = lax.ppermute(field[:, :, :width], 'gx', back)  6.09 us
    pallas_call x2, Pallas kernels, lookup(): pl.pallas_call(lambda *refs: lookup_kernel(step, extra, *refs), out_shape...  4.21 us
    all_to_all x1, starting transfers between devices, local(): band = lax.all_to_all(send, 'gy', 2, 1, tiled=True).astype(jnp.float32)  3.36 us
    unnamed x18, other arithmetic  2.56 us
  transfers between devices with their start and end apart: 13, of which 10 were waited for; matrix products, arithmetic and copies ran while one was open for 10% of the time, Pallas kernels for 3%

profile of v19, /device:TPU:0, one launch (start us, length us, event | category | flops | bytes accessed | tf_op | source)
XLA Modules:
  0.0 97.4 jit_solution(5915221728470392391)
XLA Ops:
  0.6 1.6 %shard_map.68 = (f32[10,1,24,64]{3,2,1,0:T(8,128)}, f32[1,24,64]{2,1,0:T(8,128)}, f32[1,24,64]{2,1,0:T(8,128)}) custom-call(s32[1,24,64]{2,1,0:T(8,128)} %refs_0_.1, f32[3,8]{1,0:T(4,128)} %refs_1_.3, f32[9,1,24,64]{3,2,1,0:T(8,128)} %refs_2_.1), custom_call_target="tpu_custom_call" | custom-call | tf_op jit(solution)/shard_map/pallas_call | solution.py:58
  2.2 2.9 %collective-permute-start.3 = (f32[10,1,24,64]{3,2,1,0:T(8,128)}, f32[10,1,24,64]{3,2,1,0:T(8,128)S(1)}, u32[]{:S(2)}, u32[]{:S(2)}) collective-permute-start(f32[10,1,24,64]{3,2,1,0:T(8,128)} %get-tuple-element.8), channel_id=1, source_target_pairs={{0,2},{1,3},{2,4},{3,5},{4,6},{5,7},{6,8},{7,9},{8,10},{9,11},{10,... | collective-permute-start | bytes 184328 | tf_op jit(solution)/shard_map/ppermute | solution.py:15
  5.2 4.1 %collective-permute-start.2 = (f32[10,1,24,64]{3,2,1,0:T(8,128)}, f32[10,1,24,64]{3,2,1,0:T(8,128)S(1)}, u32[]{:S(2)}, u32[]{:S(2)}) collective-permute-start(f32[10,1,24,64]{3,2,1,0:T(8,128)} %get-tuple-element.8), channel_id=1, source_target_pairs={{0,30},{1,31},{2,0},{3,1},{4,2},{5,3},{6,4},{7,5},{8,6},{9,7},{10,... | collective-permute-start | bytes 184328 | tf_op jit(solution)/shard_map/ppermute | solution.py:15
  9.2 0.8 collective-permute-start.1
  10.3 0.9 constant_dynamic-update-slice_fusion.14
  11.3 2.2 %collective-permute-done.1 = f32[10,1,24,64]{3,2,1,0:T(8,128)S(1)} collective-permute-done((f32[10,1,24,64]{3,2,1,0:T(8,128)}, f32[10,1,24,64]{3,2,1,0:T(8,128)S(1)}, u32[]{:S(2)}, u32[]{:S(2)}) %collective-permute-start.1) | collective-permute-done | bytes 61472 | tf_op jit(solution)/shard_map/ppermute | solution.py:15
  13.4 4.7 %collective-permute-done = f32[10,1,24,64]{3,2,1,0:T(8,128)S(1)} collective-permute-done((f32[10,1,24,64]{3,2,1,0:T(8,128)}, f32[10,1,24,64]{3,2,1,0:T(8,128)S(1)}, u32[]{:S(2)}, u32[]{:S(2)}) %collective-permute-start) | collective-permute-done | bytes 61472 | tf_op jit(solution)/shard_map/ppermute | solution.py:15
  18.2 0.8 maximum_bitcast_fusion.20
  19.9 0.3 copy-done.2
  20.7 0.3 copy.26
  20.9 0.3 copy.25
  21.2 0.3 copy.24
  21.5 0.3 copy.23
  21.7 0.3 copy.22
  22.0 0.3 copy.21
  22.3 0.3 copy.20
  22.5 0.3 copy.19
  22.8 0.8 concatenate.308
  23.6 0.3 copy.27
  23.9 1.0 %reshape.473 = bf16[8,2,2709]{2,1,0:T(2,128)(2,1)} reshape(bf16[56,1,18,43]{3,2,1,0:T(8,128)(2,1)S(1)} %bitcast.659) | data formatting | bytes 173376
  24.9 3.4 %all-to-all-start = ((bf16[8,2,2709]{2,1,0:T(2,128)(2,1)}), bf16[8,2,2709]{2,1,0:T(2,128)(2,1)S(1)}, u32[]{:S(2)}, u32[]{:S(2)}) async-start(bf16[8,2,2709]{2,1,0:T(2,128)(2,1)} %reshape.473), calls=%async_computation | async-start | bytes 180224 | tf_op jit(solution)/shard_map/all_to_all | solution.py:204
  28.2 2.6 %shard_map.69 = f32[12,9,24,128]{3,2,1,0:T(8,128)} custom-call(s32[9,24,128]{2,1,0:T(8,128)} %bitcast.662, f32[3,8]{1,0:T(4,128)} %refs_1_.3, f32[9,9,24,128]{3,2,1,0:T(8,128)} %bitcast.661), custom_call_target="tpu_custom_call" | custom-call | tf_op jit(solution)/shard_map/pallas_call | solution.py:58
  30.8 1.6 %fusion.275 = (f32[12,6,24,128]{3,2,1,0:T(8,128)S(1)}, f32[12,6,24,128]{3,2,1,0:T(8,128)S(1)}) fusion(f32[12,9,24,128]{3,2,1,0:T(8,128)} %shard_map.69), kind=kLoop, calls=%fused_computation.498 | loop fusion | bytes 3538944 | tf_op jit(solution)/shard_map/slice | solution.py:212
  32.4 0.5 collective-permute-start.4
  32.9 2.3 %collective-permute-start.5 = (f32[12,6,24,128]{3,2,1,0:T(8,128)S(1)}, f32[12,6,24,128]{3,2,1,0:T(8,128)S(1)}, u32[]{:S(2)}, u32[]{:S(2)}) collective-permute-start(f32[12,6,24,128]{3,2,1,0:T(8,128)S(1)} %get-tuple-element.51), channel_id=1, source_target_pairs={{0,7},{1,0},{2,1},{3,2},{4,3},{5,4},{6,5},{7,6},{8,15},{9,8},{10,9... | collective-permute-start | bytes 2654216 | tf_op jit(solution)/shard_map/ppermute | solution.py:15
  35.1 0.4 reshape.474
  35.6 0.6 convolution_bitcast_fusion.1
  36.2 2.4 %convolution_bitcast_fusion = f32[18,17,24,43]{3,1,2,0:T(8,128)S(1)} fusion(f32[18,24,7,43]{3,1,2,0:T(8,128)S(1)} %convolution_bitcast_fusion.1, f32[9,3]{0,1:T(4,128)S(1)} %select_add_fusion, f32[9,3]{0,1:T(4,128)S(1)} %broadcast.1055), kind=kOutput, calls=%fused_computation.5 | convolution fusion | flops 13264335 | bytes 1783512 | tf_op jit(solution)/shard_map/gb,cfbz->cgfz/dot_general | solution.py:227
  38.6 14.5 %collective-permute-done.4 = f32[12,6,24,128]{3,2,1,0:T(8,128)} collective-permute-done((f32[12,6,24,128]{3,2,1,0:T(8,128)S(1)}, f32[12,6,24,128]{3,2,1,0:T(8,128)}, u32[]{:S(2)}, u32[]{:S(2)}) %collective-permute-start.4) | collective-permute-done | bytes 884768 | tf_op jit(solution)/shard_map/ppermute | solution.py:15
  53.2 0.7 collective-permute-done.5
  53.9 0.2 pad_maximum_fusion.10
  54.1 2.2 %fusion = f32[18,17,24,128]{3,2,1,0:T(8,128)S(1)} fusion(f32[18,17,24,43]{3,1,2,0:T(8,128)S(1)} %convolution_bitcast_fusion, f32[128]{0:T(128)S(1)} %get-tuple-element.152, f32[128]{0:T(128)S(1)} %get-tuple-element.153, s32[128]{0:T(128)S(1)} %get-tuple-element.155, s32[128]{0:T(128)S(1)} %get-tuple-element.154), kind=kOutput, calls=%fused_computation | convolution fusion | flops 242561280 | bytes 5025344 | tf_op jit(solution)/shard_map/kz,cgfz->cgfk/dot_general | solution.py:228
  56.3 4.0 %collective-permute-start.7 = (f32[10,21,2,128]{3,2,1,0:T(2,128)S(1)}, f32[10,21,2,128]{3,2,1,0:T(2,128)S(1)}, u32[]{:S(2)}, u32[]{:S(2)}) collective-permute-start(f32[10,21,2,128]{3,2,1,0:T(2,128)S(1)} %get-tuple-element.39), channel_id=1, source_target_pairs={{8,0},{16,8},{24,16},{0,24},{9,1},{17,9},{25,17},{1,25},{10,2},{18... | collective-permute-start | bytes 645128 | tf_op jit(solution)/shard_map/ppermute | solution.py:25
  60.3 0.2 pad_maximum_fusion.1
  60.5 0.2 slice.1189
  60.7 2.8 %collective-permute-done.6 = f32[10,21,2,128]{3,2,1,0:T(2,128)S(1)} collective-permute-done((f32[10,21,2,128]{3,2,1,0:T(2,128)S(1)}, f32[10,21,2,128]{3,2,1,0:T(2,128)S(1)}, u32[]{:S(2)}, u32[]{:S(2)}) %collective-permute-start.6) | collective-permute-done | bytes 215072 | tf_op jit(solution)/shard_map/ppermute | solution.py:24
  63.6 5.1 %collective-permute-done.7 = f32[10,21,2,128]{3,2,1,0:T(2,128)S(1)} collective-permute-done((f32[10,21,2,128]{3,2,1,0:T(2,128)S(1)}, f32[10,21,2,128]{3,2,1,0:T(2,128)S(1)}, u32[]{:S(2)}, u32[]{:S(2)}) %collective-permute-start.7) | collective-permute-done | bytes 215072 | tf_op jit(solution)/shard_map/ppermute | solution.py:25
  68.8 0.6 pad_maximum_fusion
  69.4 0.2 slice_bitcast_fusion.3
  69.6 0.2 fusion.277
  69.8 0.2 fusion.276
  69.9 0.2 fusion.278
  70.1 0.2 fusion.21
  70.3 0.4 fusion.32
  70.7 0.2 slice_add_fusion
  71.1 0.2 fusion.82
  71.3 0.2 slice_bitcast_fusion.4
  71.8 0.2 fusion.71
  72.3 0.5 fusion.6
  73.0 3.8 %collective-permute-start.9 = (f32[9,17,2,128]{3,2,1,0:T(2,128)S(1)}, f32[9,17,2,128]{3,2,1,0:T(2,128)S(1)}, u32[]{:S(2)}, u32[]{:S(2)}) collective-permute-start(f32[9,17,2,128]{3,2,1,0:T(2,128)S(1)} %get-tuple-element.44), channel_id=1, source_target_pairs={{8,0},{16,8},{24,16},{0,24},{9,1},{17,9},{25,17},{1,25},{10,2},{18... | collective-permute-start | bytes 470024 | tf_op jit(solution)/shard_map/ppermute | solution.py:25
  76.9 4.9 %collective-permute-done.8 = f32[9,17,2,128]{3,2,1,0:T(2,128)S(1)} collective-permute-done((f32[9,17,2,128]{3,2,1,0:T(2,128)S(1)}, f32[9,17,2,128]{3,2,1,0:T(2,128)S(1)}, u32[]{:S(2)}, u32[]{:S(2)}) %collective-permute-start.8) | collective-permute-done | bytes 156704 | tf_op jit(solution)/shard_map/ppermute | solution.py:24
  81.8 0.7 collective-permute-done.9
  82.7 0.4 pad_maximum_fusion.2
  83.6 0.2 fusion.49
  83.7 0.2 fusion.44
  83.9 0.2 fusion.38
  84.0 0.1 slice_add_fusion.1
  85.3 0.4 fusion.12
  85.8 0.6 collective-permute-start.10
  86.5 3.3 %collective-permute-start.11 = (f32[9,13,2,128]{3,2,1,0:T(2,128)S(1)}, f32[9,13,2,128]{3,2,1,0:T(2,128)S(1)}, u32[]{:S(2)}, u32[]{:S(2)}) collective-permute-start(f32[9,13,2,128]{3,2,1,0:T(2,128)S(1)} %get-tuple-element.49), channel_id=1, source_target_pairs={{8,0},{16,8},{24,16},{0,24},{9,1},{17,9},{25,17},{1,25},{10,2},{18... | collective-permute-start | bytes 359432 | tf_op jit(solution)/shard_map/ppermute | solution.py:25
  89.8 3.7 %collective-permute-done.10 = f32[9,13,2,128]{3,2,1,0:T(2,128)S(1)} collective-permute-done((f32[9,13,2,128]{3,2,1,0:T(2,128)S(1)}, f32[9,13,2,128]{3,2,1,0:T(2,128)S(1)}, u32[]{:S(2)}, u32[]{:S(2)}) %collective-permute-start.10) | collective-permute-done | bytes 119840 | tf_op jit(solution)/shard_map/ppermute | solution.py:24
  93.5 0.3 collective-permute-done.11
  94.0 0.4 pad_maximum_fusion.3
  96.2 1.2 %fusion.16 = f32[9,24,9,128]{3,1,2,0:T(8,128)} fusion(f32[9,9,24,128]{3,2,1,0:T(8,128)S(1)} %fusion.151, f32[18,17,24,128]{3,2,1,0:T(8,128)S(1)} %fusion, f32[9,24]{1,0:T(8,128)S(1)} %slice.1310), kind=kLoop, calls=%fused_computation.25 | loop fusion | flops 1244160 | bytes 3982176 | tf_op jit(solution)/shard_map/transpose | solution.py:264
  (119 shorter events, 6.6 us)
Async XLA Ops:
  2.2 17.0 %copy-start.1 = (f32[10,1,24,64]{3,2,1,0:T(8,128)S(1)}, f32[10,1,24,64]{3,2,1,0:T(8,128)}, u32[]{:S(2)}) copy-start(f32[10,1,24,64]{3,2,1,0:T(8,128)} %get-tuple-element.8) | copy-start | bytes 184324
  2.2 17.0 %collective-permute-start.3 = (f32[10,1,24,64]{3,2,1,0:T(8,128)}, f32[10,1,24,64]{3,2,1,0:T(8,128)S(1)}, u32[]{:S(2)}, u32[]{:S(2)}) collective-permute-start(f32[10,1,24,64]{3,2,1,0:T(8,128)} %get-tuple-element.8), channel_id=1, source_target_pairs={{0,2},{1,3},{2,4},{3,5},{4,6},{5,7},{6,8},{7,9},{8,10},{9,11},{10,... | collective-permute-start | bytes 184328 | tf_op jit(solution)/shard_map/ppermute | solution.py:15
  5.2 14.2 %collective-permute-start.2 = (f32[10,1,24,64]{3,2,1,0:T(8,128)}, f32[10,1,24,64]{3,2,1,0:T(8,128)S(1)}, u32[]{:S(2)}, u32[]{:S(2)}) collective-permute-start(f32[10,1,24,64]{3,2,1,0:T(8,128)} %get-tuple-element.8), channel_id=1, source_target_pairs={{0,30},{1,31},{2,0},{3,1},{4,2},{5,3},{6,4},{7,5},{8,6},{9,7},{10,... | collective-permute-start | bytes 184328 | tf_op jit(solution)/shard_map/ppermute | solution.py:15
  9.2 4.2 %collective-permute-start.1 = (f32[10,1,24,64]{3,2,1,0:T(8,128)}, f32[10,1,24,64]{3,2,1,0:T(8,128)S(1)}, u32[]{:S(2)}, u32[]{:S(2)}) collective-permute-start(f32[10,1,24,64]{3,2,1,0:T(8,128)} %get-tuple-element.8), channel_id=1, source_target_pairs={{0,31},{1,0},{2,1},{3,2},{4,3},{5,4},{6,5},{7,6},{8,7},{9,8},{10,9... | collective-permute-start | bytes 184328 | tf_op jit(solution)/shard_map/ppermute | solution.py:15
  10.1 8.1 %collective-permute-start = (f32[10,1,24,64]{3,2,1,0:T(8,128)}, f32[10,1,24,64]{3,2,1,0:T(8,128)S(1)}, u32[]{:S(2)}, u32[]{:S(2)}) collective-permute-start(f32[10,1,24,64]{3,2,1,0:T(8,128)} %get-tuple-element.8), channel_id=1, source_target_pairs={{0,1},{1,2},{2,3},{3,4},{4,5},{5,6},{6,7},{7,8},{8,9},{9,10},{10,1... | collective-permute-start | bytes 184328 | tf_op jit(solution)/shard_map/ppermute | solution.py:15
  19.3 0.9 copy-start.2
  19.3 0.9 copy-start.3
  19.3 0.9 copy-start.4
  24.9 10.3 %all-to-all-start = ((bf16[8,2,2709]{2,1,0:T(2,128)(2,1)}), bf16[8,2,2709]{2,1,0:T(2,128)(2,1)S(1)}, u32[]{:S(2)}, u32[]{:S(2)}) async-start(bf16[8,2,2709]{2,1,0:T(2,128)(2,1)} %reshape.473), calls=%async_computation | async-start | bytes 180224 | tf_op jit(solution)/shard_map/all_to_all | solution.py:204
  32.4 20.7 %collective-permute-start.4 = (f32[12,6,24,128]{3,2,1,0:T(8,128)S(1)}, f32[12,6,24,128]{3,2,1,0:T(8,128)}, u32[]{:S(2)}, u32[]{:S(2)}) collective-permute-start(f32[12,6,24,128]{3,2,1,0:T(8,128)S(1)} %get-tuple-element.50), channel_id=1, source_target_pairs={{0,1},{1,2},{2,3},{3,4},{4,5},{5,6},{6,7},{7,0},{8,9},{9,10},{10,1... | collective-permute-start | bytes 2654216 | tf_op jit(solution)/shard_map/ppermute | solution.py:15
  32.9 21.0 %collective-permute-start.5 = (f32[12,6,24,128]{3,2,1,0:T(8,128)S(1)}, f32[12,6,24,128]{3,2,1,0:T(8,128)S(1)}, u32[]{:S(2)}, u32[]{:S(2)}) collective-permute-start(f32[12,6,24,128]{3,2,1,0:T(8,128)S(1)} %get-tuple-element.51), channel_id=1, source_target_pairs={{0,7},{1,0},{2,1},{3,2},{4,3},{5,4},{6,5},{7,6},{8,15},{9,8},{10,9... | collective-permute-start | bytes 2654216 | tf_op jit(solution)/shard_map/ppermute | solution.py:15
  38.6 15.3 %copy-start = (f32[12,9,24,128]{3,2,1,0:T(8,128)S(1)}, f32[12,9,24,128]{3,2,1,0:T(8,128)}, u32[]{:S(2)}) copy-start(f32[12,9,24,128]{3,2,1,0:T(8,128)} %shard_map.69) | copy-start | bytes 3981316
  54.1 9.5 %collective-permute-start.6 = (f32[10,21,2,128]{3,2,1,0:T(2,128)S(1)}, f32[10,21,2,128]{3,2,1,0:T(2,128)S(1)}, u32[]{:S(2)}, u32[]{:S(2)}) collective-permute-start(f32[10,21,2,128]{3,2,1,0:T(2,128)S(1)} %get-tuple-element.38), channel_id=1, source_target_pairs={{0,8},{8,16},{16,24},{24,0},{1,9},{9,17},{17,25},{25,1},{2,10},{10... | collective-permute-start | bytes 645128 | tf_op jit(solution)/shard_map/ppermute | solution.py:24
  56.3 12.4 %collective-permute-start.7 = (f32[10,21,2,128]{3,2,1,0:T(2,128)S(1)}, f32[10,21,2,128]{3,2,1,0:T(2,128)S(1)}, u32[]{:S(2)}, u32[]{:S(2)}) collective-permute-start(f32[10,21,2,128]{3,2,1,0:T(2,128)S(1)} %get-tuple-element.39), channel_id=1, source_target_pairs={{8,0},{16,8},{24,16},{0,24},{9,1},{17,9},{25,17},{1,25},{10,2},{18... | collective-permute-start | bytes 645128 | tf_op jit(solution)/shard_map/ppermute | solution.py:25
  72.9 8.8 %collective-permute-start.8 = (f32[9,17,2,128]{3,2,1,0:T(2,128)S(1)}, f32[9,17,2,128]{3,2,1,0:T(2,128)S(1)}, u32[]{:S(2)}, u32[]{:S(2)}) collective-permute-start(f32[9,17,2,128]{3,2,1,0:T(2,128)S(1)} %get-tuple-element.43), channel_id=1, source_target_pairs={{0,8},{8,16},{16,24},{24,0},{1,9},{9,17},{17,25},{25,1},{2,10},{10... | collective-permute-start | bytes 470024 | tf_op jit(solution)/shard_map/ppermute | solution.py:24
  73.0 9.5 %collective-permute-start.9 = (f32[9,17,2,128]{3,2,1,0:T(2,128)S(1)}, f32[9,17,2,128]{3,2,1,0:T(2,128)S(1)}, u32[]{:S(2)}, u32[]{:S(2)}) collective-permute-start(f32[9,17,2,128]{3,2,1,0:T(2,128)S(1)} %get-tuple-element.44), channel_id=1, source_target_pairs={{8,0},{16,8},{24,16},{0,24},{9,1},{17,9},{25,17},{1,25},{10,2},{18... | collective-permute-start | bytes 470024 | tf_op jit(solution)/shard_map/ppermute | solution.py:25
  85.8 7.7 %collective-permute-start.10 = (f32[9,13,2,128]{3,2,1,0:T(2,128)S(1)}, f32[9,13,2,128]{3,2,1,0:T(2,128)S(1)}, u32[]{:S(2)}, u32[]{:S(2)}) collective-permute-start(f32[9,13,2,128]{3,2,1,0:T(2,128)S(1)} %get-tuple-element.48), channel_id=1, source_target_pairs={{0,8},{8,16},{16,24},{24,0},{1,9},{9,17},{17,25},{25,1},{2,10},{10... | collective-permute-start | bytes 359432 | tf_op jit(solution)/shard_map/ppermute | solution.py:24
  86.4 7.6 %copy-start.5 = (f32[9,1,24,64]{3,2,1,0:T(8,128)}, f32[9,1,24,64]{3,2,1,0:T(8,128)S(1)}, u32[]{:S(2)}) copy-start(f32[9,1,24,64]{3,2,1,0:T(8,128)S(1)} %constant_dynamic-update-slice_fusion) | copy-start | bytes 165892
  86.5 7.4 %collective-permute-start.11 = (f32[9,13,2,128]{3,2,1,0:T(2,128)S(1)}, f32[9,13,2,128]{3,2,1,0:T(2,128)S(1)}, u32[]{:S(2)}, u32[]{:S(2)}) collective-permute-start(f32[9,13,2,128]{3,2,1,0:T(2,128)S(1)} %get-tuple-element.49), channel_id=1, source_target_pairs={{8,0},{16,8},{24,16},{0,24},{9,1},{17,9},{25,17},{1,25},{10,2},{18... | collective-permute-start | bytes 359432 | tf_op jit(solution)/shard_map/ppermute | solution.py:25
